TPU v7x, 32 devices: a whole 2x2x4 slice. The times are simulated.
32 devices in a mesh: grp: 2 (over y), blk: 8 (over z, x), bin: 2 (over core).
Axes of the slice: x: 2, y: 2, z: 4, core: 2. Of those that a mesh axis runs over, the one named last changes fastest.
Arguments:
- units: bfloat16 [1024, 32768], P(('grp', 'bin'), 'blk'), parts along dimension 0, may hold values from -6 to 6
- cotangent: bfloat16 [1024, 32768], P(('grp', 'bin'), 'blk'), parts along dimension 0, may hold values from -6 to 6
- left_factor: bfloat16 [64, 512, 512], P('blk', 'bin'), may hold values from -0.25 to 0.25
- right_factor: bfloat16 [512, 64, 64], P('blk', 'bin'), may hold values from -0.75 to 0.75
- session_units: int32 [128], P(('grp', 'blk')), parts along dimension 0, may hold values from 128 to 512, as said below
Outputs:
- grad_left: bfloat16 [128, 512, 512], P(('grp', 'blk'), 'bin'), parts along dimension 0
- grad_right: bfloat16 [1024, 64, 64], P(('grp', 'blk'), 'bin'), parts along dimension 0
There are 2 independent parts, one for each index of `grp`. A program takes and returns all parts, laid end to end along the dimension named above; an argument that names none is the same for every part. Nothing has to cross between parts.
Inputs may be any that keep to these rules, and one draw needn't show every extreme that they name: `session_units`: each count is a multiple of a quarter of 512; some session of every group has all 512 units live.
All inputs are finite; a program needn't handle non-finite values.
Results may differ from a plain program's by a relative error of at most 0.0049.
Values may be sent and summed in bfloat16 or wider, within the bound.
No kernel may reach another device: no remote copies, remote signals or barrier semaphores. Data moves between devices by JAX's collectives and lax.ppermute only.
A program may use at most 128 MiB of HBM per device.

v0:
```python
import jax
import jax.numpy as jnp
from jax import lax
from jax.sharding import PartitionSpec as P


def on_device(units, cotangent, left_factor, right_factor, session_units):
    row_count = units.shape[0]
    local_blocks = left_factor.shape[0]
    block_size = left_factor.shape[2]
    right_local = right_factor.shape[0]
    order_right = right_factor.shape[2]
    peer_count = lax.axis_size("blk")
    unit_mask = (jnp.arange(block_size)[None, :] < session_units[:, None]).astype(jnp.bfloat16)
    inputs = units.reshape(row_count, local_blocks, block_size) * unit_mask[None]
    left_full = lax.all_gather(left_factor, "bin", axis=1, tiled=True)
    mixed = jnp.einsum(
        "rki,kij->kjr", inputs, left_full, preferred_element_type=jnp.float32
    ).astype(jnp.bfloat16)
    mixed_sent = mixed.reshape(local_blocks, peer_count, right_local, row_count)
    mixed_got = lax.all_to_all(mixed_sent, "blk", split_axis=1, concat_axis=0, tiled=True)
    permuted = mixed_got.reshape(order_right, right_local, row_count)
    upstream = cotangent.reshape(row_count, right_local, order_right)
    right_full = lax.all_gather(right_factor, "bin", axis=1, tiled=True)
    back_grad = jnp.einsum(
        "rjm,jkm->jkr", upstream, right_full, preferred_element_type=jnp.float32
    ).astype(jnp.bfloat16)
    back_sent = back_grad.reshape(right_local, peer_count, local_blocks, row_count)
    back_got = lax.all_to_all(back_sent, "blk", split_axis=1, concat_axis=0, tiled=True)
    returned = back_got.reshape(block_size, local_blocks, row_count)
    right_term = jnp.einsum("kjr,rjm->jkm", permuted, upstream, preferred_element_type=jnp.float32)
    grad_right = lax.psum_scatter(right_term, "bin", scatter_dimension=1, tiled=True).astype(
        jnp.bfloat16
    )
    left_term = jnp.einsum("rki,jkr->kij", inputs, returned, preferred_element_type=jnp.float32)
    grad_left = lax.psum_scatter(left_term, "bin", scatter_dimension=1, tiled=True).astype(
        jnp.bfloat16
    )
    return (grad_left, grad_right)


def solution(mesh):
    placed = (
        P(("grp", "bin"), "blk"),
        P(("grp", "bin"), "blk"),
        P("blk", "bin", None),
        P("blk", "bin", None),
        P(("grp", "blk")),
    )
    return jax.shard_map(
        on_device,
        mesh=mesh,
        in_specs=placed,
        out_specs=(P(("grp", "blk"), "bin", None), P(("grp", "blk"), "bin", None)),
        check_vma=False,
    )
```

profile of v0, /device:TPU:0, one launch (start us, length us, event | category | flops | bytes accessed | tf_op | source)
XLA Modules:
  0.0 175.1 jit_solution(1585854343197089779)
XLA Ops:
  7.2 0.0 copy-start.3
  7.2 0.0 copy-start
  7.2 0.0 all-gather.2.cloned.1.call-start
  7.2 0.7 all-gather.2.cloned.1.call-update
  7.9 0.0 copy-done.3
  7.9 0.1 fusion.6
  8.0 18.0 %all-gather.2.cloned.1.call-done = bf16[8,512,512]{2,1,0:T(8,128)(2,1)} async-done(((bf16[8,256,512]{2,1,0:T(8,128)(2,1)}), bf16[8,512,512]{2,1,0:T(8,128)(2,1)}) %all-gather.2.cloned.1.call-update) | async-done | bytes 4194320 | tf_op jit(solution)/shard_map/all_gather | solution.py:16
  26.0 0.0 copy-done
  26.0 4.8 %convert_bitcast_fusion = bf16[8,512,256]{1,2,0:T(8,128)(2,1)} fusion(bf16[8,512,512]{2,1,0:T(8,128)(2,1)} %all-gather.2.cloned.1.call-done, bf16[32,8,8,512]{3,2,1,0:T(8,128)(2,1)S(1)} %bitcast.30, bf16[8,512]{1,0:T(8,128)(2,1)S(1)} %fusion.6), kind=kOutput, calls=%fused_computation.4 | convolution fusion | flops 1075838976 | bytes 8396800 | tf_op jit(solution)/shard_map/rki,kij->kjr/dot_general | solution.py:17
  30.7 2.8 %copy.24 = bf16[8,512,256]{2,1,0:T(8,128)(2,1)S(1)} copy(bf16[8,512,256]{1,2,0:T(8,128)(2,1)} %convert_bitcast_fusion) | data formatting | bytes 4194304 | tf_op jit(solution)/shard_map/convert_element_type | solution.py:19
  33.6 1.5 copy.25
  35.1 5.8 %all-to-all-start.1 = ((bf16[8,8,64,256]{3,2,0,1:T(8,128)(2,1)}), bf16[8,8,64,256]{3,2,0,1:T(8,128)(2,1)}, u32[]{:S(2)}, u32[]{:S(2)}) async-start(bf16[8,8,64,256]{3,2,0,1:T(8,128)(2,1)} %copy.25), calls=%async_computation.2 | async-start | bytes 4194304 | tf_op jit(solution)/shard_map/all_to_all | solution.py:21
  40.8 3.3 %copy.20 = bf16[256,4096]{0,1:T(8,128)(2,1)S(1)} copy(bf16[256,4096]{1,0:T(8,128)(2,1)} %param.6) | data formatting | bytes 4194304 | tf_op args[1]
  44.2 0.0 copy-done.2
  44.2 2.6 %all_gather.6 = bf16[64,64,64]{2,1,0:T(8,128)(2,1)S(1)} all-gather(bf16[64,32,64]{2,1,0:T(8,128)(2,1)S(1)} %copy-done.2), channel_id=1, replica_groups=mesh['grp'=2,'blk'=8,'bin'=2] {'bin'}, dimensions={1}, use_global_device_ids=true | all-gather | bytes 786432 | tf_op jit(solution)/shard_map/all_gather | solution.py:24
  46.7 0.7 convert_bitcast_fusion.1
  47.4 1.5 copy.21
  48.9 40.7 %all-to-all-done.1 = bf16[8,8,64,256]{3,2,0,1:T(8,128)(2,1)} async-done(((bf16[8,8,64,256]{3,2,0,1:T(8,128)(2,1)}), bf16[8,8,64,256]{3,2,0,1:T(8,128)(2,1)}, u32[]{:S(2)}, u32[]{:S(2)}) %all-to-all-start.1) | async-done | bytes 2097184 | tf_op jit(solution)/shard_map/all_to_all | solution.py:21
  89.6 4.4 %all-to-all-start = ((bf16[64,8,8,256]{3,2,0,1:T(8,128)(2,1)}), bf16[64,8,8,256]{3,2,0,1:T(8,128)(2,1)}, u32[]{:S(2)}, u32[]{:S(2)}) async-start(bf16[64,8,8,256]{3,2,0,1:T(8,128)(2,1)} %copy.21), calls=%async_computation | async-start | bytes 4194304 | tf_op jit(solution)/shard_map/all_to_all | solution.py:29
  94.0 0.0 reduce-scatter.5.cloned.1.call-start
  94.0 4.3 %fusion = f32[64,64,64]{2,1,0:T(8,128)} fusion(bf16[256,64,64]{0,2,1:T(8,128)(2,1)S(1)} %bitcast.27, bf16[8,8,1,64,256]{4,3,1,0,2:T(8,128)(2,1)} %bitcast.8), kind=kOutput, calls=%fused_computation.1 | convolution fusion | flops 134217728 | bytes 5242880 | tf_op jit(solution)/shard_map/kjr,rjm->jkm/dot_general | solution.py:31
  98.3 0.0 reduce-scatter.5.cloned.1.call-update
  98.4 0.0 reduce-scatter.3.cloned.1.call-start
  98.4 43.4 %all-to-all-done = bf16[64,8,8,256]{3,2,0,1:T(8,128)(2,1)} async-done(((bf16[64,8,8,256]{3,2,0,1:T(8,128)(2,1)}), bf16[64,8,8,256]{3,2,0,1:T(8,128)(2,1)}, u32[]{:S(2)}, u32[]{:S(2)}) %all-to-all-start) | async-done | bytes 2097184 | tf_op jit(solution)/shard_map/all_to_all | solution.py:29
  141.8 2.2 %copy.22 = bf16[8,64,1,8,256]{4,1,0,3,2:T(8,128)(2,1)S(1)} copy(bf16[8,64,1,8,256]{4,3,1,0,2:T(8,128)(2,1)} %bitcast.3) | data formatting | bytes 4194304 | tf_op jit(solution)/shard_map/all_to_all | solution.py:29
  144.1 0.0 copy-done.1
  144.1 4.7 %fusion.3 = f32[8,512,512]{2,1,0:T(8,128)} fusion(bf16[512,8,256]{2,0,1:T(8,128)(2,1)S(1)} %bitcast.29, bf16[32,8,8,512]{3,2,1,0:T(8,128)(2,1)S(1)} %bitcast.31, bf16[8,512]{1,0:T(8,128)(2,1)S(1)} %fusion.6), kind=kOutput, calls=%fused_computation.6 | convolution fusion | flops 1074790400 | bytes 12591104 | tf_op jit(solution)/shard_map/rki,jkr->kij/dot_general | solution.py:35
  148.8 0.0 reduce-scatter.3.cloned.1.call-update
  148.8 0.0 reduce-scatter.5.cloned.1.call-done
  148.8 2.1 %convert_element_type.27 = bf16[64,32,64]{2,1,0:T(8,128)(2,1)} convert(f32[64,32,64]{2,1,0:T(8,128)} %reduce-scatter.5.cloned.1.call-done) | non-fusion elementwise | flops 131072 | bytes 786432 | tf_op jit(solution)/shard_map/convert_element_type | solution.py:32
  150.9 13.8 %reduce-scatter.3.cloned.1.call-done = f32[8,256,512]{2,1,0:T(8,128)} async-done(((f32[8,512,512]{2,1,0:T(8,128)}), f32[8,256,512]{2,1,0:T(8,128)}) %reduce-scatter.3.cloned.1.call-update) | async-done | bytes 4194320 | tf_op jit(solution)/shard_map/reduce_scatter | solution.py:36
  164.8 3.8 %convert_element_type.24 = bf16[8,256,512]{2,1,0:T(8,128)(2,1)} convert(f32[8,256,512]{2,1,0:T(8,128)} %reduce-scatter.3.cloned.1.call-done) | non-fusion elementwise | flops 1048576 | bytes 6291456 | tf_op jit(solution)/shard_map/convert_element_type | solution.py:36
  (2 shorter events, 0.0 us)
Async XLA Ops:
  7.2 0.8 copy-start.3
  7.2 18.8 %copy-start = (bf16[256,4096]{1,0:T(8,128)(2,1)S(1)}, bf16[256,4096]{1,0:T(8,128)(2,1)}, u32[]{:S(2)}) copy-start(bf16[256,4096]{1,0:T(8,128)(2,1)} %param.5) | copy-start | bytes 6291460
  7.2 18.8 %all-gather.2.cloned.1.call-start = ((), (), s32[]{:S(2)}) async-start(), calls=%async_computation.5 | async-start | bytes 6291456 | tf_op jit(solution)/shard_map/all_gather | solution.py:16
  35.1 54.6 %all-to-all-start.1 = ((bf16[8,8,64,256]{3,2,0,1:T(8,128)(2,1)}), bf16[8,8,64,256]{3,2,0,1:T(8,128)(2,1)}, u32[]{:S(2)}, u32[]{:S(2)}) async-start(bf16[8,8,64,256]{3,2,0,1:T(8,128)(2,1)} %copy.25), calls=%async_computation.2 | async-start | bytes 4194304 | tf_op jit(solution)/shard_map/all_to_all | solution.py:21
  40.8 3.3 %copy-start.2 = (bf16[64,32,64]{2,1,0:T(8,128)(2,1)S(1)}, bf16[64,32,64]{2,1,0:T(8,128)(2,1)}, u32[]{:S(2)}) copy-start(bf16[64,32,64]{2,1,0:T(8,128)(2,1)} %param.8) | copy-start | bytes 786436
  89.6 52.2 %all-to-all-start = ((bf16[64,8,8,256]{3,2,0,1:T(8,128)(2,1)}), bf16[64,8,8,256]{3,2,0,1:T(8,128)(2,1)}, u32[]{:S(2)}, u32[]{:S(2)}) async-start(bf16[64,8,8,256]{3,2,0,1:T(8,128)(2,1)} %copy.21), calls=%async_computation | async-start | bytes 4194304 | tf_op jit(solution)/shard_map/all_to_all | solution.py:29
  94.0 54.8 %reduce-scatter.5.cloned.1.call-start = ((), (), s32[]{:S(2)}) async-start(), calls=%async_computation.6 | async-start | bytes 3145728 | tf_op jit(solution)/shard_map/reduce_scatter | solution.py:32
  98.4 66.4 %reduce-scatter.3.cloned.1.call-start = ((), (), s32[]{:S(2)}) async-start(), calls=%async_computation.4 | async-start | bytes 12582912 | tf_op jit(solution)/shard_map/reduce_scatter | solution.py:36
  141.8 2.2 %copy-start.1 = (bf16[256,4096]{1,0:T(8,128)(2,1)S(1)}, bf16[256,4096]{1,0:T(8,128)(2,1)}, u32[]{:S(2)}) copy-start(bf16[256,4096]{1,0:T(8,128)(2,1)} %param.5) | copy-start | bytes 6291460
Sparse Core Ops, SparseCore 0:
  9.6 16.3 all-gather.1
  98.5 10.8 reduce-scatter.4
  148.9 15.8 reduce-scatter.2
where the time goes:
time: 176 us; the launch traced here: 175 us
  waiting for transfers between devices  117 us (66%)
  matrix products  14.4 us (8%)
  between operations  13.8 us (8%)
  local copies, waits for them, and re-layouts  11.3 us (6%)
  starting transfers between devices  10.2 us (6%)
  other arithmetic  5.95 us (3%)
  blocking collectives  2.56 us (1%)
    all_to_all x1, waiting for transfers between devices, on_device(): lax.all_to_all(back_sent, 'blk', split_axis=1, concat_axis=0, tiled=True)  43.4 us
    all_to_all x1, waiting for transfers between devices, on_device(): lax.all_to_all(mixed_sent, 'blk', split_axis=1, concat_axis=0, tiled=True)  40.7 us
    all_gather x1, waiting for transfers between devices, on_device(): left_full = lax.all_gather(left_factor, 'bin', axis=1, tiled=True)  18 us
    reduce_scatter x1, waiting for transfers between devices, on_device(): lax.psum_scatter(left_term, 'bin', scatter_dimension=1, tiled=True)  13.8 us
    all_to_all x1, starting transfers between devices, on_device(): lax.all_to_all(mixed_sent, 'blk', split_axis=1, concat_axis=0, tiled=True)  5.77 us
    dot_general x1, matrix products, on_device(): jnp.einsum('rki,kij->kjr', inputs, left_full, preferred_element_type=jnp....  4.76 us
    dot_general x1, matrix products, on_device(): jnp.einsum('rki,jkr->kij', inputs, returned, preferred_element_type=jnp.f...  4.66 us
    all_to_all x1, starting transfers between devices, on_device(): lax.all_to_all(back_sent, 'blk', split_axis=1, concat_axis=0, tiled=True)  4.36 us
  transfers between devices with their start and end apart: 5, of which 4 were waited for; matrix products, arithmetic and copies ran while one was open for 11% of the time, Pallas kernels for 0%

commit v1 on v0

v1 whole, which is shorter than its diff:
```python
import jax
import jax.numpy as jnp
from jax import lax
from jax.sharding import PartitionSpec as P


def on_device(units, cotangent, left_factor, right_factor, session_units):
    row_count = units.shape[0]
    local_blocks = left_factor.shape[0]
    block_size = left_factor.shape[2]
    right_local = right_factor.shape[0]
    order_right = right_factor.shape[2]
    peer_count = lax.axis_size("blk")
    block_count = peer_count * local_blocks
    half = block_count // 2
    core = lax.axis_index("bin")

    upstream = cotangent.reshape(row_count, right_local, order_right)
    right_full = lax.all_gather(right_factor, "bin", axis=1, tiled=True)
    back_grad = jnp.einsum(
        "rjm,jkm->kjr", upstream, right_full, preferred_element_type=jnp.float32
    ).astype(jnp.bfloat16)
    back_sent = back_grad.reshape(peer_count, local_blocks, right_local, row_count)
    back_got = lax.all_to_all(back_sent, "blk", 0, 0, tiled=True)

    unit_mask = (jnp.arange(block_size)[None, :] < session_units[:, None]).astype(jnp.bfloat16)
    inputs = units.reshape(row_count, local_blocks, block_size) * unit_mask[None]
    left_full = lax.all_gather(left_factor, "bin", axis=1, tiled=True)
    mixed = jnp.einsum(
        "rki,kij->jkr", inputs, left_full, preferred_element_type=jnp.float32
    ).astype(jnp.bfloat16)
    mixed_sent = mixed.reshape(peer_count, right_local, local_blocks, row_count)
    mixed_sent, back_got = lax.optimization_barrier((mixed_sent, back_got))

    back_t = back_got.transpose(1, 0, 2, 3).reshape(local_blocks, block_size, row_count)
    left_term = jnp.einsum("rki,kjr->kij", inputs, back_t, preferred_element_type=jnp.float32)
    mixed_sent, left_term = lax.optimization_barrier((mixed_sent, left_term))
    grad_left = lax.psum_scatter(left_term, "bin", scatter_dimension=1, tiled=True).astype(
        jnp.bfloat16
    )
    mixed_got = lax.all_to_all(mixed_sent, "blk", 0, 0, tiled=True)

    mixed_t = mixed_got.transpose(1, 0, 2, 3).reshape(right_local, block_count, row_count)
    right_term = jnp.einsum("jkr,rjm->jkm", mixed_t, upstream, preferred_element_type=jnp.float32)
    mine = lax.dynamic_slice_in_dim(right_term, core * half, half, axis=1)
    theirs = lax.dynamic_slice_in_dim(right_term, (1 - core) * half, half, axis=1)
    got = lax.ppermute(theirs, "bin", [(0, 1), (1, 0)])
    grad_right = (mine + got).astype(jnp.bfloat16)
    return (grad_left, grad_right)


def solution(mesh):
    placed = (
        P(("grp", "bin"), "blk"),
        P(("grp", "bin"), "blk"),
        P("blk", "bin", None),
        P("blk", "bin", None),
        P(("grp", "blk")),
    )
    return jax.shard_map(
        on_device,
        mesh=mesh,
        in_specs=placed,
        out_specs=(P(("grp", "blk"), "bin", None), P(("grp", "blk"), "bin", None)),
        check_vma=False,
    )
```

time: 176 us -> 151 us (0.86)
  waiting for transfers between devices: 117 us -> 85.2 us
  local copies, waits for them, and re-layouts: 11.3 us -> 14.8 us
    all_gather x1, waiting for transfers between devices: 18 us -> 0.01 us  [on_device(): left_full = lax.all_gather(left_factor, 'bin', axis=1, tiled=True)]
    reduce_scatter x1, waiting for transfers between devices: 13.8 us -> 0.01 us  [on_device(): lax.psum_scatter(left_term, 'bin', scatter_dimension=1, tiled=True)]
    ppermute x0 -> x1, waiting for transfers between devices: none -> 2.64 us  [on_device(): got = lax.ppermute(theirs, 'bin', [(0, 1), (1, 0)])]
    reshape x2, local copies, waits for them, and re-layouts: 2.92 us -> 5.54 us  [the longest x1 4.08 us: on_device(): units.reshape(row_count, local_blocks, block_size) * unit_mask[None]]
    all_to_all x2, waiting for transfers between devices: 84.2 us -> 81.9 us  [the longest x1 47.8 us: on_device(): mixed_got = lax.all_to_all(mixed_sent, 'blk', 0, 0, tiled=True)]
    all_to_all x1 -> x0, local copies, waits for them, and re-layouts: 2.23 us -> none  [on_device(): lax.all_to_all(back_sent, 'blk', split_axis=1, concat_axis=0, tiled=True)]
    unnamed x9 -> x7, local copies, waits for them, and re-layouts: 3.35 us -> 4.65 us
  transfers between devices with their start and end apart: 5 -> 5, of which waited for: 4 -> 3; matrix products, arithmetic and copies ran while one was open for 11% -> 16% of each run, Pallas kernels for 0% -> 0%
where the time goes in v1:
time: 151 us; the launch traced here: 150 us
  waiting for transfers between devices  85.2 us (56%)
  matrix products  15.6 us (10%)
  local copies, waits for them, and re-layouts  14.8 us (10%)
  between operations  14.1 us (9%)
  starting transfers between devices  11.7 us (8%)
  other arithmetic  6.1 us (4%)
  blocking collectives  2.64 us (2%)
    all_to_all x1, waiting for transfers between devices, on_device(): mixed_got = lax.all_to_all(mixed_sent, 'blk', 0, 0, tiled=True)  47.8 us
    all_to_all x1, waiting for transfers between devices, on_device(): back_got = lax.all_to_all(back_sent, 'blk', 0, 0, tiled=True)  34.1 us
    all_to_all x1, starting transfers between devices, on_device(): back_got = lax.all_to_all(back_sent, 'blk', 0, 0, tiled=True)  7.17 us
    dot_general x1, matrix products, on_device(): jnp.einsum('rki,kjr->kij', inputs, back_t, preferred_element_type=jnp.flo...  6.78 us
    dot_general x1, matrix products, on_device(): jnp.einsum('rki,kij->jkr', inputs, left_full, preferred_element_type=jnp....  5.84 us
    unnamed x7, local copies, waits for them, and re-layouts  4.65 us
    convert_element_type x1, local copies, waits for them, and re-layouts, on_device(): mixed = jnp.einsum('rki,kij->jkr', inputs, left_full, preferred_element_t...  4.51 us
    all_to_all x1, starting transfers between devices, on_device(): mixed_got = lax.all_to_all(mixed_sent, 'blk', 0, 0, tiled=True)  4.37 us
  transfers between devices with their start and end apart: 5, of which 3 were waited for; matrix products, arithmetic and copies ran while one was open for 16% of the time, Pallas kernels for 0%

profile of v1, /device:TPU:0, one launch (start us, length us, event | category | flops | bytes accessed | tf_op | source)
XLA Modules:
  0.0 150.2 jit_solution(10673937830390873507)
XLA Ops:
  7.2 0.0 all-gather.2.cloned.1.call-start
  7.2 0.7 all-gather.2.cloned.1.call-update
  7.9 0.0 copy-start.1
  7.9 3.3 %copy.22 = bf16[256,4096]{0,1:T(8,128)(2,1)S(1)} copy(bf16[256,4096]{1,0:T(8,128)(2,1)} %param.6) | data formatting | bytes 4194304 | tf_op args[1]
  11.2 0.0 copy-done.1
  11.3 2.6 %all_gather.7 = bf16[64,64,64]{2,1,0:T(8,128)(2,1)S(1)} all-gather(bf16[64,32,64]{2,1,0:T(8,128)(2,1)S(1)} %copy-done.1), channel_id=1, replica_groups=mesh['grp'=2,'blk'=8,'bin'=2] {'bin'}, dimensions={1}, use_global_device_ids=true | all-gather | bytes 786432 | tf_op jit(solution)/shard_map/all_gather | solution.py:19
  13.9 0.7 convert_bitcast_fusion
  14.6 1.5 copy.23
  16.1 7.2 %all-to-all-start = ((bf16[8,8,64,256]{3,1,2,0:T(8,128)(2,1)}), bf16[8,8,64,256]{3,1,2,0:T(8,128)(2,1)}, u32[]{:S(2)}, u32[]{:S(2)}) async-start(bf16[8,8,64,256]{3,1,2,0:T(8,128)(2,1)} %copy.23), calls=%async_computation | async-start | bytes 4194304 | tf_op jit(solution)/shard_map/all_to_all | solution.py:24
  23.2 0.0 copy-start.2
  23.2 0.0 reduce-scatter.2.cloned.1.call-start
  23.3 4.1 %copy.27 = bf16[256,4096]{0,1:T(8,128)(2,1)} copy(bf16[256,4096]{1,0:T(8,128)(2,1)} %param.5) | data formatting | bytes 4194304 | tf_op jit(solution)/shard_map/reshape | solution.py:27
  27.4 0.0 copy-done.2
  27.4 0.1 fusion.9
  27.4 0.0 all-gather.2.cloned.1.call-done
  27.4 5.8 %convert_bitcast_fusion.1 = bf16[512,8,256]{0,2,1:T(8,128)(2,1)} fusion(bf16[8,512,512]{2,1,0:T(8,128)(2,1)} %all-gather.2.cloned.1.call-done, bf16[256,8,512]{0,2,1:T(8,128)(2,1)} %bitcast.26, bf16[8,512]{1,0:T(8,128)(2,1)S(1)} %fusion.9), kind=kOutput, calls=%fused_computation.6 | convolution fusion | flops 1075838976 | bytes 8396800 | tf_op jit(solution)/shard_map/rki,kij->jkr/dot_general | solution.py:29
  33.3 4.5 %copy.21 = bf16[512,8,256]{2,1,0:T(8,128)(2,1)} copy(bf16[512,8,256]{0,2,1:T(8,128)(2,1)} %convert_bitcast_fusion.1) | data formatting | bytes 4194304 | tf_op jit(solution)/shard_map/convert_element_type | solution.py:31
  37.8 34.1 %all-to-all-done = bf16[8,8,64,256]{3,1,2,0:T(8,128)(2,1)} async-done(((bf16[8,8,64,256]{3,1,2,0:T(8,128)(2,1)}), bf16[8,8,64,256]{3,1,2,0:T(8,128)(2,1)}, u32[]{:S(2)}, u32[]{:S(2)}) %all-to-all-start) | async-done | bytes 2097184 | tf_op jit(solution)/shard_map/all_to_all | solution.py:24
  71.9 6.8 %fusion.3 = f32[8,512,512]{2,1,0:T(8,128)} fusion(bf16[8,512,256]{2,0,1:T(8,128)(2,1)} %bitcast.7, bf16[256,8,512]{0,2,1:T(8,128)(2,1)} %bitcast.27, bf16[8,512]{1,0:T(8,128)(2,1)S(1)} %fusion.9), kind=kOutput, calls=%fused_computation.3 | convolution fusion | flops 1074790400 | bytes 12591104 | tf_op jit(solution)/shard_map/rki,kjr->kij/dot_general | solution.py:36
  78.6 0.0 reduce-scatter.2.cloned.1.call-update
  78.7 4.4 %all-to-all-start.1 = ((bf16[8,64,8,256]{3,2,1,0:T(8,128)(2,1)}), bf16[8,64,8,256]{3,2,1,0:T(8,128)(2,1)}, u32[]{:S(2)}, u32[]{:S(2)}) async-start(bf16[8,64,8,256]{3,2,1,0:T(8,128)(2,1)} %bitcast.25), calls=%async_computation.2 | async-start | bytes 4194304 | tf_op jit(solution)/shard_map/all_to_all | solution.py:41
  83.1 47.8 %all-to-all-done.1 = bf16[8,64,8,256]{3,2,1,0:T(8,128)(2,1)} async-done(((bf16[8,64,8,256]{3,2,1,0:T(8,128)(2,1)}), bf16[8,64,8,256]{3,2,1,0:T(8,128)(2,1)}, u32[]{:S(2)}, u32[]{:S(2)}) %all-to-all-start.1) | async-done | bytes 2097184 | tf_op jit(solution)/shard_map/all_to_all | solution.py:41
  130.9 2.3 %fusion = f32[64,64,64]{2,1,0:T(8,128)S(1)} fusion(bf16[256,64,64]{0,2,1:T(8,128)(2,1)S(1)} %bitcast.24, bf16[8,64,8,256]{3,2,1,0:T(8,128)(2,1)} %all-to-all-done.1), kind=kOutput, calls=%fused_computation | convolution fusion | flops 134217728 | bytes 5242880 | tf_op jit(solution)/shard_map/jkr,rjm->jkm/dot_general | solution.py:44
  133.1 0.0 copy-start
  133.2 1.3 copy-done
  134.5 0.1 constant_dynamic-slice_fusion
  134.6 0.1 collective-permute-start
  134.6 2.6 %collective-permute-done = f32[64,32,64]{2,1,0:T(8,128)S(1)} collective-permute-done((f32[64,32,64]{2,1,0:T(8,128)S(1)}, f32[64,32,64]{2,1,0:T(8,128)S(1)}, u32[]{:S(2)}, u32[]{:S(2)}) %collective-permute-start) | collective-permute-done | bytes 524320 | tf_op jit(solution)/shard_map/ppermute | solution.py:47
  137.3 2.2 %add_convert_fusion = bf16[64,32,64]{2,1,0:T(8,128)(2,1)} fusion(f32[64,32,64]{2,1,0:T(8,128)S(1)} %collective-permute-done, f32[64,64,64]{2,1,0:T(8,128)} %copy-done, s32[]{:T(128)S(6)} %select_n.6), kind=kLoop, calls=%fused_computation.9 | loop fusion | flops 262144 | bytes 1310724 | tf_op jit(solution)/shard_map/convert_element_type | solution.py:48
  139.5 0.0 reduce-scatter.2.cloned.1.call-done
  139.5 3.8 %convert_element_type.30 = bf16[8,256,512]{2,1,0:T(8,128)(2,1)} convert(f32[8,256,512]{2,1,0:T(8,128)} %reduce-scatter.2.cloned.1.call-done) | non-fusion elementwise | flops 1048576 | bytes 6291456 | tf_op jit(solution)/shard_map/convert_element_type | solution.py:38
Async XLA Ops:
  7.2 20.3 %all-gather.2.cloned.1.call-start = ((), (), s32[]{:S(2)}) async-start(), calls=%async_computation.3 | async-start | bytes 6291456 | tf_op jit(solution)/shard_map/all_gather | solution.py:28
  7.9 3.4 %copy-start.1 = (bf16[64,32,64]{2,1,0:T(8,128)(2,1)S(1)}, bf16[64,32,64]{2,1,0:T(8,128)(2,1)}, u32[]{:S(2)}) copy-start(bf16[64,32,64]{2,1,0:T(8,128)(2,1)} %param.8) | copy-start | bytes 786436
  16.1 55.8 %all-to-all-start = ((bf16[8,8,64,256]{3,1,2,0:T(8,128)(2,1)}), bf16[8,8,64,256]{3,1,2,0:T(8,128)(2,1)}, u32[]{:S(2)}, u32[]{:S(2)}) async-start(bf16[8,8,64,256]{3,1,2,0:T(8,128)(2,1)} %copy.23), calls=%async_computation | async-start | bytes 4194304 | tf_op jit(solution)/shard_map/all_to_all | solution.py:24
  23.2 4.1 %copy-start.2 = (s32[8]{0:T(128)S(1)}, s32[8]{0:T(128)}, u32[]{:S(2)}) copy-start(s32[8]{0:T(128)} %param.9) | copy-start | bytes 100
  23.2 116.3 %reduce-scatter.2.cloned.1.call-start = ((), (), s32[]{:S(2)}) async-start(), calls=%async_computation.4 | async-start | bytes 12582912 | tf_op jit(solution)/shard_map/reduce_scatter | solution.py:38
  78.7 52.2 %all-to-all-start.1 = ((bf16[8,64,8,256]{3,2,1,0:T(8,128)(2,1)}), bf16[8,64,8,256]{3,2,1,0:T(8,128)(2,1)}, u32[]{:S(2)}, u32[]{:S(2)}) async-start(bf16[8,64,8,256]{3,2,1,0:T(8,128)(2,1)} %bitcast.25), calls=%async_computation.2 | async-start | bytes 4194304 | tf_op jit(solution)/shard_map/all_to_all | solution.py:41
  133.1 1.3 copy-start
  134.6 2.7 %collective-permute-start = (f32[64,32,64]{2,1,0:T(8,128)S(1)}, f32[64,32,64]{2,1,0:T(8,128)S(1)}, u32[]{:S(2)}, u32[]{:S(2)}) collective-permute-start(f32[64,32,64]{2,1,0:T(8,128)S(1)} %constant_dynamic-slice_fusion), channel_id=1, source_target_pairs={{0,1},{1,0},{2,3},{3,2},{4,5},{5,4},{6,7},{7,6},{8,9},{9,8},{10,11... | collective-permute-start | bytes 1572872 | tf_op jit(solution)/shard_map/ppermute | solution.py:47
Sparse Core Ops, SparseCore 0:
  9.5 16.3 all-gather.1
  78.8 15.8 reduce-scatter.1

commit v2 on v1

--- a/solution.py
+++ b/solution.py
@@ -2,6 +2,22 @@
 import jax.numpy as jnp
 from jax import lax
 from jax.sharding import PartitionSpec as P
+
+
+def swap_halves(local, axis):
+    other = lax.ppermute(local, "bin", [(0, 1), (1, 0)])
+    core = lax.axis_index("bin")
+    first = jnp.where(core == 0, local, other)
+    second = jnp.where(core == 0, other, local)
+    return jnp.concatenate([first, second], axis=axis)
+
+
+def sum_halves(term, axis):
+    half = term.shape[axis] // 2
+    core = lax.axis_index("bin")
+    mine = lax.dynamic_slice_in_dim(term, core * half, half, axis=axis)
+    theirs = lax.dynamic_slice_in_dim(term, (1 - core) * half, half, axis=axis)
+    return mine + lax.ppermute(theirs, "bin", [(0, 1), (1, 0)])
 
 
 def on_device(units, cotangent, left_factor, right_factor, session_units):
@@ -12,11 +28,9 @@
     order_right = right_factor.shape[2]
     peer_count = lax.axis_size("blk")
     block_count = peer_count * local_blocks
-    half = block_count // 2
-    core = lax.axis_index("bin")
 
     upstream = cotangent.reshape(row_count, right_local, order_right)
-    right_full = lax.all_gather(right_factor, "bin", axis=1, tiled=True)
+    right_full = swap_halves(right_factor, 1)
     back_grad = jnp.einsum(
         "rjm,jkm->kjr", upstream, right_full, preferred_element_type=jnp.float32
     ).astype(jnp.bfloat16)
@@ -25,7 +39,7 @@
 
     unit_mask = (jnp.arange(block_size)[None, :] < session_units[:, None]).astype(jnp.bfloat16)
     inputs = units.reshape(row_count, local_blocks, block_size) * unit_mask[None]
-    left_full = lax.all_gather(left_factor, "bin", axis=1, tiled=True)
+    left_full = swap_halves(left_factor, 1)
     mixed = jnp.einsum(
         "rki,kij->jkr", inputs, left_full, preferred_element_type=jnp.float32
     ).astype(jnp.bfloat16)
@@ -35,17 +49,12 @@
     back_t = back_got.transpose(1, 0, 2, 3).reshape(local_blocks, block_size, row_count)
     left_term = jnp.einsum("rki,kjr->kij", inputs, back_t, preferred_element_type=jnp.float32)
     mixed_sent, left_term = lax.optimization_barrier((mixed_sent, left_term))
-    grad_left = lax.psum_scatter(left_term, "bin", scatter_dimension=1, tiled=True).astype(
-        jnp.bfloat16
-    )
+    grad_left = sum_halves(left_term, 1).astype(jnp.bfloat16)
     mixed_got = lax.all_to_all(mixed_sent, "blk", 0, 0, tiled=True)
 
     mixed_t = mixed_got.transpose(1, 0, 2, 3).reshape(right_local, block_count, row_count)
     right_term = jnp.einsum("jkr,rjm->jkm", mixed_t, upstream, preferred_element_type=jnp.float32)
-    mine = lax.dynamic_slice_in_dim(right_term, core * half, half, axis=1)
-    theirs = lax.dynamic_slice_in_dim(right_term, (1 - core) * half, half, axis=1)
-    got = lax.ppermute(theirs, "bin", [(0, 1), (1, 0)])
-    grad_right = (mine + got).astype(jnp.bfloat16)
+    grad_right = sum_halves(right_term, 1).astype(jnp.bfloat16)
     return (grad_left, grad_right)
 
 

time: 151 us -> 139 us (0.921)
  between operations: 14.1 us -> 0.72 us
  local copies, waits for them, and re-layouts: 14.8 us -> 20.3 us
  other arithmetic: 6.1 us -> 10.5 us
  waiting for transfers between devices: 85.2 us -> 81.5 us
  blocking collectives: 2.64 us -> 0 us
  matrix products: 15.6 us -> 13.2 us
    dynamic_slice x1 -> x2, local copies, waits for them, and re-layouts: 0.09 us -> 4.65 us  [sum_halves(): theirs = lax.dynamic_slice_in_dim(term, (1 - core) * half, half, axis=axis)]
    convert_element_type x1 -> x0, local copies, waits for them, and re-layouts: 4.51 us -> none  [on_device(): mixed = jnp.einsum('rki,kij->jkr', inputs, left_full, preferred_element_t...]
    all_to_all x1, waiting for transfers between devices: 47.8 us -> 43.5 us  [on_device(): mixed_got = lax.all_to_all(mixed_sent, 'blk', 0, 0, tiled=True)]
    unnamed x7 -> x12, local copies, waits for them, and re-layouts: 4.65 us -> 8.66 us
    dot_general x1, matrix products: 5.84 us -> 2.66 us  [on_device(): jnp.einsum('rki,kij->jkr', inputs, left_full, preferred_element_type=jnp....]
    select_n x0 -> x2, other arithmetic: none -> 2.69 us  [swap_halves(): first = jnp.where(core == 0, local, other)]
    all_gather x1 -> x0, blocking collectives: 2.64 us -> none  [on_device(): right_full = lax.all_gather(right_factor, 'bin', axis=1, tiled=True)]
    convert_element_type x2, other arithmetic: 6.02 us -> 7.77 us  [the longest x1 5.52 us: on_device(): grad_left = sum_halves(left_term, 1).astype(jnp.bfloat16)]
  transfers between devices with their start and end apart: 5 -> 6, of which waited for: 3 -> 4; matrix products, arithmetic and copies ran while one was open for 16% -> 19% of each run, Pallas kernels for 0% -> 0%
where the time goes in v2:
time: 139 us; the launch traced here: 138 us
  waiting for transfers between devices  81.5 us (59%)
  local copies, waits for them, and re-layouts  20.3 us (15%)
  matrix products  13.2 us (9%)
  starting transfers between devices  12 us (9%)
  other arithmetic  10.5 us (8%)
    all_to_all x1, waiting for transfers between devices, on_device(): mixed_got = lax.all_to_all(mixed_sent, 'blk', 0, 0, tiled=True)  43.5 us
    all_to_all x1, waiting for transfers between devices, on_device(): back_got = lax.all_to_all(back_sent, 'blk', 0, 0, tiled=True)  35.2 us
    unnamed x12, local copies, waits for them, and re-layouts  8.66 us
    dot_general x1, matrix products, on_device(): jnp.einsum('rki,kjr->kij', inputs, back_t, preferred_element_type=jnp.flo...  6.93 us
    all_to_all x1, starting transfers between devices, on_device(): back_got = lax.all_to_all(back_sent, 'blk', 0, 0, tiled=True)  6.84 us
    convert_element_type x1, other arithmetic, on_device(): grad_left = sum_halves(left_term, 1).astype(jnp.bfloat16)  5.52 us
    dynamic_slice x2, local copies, waits for them, and re-layouts, sum_halves(): theirs = lax.dynamic_slice_in_dim(term, (1 - core) * half, half, axis=axis)  4.65 us
    all_to_all x1, starting transfers between devices, on_device(): mixed_got = lax.all_to_all(mixed_sent, 'blk', 0, 0, tiled=True)  4.35 us
  transfers between devices with their start and end apart: 6, of which 4 were waited for; matrix products, arithmetic and copies ran while one was open for 19% of the time, Pallas kernels for 0%

profile of v2, /device:TPU:0, one launch (start us, length us, event | category | flops | bytes accessed | tf_op | source)
XLA Modules:
  0.0 138.2 jit_solution(8845622284190052936)
XLA Ops:
  0.6 0.5 collective-permute-start.1
  1.1 3.3 %copy.29 = bf16[256,4096]{0,1:T(8,128)(2,1)S(1)} copy(bf16[256,4096]{1,0:T(8,128)(2,1)} %param.6) | data formatting | bytes 4194304 | tf_op args[1]
  4.5 0.0 collective-permute-done.1
  4.5 0.0 copy-done.3
  4.5 0.1 broadcast_select_fusion.3
  4.6 0.7 convert_bitcast_fusion
  5.3 1.5 %copy.30 = bf16[8,8,64,256]{3,1,2,0:T(8,128)(2,1)} copy(bf16[8,8,64,256]{3,1,0,2:T(8,128)(2,1)S(1)} %convert_bitcast_fusion) | data formatting | bytes 4194304 | tf_op jit(solution)/shard_map/reshape | solution.py:37
  6.7 6.8 %all-to-all-start = ((bf16[8,8,64,256]{3,1,2,0:T(8,128)(2,1)}), bf16[8,8,64,256]{3,1,2,0:T(8,128)(2,1)}, u32[]{:S(2)}, u32[]{:S(2)}) async-start(bf16[8,8,64,256]{3,1,2,0:T(8,128)(2,1)} %copy.30), calls=%async_computation | async-start | bytes 4194304 | tf_op jit(solution)/shard_map/all_to_all | solution.py:38
  13.6 3.9 %copy.25 = bf16[8,256,512]{1,2,0:T(8,128)(2,1)} copy(bf16[8,256,512]{2,1,0:T(8,128)(2,1)} %param.7) | data formatting | bytes 4194304 | tf_op args[2]
  17.5 0.2 collective-permute-start
  17.7 4.1 %copy.35 = bf16[256,4096]{0,1:T(8,128)(2,1)} copy(bf16[256,4096]{1,0:T(8,128)(2,1)} %param.5) | data formatting | bytes 4194304 | tf_op jit(solution)/shard_map/reshape | solution.py:41
  21.8 0.0 copy-done.4
  21.8 0.1 fusion.19
  21.8 0.2 collective-permute-done
  22.0 2.6 %broadcast_select_fusion.1 = (bf16[8,256,512]{1,2,0:T(8,128)(2,1)S(1)}, bf16[8,256,512]{1,2,0:T(8,128)(2,1)S(1)}) fusion(bf16[8,256,512]{1,2,0:T(8,128)(2,1)} %copy.25, bf16[8,256,512]{1,2,0:T(8,128)(2,1)} %collective-permute-done, pred[]{:T(512)S(6)} %eq.2), kind=kLoop, calls=%fused_computation.12 | loop fusion | flops 2097152 | bytes 8388609 | tf_op jit(solution)/shard_map/jit(_where)/select_n | solution.py:10
  24.6 0.1 copy-done.1
  24.7 2.7 %fusion.9 = bf16[8,512,256]{2,1,0:T(8,128)(2,1)} fusion(bf16[8,256,512]{1,2,0:T(8,128)(2,1)S(1)} %get-tuple-element.11, bf16[8,256,512]{1,2,0:T(8,128)(2,1)S(1)} %get-tuple-element.10, bf16[256,8,512]{0,2,1:T(8,128)(2,1)S(1)} %bitcast.21, bf16[8,512]{1,0:T(8,128)(2,1)S(1)} %fusion.19), kind=kOutput, calls=%fused_computation.13 | convolution fusion | flops 1084227584 | bytes 8396800 | tf_op jit(solution)/shard_map/rki,kij->jkr/dot_general | solution.py:43
  27.4 35.2 %all-to-all-done = bf16[8,8,64,256]{3,1,2,0:T(8,128)(2,1)} async-done(((bf16[8,8,64,256]{3,1,2,0:T(8,128)(2,1)}), bf16[8,8,64,256]{3,1,2,0:T(8,128)(2,1)}, u32[]{:S(2)}, u32[]{:S(2)}) %all-to-all-start) | async-done | bytes 2097184 | tf_op jit(solution)/shard_map/all_to_all | solution.py:38
  62.6 6.9 %fusion.7 = f32[8,512,512]{2,1,0:T(8,128)} fusion(bf16[8,512,256]{2,0,1:T(8,128)(2,1)} %bitcast.7, bf16[256,8,512]{0,2,1:T(8,128)(2,1)} %bitcast.20, bf16[8,512]{1,0:T(8,128)(2,1)S(1)} %fusion.19), kind=kOutput, calls=%fused_computation.8 | convolution fusion | flops 1074790400 | bytes 12591104 | tf_op jit(solution)/shard_map/rki,kjr->kij/dot_general | solution.py:50
  69.5 1.5 %copy.32 = bf16[8,64,8,256]{3,1,2,0:T(8,128)(2,1)} copy(bf16[8,64,8,256]{3,1,0,2:T(8,128)(2,1)S(1)} %bitcast.22) | data formatting | bytes 4194304 | tf_op jit(solution)/shard_map/optimization_barrier | solution.py:51
  70.9 4.4 %all-to-all-start.1 = ((bf16[8,64,8,256]{3,1,2,0:T(8,128)(2,1)}), bf16[8,64,8,256]{3,1,2,0:T(8,128)(2,1)}, u32[]{:S(2)}, u32[]{:S(2)}) async-start(bf16[8,64,8,256]{3,1,2,0:T(8,128)(2,1)} %copy.32), calls=%async_computation.1 | async-start | bytes 4194304 | tf_op jit(solution)/shard_map/all_to_all | solution.py:53
  75.3 4.6 %constant_dynamic-slice_fusion.1 = f32[8,256,512]{2,1,0:T(8,128)} fusion(f32[8,512,512]{2,1,0:T(8,128)} %fusion.7, s32[]{:T(128)S(6)} %select_n.43), kind=kLoop, calls=%fused_computation.27 | loop fusion | bytes 8388612 | tf_op jit(solution)/shard_map/dynamic_slice | solution.py:19
  79.9 0.0 collective-permute-start.2
  79.9 43.5 %all-to-all-done.1 = bf16[8,64,8,256]{3,1,2,0:T(8,128)(2,1)} async-done(((bf16[8,64,8,256]{3,1,2,0:T(8,128)(2,1)}), bf16[8,64,8,256]{3,1,2,0:T(8,128)(2,1)}, u32[]{:S(2)}, u32[]{:S(2)}) %all-to-all-start.1) | async-done | bytes 2097184 | tf_op jit(solution)/shard_map/all_to_all | solution.py:53
  123.4 3.0 %fusion.4 = f32[64,64,64]{2,1,0:T(8,128)S(1)} fusion(bf16[256,64,64]{0,2,1:T(8,128)(2,1)S(1)} %bitcast.19, bf16[64,8,8,256]{3,0,2,1:T(8,128)(2,1)} %bitcast.8), kind=kOutput, calls=%fused_computation.5 | convolution fusion | flops 134217728 | bytes 5242880 | tf_op jit(solution)/shard_map/jkr,rjm->jkm/dot_general | solution.py:56
  126.3 1.3 copy-done
  127.7 0.1 constant_dynamic-slice_fusion
  127.7 0.1 collective-permute-start.3
  127.8 2.6 %collective-permute-done.3 = f32[64,32,64]{2,1,0:T(8,128)S(1)} collective-permute-done((f32[64,32,64]{2,1,0:T(8,128)S(1)}, f32[64,32,64]{2,1,0:T(8,128)S(1)}, u32[]{:S(2)}, u32[]{:S(2)}) %collective-permute-start.3) | collective-permute-done | bytes 524320 | tf_op jit(solution)/shard_map/ppermute | solution.py:20
  130.5 2.2 %add_convert_fusion.1 = bf16[64,32,64]{2,1,0:T(8,128)(2,1)} fusion(f32[64,32,64]{2,1,0:T(8,128)S(1)} %collective-permute-done.3, f32[64,64,64]{2,1,0:T(8,128)} %copy-done, s32[]{:T(128)S(6)} %select_n.44), kind=kLoop, calls=%fused_computation.19 | loop fusion | flops 262144 | bytes 1310724 | tf_op jit(solution)/shard_map/convert_element_type | solution.py:57
  132.7 0.0 collective-permute-done.2
  132.7 5.5 %add_convert_fusion = bf16[8,256,512]{2,1,0:T(8,128)(2,1)} fusion(f32[8,256,512]{2,1,0:T(8,128)} %collective-permute-done.2, f32[8,512,512]{2,1,0:T(8,128)} %fusion.7, s32[]{:T(128)S(6)} %select_n.42), kind=kLoop, calls=%fused_computation.4 | loop fusion | flops 2097152 | bytes 10485764 | tf_op jit(solution)/shard_map/convert_element_type | solution.py:52
  (6 shorter events, 0.0 us)
Async XLA Ops:
  0.6 3.9 %collective-permute-start.1 = (bf16[64,32,64]{2,1,0:T(8,128)(2,1)}, bf16[64,32,64]{2,1,0:T(8,128)(2,1)S(1)}, u32[]{:S(2)}, u32[]{:S(2)}) collective-permute-start(bf16[64,32,64]{2,1,0:T(8,128)(2,1)} %param.8), channel_id=1, source_target_pairs={{0,1},{1,0},{2,3},{3,2},{4,5},{5,4},{6,7},{7,6},{8,9},{9,8},{10,11... | collective-permute-start | bytes 786440 | tf_op jit(solution)/shard_map/ppermute | solution.py:8
  1.1 3.4 %copy-start.3 = (bf16[64,32,64]{2,1,0:T(8,128)(2,1)S(1)}, bf16[64,32,64]{2,1,0:T(8,128)(2,1)}, u32[]{:S(2)}) copy-start(bf16[64,32,64]{2,1,0:T(8,128)(2,1)} %param.8) | copy-start | bytes 786436
  6.7 55.8 %all-to-all-start = ((bf16[8,8,64,256]{3,1,2,0:T(8,128)(2,1)}), bf16[8,8,64,256]{3,1,2,0:T(8,128)(2,1)}, u32[]{:S(2)}, u32[]{:S(2)}) async-start(bf16[8,8,64,256]{3,1,2,0:T(8,128)(2,1)} %copy.30), calls=%async_computation | async-start | bytes 4194304 | tf_op jit(solution)/shard_map/all_to_all | solution.py:38
  17.5 4.3 %copy-start.4 = (s32[8]{0:T(128)S(1)}, s32[8]{0:T(128)}, u32[]{:S(2)}) copy-start(s32[8]{0:T(128)} %param.9) | copy-start | bytes 100
  17.5 4.5 %collective-permute-start = (bf16[8,256,512]{1,2,0:T(8,128)(2,1)}, bf16[8,256,512]{1,2,0:T(8,128)(2,1)}, u32[]{:S(2)}, u32[]{:S(2)}) collective-permute-start(bf16[8,256,512]{1,2,0:T(8,128)(2,1)} %copy.25), channel_id=1, source_target_pairs={{0,1},{1,0},{2,3},{3,2},{4,5},{5,4},{6,7},{7,6},{8,9},{9,8},{10,11... | collective-permute-start | bytes 6291464 | tf_op jit(solution)/shard_map/ppermute | solution.py:8
  21.8 2.9 %copy-start.1 = (bf16[256,4096]{0,1:T(8,128)(2,1)S(1)}, bf16[256,4096]{0,1:T(8,128)(2,1)}, u32[]{:S(2)}) copy-start(bf16[256,4096]{0,1:T(8,128)(2,1)} %copy.35) | copy-start | bytes 6291460
  62.6 6.9 %copy-start.2 = (bf16[8,512,256]{2,1,0:T(8,128)(2,1)S(1)}, bf16[8,512,256]{2,1,0:T(8,128)(2,1)}, u32[]{:S(2)}) copy-start(bf16[8,512,256]{2,1,0:T(8,128)(2,1)} %fusion.9) | copy-start | bytes 6291460
  70.9 52.4 %all-to-all-start.1 = ((bf16[8,64,8,256]{3,1,2,0:T(8,128)(2,1)}), bf16[8,64,8,256]{3,1,2,0:T(8,128)(2,1)}, u32[]{:S(2)}, u32[]{:S(2)}) async-start(bf16[8,64,8,256]{3,1,2,0:T(8,128)(2,1)} %copy.32), calls=%async_computation.1 | async-start | bytes 4194304 | tf_op jit(solution)/shard_map/all_to_all | solution.py:53
  79.9 52.9 %collective-permute-start.2 = (f32[8,256,512]{2,1,0:T(8,128)}, f32[8,256,512]{2,1,0:T(8,128)}, u32[]{:S(2)}, u32[]{:S(2)}) collective-permute-start(f32[8,256,512]{2,1,0:T(8,128)} %constant_dynamic-slice_fusion.1), channel_id=1, source_target_pairs={{0,1},{1,0},{2,3},{3,2},{4,5},{5,4},{6,7},{7,6},{8,9},{9,8},{10,11... | collective-permute-start | bytes 12582920 | tf_op jit(solution)/shard_map/ppermute | solution.py:20
  126.3 1.3 copy-start
  127.7 2.7 %collective-permute-start.3 = (f32[64,32,64]{2,1,0:T(8,128)S(1)}, f32[64,32,64]{2,1,0:T(8,128)S(1)}, u32[]{:S(2)}, u32[]{:S(2)}) collective-permute-start(f32[64,32,64]{2,1,0:T(8,128)S(1)} %constant_dynamic-slice_fusion), channel_id=1, source_target_pairs={{0,1},{1,0},{2,3},{3,2},{4,5},{5,4},{6,7},{7,6},{8,9},{9,8},{10,11... | collective-permute-start | bytes 1572872 | tf_op jit(solution)/shard_map/ppermute | solution.py:20

commit v3 on v2

--- a/solution.py
+++ b/solution.py
@@ -43,16 +43,25 @@
     mixed = jnp.einsum(
         "rki,kij->jkr", inputs, left_full, preferred_element_type=jnp.float32
     ).astype(jnp.bfloat16)
-    mixed_sent = mixed.reshape(peer_count, right_local, local_blocks, row_count)
+    mixed_sent = mixed.reshape(peer_count, right_local, local_blocks, row_count).transpose(0, 2, 1, 3)
     mixed_sent, back_got = lax.optimization_barrier((mixed_sent, back_got))
 
+    half_size = block_size // 2
+    core = lax.axis_index("bin")
     back_t = back_got.transpose(1, 0, 2, 3).reshape(local_blocks, block_size, row_count)
-    left_term = jnp.einsum("rki,kjr->kij", inputs, back_t, preferred_element_type=jnp.float32)
-    mixed_sent, left_term = lax.optimization_barrier((mixed_sent, left_term))
-    grad_left = sum_halves(left_term, 1).astype(jnp.bfloat16)
+
+    def left_of(start):
+        rows = lax.dynamic_slice_in_dim(inputs, start, half_size, axis=2)
+        return jnp.einsum("rki,kjr->kij", rows, back_t, preferred_element_type=jnp.float32)
+
+    theirs = left_of((1 - core) * half_size)
+    mixed_sent, theirs = lax.optimization_barrier((mixed_sent, theirs))
     mixed_got = lax.all_to_all(mixed_sent, "blk", 0, 0, tiled=True)
+    got_left = lax.ppermute(theirs, "bin", [(0, 1), (1, 0)])
+    grad_left = (left_of(core * half_size) + got_left).astype(jnp.bfloat16)
 
-    mixed_t = mixed_got.transpose(1, 0, 2, 3).reshape(right_local, block_count, row_count)
+    mixed_t = mixed_got.transpose(2, 0, 1, 3).reshape(right_local, block_count, row_count)
+    grad_left, mixed_t = lax.optimization_barrier((grad_left, mixed_t))
     right_term = jnp.einsum("jkr,rjm->jkm", mixed_t, upstream, preferred_element_type=jnp.float32)
     grad_right = sum_halves(right_term, 1).astype(jnp.bfloat16)
     return (grad_left, grad_right)

time: 139 us -> 131 us (0.942)
  local copies, waits for them, and re-layouts: 20.3 us -> 15.9 us
  other arithmetic: 10.5 us -> 7.26 us
  waiting for transfers between devices: 81.5 us -> 79.2 us
  matrix products: 13.2 us -> 15.2 us
    convert_element_type x1 -> x0, other arithmetic: 5.52 us -> none  [on_device(): grad_left = sum_halves(left_term, 1).astype(jnp.bfloat16)]
    dynamic_slice x2 -> x1, local copies, waits for them, and re-layouts: 4.65 us -> 0.09 us  [sum_halves(): theirs = lax.dynamic_slice_in_dim(term, (1 - core) * half, half, axis=axis)]
    unnamed x12 -> x13, local copies, waits for them, and re-layouts: 8.66 us -> 12.8 us
    dot_general x1 -> x2, matrix products: 6.93 us -> 10.3 us  [left_of(): jnp.einsum('rki,kjr->kij', rows, back_t, preferred_element_type=jnp.float32)]
    ppermute x0 -> x1, waiting for transfers between devices: none -> 3.12 us  [on_device(): got_left = lax.ppermute(theirs, 'bin', [(0, 1), (1, 0)])]
    all_to_all x1, waiting for transfers between devices: 43.5 us -> 40.6 us  [on_device(): mixed_got = lax.all_to_all(mixed_sent, 'blk', 0, 0, tiled=True)]
    reshape x1, local copies, waits for them, and re-layouts: 4.08 us -> 1.57 us  [on_device(): mixed.reshape(peer_count, right_local, local_blocks, row_count)]
    all_to_all x1, waiting for transfers between devices: 35.2 us -> 32.9 us  [on_device(): back_got = lax.all_to_all(back_sent, 'blk', 0, 0, tiled=True)]
where the time goes in v3:
time: 131 us; the launch traced here: 130 us
  waiting for transfers between devices  79.2 us (60%)
  local copies, waits for them, and re-layouts  15.9 us (12%)
  matrix products  15.2 us (12%)
  starting transfers between devices  12 us (9%)
  other arithmetic  7.26 us (6%)
    all_to_all x1, waiting for transfers between devices, on_device(): mixed_got = lax.all_to_all(mixed_sent, 'blk', 0, 0, tiled=True)  40.6 us
    all_to_all x1, waiting for transfers between devices, on_device(): back_got = lax.all_to_all(back_sent, 'blk', 0, 0, tiled=True)  32.9 us
    unnamed x13, local copies, waits for them, and re-layouts  12.8 us
    dot_general x2, matrix products, left_of(): jnp.einsum('rki,kjr->kij', rows, back_t, preferred_element_type=jnp.float32)  10.3 us
    all_to_all x1, starting transfers between devices, on_device(): back_got = lax.all_to_all(back_sent, 'blk', 0, 0, tiled=True)  6.84 us
    all_to_all x1, starting transfers between devices, on_device(): mixed_got = lax.all_to_all(mixed_sent, 'blk', 0, 0, tiled=True)  4.36 us
    ppermute x1, waiting for transfers between devices, on_device(): got_left = lax.ppermute(theirs, 'bin', [(0, 1), (1, 0)])  3.12 us
    dot_general x1, matrix products, on_device(): jnp.einsum('jkr,rjm->jkm', mixed_t, upstream, preferred_element_type=jnp....  2.97 us
  transfers between devices with their start and end apart: 6, of which 4 were waited for; matrix products, arithmetic and copies ran while one was open for 19% of the time, Pallas kernels for 0%

profile of v3, /device:TPU:0, one launch (start us, length us, event | category | flops | bytes accessed | tf_op | source)
XLA Modules:
  0.0 130.3 jit_solution(8423999949729916826)
XLA Ops:
  0.6 0.5 collective-permute-start.1
  1.1 3.3 %copy.30 = bf16[256,4096]{0,1:T(8,128)(2,1)S(1)} copy(bf16[256,4096]{1,0:T(8,128)(2,1)} %param.6) | data formatting | bytes 4194304 | tf_op args[1]
  4.5 0.0 collective-permute-done.1
  4.5 0.0 copy-done.3
  4.5 0.1 broadcast_select_fusion.3
  4.6 0.7 convert_bitcast_fusion
  5.3 1.5 %copy.31 = bf16[8,8,64,256]{3,1,2,0:T(8,128)(2,1)} copy(bf16[8,8,64,256]{3,1,0,2:T(8,128)(2,1)S(1)} %convert_bitcast_fusion) | data formatting | bytes 4194304 | tf_op jit(solution)/shard_map/reshape | solution.py:37
  6.7 6.8 %all-to-all-start = ((bf16[8,8,64,256]{3,1,2,0:T(8,128)(2,1)}), bf16[8,8,64,256]{3,1,2,0:T(8,128)(2,1)}, u32[]{:S(2)}, u32[]{:S(2)}) async-start(bf16[8,8,64,256]{3,1,2,0:T(8,128)(2,1)} %copy.31), calls=%async_computation | async-start | bytes 4194304 | tf_op jit(solution)/shard_map/all_to_all | solution.py:38
  13.6 3.9 %copy.26 = bf16[8,256,512]{1,2,0:T(8,128)(2,1)} copy(bf16[8,256,512]{2,1,0:T(8,128)(2,1)} %param.7) | data formatting | bytes 4194304 | tf_op args[2]
  17.5 0.2 collective-permute-start
  17.7 4.1 %copy.24 = bf16[256,4096]{0,1:T(8,128)(2,1)} copy(bf16[256,4096]{1,0:T(8,128)(2,1)} %param.5) | data formatting | bytes 4194304 | tf_op args[0]
  21.8 0.1 fusion.17
  21.8 2.1 %broadcast_multiply_fusion = bf16[256,8,512]{0,2,1:T(8,128)(2,1)S(1)} fusion(bf16[256,8,512]{0,2,1:T(8,128)(2,1)} %bitcast.24, bf16[8,512]{1,0:T(8,128)(2,1)S(1)} %fusion.17), kind=kLoop, calls=%fused_computation.21 | loop fusion | flops 1048576 | bytes 4202496 | tf_op jit(solution)/shard_map/mul | solution.py:41
  23.9 0.0 collective-permute-done
  24.0 0.1 copy-done.2
  24.1 2.8 %broadcast_select_fusion.1 = (bf16[8,256,512]{1,2,0:T(8,128)(2,1)S(1)}, bf16[8,256,512]{1,2,0:T(8,128)(2,1)S(1)}) fusion(bf16[8,256,512]{1,2,0:T(8,128)(2,1)S(1)} %copy-done.2, bf16[8,256,512]{1,2,0:T(8,128)(2,1)} %collective-permute-done, pred[]{:T(512)S(6)} %eq.2), kind=kLoop, calls=%fused_computation.10 | loop fusion | flops 2097152 | bytes 8388609 | tf_op jit(solution)/shard_map/jit(_where)/select_n | solution.py:10
  26.8 0.0 copy-done.1
  26.8 1.3 fusion.6
  28.1 1.6 %copy.43 = bf16[8,64,8,256]{3,1,2,0:T(8,128)(2,1)} copy(bf16[8,64,8,256]{3,1,0,2:T(8,128)(2,1)S(1)} %bitcast.25) | data formatting | bytes 4194304 | tf_op jit(solution)/shard_map/reshape | solution.py:46
  29.7 32.9 %all-to-all-done = bf16[8,8,64,256]{3,1,2,0:T(8,128)(2,1)} async-done(((bf16[8,8,64,256]{3,1,2,0:T(8,128)(2,1)}), bf16[8,8,64,256]{3,1,2,0:T(8,128)(2,1)}, u32[]{:S(2)}, u32[]{:S(2)}) %all-to-all-start) | async-done | bytes 2097184 | tf_op jit(solution)/shard_map/all_to_all | solution.py:38
  62.6 4.8 %fusion.9 = f32[8,256,512]{2,1,0:T(8,128)} fusion(bf16[8,512,256]{2,0,1:T(8,128)(2,1)} %bitcast.8, bf16[256,8,512]{0,2,1:T(8,128)(2,1)} %copy-done.1, s32[]{:T(128)S(6)} %select_n.43), kind=kOutput, calls=%fused_computation.12 | convolution fusion | flops 536870912 | bytes 7340036 | tf_op jit(solution)/shard_map/rki,kjr->kij/dot_general | solution.py:55
  67.4 0.0 collective-permute-start.2
  67.4 4.4 %all-to-all-start.1 = ((bf16[8,8,64,256]{3,2,1,0:T(8,128)(2,1)}), bf16[8,8,64,256]{3,2,1,0:T(8,128)(2,1)}, u32[]{:S(2)}, u32[]{:S(2)}) async-start(bf16[8,8,64,256]{3,2,1,0:T(8,128)(2,1)} %bitcast.23), calls=%async_computation.1 | async-start | bytes 4194304 | tf_op jit(solution)/shard_map/all_to_all | solution.py:59
  71.8 3.1 %collective-permute-done.2 = f32[8,256,512]{2,1,0:T(8,128)} collective-permute-done((f32[8,256,512]{2,1,0:T(8,128)}, f32[8,256,512]{2,1,0:T(8,128)}, u32[]{:S(2)}, u32[]{:S(2)}) %collective-permute-start.2) | collective-permute-done | bytes 4194336 | tf_op jit(solution)/shard_map/ppermute | solution.py:60
  74.9 5.5 %add_convert_fusion = bf16[8,256,512]{2,1,0:T(8,128)(2,1)} fusion(f32[8,256,512]{2,1,0:T(8,128)} %collective-permute-done.2, bf16[8,512,256]{2,0,1:T(8,128)(2,1)} %bitcast.8, bf16[256,8,512]{0,2,1:T(8,128)(2,1)} %copy-done.1, s32[]{:T(128)S(6)} %select_n.36), kind=kOutput, calls=%fused_computation.4 | convolution fusion | flops 538968064 | bytes 9437188 | tf_op jit(solution)/shard_map/rki,kjr->kij/dot_general | solution.py:55
  80.4 40.6 %all-to-all-done.1 = bf16[8,8,64,256]{3,2,1,0:T(8,128)(2,1)} async-done(((bf16[8,8,64,256]{3,2,1,0:T(8,128)(2,1)}), bf16[8,8,64,256]{3,2,1,0:T(8,128)(2,1)}, u32[]{:S(2)}, u32[]{:S(2)}) %all-to-all-start.1) | async-done | bytes 2097184 | tf_op jit(solution)/shard_map/all_to_all | solution.py:59
  120.9 3.0 %fusion.4 = f32[64,64,64]{2,1,0:T(8,128)S(1)} fusion(bf16[256,64,64]{0,2,1:T(8,128)(2,1)S(1)} %bitcast.22, bf16[64,64,256]{2,0,1:T(8,128)(2,1)} %bitcast.11), kind=kOutput, calls=%fused_computation.5 | convolution fusion | flops 134217728 | bytes 5242880 | tf_op jit(solution)/shard_map/jkr,rjm->jkm/dot_general | solution.py:65
  123.9 1.4 %copy-done = f32[64,64,64]{2,1,0:T(8,128)} copy-done((f32[64,64,64]{2,1,0:T(8,128)}, f32[64,64,64]{2,1,0:T(8,128)S(1)}, u32[]{:S(2)}) %copy-start) | copy-done | bytes 1048600
  125.2 0.1 constant_dynamic-slice_fusion
  125.3 0.1 collective-permute-start.3
  125.4 2.6 %collective-permute-done.3 = f32[64,32,64]{2,1,0:T(8,128)S(1)} collective-permute-done((f32[64,32,64]{2,1,0:T(8,128)S(1)}, f32[64,32,64]{2,1,0:T(8,128)S(1)}, u32[]{:S(2)}, u32[]{:S(2)}) %collective-permute-start.3) | collective-permute-done | bytes 524320 | tf_op jit(solution)/shard_map/ppermute | solution.py:20
  128.1 2.2 %add_convert_fusion.1 = bf16[64,32,64]{2,1,0:T(8,128)(2,1)} fusion(f32[64,32,64]{2,1,0:T(8,128)S(1)} %collective-permute-done.3, f32[64,64,64]{2,1,0:T(8,128)} %copy-done, s32[]{:T(128)S(6)} %select_n.44), kind=kLoop, calls=%fused_computation.18 | loop fusion | flops 262144 | bytes 1310724 | tf_op jit(solution)/shard_map/convert_element_type | solution.py:66
  (6 shorter events, 0.0 us)
Async XLA Ops:
  0.6 3.9 %collective-permute-start.1 = (bf16[64,32,64]{2,1,0:T(8,128)(2,1)}, bf16[64,32,64]{2,1,0:T(8,128)(2,1)S(1)}, u32[]{:S(2)}, u32[]{:S(2)}) collective-permute-start(bf16[64,32,64]{2,1,0:T(8,128)(2,1)} %param.8), channel_id=1, source_target_pairs={{0,1},{1,0},{2,3},{3,2},{4,5},{5,4},{6,7},{7,6},{8,9},{9,8},{10,11... | collective-permute-start | bytes 786440 | tf_op jit(solution)/shard_map/ppermute | solution.py:8
  1.1 3.4 %copy-start.3 = (bf16[64,32,64]{2,1,0:T(8,128)(2,1)S(1)}, bf16[64,32,64]{2,1,0:T(8,128)(2,1)}, u32[]{:S(2)}) copy-start(bf16[64,32,64]{2,1,0:T(8,128)(2,1)} %param.8) | copy-start | bytes 786436
  6.7 55.8 %all-to-all-start = ((bf16[8,8,64,256]{3,1,2,0:T(8,128)(2,1)}), bf16[8,8,64,256]{3,1,2,0:T(8,128)(2,1)}, u32[]{:S(2)}, u32[]{:S(2)}) async-start(bf16[8,8,64,256]{3,1,2,0:T(8,128)(2,1)} %copy.31), calls=%async_computation | async-start | bytes 4194304 | tf_op jit(solution)/shard_map/all_to_all | solution.py:38
  17.5 4.3 %copy-start.4 = (s32[8]{0:T(128)S(1)}, s32[8]{0:T(128)}, u32[]{:S(2)}) copy-start(s32[8]{0:T(128)} %param.9) | copy-start | bytes 100
  17.5 6.5 %collective-permute-start = (bf16[8,256,512]{1,2,0:T(8,128)(2,1)}, bf16[8,256,512]{1,2,0:T(8,128)(2,1)}, u32[]{:S(2)}, u32[]{:S(2)}) collective-permute-start(bf16[8,256,512]{1,2,0:T(8,128)(2,1)} %copy.26), channel_id=1, source_target_pairs={{0,1},{1,0},{2,3},{3,2},{4,5},{5,4},{6,7},{7,6},{8,9},{9,8},{10,11... | collective-permute-start | bytes 6291464 | tf_op jit(solution)/shard_map/ppermute | solution.py:8
  21.8 2.2 %copy-start.2 = (bf16[8,256,512]{1,2,0:T(8,128)(2,1)S(1)}, bf16[8,256,512]{1,2,0:T(8,128)(2,1)}, u32[]{:S(2)}) copy-start(bf16[8,256,512]{1,2,0:T(8,128)(2,1)} %copy.26) | copy-start | bytes 6291460
  23.9 2.9 %copy-start.1 = (bf16[256,8,512]{0,2,1:T(8,128)(2,1)}, bf16[256,8,512]{0,2,1:T(8,128)(2,1)S(1)}, u32[]{:S(2)}) copy-start(bf16[256,8,512]{0,2,1:T(8,128)(2,1)S(1)} %broadcast_multiply_fusion) | copy-start | bytes 6291460
  67.4 7.5 %collective-permute-start.2 = (f32[8,256,512]{2,1,0:T(8,128)}, f32[8,256,512]{2,1,0:T(8,128)}, u32[]{:S(2)}, u32[]{:S(2)}) collective-permute-start(f32[8,256,512]{2,1,0:T(8,128)} %fusion.9), channel_id=1, source_target_pairs={{0,1},{1,0},{2,3},{3,2},{4,5},{5,4},{6,7},{7,6},{8,9},{9,8},{10,11... | collective-permute-start | bytes 12582920 | tf_op jit(solution)/shard_map/ppermute | solution.py:60
  67.4 53.6 %all-to-all-start.1 = ((bf16[8,8,64,256]{3,2,1,0:T(8,128)(2,1)}), bf16[8,8,64,256]{3,2,1,0:T(8,128)(2,1)}, u32[]{:S(2)}, u32[]{:S(2)}) async-start(bf16[8,8,64,256]{3,2,1,0:T(8,128)(2,1)} %bitcast.23), calls=%async_computation.1 | async-start | bytes 4194304 | tf_op jit(solution)/shard_map/all_to_all | solution.py:59
  123.9 1.4 %copy-start = (f32[64,64,64]{2,1,0:T(8,128)}, f32[64,64,64]{2,1,0:T(8,128)S(1)}, u32[]{:S(2)}) copy-start(f32[64,64,64]{2,1,0:T(8,128)S(1)} %fusion.4) | copy-start | bytes 3145732
  125.3 2.7 %collective-permute-start.3 = (f32[64,32,64]{2,1,0:T(8,128)S(1)}, f32[64,32,64]{2,1,0:T(8,128)S(1)}, u32[]{:S(2)}, u32[]{:S(2)}) collective-permute-start(f32[64,32,64]{2,1,0:T(8,128)S(1)} %constant_dynamic-slice_fusion), channel_id=1, source_target_pairs={{0,1},{1,0},{2,3},{3,2},{4,5},{5,4},{6,7},{7,6},{8,9},{9,8},{10,11... | collective-permute-start | bytes 1572872 | tf_op jit(solution)/shard_map/ppermute | solution.py:20

commit v4 on v3

--- a/solution.py
+++ b/solution.py
@@ -10,14 +10,6 @@
     first = jnp.where(core == 0, local, other)
     second = jnp.where(core == 0, other, local)
     return jnp.concatenate([first, second], axis=axis)
-
-
-def sum_halves(term, axis):
-    half = term.shape[axis] // 2
-    core = lax.axis_index("bin")
-    mine = lax.dynamic_slice_in_dim(term, core * half, half, axis=axis)
-    theirs = lax.dynamic_slice_in_dim(term, (1 - core) * half, half, axis=axis)
-    return mine + lax.ppermute(theirs, "bin", [(0, 1), (1, 0)])
 
 
 def on_device(units, cotangent, left_factor, right_factor, session_units):
@@ -58,12 +50,19 @@
     mixed_sent, theirs = lax.optimization_barrier((mixed_sent, theirs))
     mixed_got = lax.all_to_all(mixed_sent, "blk", 0, 0, tiled=True)
     got_left = lax.ppermute(theirs, "bin", [(0, 1), (1, 0)])
-    grad_left = (left_of(core * half_size) + got_left).astype(jnp.bfloat16)
+    grad_left = (lax.optimization_barrier(left_of(core * half_size)) + got_left).astype(jnp.bfloat16)
+    grad_left, mixed_got = lax.optimization_barrier((grad_left, mixed_got))
+    half_peers = peer_count // 2
 
-    mixed_t = mixed_got.transpose(2, 0, 1, 3).reshape(right_local, block_count, row_count)
-    grad_left, mixed_t = lax.optimization_barrier((grad_left, mixed_t))
-    right_term = jnp.einsum("jkr,rjm->jkm", mixed_t, upstream, preferred_element_type=jnp.float32)
-    grad_right = sum_halves(right_term, 1).astype(jnp.bfloat16)
+    def right_of(start):
+        blocks = lax.dynamic_slice_in_dim(mixed_got, start, half_peers, axis=0)
+        blocks = blocks.transpose(2, 0, 1, 3).reshape(right_local, half_peers * local_blocks, row_count)
+        return jnp.einsum("jkr,rjm->jkm", blocks, upstream, preferred_element_type=jnp.float32)
+
+    got_right = lax.ppermute(right_of((1 - core) * half_peers), "bin", [(0, 1), (1, 0)])
+    grad_right = (lax.optimization_barrier(right_of(core * half_peers)) + got_right).astype(
+        jnp.bfloat16
+    )
     return (grad_left, grad_right)
 
 

time: 131 us -> 128 us (0.977)
  matrix products: 15.2 us -> 11.2 us
  other arithmetic: 7.26 us -> 10.3 us
  waiting for transfers between devices: 79.2 us -> 76.8 us
    convert_element_type x1 -> x2, other arithmetic: 2.25 us -> 5.27 us  [the longest x1 4.25 us: on_device(): (lax.optimization_barrier(left_of(core * half_size)) + got_left).astype(j...]
    ppermute x1, waiting for transfers between devices: 3.12 us -> 0.27 us  [on_device(): got_left = lax.ppermute(theirs, 'bin', [(0, 1), (1, 0)])]
    dot_general x2, matrix products: 10.3 us -> 7.63 us  [left_of(): jnp.einsum('rki,kjr->kij', rows, back_t, preferred_element_type=jnp.float32)]
    transpose x0 -> x1, local copies, waits for them, and re-layouts: none -> 1.68 us  [right_of(): blocks.transpose(2, 0, 1, 3)]
    unnamed x13 -> x11, local copies, waits for them, and re-layouts: 12.8 us -> 11.4 us
    dot_general x1 -> x2, matrix products: 2.97 us -> 1.68 us  [right_of(): jnp.einsum('jkr,rjm->jkm', blocks, upstream, preferred_element_type=jnp.f...]
  transfers between devices with their start and end apart: 6 -> 6, of which waited for: 4 -> 4; matrix products, arithmetic and copies ran while one was open for 19% -> 21% of each run, Pallas kernels for 0% -> 0%
where the time goes in v4:
time: 128 us; the launch traced here: 127 us
  waiting for transfers between devices  76.8 us (60%)
  local copies, waits for them, and re-layouts  16.2 us (13%)
  starting transfers between devices  12 us (9%)
  matrix products  11.2 us (9%)
  other arithmetic  10.3 us (8%)
    all_to_all x1, waiting for transfers between devices, on_device(): mixed_got = lax.all_to_all(mixed_sent, 'blk', 0, 0, tiled=True)  41.8 us
    all_to_all x1, waiting for transfers between devices, on_device(): back_got = lax.all_to_all(back_sent, 'blk', 0, 0, tiled=True)  32.9 us
    unnamed x11, local copies, waits for them, and re-layouts  11.4 us
    dot_general x2, matrix products, left_of(): jnp.einsum('rki,kjr->kij', rows, back_t, preferred_element_type=jnp.float32)  7.63 us
    all_to_all x1, starting transfers between devices, on_device(): back_got = lax.all_to_all(back_sent, 'blk', 0, 0, tiled=True)  6.84 us
    all_to_all x1, starting transfers between devices, on_device(): mixed_got = lax.all_to_all(mixed_sent, 'blk', 0, 0, tiled=True)  4.36 us
    convert_element_type x1, other arithmetic, on_device(): (lax.optimization_barrier(left_of(core * half_size)) + got_left).astype(j...  4.25 us
    select_n x2, other arithmetic, swap_halves(): first = jnp.where(core == 0, local, other)  2.85 us
  transfers between devices with their start and end apart: 6, of which 4 were waited for; matrix products, arithmetic and copies ran while one was open for 21% of the time, Pallas kernels for 0%

profile of v4, /device:TPU:0, one launch (start us, length us, event | category | flops | bytes accessed | tf_op | source)
XLA Modules:
  0.0 127.2 jit_solution(15093464489477778336)
XLA Ops:
  0.6 0.5 collective-permute-start.1
  1.1 3.3 %copy.33 = bf16[256,4096]{0,1:T(8,128)(2,1)S(1)} copy(bf16[256,4096]{1,0:T(8,128)(2,1)} %param.6) | data formatting | bytes 4194304 | tf_op args[1]
  4.5 0.0 collective-permute-done.1
  4.5 0.0 copy-done.2
  4.5 0.1 broadcast_select_fusion.3
  4.6 0.7 convert_bitcast_fusion
  5.3 1.5 %copy.34 = bf16[8,8,64,256]{3,1,2,0:T(8,128)(2,1)} copy(bf16[8,8,64,256]{3,1,0,2:T(8,128)(2,1)S(1)} %convert_bitcast_fusion) | data formatting | bytes 4194304 | tf_op jit(solution)/shard_map/reshape | solution.py:29
  6.7 6.8 %all-to-all-start = ((bf16[8,8,64,256]{3,1,2,0:T(8,128)(2,1)}), bf16[8,8,64,256]{3,1,2,0:T(8,128)(2,1)}, u32[]{:S(2)}, u32[]{:S(2)}) async-start(bf16[8,8,64,256]{3,1,2,0:T(8,128)(2,1)} %copy.34), calls=%async_computation | async-start | bytes 4194304 | tf_op jit(solution)/shard_map/all_to_all | solution.py:30
  13.6 3.9 %copy.29 = bf16[8,256,512]{1,2,0:T(8,128)(2,1)} copy(bf16[8,256,512]{2,1,0:T(8,128)(2,1)} %param.7) | data formatting | bytes 4194304 | tf_op args[2]
  17.5 0.2 collective-permute-start
  17.7 4.1 %copy.27 = bf16[256,4096]{0,1:T(8,128)(2,1)} copy(bf16[256,4096]{1,0:T(8,128)(2,1)} %param.5) | data formatting | bytes 4194304 | tf_op args[0]
  21.8 0.1 fusion.22
  21.9 2.1 %broadcast_multiply_fusion = bf16[256,8,512]{0,2,1:T(8,128)(2,1)S(1)} fusion(bf16[256,8,512]{0,2,1:T(8,128)(2,1)} %bitcast.33, bf16[8,512]{1,0:T(8,128)(2,1)S(1)} %fusion.22), kind=kLoop, calls=%fused_computation.28 | loop fusion | flops 1048576 | bytes 4202496 | tf_op jit(solution)/shard_map/mul | solution.py:33
  24.0 0.0 collective-permute-done
  24.0 0.1 copy-done
  24.1 2.8 %broadcast_select_fusion.1 = (bf16[8,256,512]{1,2,0:T(8,128)(2,1)S(1)}, bf16[8,256,512]{1,2,0:T(8,128)(2,1)S(1)}) fusion(bf16[8,256,512]{1,2,0:T(8,128)(2,1)S(1)} %copy-done, bf16[8,256,512]{1,2,0:T(8,128)(2,1)} %collective-permute-done, pred[]{:T(512)S(6)} %eq.2), kind=kLoop, calls=%fused_computation.8 | loop fusion | flops 2097152 | bytes 8388609 | tf_op jit(solution)/shard_map/jit(_where)/select_n | solution.py:10
  26.9 1.3 fusion.4
  28.1 1.6 %copy.53 = bf16[8,64,8,256]{3,1,2,0:T(8,128)(2,1)} copy(bf16[8,64,8,256]{3,1,0,2:T(8,128)(2,1)S(1)} %bitcast.34) | data formatting | bytes 4194304 | tf_op jit(solution)/shard_map/reshape | solution.py:38
  29.7 32.9 %all-to-all-done = bf16[8,8,64,256]{3,1,2,0:T(8,128)(2,1)} async-done(((bf16[8,8,64,256]{3,1,2,0:T(8,128)(2,1)}), bf16[8,8,64,256]{3,1,2,0:T(8,128)(2,1)}, u32[]{:S(2)}, u32[]{:S(2)}) %all-to-all-start) | async-done | bytes 2097184 | tf_op jit(solution)/shard_map/all_to_all | solution.py:30
  62.6 4.8 %fusion.7 = f32[8,256,512]{2,1,0:T(8,128)} fusion(bf16[8,512,256]{2,0,1:T(8,128)(2,1)} %bitcast.8, bf16[256,8,512]{0,2,1:T(8,128)(2,1)} %copy-done.1, s32[]{:T(128)S(6)} %select_n.43), kind=kOutput, calls=%fused_computation.10 | convolution fusion | flops 536870912 | bytes 7340036 | tf_op jit(solution)/shard_map/rki,kjr->kij/dot_general | solution.py:47
  67.3 0.0 collective-permute-start.2
  67.3 4.4 %all-to-all-start.1 = ((bf16[8,8,64,256]{3,2,1,0:T(8,128)(2,1)}), bf16[8,8,64,256]{3,2,1,0:T(8,128)(2,1)}, u32[]{:S(2)}, u32[]{:S(2)}) async-start(bf16[8,8,64,256]{3,2,1,0:T(8,128)(2,1)} %bitcast.32), calls=%async_computation.1 | async-start | bytes 4194304 | tf_op jit(solution)/shard_map/all_to_all | solution.py:51
  71.7 2.8 %fusion.9 = f32[8,256,512]{2,1,0:T(8,128)S(1)} fusion(bf16[8,512,256]{2,0,1:T(8,128)(2,1)} %bitcast.8, bf16[256,8,512]{0,2,1:T(8,128)(2,1)} %copy-done.1, s32[]{:T(128)S(6)} %select_n.36), kind=kOutput, calls=%fused_computation.12 | convolution fusion | flops 536870912 | bytes 7340036 | tf_op jit(solution)/shard_map/rki,kjr->kij/dot_general | solution.py:47
  74.6 0.3 collective-permute-done.2
  74.8 4.2 %add_convert_fusion = bf16[8,256,512]{2,1,0:T(8,128)(2,1)} fusion(f32[8,256,512]{2,1,0:T(8,128)S(1)} %fusion.9, f32[8,256,512]{2,1,0:T(8,128)} %collective-permute-done.2), kind=kLoop, calls=%fused_computation.4 | loop fusion | flops 2097152 | bytes 10485760 | tf_op jit(solution)/shard_map/convert_element_type | solution.py:53
  79.1 41.8 %all-to-all-done.1 = bf16[8,8,64,256]{3,2,1,0:T(8,128)(2,1)} async-done(((bf16[8,8,64,256]{3,2,1,0:T(8,128)(2,1)}), bf16[8,8,64,256]{3,2,1,0:T(8,128)(2,1)}, u32[]{:S(2)}, u32[]{:S(2)}) %all-to-all-start.1) | async-done | bytes 2097184 | tf_op jit(solution)/shard_map/all_to_all | solution.py:51
  120.9 1.7 %dynamic-slice_bitcast_fusion = (bf16[64,4,8,256]{3,0,2,1:T(8,128)(2,1)S(1)}, bf16[64,4,8,256]{3,0,2,1:T(8,128)(2,1)S(1)}) fusion(bf16[8,8,64,256]{3,2,1,0:T(8,128)(2,1)} %all-to-all-done.1, s32[]{:T(128)S(6)} %select_n.45, s32[]{:T(128)S(6)} %select_n.44), kind=kLoop, calls=%fused_computation.24 | loop fusion | bytes 4194312 | tf_op jit(solution)/shard_map/transpose | solution.py:59
  122.6 0.8 fusion.14
  123.4 0.1 collective-permute-start.3
  123.5 0.8 fusion.16
  124.3 1.8 %collective-permute-done.3 = f32[64,32,64]{2,1,0:T(8,128)S(1)} collective-permute-done((f32[64,32,64]{2,1,0:T(8,128)S(1)}, f32[64,32,64]{2,1,0:T(8,128)S(1)}, u32[]{:S(2)}, u32[]{:S(2)}) %collective-permute-start.3) | collective-permute-done | bytes 524320 | tf_op jit(solution)/shard_map/ppermute | solution.py:62
  126.1 1.0 add_convert_fusion.1
  (6 shorter events, 0.0 us)
Async XLA Ops:
  0.6 3.9 %collective-permute-start.1 = (bf16[64,32,64]{2,1,0:T(8,128)(2,1)}, bf16[64,32,64]{2,1,0:T(8,128)(2,1)S(1)}, u32[]{:S(2)}, u32[]{:S(2)}) collective-permute-start(bf16[64,32,64]{2,1,0:T(8,128)(2,1)} %param.8), channel_id=1, source_target_pairs={{0,1},{1,0},{2,3},{3,2},{4,5},{5,4},{6,7},{7,6},{8,9},{9,8},{10,11... | collective-permute-start | bytes 786440 | tf_op jit(solution)/shard_map/ppermute | solution.py:8
  1.1 3.4 %copy-start.2 = (bf16[64,32,64]{2,1,0:T(8,128)(2,1)S(1)}, bf16[64,32,64]{2,1,0:T(8,128)(2,1)}, u32[]{:S(2)}) copy-start(bf16[64,32,64]{2,1,0:T(8,128)(2,1)} %param.8) | copy-start | bytes 786436
  6.7 55.8 %all-to-all-start = ((bf16[8,8,64,256]{3,1,2,0:T(8,128)(2,1)}), bf16[8,8,64,256]{3,1,2,0:T(8,128)(2,1)}, u32[]{:S(2)}, u32[]{:S(2)}) async-start(bf16[8,8,64,256]{3,1,2,0:T(8,128)(2,1)} %copy.34), calls=%async_computation | async-start | bytes 4194304 | tf_op jit(solution)/shard_map/all_to_all | solution.py:30
  17.5 6.5 %collective-permute-start = (bf16[8,256,512]{1,2,0:T(8,128)(2,1)}, bf16[8,256,512]{1,2,0:T(8,128)(2,1)}, u32[]{:S(2)}, u32[]{:S(2)}) collective-permute-start(bf16[8,256,512]{1,2,0:T(8,128)(2,1)} %copy.29), channel_id=1, source_target_pairs={{0,1},{1,0},{2,3},{3,2},{4,5},{5,4},{6,7},{7,6},{8,9},{9,8},{10,11... | collective-permute-start | bytes 6291464 | tf_op jit(solution)/shard_map/ppermute | solution.py:8
  17.7 4.1 %copy-start.3 = (s32[8]{0:T(128)S(1)}, s32[8]{0:T(128)}, u32[]{:S(2)}) copy-start(s32[8]{0:T(128)} %param.9) | copy-start | bytes 100
  21.9 2.2 %copy-start = (bf16[8,256,512]{1,2,0:T(8,128)(2,1)S(1)}, bf16[8,256,512]{1,2,0:T(8,128)(2,1)}, u32[]{:S(2)}) copy-start(bf16[8,256,512]{1,2,0:T(8,128)(2,1)} %copy.29) | copy-start | bytes 6291460
  23.9 2.9 %copy-start.1 = (bf16[256,8,512]{0,2,1:T(8,128)(2,1)}, bf16[256,8,512]{0,2,1:T(8,128)(2,1)S(1)}, u32[]{:S(2)}) copy-start(bf16[256,8,512]{0,2,1:T(8,128)(2,1)S(1)} %broadcast_multiply_fusion) | copy-start | bytes 6291460
  67.3 7.5 %collective-permute-start.2 = (f32[8,256,512]{2,1,0:T(8,128)}, f32[8,256,512]{2,1,0:T(8,128)}, u32[]{:S(2)}, u32[]{:S(2)}) collective-permute-start(f32[8,256,512]{2,1,0:T(8,128)} %fusion.7), channel_id=1, source_target_pairs={{0,1},{1,0},{2,3},{3,2},{4,5},{5,4},{6,7},{7,6},{8,9},{9,8},{10,11... | collective-permute-start | bytes 12582920 | tf_op jit(solution)/shard_map/ppermute | solution.py:52
  67.3 53.6 %all-to-all-start.1 = ((bf16[8,8,64,256]{3,2,1,0:T(8,128)(2,1)}), bf16[8,8,64,256]{3,2,1,0:T(8,128)(2,1)}, u32[]{:S(2)}, u32[]{:S(2)}) async-start(bf16[8,8,64,256]{3,2,1,0:T(8,128)(2,1)} %bitcast.32), calls=%async_computation.1 | async-start | bytes 4194304 | tf_op jit(solution)/shard_map/all_to_all | solution.py:51
  123.4 2.7 %collective-permute-start.3 = (f32[64,32,64]{2,1,0:T(8,128)S(1)}, f32[64,32,64]{2,1,0:T(8,128)S(1)}, u32[]{:S(2)}, u32[]{:S(2)}) collective-permute-start(f32[64,32,64]{2,1,0:T(8,128)S(1)} %fusion.14), channel_id=1, source_target_pairs={{0,1},{1,0},{2,3},{3,2},{4,5},{5,4},{6,7},{7,6},{8,9},{9,8},{10,11... | collective-permute-start | bytes 1572872 | tf_op jit(solution)/shard_map/ppermute | solution.py:62

commit v5 on v4

--- a/solution.py
+++ b/solution.py
@@ -42,15 +42,20 @@
     core = lax.axis_index("bin")
     back_t = back_got.transpose(1, 0, 2, 3).reshape(local_blocks, block_size, row_count)
 
-    def left_of(start):
+    def left_of(start, back_part):
         rows = lax.dynamic_slice_in_dim(inputs, start, half_size, axis=2)
-        return jnp.einsum("rki,kjr->kij", rows, back_t, preferred_element_type=jnp.float32)
+        return jnp.einsum("rki,kjr->kij", rows, back_part, preferred_element_type=jnp.float32)
 
-    theirs = left_of((1 - core) * half_size)
-    mixed_sent, theirs = lax.optimization_barrier((mixed_sent, theirs))
+    half_cols = block_size // 2
+    theirs_start = (1 - core) * half_size
+    theirs_a = left_of(theirs_start, back_t[:, :half_cols])
+    mixed_sent, theirs_a = lax.optimization_barrier((mixed_sent, theirs_a))
     mixed_got = lax.all_to_all(mixed_sent, "blk", 0, 0, tiled=True)
-    got_left = lax.ppermute(theirs, "bin", [(0, 1), (1, 0)])
-    grad_left = (lax.optimization_barrier(left_of(core * half_size)) + got_left).astype(jnp.bfloat16)
+    got_a = lax.ppermute(theirs_a, "bin", [(0, 1), (1, 0)])
+    got_b = lax.ppermute(left_of(theirs_start, back_t[:, half_cols:]), "bin", [(0, 1), (1, 0)])
+    got_left = jnp.concatenate([got_a, got_b], axis=2)
+    mine = lax.optimization_barrier(left_of(core * half_size, back_t))
+    grad_left = (mine + got_left).astype(jnp.bfloat16)
     grad_left, mixed_got = lax.optimization_barrier((grad_left, mixed_got))
     half_peers = peer_count // 2
 

time: 128 us -> 127 us (level)
  waiting for transfers between devices: 76.8 us -> 71.9 us
  local copies, waits for them, and re-layouts: 16.2 us -> 19.7 us
    all_to_all x1, waiting for transfers between devices: 41.8 us -> 32.9 us  [on_device(): mixed_got = lax.all_to_all(mixed_sent, 'blk', 0, 0, tiled=True)]
    ppermute x1 -> x2, waiting for transfers between devices: 0.27 us -> 4.33 us  [the longest x1 3 us: on_device(): lax.ppermute(left_of(theirs_start, back_t[:, half_cols:]), 'bin', [(0, 1)...]
    transpose x0 -> x1, local copies, waits for them, and re-layouts: none -> 2.23 us  [on_device(): back_got.transpose(1, 0, 2, 3).reshape(local_blocks, block_size, row_count)]
    unnamed x11 -> x15, local copies, waits for them, and re-layouts: 11.4 us -> 12.8 us
    dot_general x2 -> x3, matrix products: 7.63 us -> 7.89 us  [left_of(): jnp.einsum('rki,kjr->kij', rows, back_part, preferred_element_type=jnp.fl...]
  transfers between devices with their start and end apart: 6 -> 7, of which waited for: 4 -> 5; matrix products, arithmetic and copies ran while one was open for 21% -> 24% of each run, Pallas kernels for 0% -> 0%
where the time goes in v5:
time: 127 us
  waiting for transfers between devices  71.9 us (57%)
  local copies, waits for them, and re-layouts  19.7 us (16%)
  starting transfers between devices  12.5 us (10%)
  matrix products  11.5 us (9%)
  other arithmetic  10.2 us (8%)
    all_to_all x1, waiting for transfers between devices, on_device(): mixed_got = lax.all_to_all(mixed_sent, 'blk', 0, 0, tiled=True)  32.9 us
    all_to_all x1, waiting for transfers between devices, on_device(): back_got = lax.all_to_all(back_sent, 'blk', 0, 0, tiled=True)  32.8 us
    unnamed x15, local copies, waits for them, and re-layouts  12.8 us
    dot_general x3, matrix products, left_of(): jnp.einsum('rki,kjr->kij', rows, back_part, preferred_element_type=jnp.fl...  7.89 us
    all_to_all x1, starting transfers between devices, on_device(): back_got = lax.all_to_all(back_sent, 'blk', 0, 0, tiled=True)  6.84 us
    all_to_all x1, starting transfers between devices, on_device(): mixed_got = lax.all_to_all(mixed_sent, 'blk', 0, 0, tiled=True)  4.36 us
    convert_element_type x1, other arithmetic, on_device(): grad_left = (mine + got_left).astype(jnp.bfloat16)  4.18 us
    ppermute x1, waiting for transfers between devices, on_device(): lax.ppermute(left_of(theirs_start, back_t[:, half_cols:]), 'bin', [(0, 1)...  3 us
  transfers between devices with their start and end apart: 7, of which 5 were waited for; matrix products, arithmetic and copies ran while one was open for 24% of the time, Pallas kernels for 0%

profile of v5, /device:TPU:0, one launch (start us, length us, event | category | flops | bytes accessed | tf_op | source)
XLA Modules:
  0.0 126.6 jit_solution(7071172929635253300)
XLA Ops:
  0.6 0.5 collective-permute-start.1
  1.1 3.3 %copy.33 = bf16[256,4096]{0,1:T(8,128)(2,1)S(1)} copy(bf16[256,4096]{1,0:T(8,128)(2,1)} %param.6) | data formatting | bytes 4194304 | tf_op args[1]
  4.5 0.1 broadcast_select_fusion.3
  4.6 0.7 convert_bitcast_fusion
  5.3 1.5 %copy.34 = bf16[8,8,64,256]{3,1,2,0:T(8,128)(2,1)} copy(bf16[8,8,64,256]{3,1,0,2:T(8,128)(2,1)S(1)} %convert_bitcast_fusion) | data formatting | bytes 4194304 | tf_op jit(solution)/shard_map/reshape | solution.py:29
  6.7 6.8 %all-to-all-start = ((bf16[8,8,64,256]{3,1,2,0:T(8,128)(2,1)}), bf16[8,8,64,256]{3,1,2,0:T(8,128)(2,1)}, u32[]{:S(2)}, u32[]{:S(2)}) async-start(bf16[8,8,64,256]{3,1,2,0:T(8,128)(2,1)} %copy.34), calls=%async_computation | async-start | bytes 4194304 | tf_op jit(solution)/shard_map/all_to_all | solution.py:30
  13.6 3.9 %copy.29 = bf16[8,256,512]{1,2,0:T(8,128)(2,1)} copy(bf16[8,256,512]{2,1,0:T(8,128)(2,1)} %param.7) | data formatting | bytes 4194304 | tf_op args[2]
  17.5 0.2 collective-permute-start
  17.7 4.1 %copy.27 = bf16[256,4096]{0,1:T(8,128)(2,1)} copy(bf16[256,4096]{1,0:T(8,128)(2,1)} %param.5) | data formatting | bytes 4194304 | tf_op args[0]
  21.8 0.1 fusion.25
  21.9 2.1 %broadcast_multiply_fusion = bf16[256,8,512]{0,2,1:T(8,128)(2,1)S(1)} fusion(bf16[256,8,512]{0,2,1:T(8,128)(2,1)} %bitcast.36, bf16[8,512]{1,0:T(8,128)(2,1)S(1)} %fusion.25), kind=kLoop, calls=%fused_computation.29 | loop fusion | flops 1048576 | bytes 4202496 | tf_op jit(solution)/shard_map/mul | solution.py:33
  24.0 0.1 copy-done.3
  24.1 2.8 %broadcast_select_fusion.1 = (bf16[8,256,512]{1,2,0:T(8,128)(2,1)S(1)}, bf16[8,256,512]{1,2,0:T(8,128)(2,1)S(1)}) fusion(bf16[8,256,512]{1,2,0:T(8,128)(2,1)S(1)} %copy-done.3, bf16[8,256,512]{1,2,0:T(8,128)(2,1)} %collective-permute-done, pred[]{:T(512)S(6)} %eq.2), kind=kLoop, calls=%fused_computation.9 | loop fusion | flops 2097152 | bytes 8388609 | tf_op jit(solution)/shard_map/jit(_where)/select_n | solution.py:10
  26.9 1.3 fusion.5
  28.1 1.6 %copy.48 = bf16[8,64,8,256]{3,1,2,0:T(8,128)(2,1)} copy(bf16[8,64,8,256]{3,1,0,2:T(8,128)(2,1)S(1)} %bitcast.37) | data formatting | bytes 4194304 | tf_op jit(solution)/shard_map/reshape | solution.py:38
  29.7 32.8 %all-to-all-done = bf16[8,8,64,256]{3,1,2,0:T(8,128)(2,1)} async-done(((bf16[8,8,64,256]{3,1,2,0:T(8,128)(2,1)}), bf16[8,8,64,256]{3,1,2,0:T(8,128)(2,1)}, u32[]{:S(2)}, u32[]{:S(2)}) %all-to-all-start) | async-done | bytes 2097184 | tf_op jit(solution)/shard_map/all_to_all | solution.py:30
  62.6 2.2 %copy.35 = bf16[8,8,64,256]{3,2,1,0:T(8,128)(2,1)S(1)} copy(bf16[8,8,64,256]{3,0,2,1:T(8,128)(2,1)} %bitcast.7) | data formatting | bytes 4194304 | tf_op jit(solution)/shard_map/transpose | solution.py:43
  64.8 1.3 %copy-done = bf16[8,8,64,256]{3,2,1,0:T(8,128)(2,1)} copy-done((bf16[8,8,64,256]{3,2,1,0:T(8,128)(2,1)}, bf16[8,8,64,256]{3,2,1,0:T(8,128)(2,1)S(1)}, u32[]{:S(2)}) %copy-start) | copy-done | bytes 2097176
  66.1 1.8 %fusion.10 = f32[8,256,256]{2,1,0:T(8,128)} fusion(bf16[8,512,256]{2,1,0:T(8,128)(2,1)S(1)} %bitcast.32, bf16[256,8,512]{0,2,1:T(8,128)(2,1)S(1)} %copy-done.2, s32[]{:T(128)S(6)} %select_n.44), kind=kOutput, calls=%fused_computation.13 | convolution fusion | flops 268435456 | bytes 4194308 | tf_op jit(solution)/shard_map/rki,kjr->kij/dot_general | solution.py:47
  67.9 4.4 %all-to-all-start.1 = ((bf16[8,8,64,256]{3,2,1,0:T(8,128)(2,1)}), bf16[8,8,64,256]{3,2,1,0:T(8,128)(2,1)}, u32[]{:S(2)}, u32[]{:S(2)}) async-start(bf16[8,8,64,256]{3,2,1,0:T(8,128)(2,1)} %bitcast.35), calls=%async_computation.1 | async-start | bytes 4194304 | tf_op jit(solution)/shard_map/all_to_all | solution.py:53
  72.3 3.4 %fusion.8 = f32[8,256,256]{2,1,0:T(8,128)} fusion(bf16[8,512,256]{2,1,0:T(8,128)(2,1)} %bitcast.33, bf16[256,8,512]{0,2,1:T(8,128)(2,1)} %copy-done.1, s32[]{:T(128)S(6)} %select_n.44), kind=kOutput, calls=%fused_computation.11 | convolution fusion | flops 268435456 | bytes 4194308 | tf_op jit(solution)/shard_map/rki,kjr->kij/dot_general | solution.py:47
  75.7 0.5 collective-permute-start.3
  76.2 2.7 %fusion.21 = f32[8,256,512]{2,1,0:T(8,128)S(1)} fusion(bf16[8,512,256]{2,1,0:T(8,128)(2,1)} %bitcast.34, bf16[256,8,512]{0,2,1:T(8,128)(2,1)} %copy-done.1, s32[]{:T(128)S(6)} %select_n.37), kind=kOutput, calls=%fused_computation.27 | convolution fusion | flops 536870912 | bytes 7340036 | tf_op jit(solution)/shard_map/rki,kjr->kij/dot_general | solution.py:47
  78.9 1.3 %collective-permute-done.2 = f32[8,256,256]{2,1,0:T(8,128)} collective-permute-done((f32[8,256,256]{2,1,0:T(8,128)}, f32[8,256,256]{2,1,0:T(8,128)}, u32[]{:S(2)}, u32[]{:S(2)}) %collective-permute-start.2) | collective-permute-done | bytes 2097184 | tf_op jit(solution)/shard_map/ppermute | solution.py:54
  80.2 3.0 %collective-permute-done.3 = f32[8,256,256]{2,1,0:T(8,128)} collective-permute-done((f32[8,256,256]{2,1,0:T(8,128)}, f32[8,256,256]{2,1,0:T(8,128)}, u32[]{:S(2)}, u32[]{:S(2)}) %collective-permute-start.3) | collective-permute-done | bytes 2097184 | tf_op jit(solution)/shard_map/ppermute | solution.py:55
  83.2 4.2 %fusion.4 = bf16[8,256,512]{2,1,0:T(8,128)(2,1)} fusion(f32[8,256,512]{2,1,0:T(8,128)S(1)} %fusion.21, f32[8,256,256]{2,1,0:T(8,128)} %collective-permute-done.3, f32[8,256,256]{2,1,0:T(8,128)} %collective-permute-done.2), kind=kLoop, calls=%fused_computation.5 | loop fusion | flops 3145728 | bytes 10485760 | tf_op jit(solution)/shard_map/convert_element_type | solution.py:58
  87.4 32.9 %all-to-all-done.1 = bf16[8,8,64,256]{3,2,1,0:T(8,128)(2,1)} async-done(((bf16[8,8,64,256]{3,2,1,0:T(8,128)(2,1)}), bf16[8,8,64,256]{3,2,1,0:T(8,128)(2,1)}, u32[]{:S(2)}, u32[]{:S(2)}) %all-to-all-start.1) | async-done | bytes 2097184 | tf_op jit(solution)/shard_map/all_to_all | solution.py:53
  120.3 1.7 %dynamic-slice_bitcast_fusion = (bf16[64,4,8,256]{3,0,2,1:T(8,128)(2,1)S(1)}, bf16[64,4,8,256]{3,0,2,1:T(8,128)(2,1)S(1)}) fusion(bf16[8,8,64,256]{3,2,1,0:T(8,128)(2,1)} %all-to-all-done.1, s32[]{:T(128)S(6)} %select_n.46, s32[]{:T(128)S(6)} %select_n.45), kind=kLoop, calls=%fused_computation.25 | loop fusion | bytes 4194312 | tf_op jit(solution)/shard_map/transpose | solution.py:64
  122.0 0.8 fusion.15
  122.9 0.8 fusion.17
  123.8 1.8 %collective-permute-done.4 = f32[64,32,64]{2,1,0:T(8,128)S(1)} collective-permute-done((f32[64,32,64]{2,1,0:T(8,128)S(1)}, f32[64,32,64]{2,1,0:T(8,128)S(1)}, u32[]{:S(2)}, u32[]{:S(2)}) %collective-permute-start.4) | collective-permute-done | bytes 524320 | tf_op jit(solution)/shard_map/ppermute | solution.py:67
  125.6 1.0 add_convert_fusion
  (14 shorter events, 0.1 us)
Async XLA Ops:
  0.6 3.9 %collective-permute-start.1 = (bf16[64,32,64]{2,1,0:T(8,128)(2,1)}, bf16[64,32,64]{2,1,0:T(8,128)(2,1)S(1)}, u32[]{:S(2)}, u32[]{:S(2)}) collective-permute-start(bf16[64,32,64]{2,1,0:T(8,128)(2,1)} %param.8), channel_id=1, source_target_pairs={{0,1},{1,0},{2,3},{3,2},{4,5},{5,4},{6,7},{7,6},{8,9},{9,8},{10,11... | collective-permute-start | bytes 786440 | tf_op jit(solution)/shard_map/ppermute | solution.py:8
  1.1 3.4 %copy-start.4 = (bf16[64,32,64]{2,1,0:T(8,128)(2,1)S(1)}, bf16[64,32,64]{2,1,0:T(8,128)(2,1)}, u32[]{:S(2)}) copy-start(bf16[64,32,64]{2,1,0:T(8,128)(2,1)} %param.8) | copy-start | bytes 786436
  6.7 55.8 %all-to-all-start = ((bf16[8,8,64,256]{3,1,2,0:T(8,128)(2,1)}), bf16[8,8,64,256]{3,1,2,0:T(8,128)(2,1)}, u32[]{:S(2)}, u32[]{:S(2)}) async-start(bf16[8,8,64,256]{3,1,2,0:T(8,128)(2,1)} %copy.34), calls=%async_computation | async-start | bytes 4194304 | tf_op jit(solution)/shard_map/all_to_all | solution.py:30
  17.5 6.5 %collective-permute-start = (bf16[8,256,512]{1,2,0:T(8,128)(2,1)}, bf16[8,256,512]{1,2,0:T(8,128)(2,1)}, u32[]{:S(2)}, u32[]{:S(2)}) collective-permute-start(bf16[8,256,512]{1,2,0:T(8,128)(2,1)} %copy.29), channel_id=1, source_target_pairs={{0,1},{1,0},{2,3},{3,2},{4,5},{5,4},{6,7},{7,6},{8,9},{9,8},{10,11... | collective-permute-start | bytes 6291464 | tf_op jit(solution)/shard_map/ppermute | solution.py:8
  17.7 4.1 %copy-start.5 = (s32[8]{0:T(128)S(1)}, s32[8]{0:T(128)}, u32[]{:S(2)}) copy-start(s32[8]{0:T(128)} %param.9) | copy-start | bytes 100
  21.9 2.2 %copy-start.3 = (bf16[8,256,512]{1,2,0:T(8,128)(2,1)S(1)}, bf16[8,256,512]{1,2,0:T(8,128)(2,1)}, u32[]{:S(2)}) copy-start(bf16[8,256,512]{1,2,0:T(8,128)(2,1)} %copy.29) | copy-start | bytes 6291460
  24.0 2.9 %copy-start.1 = (bf16[256,8,512]{0,2,1:T(8,128)(2,1)}, bf16[256,8,512]{0,2,1:T(8,128)(2,1)S(1)}, u32[]{:S(2)}) copy-start(bf16[256,8,512]{0,2,1:T(8,128)(2,1)S(1)} %broadcast_multiply_fusion) | copy-start | bytes 6291460
  62.6 3.6 %copy-start.2 = (bf16[256,8,512]{0,2,1:T(8,128)(2,1)S(1)}, bf16[256,8,512]{0,2,1:T(8,128)(2,1)}, u32[]{:S(2)}) copy-start(bf16[256,8,512]{0,2,1:T(8,128)(2,1)} %copy-done.1) | copy-start | bytes 6291460
  64.8 1.3 %copy-start = (bf16[8,8,64,256]{3,2,1,0:T(8,128)(2,1)}, bf16[8,8,64,256]{3,2,1,0:T(8,128)(2,1)S(1)}, u32[]{:S(2)}) copy-start(bf16[8,8,64,256]{3,2,1,0:T(8,128)(2,1)S(1)} %copy.35) | copy-start | bytes 6291460
  67.9 52.4 %all-to-all-start.1 = ((bf16[8,8,64,256]{3,2,1,0:T(8,128)(2,1)}), bf16[8,8,64,256]{3,2,1,0:T(8,128)(2,1)}, u32[]{:S(2)}, u32[]{:S(2)}) async-start(bf16[8,8,64,256]{3,2,1,0:T(8,128)(2,1)} %bitcast.35), calls=%async_computation.1 | async-start | bytes 4194304 | tf_op jit(solution)/shard_map/all_to_all | solution.py:53
  75.7 4.5 %collective-permute-start.2 = (f32[8,256,256]{2,1,0:T(8,128)}, f32[8,256,256]{2,1,0:T(8,128)}, u32[]{:S(2)}, u32[]{:S(2)}) collective-permute-start(f32[8,256,256]{2,1,0:T(8,128)} %fusion.10), channel_id=1, source_target_pairs={{0,1},{1,0},{2,3},{3,2},{4,5},{5,4},{6,7},{7,6},{8,9},{9,8},{10,11... | collective-permute-start | bytes 6291464 | tf_op jit(solution)/shard_map/ppermute | solution.py:54
  75.7 7.5 %collective-permute-start.3 = (f32[8,256,256]{2,1,0:T(8,128)}, f32[8,256,256]{2,1,0:T(8,128)}, u32[]{:S(2)}, u32[]{:S(2)}) collective-permute-start(f32[8,256,256]{2,1,0:T(8,128)} %fusion.8), channel_id=1, source_target_pairs={{0,1},{1,0},{2,3},{3,2},{4,5},{5,4},{6,7},{7,6},{8,9},{9,8},{10,11... | collective-permute-start | bytes 6291464 | tf_op jit(solution)/shard_map/ppermute | solution.py:55
  122.9 2.7 %collective-permute-start.4 = (f32[64,32,64]{2,1,0:T(8,128)S(1)}, f32[64,32,64]{2,1,0:T(8,128)S(1)}, u32[]{:S(2)}, u32[]{:S(2)}) collective-permute-start(f32[64,32,64]{2,1,0:T(8,128)S(1)} %fusion.15), channel_id=1, source_target_pairs={{0,1},{1,0},{2,3},{3,2},{4,5},{5,4},{6,7},{7,6},{8,9},{9,8},{10,11... | collective-permute-start | bytes 1572872 | tf_op jit(solution)/shard_map/ppermute | solution.py:67

commit v6 on v5

--- a/solution.py
+++ b/solution.py
@@ -1,7 +1,49 @@
+import functools
+
 import jax
 import jax.numpy as jnp
 from jax import lax
 from jax.sharding import PartitionSpec as P
+from jax.experimental import pallas as pl
+from jax.experimental.pallas import tpu as pltpu
+
+
+def _back_kernel(peer_count, local_blocks, group, cot_ref, right_ref, out_ref):
+    right_local, block_count, order = right_ref.shape
+    row_count = cot_ref.shape[0]
+    width = group * order
+
+    def body(step, carry):
+        start = pl.multiple_of(step * width, width)
+        cols = cot_ref[:, pl.ds(start, width)]
+        for h in range(group):
+            j = step * group + h
+            part = cols[:, h * order:(h + 1) * order]
+            res = lax.dot_general(
+                right_ref[j], part, (((1,), (1,)), ((), ())), preferred_element_type=jnp.float32
+            )
+            for p in range(peer_count):
+                out_ref[p, j] = res[p * local_blocks:(p + 1) * local_blocks].astype(out_ref.dtype)
+        return carry
+
+    lax.fori_loop(0, right_local // group, body, 0)
+
+
+def back_grads(cotangent, right_full, peer_count, local_blocks):
+    right_local, block_count, order = right_full.shape
+    row_count = cotangent.shape[0]
+    group = max(1, 128 // order)
+    return pl.pallas_call(
+        functools.partial(_back_kernel, peer_count, local_blocks, group),
+        out_shape=jax.ShapeDtypeStruct((peer_count, right_local, local_blocks, row_count), jnp.bfloat16),
+        in_specs=[pl.BlockSpec(memory_space=pltpu.VMEM)] * 2,
+        out_specs=pl.BlockSpec(memory_space=pltpu.VMEM),
+        cost_estimate=pl.CostEstimate(
+            flops=2 * row_count * right_local * block_count * order,
+            bytes_accessed=2 * (cotangent.size + right_full.size + row_count * right_local * block_count),
+            transcendentals=0,
+        ),
+    )(cotangent, right_full)
 
 
 def swap_halves(local, axis):
@@ -23,10 +65,7 @@
 
     upstream = cotangent.reshape(row_count, right_local, order_right)
     right_full = swap_halves(right_factor, 1)
-    back_grad = jnp.einsum(
-        "rjm,jkm->kjr", upstream, right_full, preferred_element_type=jnp.float32
-    ).astype(jnp.bfloat16)
-    back_sent = back_grad.reshape(peer_count, local_blocks, right_local, row_count)
+    back_sent = back_grads(cotangent, right_full, peer_count, local_blocks).transpose(0, 2, 1, 3)
     back_got = lax.all_to_all(back_sent, "blk", 0, 0, tiled=True)
 
     unit_mask = (jnp.arange(block_size)[None, :] < session_units[:, None]).astype(jnp.bfloat16)

time: 127 us -> 135 us (1.063)
  Pallas kernels: 0 us -> 10.7 us
  local copies, waits for them, and re-layouts: 19.7 us -> 17.3 us
  other arithmetic: 10.2 us -> 12.5 us
  waiting for transfers between devices: 71.9 us -> 70 us
    pallas_call x0 -> x1, Pallas kernels: none -> 10.7 us  [back_grads(): pl.pallas_call(functools.partial(_back_kernel, peer_count, local_blocks,...]
    transpose x1 -> x0, local copies, waits for them, and re-layouts: 2.23 us -> none  [on_device(): back_got.transpose(1, 0, 2, 3).reshape(local_blocks, block_size, row_count)]
    ppermute x1, waiting for transfers between devices: 3 us -> 0.85 us  [on_device(): lax.ppermute(left_of(theirs_start, back_t[:, half_cols:]), 'bin', [(0, 1)...]
    ppermute x2, waiting for transfers between devices: 0.01 us -> 1.75 us  [swap_halves(): other = lax.ppermute(local, 'bin', [(0, 1), (1, 0)])]
    unnamed x15 -> x17, local copies, waits for them, and re-layouts: 12.8 us -> 13.6 us
  transfers between devices with their start and end apart: 7 -> 7, of which waited for: 5 -> 5; matrix products, arithmetic and copies ran while one was open for 24% -> 22% of each run, Pallas kernels for 0% -> 0%
where the time goes in v6:
time: 135 us
  waiting for transfers between devices  70 us (52%)
  local copies, waits for them, and re-layouts  17.3 us (13%)
  starting transfers between devices  12.7 us (9%)
  other arithmetic  12.5 us (9%)
  Pallas kernels  10.7 us (8%)
  matrix products  10.7 us (8%)
    all_to_all x1, waiting for transfers between devices, on_device(): mixed_got = lax.all_to_all(mixed_sent, 'blk', 0, 0, tiled=True)  33 us
    all_to_all x1, waiting for transfers between devices, on_device(): back_got = lax.all_to_all(back_sent, 'blk', 0, 0, tiled=True)  32.6 us
    unnamed x17, local copies, waits for them, and re-layouts  13.6 us
    pallas_call x1, Pallas kernels, back_grads(): pl.pallas_call(functools.partial(_back_kernel, peer_count, local_blocks,...  10.7 us
    dot_general x3, matrix products, left_of(): jnp.einsum('rki,kjr->kij', rows, back_part, preferred_element_type=jnp.fl...  7.79 us
    all_to_all x1, starting transfers between devices, on_device(): back_got = lax.all_to_all(back_sent, 'blk', 0, 0, tiled=True)  7.17 us
    all_to_all x1, starting transfers between devices, on_device(): mixed_got = lax.all_to_all(mixed_sent, 'blk', 0, 0, tiled=True)  4.49 us
    convert_element_type x1, other arithmetic, on_device(): grad_left = (mine + got_left).astype(jnp.bfloat16)  4.18 us
  transfers between devices with their start and end apart: 7, of which 5 were waited for; matrix products, arithmetic and copies ran while one was open for 22% of the time, Pallas kernels for 0%

profile of v6, /device:TPU:0, one launch (start us, length us, event | category | flops | bytes accessed | tf_op | source)
XLA Modules:
  0.0 134.8 jit_solution(18125833555990964081)
XLA Ops:
  0.6 0.5 collective-permute-start.1
  1.1 1.7 %collective-permute-done.1 = bf16[64,32,64]{2,1,0:T(8,128)(2,1)S(1)} collective-permute-done((bf16[64,32,64]{2,1,0:T(8,128)(2,1)}, bf16[64,32,64]{2,1,0:T(8,128)(2,1)S(1)}, u32[]{:S(2)}, u32[]{:S(2)}) %collective-permute-start.1) | collective-permute-done | bytes 262176 | tf_op jit(solution)/shard_map/ppermute | solution.py:50
  2.9 1.1 broadcast_select_fusion.3
  4.0 1.3 pad_maximum_fusion.right_ref
  5.3 10.7 %shard_map.68 = bf16[8,64,8,256]{3,2,1,0:T(8,128)(2,1)} custom-call(bf16[256,4096]{1,0:T(8,128)(2,1)} %cot_ref.1, bf16[64,64,64]{2,1,0:T(8,128)(2,1)} %pad_maximum_fusion.right_ref), custom_call_target="tpu_custom_call" | custom-call | flops 134217728 | bytes 4718592 | tf_op jit(solution)/shard_map/pallas_call | solution.py:36
  16.0 7.2 %all-to-all-start = ((bf16[8,8,64,256]{3,1,2,0:T(8,128)(2,1)}), bf16[8,8,64,256]{3,1,2,0:T(8,128)(2,1)S(1)}, u32[]{:S(2)}, u32[]{:S(2)}) async-start(bf16[8,8,64,256]{3,1,2,0:T(8,128)(2,1)} %bitcast.30), calls=%async_computation | async-start | bytes 4194304 | tf_op jit(solution)/shard_map/all_to_all | solution.py:69
  23.2 3.9 %copy.32 = bf16[8,256,512]{1,2,0:T(8,128)(2,1)} copy(bf16[8,256,512]{2,1,0:T(8,128)(2,1)} %param.7) | data formatting | bytes 4194304 | tf_op args[2]
  27.1 4.1 %copy.30 = bf16[256,4096]{0,1:T(8,128)(2,1)} copy(bf16[256,4096]{1,0:T(8,128)(2,1)} %param.5) | data formatting | bytes 4194304 | tf_op args[0]
  31.2 0.1 fusion.22
  31.3 2.1 %broadcast_multiply_fusion = bf16[256,8,512]{0,2,1:T(8,128)(2,1)S(1)} fusion(bf16[256,8,512]{0,2,1:T(8,128)(2,1)} %bitcast.31, bf16[8,512]{1,0:T(8,128)(2,1)S(1)} %fusion.22), kind=kLoop, calls=%fused_computation.26 | loop fusion | flops 1048576 | bytes 4202496 | tf_op jit(solution)/shard_map/mul | solution.py:72
  33.4 0.1 copy-done.5
  33.5 2.8 %broadcast_select_fusion.1 = (bf16[8,256,512]{1,2,0:T(8,128)(2,1)S(1)}, bf16[8,256,512]{1,2,0:T(8,128)(2,1)S(1)}) fusion(bf16[8,256,512]{1,2,0:T(8,128)(2,1)S(1)} %copy-done.5, bf16[8,256,512]{1,2,0:T(8,128)(2,1)} %collective-permute-done, pred[]{:T(512)S(6)} %eq.2), kind=kLoop, calls=%fused_computation.8 | loop fusion | flops 2097152 | bytes 8388609 | tf_op jit(solution)/shard_map/jit(_where)/select_n | solution.py:52
  36.3 1.3 fusion.5
  37.5 1.6 %copy.54 = bf16[8,64,8,256]{3,1,2,0:T(8,128)(2,1)} copy(bf16[8,64,8,256]{3,1,0,2:T(8,128)(2,1)S(1)} %bitcast.32) | data formatting | bytes 4194304 | tf_op jit(solution)/shard_map/reshape | solution.py:77
  39.1 32.6 %all-to-all-done = bf16[8,8,64,256]{3,1,2,0:T(8,128)(2,1)S(1)} async-done(((bf16[8,8,64,256]{3,1,2,0:T(8,128)(2,1)}), bf16[8,8,64,256]{3,1,2,0:T(8,128)(2,1)S(1)}, u32[]{:S(2)}, u32[]{:S(2)}) %all-to-all-start) | async-done | bytes 2097184 | tf_op jit(solution)/shard_map/all_to_all | solution.py:69
  71.7 0.4 copy.36
  72.1 0.9 copy-done
  73.1 1.3 copy-done.4
  74.4 1.8 %fusion.10 = f32[8,256,256]{2,1,0:T(8,128)} fusion(bf16[8,512,256]{2,1,0:T(8,128)(2,1)S(1)} %copy.36, bf16[256,8,512]{0,2,1:T(8,128)(2,1)S(1)} %copy-done.2, s32[]{:T(128)S(6)} %select_n.44), kind=kOutput, calls=%fused_computation.12 | convolution fusion | flops 268435456 | bytes 4194308 | tf_op jit(solution)/shard_map/rki,kjr->kij/dot_general | solution.py:86
  76.2 4.5 %all-to-all-start.1 = ((bf16[8,8,64,256]{3,2,1,0:T(8,128)(2,1)}), bf16[8,8,64,256]{3,2,1,0:T(8,128)(2,1)}, u32[]{:S(2)}, u32[]{:S(2)}) async-start(bf16[8,8,64,256]{3,2,1,0:T(8,128)(2,1)} %bitcast.29), calls=%async_computation.1 | async-start | bytes 4194304 | tf_op jit(solution)/shard_map/all_to_all | solution.py:92
  80.7 3.1 %fusion.8 = f32[8,256,256]{2,1,0:T(8,128)} fusion(bf16[8,512,256]{2,1,0:T(8,128)(2,1)} %copy-done.4, bf16[256,8,512]{0,2,1:T(8,128)(2,1)S(1)} %copy-done.3, s32[]{:T(128)S(6)} %select_n.44), kind=kOutput, calls=%fused_computation.10 | convolution fusion | flops 268435456 | bytes 4194308 | tf_op jit(solution)/shard_map/rki,kjr->kij/dot_general | solution.py:86
  83.9 0.5 collective-permute-start.3
  84.4 3.3 %copy.40 = bf16[256,4096]{0,1:T(8,128)(2,1)S(1)} copy(bf16[256,4096]{1,0:T(8,128)(2,1)} %cot_ref.1) | data formatting | bytes 4194304 | tf_op args[1]
  87.6 2.9 %fusion.18 = f32[8,256,512]{2,1,0:T(8,128)S(1)} fusion(bf16[256,8,512]{0,2,1:T(8,128)(2,1)} %copy-done.1, s32[]{:T(128)S(6)} %select_n.37, bf16[8,512,256]{2,0,1:T(8,128)(2,1)} %bitcast.28), kind=kOutput, calls=%fused_computation.24 | convolution fusion | flops 536870912 | bytes 7340036 | tf_op jit(solution)/shard_map/rki,kjr->kij/dot_general | solution.py:86
  90.5 0.8 collective-permute-done.3
  91.4 4.2 %fusion.4 = bf16[8,256,512]{2,1,0:T(8,128)(2,1)} fusion(f32[8,256,512]{2,1,0:T(8,128)S(1)} %fusion.18, f32[8,256,256]{2,1,0:T(8,128)} %collective-permute-done.3, f32[8,256,256]{2,1,0:T(8,128)} %collective-permute-done.2), kind=kLoop, calls=%fused_computation.5 | loop fusion | flops 3145728 | bytes 10485760 | tf_op jit(solution)/shard_map/convert_element_type | solution.py:97
  95.5 33.0 %all-to-all-done.1 = bf16[8,8,64,256]{3,2,1,0:T(8,128)(2,1)} async-done(((bf16[8,8,64,256]{3,2,1,0:T(8,128)(2,1)}), bf16[8,8,64,256]{3,2,1,0:T(8,128)(2,1)}, u32[]{:S(2)}, u32[]{:S(2)}) %all-to-all-start.1) | async-done | bytes 2097184 | tf_op jit(solution)/shard_map/all_to_all | solution.py:92
  128.5 1.7 %dynamic-slice_bitcast_fusion = (bf16[64,4,8,256]{3,0,2,1:T(8,128)(2,1)S(1)}, bf16[64,4,8,256]{3,0,2,1:T(8,128)(2,1)S(1)}) fusion(bf16[8,8,64,256]{3,2,1,0:T(8,128)(2,1)} %all-to-all-done.1, s32[]{:T(128)S(6)} %select_n.46, s32[]{:T(128)S(6)} %select_n.45), kind=kLoop, calls=%fused_computation.22 | loop fusion | bytes 4194312 | tf_op jit(solution)/shard_map/transpose | solution.py:103
  130.2 0.8 fusion.12
  131.1 0.8 fusion.14
  132.0 1.8 %collective-permute-done.4 = f32[64,32,64]{2,1,0:T(8,128)S(1)} collective-permute-done((f32[64,32,64]{2,1,0:T(8,128)S(1)}, f32[64,32,64]{2,1,0:T(8,128)S(1)}, u32[]{:S(2)}, u32[]{:S(2)}) %collective-permute-start.4) | collective-permute-done | bytes 524320 | tf_op jit(solution)/shard_map/ppermute | solution.py:106
  133.8 1.0 add_convert_fusion
  (16 shorter events, 0.1 us)
Async XLA Ops:
  0.6 2.3 %collective-permute-start.1 = (bf16[64,32,64]{2,1,0:T(8,128)(2,1)}, bf16[64,32,64]{2,1,0:T(8,128)(2,1)S(1)}, u32[]{:S(2)}, u32[]{:S(2)}) collective-permute-start(bf16[64,32,64]{2,1,0:T(8,128)(2,1)} %param.8), channel_id=1, source_target_pairs={{0,1},{1,0},{2,3},{3,2},{4,5},{5,4},{6,7},{7,6},{8,9},{9,8},{10,11... | collective-permute-start | bytes 786440 | tf_op jit(solution)/shard_map/ppermute | solution.py:50
  16.0 55.7 %all-to-all-start = ((bf16[8,8,64,256]{3,1,2,0:T(8,128)(2,1)}), bf16[8,8,64,256]{3,1,2,0:T(8,128)(2,1)S(1)}, u32[]{:S(2)}, u32[]{:S(2)}) async-start(bf16[8,8,64,256]{3,1,2,0:T(8,128)(2,1)} %bitcast.30), calls=%async_computation | async-start | bytes 4194304 | tf_op jit(solution)/shard_map/all_to_all | solution.py:69
  27.1 4.1 %copy-start.6 = (s32[8]{0:T(128)S(1)}, s32[8]{0:T(128)}, u32[]{:S(2)}) copy-start(s32[8]{0:T(128)} %param.9) | copy-start | bytes 100
  27.1 6.3 %collective-permute-start = (bf16[8,256,512]{1,2,0:T(8,128)(2,1)}, bf16[8,256,512]{1,2,0:T(8,128)(2,1)}, u32[]{:S(2)}, u32[]{:S(2)}) collective-permute-start(bf16[8,256,512]{1,2,0:T(8,128)(2,1)} %copy.32), channel_id=1, source_target_pairs={{0,1},{1,0},{2,3},{3,2},{4,5},{5,4},{6,7},{7,6},{8,9},{9,8},{10,11... | collective-permute-start | bytes 6291464 | tf_op jit(solution)/shard_map/ppermute | solution.py:50
  31.3 2.2 %copy-start.5 = (bf16[8,256,512]{1,2,0:T(8,128)(2,1)S(1)}, bf16[8,256,512]{1,2,0:T(8,128)(2,1)}, u32[]{:S(2)}) copy-start(bf16[8,256,512]{1,2,0:T(8,128)(2,1)} %copy.32) | copy-start | bytes 6291460
  33.4 2.9 %copy-start.1 = (bf16[256,8,512]{0,2,1:T(8,128)(2,1)}, bf16[256,8,512]{0,2,1:T(8,128)(2,1)S(1)}, u32[]{:S(2)}) copy-start(bf16[256,8,512]{0,2,1:T(8,128)(2,1)S(1)} %broadcast_multiply_fusion) | copy-start | bytes 6291460
  71.7 1.4 %copy-start = (bf16[8,8,64,256]{3,1,2,0:T(8,128)(2,1)}, bf16[8,8,64,256]{3,1,2,0:T(8,128)(2,1)S(1)}, u32[]{:S(2)}) copy-start(bf16[8,8,64,256]{3,1,2,0:T(8,128)(2,1)S(1)} %all-to-all-done) | copy-start | bytes 6291460
  71.7 2.7 %copy-start.2 = (bf16[256,8,512]{0,2,1:T(8,128)(2,1)S(1)}, bf16[256,8,512]{0,2,1:T(8,128)(2,1)}, u32[]{:S(2)}) copy-start(bf16[256,8,512]{0,2,1:T(8,128)(2,1)} %copy-done.1) | copy-start | bytes 6291460
  73.1 1.3 copy-start.4
  76.2 4.5 %copy-start.3 = (bf16[256,8,512]{0,2,1:T(8,128)(2,1)S(1)}, bf16[256,8,512]{0,2,1:T(8,128)(2,1)}, u32[]{:S(2)}) copy-start(bf16[256,8,512]{0,2,1:T(8,128)(2,1)} %copy-done.1) | copy-start | bytes 6291460
  76.2 52.3 %all-to-all-start.1 = ((bf16[8,8,64,256]{3,2,1,0:T(8,128)(2,1)}), bf16[8,8,64,256]{3,2,1,0:T(8,128)(2,1)}, u32[]{:S(2)}, u32[]{:S(2)}) async-start(bf16[8,8,64,256]{3,2,1,0:T(8,128)(2,1)} %bitcast.29), calls=%async_computation.1 | async-start | bytes 4194304 | tf_op jit(solution)/shard_map/all_to_all | solution.py:92
  83.9 6.6 %collective-permute-start.2 = (f32[8,256,256]{2,1,0:T(8,128)}, f32[8,256,256]{2,1,0:T(8,128)}, u32[]{:S(2)}, u32[]{:S(2)}) collective-permute-start(f32[8,256,256]{2,1,0:T(8,128)} %fusion.10), channel_id=1, source_target_pairs={{0,1},{1,0},{2,3},{3,2},{4,5},{5,4},{6,7},{7,6},{8,9},{9,8},{10,11... | collective-permute-start | bytes 6291464 | tf_op jit(solution)/shard_map/ppermute | solution.py:93
  83.9 7.5 %collective-permute-start.3 = (f32[8,256,256]{2,1,0:T(8,128)}, f32[8,256,256]{2,1,0:T(8,128)}, u32[]{:S(2)}, u32[]{:S(2)}) collective-permute-start(f32[8,256,256]{2,1,0:T(8,128)} %fusion.8), channel_id=1, source_target_pairs={{0,1},{1,0},{2,3},{3,2},{4,5},{5,4},{6,7},{7,6},{8,9},{9,8},{10,11... | collective-permute-start | bytes 6291464 | tf_op jit(solution)/shard_map/ppermute | solution.py:94
  131.1 2.7 %collective-permute-start.4 = (f32[64,32,64]{2,1,0:T(8,128)S(1)}, f32[64,32,64]{2,1,0:T(8,128)S(1)}, u32[]{:S(2)}, u32[]{:S(2)}) collective-permute-start(f32[64,32,64]{2,1,0:T(8,128)S(1)} %fusion.12), channel_id=1, source_target_pairs={{0,1},{1,0},{2,3},{3,2},{4,5},{5,4},{6,7},{7,6},{8,9},{9,8},{10,11... | collective-permute-start | bytes 1572872 | tf_op jit(solution)/shard_map/ppermute | solution.py:106

commit v7 on v4

--- a/solution.py
+++ b/solution.py
@@ -40,17 +40,18 @@
 
     half_size = block_size // 2
     core = lax.axis_index("bin")
+    swap = [(0, 1), (1, 0)]
+    own_part = lax.dynamic_slice_in_dim(inputs, core * half_size, half_size, axis=2)
+    their_part = lax.dynamic_slice_in_dim(inputs, (1 - core) * half_size, half_size, axis=2)
+    partner_part = lax.ppermute(their_part, "bin", swap)
     back_t = back_got.transpose(1, 0, 2, 3).reshape(local_blocks, block_size, row_count)
-
-    def left_of(start):
-        rows = lax.dynamic_slice_in_dim(inputs, start, half_size, axis=2)
-        return jnp.einsum("rki,kjr->kij", rows, back_t, preferred_element_type=jnp.float32)
-
-    theirs = left_of((1 - core) * half_size)
-    mixed_sent, theirs = lax.optimization_barrier((mixed_sent, theirs))
+    partner_back = lax.ppermute(back_t, "bin", swap)
     mixed_got = lax.all_to_all(mixed_sent, "blk", 0, 0, tiled=True)
-    got_left = lax.ppermute(theirs, "bin", [(0, 1), (1, 0)])
-    grad_left = (lax.optimization_barrier(left_of(core * half_size)) + got_left).astype(jnp.bfloat16)
+    left_term = jnp.einsum("rki,kjr->kij", own_part, back_t, preferred_element_type=jnp.float32)
+    left_term = left_term + jnp.einsum(
+        "rki,kjr->kij", partner_part, partner_back, preferred_element_type=jnp.float32
+    )
+    grad_left = left_term.astype(jnp.bfloat16)
     grad_left, mixed_got = lax.optimization_barrier((grad_left, mixed_got))
     half_peers = peer_count // 2
 

time: 128 us -> 122 us (0.953)
  waiting for transfers between devices: 76.8 us -> 70.1 us
  local copies, waits for them, and re-layouts: 16.2 us -> 21.9 us
  other arithmetic: 10.3 us -> 6.02 us
    all_to_all x1, waiting for transfers between devices: 41.8 us -> 35 us  [on_device(): mixed_got = lax.all_to_all(mixed_sent, 'blk', 0, 0, tiled=True)]
    convert_element_type x1 -> x0, other arithmetic: 4.25 us -> none  [on_device(): (lax.optimization_barrier(left_of(core * half_size)) + got_left).astype(j...]
    transpose x0 -> x1, local copies, waits for them, and re-layouts: none -> 3.41 us  [on_device(): back_got.transpose(1, 0, 2, 3).reshape(local_blocks, block_size, row_count)]
    dynamic_slice x0 -> x1, local copies, waits for them, and re-layouts: none -> 2.35 us  [on_device(): lax.dynamic_slice_in_dim(inputs, (1 - core) * half_size, half_size, axis=2)]
  transfers between devices with their start and end apart: 6 -> 7, of which waited for: 4 -> 4; matrix products, arithmetic and copies ran while one was open for 21% -> 26% of each run, Pallas kernels for 0% -> 0%
where the time goes in v7:
time: 122 us; the launch traced here: 121 us
  waiting for transfers between devices  70.1 us (57%)
  local copies, waits for them, and re-layouts  21.9 us (18%)
  starting transfers between devices  12.5 us (10%)
  matrix products  9.99 us (8%)
  other arithmetic  6.02 us (5%)
    all_to_all x1, waiting for transfers between devices, on_device(): mixed_got = lax.all_to_all(mixed_sent, 'blk', 0, 0, tiled=True)  35 us
    all_to_all x1, waiting for transfers between devices, on_device(): back_got = lax.all_to_all(back_sent, 'blk', 0, 0, tiled=True)  32.9 us
    unnamed x11, local copies, waits for them, and re-layouts  11.4 us
    all_to_all x1, starting transfers between devices, on_device(): back_got = lax.all_to_all(back_sent, 'blk', 0, 0, tiled=True)  6.84 us
    all_to_all x1, starting transfers between devices, on_device(): mixed_got = lax.all_to_all(mixed_sent, 'blk', 0, 0, tiled=True)  4.35 us
    dot_general x1, matrix products, on_device(): jnp.einsum('rki,kjr->kij', partner_part, partner_back, preferred_element_...  3.72 us
    transpose x1, local copies, waits for them, and re-layouts, on_device(): back_got.transpose(1, 0, 2, 3).reshape(local_blocks, block_size, row_count)  3.41 us
    select_n x2, other arithmetic, swap_halves(): first = jnp.where(core == 0, local, other)  2.85 us
  transfers between devices with their start and end apart: 7, of which 4 were waited for; matrix products, arithmetic and copies ran while one was open for 26% of the time, Pallas kernels for 0%

profile of v7, /device:TPU:0, one launch (start us, length us, event | category | flops | bytes accessed | tf_op | source)
XLA Modules:
  0.0 121.2 jit_solution(646237240185272340)
XLA Ops:
  0.6 0.5 collective-permute-start.1
  1.1 3.3 %copy.33 = bf16[256,4096]{0,1:T(8,128)(2,1)S(1)} copy(bf16[256,4096]{1,0:T(8,128)(2,1)} %param.6) | data formatting | bytes 4194304 | tf_op args[1]
  4.5 0.0 collective-permute-done.1
  4.5 0.1 broadcast_select_fusion.3
  4.6 0.7 convert_bitcast_fusion
  5.3 1.5 %copy.34 = bf16[8,8,64,256]{3,1,2,0:T(8,128)(2,1)} copy(bf16[8,8,64,256]{3,1,0,2:T(8,128)(2,1)S(1)} %convert_bitcast_fusion) | data formatting | bytes 4194304 | tf_op jit(solution)/shard_map/reshape | solution.py:29
  6.7 6.8 %all-to-all-start = ((bf16[8,8,64,256]{3,1,2,0:T(8,128)(2,1)}), bf16[8,8,64,256]{3,1,2,0:T(8,128)(2,1)}, u32[]{:S(2)}, u32[]{:S(2)}) async-start(bf16[8,8,64,256]{3,1,2,0:T(8,128)(2,1)} %copy.34), calls=%async_computation | async-start | bytes 4194304 | tf_op jit(solution)/shard_map/all_to_all | solution.py:30
  13.6 3.9 %copy.29 = bf16[8,256,512]{1,2,0:T(8,128)(2,1)} copy(bf16[8,256,512]{2,1,0:T(8,128)(2,1)} %param.7) | data formatting | bytes 4194304 | tf_op args[2]
  17.5 0.2 collective-permute-start
  17.7 4.1 %copy.27 = bf16[256,4096]{0,1:T(8,128)(2,1)} copy(bf16[256,4096]{1,0:T(8,128)(2,1)} %param.5) | data formatting | bytes 4194304 | tf_op args[0]
  21.8 0.1 fusion.18
  21.8 2.1 %broadcast_multiply_fusion = bf16[256,8,512]{0,2,1:T(8,128)(2,1)S(1)} fusion(bf16[256,8,512]{0,2,1:T(8,128)(2,1)} %bitcast.35, bf16[8,512]{1,0:T(8,128)(2,1)S(1)} %fusion.18), kind=kLoop, calls=%fused_computation.24 | loop fusion | flops 1048576 | bytes 4202496 | tf_op jit(solution)/shard_map/mul | solution.py:33
  23.9 0.0 collective-permute-done
  23.9 0.1 copy-done.1
  24.1 2.8 %broadcast_select_fusion.1 = (bf16[8,256,512]{1,2,0:T(8,128)(2,1)S(1)}, bf16[8,256,512]{1,2,0:T(8,128)(2,1)S(1)}) fusion(bf16[8,256,512]{1,2,0:T(8,128)(2,1)S(1)} %copy-done.1, bf16[8,256,512]{1,2,0:T(8,128)(2,1)} %collective-permute-done, pred[]{:T(512)S(6)} %eq.2), kind=kLoop, calls=%fused_computation.8 | loop fusion | flops 2097152 | bytes 8388609 | tf_op jit(solution)/shard_map/jit(_where)/select_n | solution.py:10
  26.8 1.3 %fusion.4 = bf16[8,512,256]{2,1,0:T(8,128)(2,1)S(1)} fusion(bf16[256,8,512]{0,2,1:T(8,128)(2,1)S(1)} %broadcast_multiply_fusion, bf16[8,256,512]{1,2,0:T(8,128)(2,1)S(1)} %get-tuple-element.11, bf16[8,256,512]{1,2,0:T(8,128)(2,1)S(1)} %get-tuple-element.10), kind=kOutput, calls=%fused_computation.9 | convolution fusion | flops 1083179008 | bytes 8388608 | tf_op jit(solution)/shard_map/rki,kij->jkr/dot_general | solution.py:35
  28.1 1.6 %copy.48 = bf16[8,64,8,256]{3,1,2,0:T(8,128)(2,1)} copy(bf16[8,64,8,256]{3,1,0,2:T(8,128)(2,1)S(1)} %bitcast.36) | data formatting | bytes 4194304 | tf_op jit(solution)/shard_map/reshape | solution.py:38
  29.7 32.9 %all-to-all-done = bf16[8,8,64,256]{3,1,2,0:T(8,128)(2,1)} async-done(((bf16[8,8,64,256]{3,1,2,0:T(8,128)(2,1)}), bf16[8,8,64,256]{3,1,2,0:T(8,128)(2,1)}, u32[]{:S(2)}, u32[]{:S(2)}) %all-to-all-start) | async-done | bytes 2097184 | tf_op jit(solution)/shard_map/all_to_all | solution.py:30
  62.6 4.3 %all-to-all-start.1 = ((bf16[8,8,64,256]{3,2,1,0:T(8,128)(2,1)}), bf16[8,8,64,256]{3,2,1,0:T(8,128)(2,1)}, u32[]{:S(2)}, u32[]{:S(2)}) async-start(bf16[8,8,64,256]{3,2,1,0:T(8,128)(2,1)} %bitcast.34), calls=%async_computation.1 | async-start | bytes 4194304 | tf_op jit(solution)/shard_map/all_to_all | solution.py:49
  66.9 3.4 %copy.35 = bf16[8,8,64,256]{3,2,1,0:T(8,128)(2,1)} copy(bf16[8,8,64,256]{3,0,2,1:T(8,128)(2,1)} %bitcast.7) | data formatting | bytes 4194304 | tf_op jit(solution)/shard_map/transpose | solution.py:47
  70.3 2.4 %constant_dynamic-slice_fusion = bf16[256,8,256]{0,2,1:T(8,128)(2,1)} fusion(bf16[256,8,512]{0,2,1:T(8,128)(2,1)} %copy-done, s32[]{:T(128)S(6)} %select_n.43), kind=kLoop, calls=%fused_computation.29 | loop fusion | bytes 2097156 | tf_op jit(solution)/shard_map/dynamic_slice | solution.py:45
  72.7 0.5 collective-permute-start.2
  73.2 2.7 %fusion.16 = f32[8,256,512]{2,1,0:T(8,128)S(1)} fusion(bf16[8,512,256]{2,1,0:T(8,128)(2,1)} %bitcast.8, bf16[256,8,512]{0,2,1:T(8,128)(2,1)} %copy-done, s32[]{:T(128)S(6)} %select_n.36), kind=kOutput, calls=%fused_computation.22 | convolution fusion | flops 536870912 | bytes 7340036 | tf_op jit(solution)/shard_map/rki,kjr->kij/dot_general | solution.py:50
  75.9 0.3 collective-permute-done.2
  76.2 3.7 %add_convert_fusion = bf16[8,256,512]{2,1,0:T(8,128)(2,1)} fusion(f32[8,256,512]{2,1,0:T(8,128)S(1)} %fusion.16, bf16[256,8,256]{0,2,1:T(8,128)(2,1)S(1)} %collective-permute-done.2, bf16[8,512,256]{2,1,0:T(8,128)(2,1)} %collective-permute-done.3), kind=kOutput, calls=%fused_computation.4 | convolution fusion | flops 538968064 | bytes 9437184 | tf_op jit(solution)/shard_map/rki,kjr->kij/dot_general | solution.py:51
  79.9 35.0 %all-to-all-done.1 = bf16[8,8,64,256]{3,2,1,0:T(8,128)(2,1)} async-done(((bf16[8,8,64,256]{3,2,1,0:T(8,128)(2,1)}), bf16[8,8,64,256]{3,2,1,0:T(8,128)(2,1)}, u32[]{:S(2)}, u32[]{:S(2)}) %all-to-all-start.1) | async-done | bytes 2097184 | tf_op jit(solution)/shard_map/all_to_all | solution.py:49
  115.0 1.7 %dynamic-slice_bitcast_fusion = (bf16[64,4,8,256]{3,0,2,1:T(8,128)(2,1)S(1)}, bf16[64,4,8,256]{3,0,2,1:T(8,128)(2,1)S(1)}) fusion(bf16[8,8,64,256]{3,2,1,0:T(8,128)(2,1)} %all-to-all-done.1, s32[]{:T(128)S(6)} %select_n.45, s32[]{:T(128)S(6)} %select_n.44), kind=kLoop, calls=%fused_computation.20 | loop fusion | bytes 4194312 | tf_op jit(solution)/shard_map/transpose | solution.py:60
  116.6 0.8 fusion.10
  117.5 0.1 collective-permute-start.4
  117.5 0.8 fusion.12
  118.4 1.8 %collective-permute-done.4 = f32[64,32,64]{2,1,0:T(8,128)S(1)} collective-permute-done((f32[64,32,64]{2,1,0:T(8,128)S(1)}, f32[64,32,64]{2,1,0:T(8,128)S(1)}, u32[]{:S(2)}, u32[]{:S(2)}) %collective-permute-start.4) | collective-permute-done | bytes 524320 | tf_op jit(solution)/shard_map/ppermute | solution.py:63
  120.2 1.0 add_convert_fusion.1
  (9 shorter events, 0.0 us)
Async XLA Ops:
  0.6 3.9 %collective-permute-start.1 = (bf16[64,32,64]{2,1,0:T(8,128)(2,1)}, bf16[64,32,64]{2,1,0:T(8,128)(2,1)S(1)}, u32[]{:S(2)}, u32[]{:S(2)}) collective-permute-start(bf16[64,32,64]{2,1,0:T(8,128)(2,1)} %param.8), channel_id=1, source_target_pairs={{0,1},{1,0},{2,3},{3,2},{4,5},{5,4},{6,7},{7,6},{8,9},{9,8},{10,11... | collective-permute-start | bytes 786440 | tf_op jit(solution)/shard_map/ppermute | solution.py:8
  1.1 3.4 %copy-start.2 = (bf16[64,32,64]{2,1,0:T(8,128)(2,1)S(1)}, bf16[64,32,64]{2,1,0:T(8,128)(2,1)}, u32[]{:S(2)}) copy-start(bf16[64,32,64]{2,1,0:T(8,128)(2,1)} %param.8) | copy-start | bytes 786436
  6.7 55.8 %all-to-all-start = ((bf16[8,8,64,256]{3,1,2,0:T(8,128)(2,1)}), bf16[8,8,64,256]{3,1,2,0:T(8,128)(2,1)}, u32[]{:S(2)}, u32[]{:S(2)}) async-start(bf16[8,8,64,256]{3,1,2,0:T(8,128)(2,1)} %copy.34), calls=%async_computation | async-start | bytes 4194304 | tf_op jit(solution)/shard_map/all_to_all | solution.py:30
  17.5 4.3 %copy-start.3 = (s32[8]{0:T(128)S(1)}, s32[8]{0:T(128)}, u32[]{:S(2)}) copy-start(s32[8]{0:T(128)} %param.9) | copy-start | bytes 100
  17.5 6.5 %collective-permute-start = (bf16[8,256,512]{1,2,0:T(8,128)(2,1)}, bf16[8,256,512]{1,2,0:T(8,128)(2,1)}, u32[]{:S(2)}, u32[]{:S(2)}) collective-permute-start(bf16[8,256,512]{1,2,0:T(8,128)(2,1)} %copy.29), channel_id=1, source_target_pairs={{0,1},{1,0},{2,3},{3,2},{4,5},{5,4},{6,7},{7,6},{8,9},{9,8},{10,11... | collective-permute-start | bytes 6291464 | tf_op jit(solution)/shard_map/ppermute | solution.py:8
  21.8 2.2 %copy-start.1 = (bf16[8,256,512]{1,2,0:T(8,128)(2,1)S(1)}, bf16[8,256,512]{1,2,0:T(8,128)(2,1)}, u32[]{:S(2)}) copy-start(bf16[8,256,512]{1,2,0:T(8,128)(2,1)} %copy.29) | copy-start | bytes 6291460
  23.9 2.9 %copy-start = (bf16[256,8,512]{0,2,1:T(8,128)(2,1)}, bf16[256,8,512]{0,2,1:T(8,128)(2,1)S(1)}, u32[]{:S(2)}) copy-start(bf16[256,8,512]{0,2,1:T(8,128)(2,1)S(1)} %broadcast_multiply_fusion) | copy-start | bytes 6291460
  62.6 52.4 %all-to-all-start.1 = ((bf16[8,8,64,256]{3,2,1,0:T(8,128)(2,1)}), bf16[8,8,64,256]{3,2,1,0:T(8,128)(2,1)}, u32[]{:S(2)}, u32[]{:S(2)}) async-start(bf16[8,8,64,256]{3,2,1,0:T(8,128)(2,1)} %bitcast.34), calls=%async_computation.1 | async-start | bytes 4194304 | tf_op jit(solution)/shard_map/all_to_all | solution.py:49
  70.3 5.9 %collective-permute-start.3 = (bf16[8,512,256]{2,1,0:T(8,128)(2,1)}, bf16[8,512,256]{2,1,0:T(8,128)(2,1)}, u32[]{:S(2)}, u32[]{:S(2)}) collective-permute-start(bf16[8,512,256]{2,1,0:T(8,128)(2,1)} %bitcast.8), channel_id=1, source_target_pairs={{0,1},{1,0},{2,3},{3,2},{4,5},{5,4},{6,7},{7,6},{8,9},{9,8},{10,11... | collective-permute-start | bytes 6291464 | tf_op jit(solution)/shard_map/ppermute | solution.py:48
  72.7 3.5 %collective-permute-start.2 = (bf16[256,8,256]{0,2,1:T(8,128)(2,1)}, bf16[256,8,256]{0,2,1:T(8,128)(2,1)S(1)}, u32[]{:S(2)}, u32[]{:S(2)}) collective-permute-start(bf16[256,8,256]{0,2,1:T(8,128)(2,1)} %constant_dynamic-slice_fusion), channel_id=1, source_target_pairs={{0,1},{1,0},{2,3},{3,2},{4,5},{5,4},{6,7},{7,6},{8,9},{9,8},{10,11... | collective-permute-start | bytes 3145736 | tf_op jit(solution)/shard_map/ppermute | solution.py:46
  117.5 2.7 %collective-permute-start.4 = (f32[64,32,64]{2,1,0:T(8,128)S(1)}, f32[64,32,64]{2,1,0:T(8,128)S(1)}, u32[]{:S(2)}, u32[]{:S(2)}) collective-permute-start(f32[64,32,64]{2,1,0:T(8,128)S(1)} %fusion.10), channel_id=1, source_target_pairs={{0,1},{1,0},{2,3},{3,2},{4,5},{5,4},{6,7},{7,6},{8,9},{9,8},{10,11... | collective-permute-start | bytes 1572872 | tf_op jit(solution)/shard_map/ppermute | solution.py:63

commit v8 on v7

--- a/solution.py
+++ b/solution.py
@@ -10,6 +10,17 @@
     first = jnp.where(core == 0, local, other)
     second = jnp.where(core == 0, other, local)
     return jnp.concatenate([first, second], axis=axis)
+
+
+def exchange(sent):
+    peer_count = sent.shape[0]
+    me = lax.axis_index("blk")
+    pieces = [lax.dynamic_index_in_dim(sent, me, 0, keepdims=False)]
+    for shift in range(1, peer_count):
+        piece = lax.dynamic_index_in_dim(sent, (me + shift) % peer_count, 0, keepdims=False)
+        pairs = [(i, (i + shift) % peer_count) for i in range(peer_count)]
+        pieces.append(lax.ppermute(piece, "blk", pairs))
+    return jnp.take(jnp.stack(pieces), (me - jnp.arange(peer_count)) % peer_count, axis=0)
 
 
 def on_device(units, cotangent, left_factor, right_factor, session_units):
@@ -27,7 +38,7 @@
         "rjm,jkm->kjr", upstream, right_full, preferred_element_type=jnp.float32
     ).astype(jnp.bfloat16)
     back_sent = back_grad.reshape(peer_count, local_blocks, right_local, row_count)
-    back_got = lax.all_to_all(back_sent, "blk", 0, 0, tiled=True)
+    back_got = exchange(back_sent)
 
     unit_mask = (jnp.arange(block_size)[None, :] < session_units[:, None]).astype(jnp.bfloat16)
     inputs = units.reshape(row_count, local_blocks, block_size) * unit_mask[None]
@@ -36,7 +47,6 @@
         "rki,kij->jkr", inputs, left_full, preferred_element_type=jnp.float32
     ).astype(jnp.bfloat16)
     mixed_sent = mixed.reshape(peer_count, right_local, local_blocks, row_count).transpose(0, 2, 1, 3)
-    mixed_sent, back_got = lax.optimization_barrier((mixed_sent, back_got))
 
     half_size = block_size // 2
     core = lax.axis_index("bin")

time: 122 us -> 128 us (1.049)
  waiting for transfers between devices: 70.1 us -> 49.5 us
  starting transfers between devices: 12.5 us -> 27.7 us
  local copies, waits for them, and re-layouts: 21.9 us -> 31.4 us
  other arithmetic: 6.02 us -> 7.61 us
    all_to_all x1 -> x0, waiting for transfers between devices: 32.9 us -> none  [on_device(): back_got = lax.all_to_all(back_sent, 'blk', 0, 0, tiled=True)]
    ppermute x0 -> x7, waiting for transfers between devices: none -> 23.4 us  [exchange(): pieces.append(lax.ppermute(piece, 'blk', pairs))]
    ppermute x0 -> x7, starting transfers between devices: none -> 19.5 us  [exchange(): pieces.append(lax.ppermute(piece, 'blk', pairs))]
    all_to_all x1, waiting for transfers between devices: 35 us -> 23.9 us  [on_device(): mixed_got = lax.all_to_all(mixed_sent, 'blk', 0, 0, tiled=True)]
    all_to_all x1 -> x0, starting transfers between devices: 6.84 us -> none  [on_device(): back_got = lax.all_to_all(back_sent, 'blk', 0, 0, tiled=True)]
    unnamed x11 -> x15, local copies, waits for them, and re-layouts: 11.4 us -> 17.5 us
    gather x0 -> x1, local copies, waits for them, and re-layouts: none -> 3.78 us  [exchange(): jnp.take(jnp.stack(pieces), (me - jnp.arange(peer_count)) % peer_count, a...]
    transpose x1 -> x0, local copies, waits for them, and re-layouts: 3.41 us -> none  [on_device(): back_got.transpose(1, 0, 2, 3).reshape(local_blocks, block_size, row_count)]
  transfers between devices with their start and end apart: 7 -> 13, of which waited for: 4 -> 6; matrix products, arithmetic and copies ran while one was open for 26% -> 36% of each run, Pallas kernels for 0% -> 0%
where the time goes in v8:
time: 128 us; the launch traced here: 127 us
  waiting for transfers between devices  49.5 us (39%)
  local copies, waits for them, and re-layouts  31.4 us (25%)
  starting transfers between devices  27.7 us (22%)
  matrix products  10 us (8%)
  other arithmetic  7.61 us (6%)
    all_to_all x1, waiting for transfers between devices, on_device(): mixed_got = lax.all_to_all(mixed_sent, 'blk', 0, 0, tiled=True)  23.9 us
    ppermute x7, waiting for transfers between devices, exchange(): pieces.append(lax.ppermute(piece, 'blk', pairs))  23.4 us
    ppermute x7, starting transfers between devices, exchange(): pieces.append(lax.ppermute(piece, 'blk', pairs))  19.5 us
    unnamed x15, local copies, waits for them, and re-layouts  17.5 us
    all_to_all x1, starting transfers between devices, on_device(): mixed_got = lax.all_to_all(mixed_sent, 'blk', 0, 0, tiled=True)  7.07 us
    gather x1, local copies, waits for them, and re-layouts, exchange(): jnp.take(jnp.stack(pieces), (me - jnp.arange(peer_count)) % peer_count, a...  3.78 us
    dot_general x1, matrix products, on_device(): jnp.einsum('rki,kjr->kij', partner_part, partner_back, preferred_element_...  3.72 us
    dot_general x1, matrix products, on_device(): jnp.einsum('rki,kjr->kij', own_part, back_t, preferred_element_type=jnp.f...  2.66 us
  transfers between devices with their start and end apart: 13, of which 6 were waited for; matrix products, arithmetic and copies ran while one was open for 36% of the time, Pallas kernels for 0%

profile of v8, /device:TPU:0, one launch (start us, length us, event | category | flops | bytes accessed | tf_op | source)
XLA Modules:
  0.0 126.9 jit_solution(14182621869370184533)
XLA Ops:
  1.2 3.9 %copy.31 = bf16[8,256,512]{1,2,0:T(8,128)(2,1)} copy(bf16[8,256,512]{2,1,0:T(8,128)(2,1)} %param.7) | data formatting | bytes 4194304 | tf_op args[2]
  5.2 3.3 %copy.28 = bf16[256,4096]{0,1:T(8,128)(2,1)S(1)} copy(bf16[256,4096]{1,0:T(8,128)(2,1)} %param.6) | data formatting | bytes 4194304 | tf_op args[1]
  8.5 4.1 %copy.27 = bf16[256,4096]{0,1:T(8,128)(2,1)} copy(bf16[256,4096]{1,0:T(8,128)(2,1)} %param.5) | data formatting | bytes 4194304 | tf_op args[0]
  12.6 2.0 %broadcast_multiply_fusion = bf16[256,8,512]{0,2,1:T(8,128)(2,1)S(1)} fusion(bf16[256,8,512]{0,2,1:T(8,128)(2,1)} %bitcast.66, bf16[8,512]{1,0:T(8,128)(2,1)S(1)} %fusion.18), kind=kLoop, calls=%fused_computation.26 | loop fusion | flops 1048576 | bytes 4202496 | tf_op jit(solution)/shard_map/mul | solution.py:44
  15.5 1.0 dynamic-slice_bitcast_fusion.2
  16.4 2.9 %collective-permute-start.1 = (bf16[8,64,256]{2,0,1:T(8,128)(2,1)S(1)}, bf16[8,64,256]{2,0,1:T(8,128)(2,1)S(1)}, u32[]{:S(2)}, u32[]{:S(2)}) collective-permute-start(bf16[8,64,256]{2,0,1:T(8,128)(2,1)S(1)} %get-tuple-element.16), channel_id=1, source_target_pairs={{0,2},{2,4},{4,6},{6,8},{8,10},{10,12},{12,14},{14,0},{1,3},{3,5},... | collective-permute-start | bytes 786440 | tf_op jit(solution)/shard_map/ppermute | solution.py:22
  19.4 1.6 %collective-permute-start.2 = (bf16[8,64,256]{2,0,1:T(8,128)(2,1)S(1)}, bf16[8,64,256]{2,0,1:T(8,128)(2,1)S(1)}, u32[]{:S(2)}, u32[]{:S(2)}) collective-permute-start(bf16[8,64,256]{2,0,1:T(8,128)(2,1)S(1)} %get-tuple-element.15), channel_id=1, source_target_pairs={{0,4},{2,6},{4,8},{6,10},{8,12},{10,14},{12,0},{14,2},{1,5},{3,7},... | collective-permute-start | bytes 786440 | tf_op jit(solution)/shard_map/ppermute | solution.py:22
  21.1 2.6 %collective-permute-start.3 = (bf16[8,64,256]{2,0,1:T(8,128)(2,1)S(1)}, bf16[8,64,256]{2,0,1:T(8,128)(2,1)S(1)}, u32[]{:S(2)}, u32[]{:S(2)}) collective-permute-start(bf16[8,64,256]{2,0,1:T(8,128)(2,1)S(1)} %get-tuple-element.14), channel_id=1, source_target_pairs={{0,6},{2,8},{4,10},{6,12},{8,14},{10,0},{12,2},{14,4},{1,7},{3,9},... | collective-permute-start | bytes 786440 | tf_op jit(solution)/shard_map/ppermute | solution.py:22
  23.7 1.2 collective-permute-start.4
  24.9 4.7 %collective-permute-done.1 = bf16[8,64,256]{2,0,1:T(8,128)(2,1)S(1)} collective-permute-done((bf16[8,64,256]{2,0,1:T(8,128)(2,1)S(1)}, bf16[8,64,256]{2,0,1:T(8,128)(2,1)S(1)}, u32[]{:S(2)}, u32[]{:S(2)}) %collective-permute-start.1) | collective-permute-done | bytes 262176 | tf_op jit(solution)/shard_map/ppermute | solution.py:22
  30.6 1.7 %collective-permute-start.6 = (bf16[8,64,256]{2,0,1:T(8,128)(2,1)S(1)}, bf16[8,64,256]{2,0,1:T(8,128)(2,1)}, u32[]{:S(2)}, u32[]{:S(2)}) collective-permute-start(bf16[8,64,256]{2,0,1:T(8,128)(2,1)S(1)} %get-tuple-element.11), channel_id=1, source_target_pairs={{0,12},{2,14},{4,0},{6,2},{8,4},{10,6},{12,8},{14,10},{1,13},{3,15... | collective-permute-start | bytes 786440 | tf_op jit(solution)/shard_map/ppermute | solution.py:22
  33.0 18.5 %collective-permute-done.3 = bf16[8,64,256]{2,0,1:T(8,128)(2,1)S(1)} collective-permute-done((bf16[8,64,256]{2,0,1:T(8,128)(2,1)S(1)}, bf16[8,64,256]{2,0,1:T(8,128)(2,1)S(1)}, u32[]{:S(2)}, u32[]{:S(2)}) %collective-permute-start.3) | collective-permute-done | bytes 262176 | tf_op jit(solution)/shard_map/ppermute | solution.py:22
  51.5 9.3 %collective-permute-start.7 = (bf16[8,64,256]{2,0,1:T(8,128)(2,1)S(1)}, bf16[8,64,256]{2,0,1:T(8,128)(2,1)}, u32[]{:S(2)}, u32[]{:S(2)}) collective-permute-start(bf16[8,64,256]{2,0,1:T(8,128)(2,1)S(1)} %get-tuple-element.10), channel_id=1, source_target_pairs={{0,14},{2,0},{4,2},{6,4},{8,6},{10,8},{12,10},{14,12},{1,15},{3,1}... | collective-permute-start | bytes 786440 | tf_op jit(solution)/shard_map/ppermute | solution.py:22
  61.5 2.5 %broadcast_select_fusion.1 = (bf16[8,256,512]{1,2,0:T(8,128)(2,1)S(1)}, bf16[8,256,512]{1,2,0:T(8,128)(2,1)S(1)}) fusion(bf16[8,256,512]{1,2,0:T(8,128)(2,1)} %copy.31, bf16[8,256,512]{1,2,0:T(8,128)(2,1)} %collective-permute-done.10, pred[]{:T(512)S(6)} %eq.16), kind=kLoop, calls=%fused_computation.10 | loop fusion | flops 2097152 | bytes 8388609 | tf_op jit(solution)/shard_map/jit(_where)/select_n | solution.py:10
  64.1 1.3 fusion.4
  65.3 1.6 %copy.47 = bf16[8,64,8,256]{3,1,2,0:T(8,128)(2,1)} copy(bf16[8,64,8,256]{3,1,0,2:T(8,128)(2,1)S(1)} %bitcast.67) | data formatting | bytes 4194304 | tf_op jit(solution)/shard_map/reshape | solution.py:49
  66.9 7.1 %all-to-all-start = ((bf16[8,8,64,256]{3,2,1,0:T(8,128)(2,1)}), bf16[8,8,64,256]{3,2,1,0:T(8,128)(2,1)}, u32[]{:S(2)}, u32[]{:S(2)}) async-start(bf16[8,8,64,256]{3,2,1,0:T(8,128)(2,1)} %bitcast.65), calls=%async_computation | async-start | bytes 4194304 | tf_op jit(solution)/shard_map/all_to_all | solution.py:59
  74.7 1.7 %bitcast_dynamic-update-slice_fusion.2 = bf16[8,8,64,256]{3,1,0,2:T(8,128)(2,1)} fusion(bf16[8,8,64,256]{3,1,0,2:T(8,128)(2,1)} %bitcast_dynamic-update-slice_fusion.3, bf16[8,64,256]{2,0,1:T(8,128)(2,1)} %collective-permute-done.5), kind=kLoop, calls=%fused_computation.31 | loop fusion | bytes 524288
  76.4 1.7 %bitcast_dynamic-update-slice_fusion.1 = bf16[8,8,64,256]{3,1,0,2:T(8,128)(2,1)} fusion(bf16[8,8,64,256]{3,1,0,2:T(8,128)(2,1)} %bitcast_dynamic-update-slice_fusion.2, bf16[8,64,256]{2,0,1:T(8,128)(2,1)} %collective-permute-done.6), kind=kLoop, calls=%fused_computation.30 | loop fusion | bytes 524288
  78.1 1.7 %bitcast_dynamic-update-slice_fusion = bf16[8,8,64,256]{3,1,0,2:T(8,128)(2,1)} fusion(bf16[8,8,64,256]{3,1,0,2:T(8,128)(2,1)} %bitcast_dynamic-update-slice_fusion.1, bf16[8,64,256]{2,0,1:T(8,128)(2,1)} %collective-permute-done.7), kind=kLoop, calls=%fused_computation.29 | loop fusion | bytes 524288 | tf_op jit(solution)/shard_map/stack | solution.py:23
  79.7 3.8 %gather_fusion = bf16[8,8,64,256]{3,1,2,0:T(8,128)(2,1)} fusion(bf16[8,8,64,256]{3,1,0,2:T(8,128)(2,1)} %bitcast_dynamic-update-slice_fusion, s32[1024]{0:T(1024)S(1)} %pad_clamp_fusion), kind=kCustom, calls=%fused_computation | custom fusion | bytes 4194336 | tf_op jit(solution)/shard_map/jit(_take)/gather | solution.py:23
  83.5 1.9 %select_bitcast_fusion = bf16[8,8,64,256]{3,0,2,1:T(8,128)(2,1)S(1)} fusion(bf16[8,8,64,256]{3,1,2,0:T(8,128)(2,1)} %gather_fusion, pred[8]{0:T(512)(128)(4,1)S(1)} %compare_and_fusion), kind=kLoop, calls=%fused_computation.7 | loop fusion | flops 1048576 | bytes 4194312 | tf_op jit(solution)/shard_map/jit(_take)/select_n | solution.py:23
  85.4 1.8 %copy.29 = bf16[8,8,64,256]{3,2,1,0:T(8,128)(2,1)} copy(bf16[8,8,64,256]{3,0,2,1:T(8,128)(2,1)S(1)} %select_bitcast_fusion) | data formatting | bytes 4194304 | tf_op jit(solution)/shard_map/jit(_take)/select_n | solution.py:23
  87.2 2.4 %constant_dynamic-slice_fusion = bf16[256,8,256]{0,2,1:T(8,128)(2,1)} fusion(bf16[256,8,512]{0,2,1:T(8,128)(2,1)} %copy-done, s32[]{:T(128)S(6)} %select_n.158), kind=kLoop, calls=%fused_computation.47 | loop fusion | bytes 2097156 | tf_op jit(solution)/shard_map/dynamic_slice | solution.py:55
  90.1 2.7 %fusion.16 = f32[8,256,512]{2,1,0:T(8,128)S(1)} fusion(bf16[8,512,256]{2,1,0:T(8,128)(2,1)} %bitcast.21, bf16[256,8,512]{0,2,1:T(8,128)(2,1)} %copy-done, s32[]{:T(128)S(6)} %select_n.133), kind=kOutput, calls=%fused_computation.24 | convolution fusion | flops 536870912 | bytes 7340036 | tf_op jit(solution)/shard_map/rki,kjr->kij/dot_general | solution.py:60
  93.0 3.7 %add_convert_fusion = bf16[8,256,512]{2,1,0:T(8,128)(2,1)} fusion(f32[8,256,512]{2,1,0:T(8,128)S(1)} %fusion.16, bf16[256,8,256]{0,2,1:T(8,128)(2,1)S(1)} %collective-permute-done.8, bf16[8,512,256]{2,1,0:T(8,128)(2,1)} %collective-permute-done.9), kind=kOutput, calls=%fused_computation.5 | convolution fusion | flops 538968064 | bytes 9437184 | tf_op jit(solution)/shard_map/rki,kjr->kij/dot_general | solution.py:61
  96.8 23.9 %all-to-all-done = bf16[8,8,64,256]{3,2,1,0:T(8,128)(2,1)} async-done(((bf16[8,8,64,256]{3,2,1,0:T(8,128)(2,1)}), bf16[8,8,64,256]{3,2,1,0:T(8,128)(2,1)}, u32[]{:S(2)}, u32[]{:S(2)}) %all-to-all-start) | async-done | bytes 2097184 | tf_op jit(solution)/shard_map/all_to_all | solution.py:59
  120.7 1.7 %dynamic-slice_bitcast_fusion = (bf16[64,4,8,256]{3,0,2,1:T(8,128)(2,1)S(1)}, bf16[64,4,8,256]{3,0,2,1:T(8,128)(2,1)S(1)}) fusion(bf16[8,8,64,256]{3,2,1,0:T(8,128)(2,1)} %all-to-all-done, s32[]{:T(128)S(6)} %select_n.163, s32[]{:T(128)S(6)} %select_n.162), kind=kLoop, calls=%fused_computation.22 | loop fusion | bytes 4194312 | tf_op jit(solution)/shard_map/transpose | solution.py:70
  122.4 0.8 fusion.10
  123.3 0.8 fusion.12
  124.1 1.8 %collective-permute-done.11 = f32[64,32,64]{2,1,0:T(8,128)S(1)} collective-permute-done((f32[64,32,64]{2,1,0:T(8,128)S(1)}, f32[64,32,64]{2,1,0:T(8,128)S(1)}, u32[]{:S(2)}, u32[]{:S(2)}) %collective-permute-start.11) | collective-permute-done | bytes 524320 | tf_op jit(solution)/shard_map/ppermute | solution.py:73
  125.9 1.0 add_convert_fusion.1
  (31 shorter events, 5.5 us)
Async XLA Ops:
  0.6 4.5 %copy-start.2 = (s32[8]{0:T(128)S(1)}, s32[8]{0:T(128)}, u32[]{:S(2)}) copy-start(s32[8]{0:T(128)} %param.9) | copy-start | bytes 100
  0.6 14.0 %collective-permute-start = (bf16[64,32,64]{2,1,0:T(8,128)(2,1)}, bf16[64,32,64]{2,1,0:T(8,128)(2,1)S(1)}, u32[]{:S(2)}, u32[]{:S(2)}) collective-permute-start(bf16[64,32,64]{2,1,0:T(8,128)(2,1)} %param.8), channel_id=1, source_target_pairs={{0,1},{1,0},{2,3},{3,2},{4,5},{5,4},{6,7},{7,6},{8,9},{9,8},{10,11... | collective-permute-start | bytes 786440 | tf_op jit(solution)/shard_map/ppermute | solution.py:8
  5.1 56.5 %collective-permute-start.10 = (bf16[8,256,512]{1,2,0:T(8,128)(2,1)}, bf16[8,256,512]{1,2,0:T(8,128)(2,1)}, u32[]{:S(2)}, u32[]{:S(2)}) collective-permute-start(bf16[8,256,512]{1,2,0:T(8,128)(2,1)} %copy.31), channel_id=1, source_target_pairs={{0,1},{1,0},{2,3},{3,2},{4,5},{5,4},{6,7},{7,6},{8,9},{9,8},{10,11... | collective-permute-start | bytes 6291464 | tf_op jit(solution)/shard_map/ppermute | solution.py:8
  12.6 2.0 %copy-start.1 = (bf16[64,32,64]{2,1,0:T(8,128)(2,1)S(1)}, bf16[64,32,64]{2,1,0:T(8,128)(2,1)}, u32[]{:S(2)}) copy-start(bf16[64,32,64]{2,1,0:T(8,128)(2,1)} %param.8) | copy-start | bytes 786436
  14.6 49.5 %copy-start = (bf16[256,8,512]{0,2,1:T(8,128)(2,1)}, bf16[256,8,512]{0,2,1:T(8,128)(2,1)S(1)}, u32[]{:S(2)}) copy-start(bf16[256,8,512]{0,2,1:T(8,128)(2,1)S(1)} %broadcast_multiply_fusion) | copy-start | bytes 6291460
  16.4 13.2 %collective-permute-start.1 = (bf16[8,64,256]{2,0,1:T(8,128)(2,1)S(1)}, bf16[8,64,256]{2,0,1:T(8,128)(2,1)S(1)}, u32[]{:S(2)}, u32[]{:S(2)}) collective-permute-start(bf16[8,64,256]{2,0,1:T(8,128)(2,1)S(1)} %get-tuple-element.16), channel_id=1, source_target_pairs={{0,2},{2,4},{4,6},{6,8},{8,10},{10,12},{12,14},{14,0},{1,3},{3,5},... | collective-permute-start | bytes 786440 | tf_op jit(solution)/shard_map/ppermute | solution.py:22
  19.4 11.1 %collective-permute-start.2 = (bf16[8,64,256]{2,0,1:T(8,128)(2,1)S(1)}, bf16[8,64,256]{2,0,1:T(8,128)(2,1)S(1)}, u32[]{:S(2)}, u32[]{:S(2)}) collective-permute-start(bf16[8,64,256]{2,0,1:T(8,128)(2,1)S(1)} %get-tuple-element.15), channel_id=1, source_target_pairs={{0,4},{2,6},{4,8},{6,10},{8,12},{10,14},{12,0},{14,2},{1,5},{3,7},... | collective-permute-start | bytes 786440 | tf_op jit(solution)/shard_map/ppermute | solution.py:22
  21.1 30.5 %collective-permute-start.3 = (bf16[8,64,256]{2,0,1:T(8,128)(2,1)S(1)}, bf16[8,64,256]{2,0,1:T(8,128)(2,1)S(1)}, u32[]{:S(2)}, u32[]{:S(2)}) collective-permute-start(bf16[8,64,256]{2,0,1:T(8,128)(2,1)S(1)} %get-tuple-element.14), channel_id=1, source_target_pairs={{0,6},{2,8},{4,10},{6,12},{8,14},{10,0},{12,2},{14,4},{1,7},{3,9},... | collective-permute-start | bytes 786440 | tf_op jit(solution)/shard_map/ppermute | solution.py:22
  23.7 50.3 %collective-permute-start.4 = (bf16[8,64,256]{2,0,1:T(8,128)(2,1)S(1)}, bf16[8,64,256]{2,0,1:T(8,128)(2,1)S(1)}, u32[]{:S(2)}, u32[]{:S(2)}) collective-permute-start(bf16[8,64,256]{2,0,1:T(8,128)(2,1)S(1)} %get-tuple-element.13), channel_id=1, source_target_pairs={{0,8},{2,10},{4,12},{6,14},{8,0},{10,2},{12,4},{14,6},{1,9},{3,11}... | collective-permute-start | bytes 786440 | tf_op jit(solution)/shard_map/ppermute | solution.py:22
  29.6 45.1 %collective-permute-start.5 = (bf16[8,64,256]{2,0,1:T(8,128)(2,1)S(1)}, bf16[8,64,256]{2,0,1:T(8,128)(2,1)}, u32[]{:S(2)}, u32[]{:S(2)}) collective-permute-start(bf16[8,64,256]{2,0,1:T(8,128)(2,1)S(1)} %get-tuple-element.12), channel_id=1, source_target_pairs={{0,10},{2,12},{4,14},{6,0},{8,2},{10,4},{12,6},{14,8},{1,11},{3,13... | collective-permute-start | bytes 786440 | tf_op jit(solution)/shard_map/ppermute | solution.py:22
  30.6 45.8 %collective-permute-start.6 = (bf16[8,64,256]{2,0,1:T(8,128)(2,1)S(1)}, bf16[8,64,256]{2,0,1:T(8,128)(2,1)}, u32[]{:S(2)}, u32[]{:S(2)}) collective-permute-start(bf16[8,64,256]{2,0,1:T(8,128)(2,1)S(1)} %get-tuple-element.11), channel_id=1, source_target_pairs={{0,12},{2,14},{4,0},{6,2},{8,4},{10,6},{12,8},{14,10},{1,13},{3,15... | collective-permute-start | bytes 786440 | tf_op jit(solution)/shard_map/ppermute | solution.py:22
  51.5 26.5 %collective-permute-start.7 = (bf16[8,64,256]{2,0,1:T(8,128)(2,1)S(1)}, bf16[8,64,256]{2,0,1:T(8,128)(2,1)}, u32[]{:S(2)}, u32[]{:S(2)}) collective-permute-start(bf16[8,64,256]{2,0,1:T(8,128)(2,1)S(1)} %get-tuple-element.10), channel_id=1, source_target_pairs={{0,14},{2,0},{4,2},{6,4},{8,6},{10,8},{12,10},{14,12},{1,15},{3,1}... | collective-permute-start | bytes 786440 | tf_op jit(solution)/shard_map/ppermute | solution.py:22
  66.9 53.8 %all-to-all-start = ((bf16[8,8,64,256]{3,2,1,0:T(8,128)(2,1)}), bf16[8,8,64,256]{3,2,1,0:T(8,128)(2,1)}, u32[]{:S(2)}, u32[]{:S(2)}) async-start(bf16[8,8,64,256]{3,2,1,0:T(8,128)(2,1)} %bitcast.65), calls=%async_computation | async-start | bytes 4194304 | tf_op jit(solution)/shard_map/all_to_all | solution.py:59
  87.2 5.9 %collective-permute-start.9 = (bf16[8,512,256]{2,1,0:T(8,128)(2,1)}, bf16[8,512,256]{2,1,0:T(8,128)(2,1)}, u32[]{:S(2)}, u32[]{:S(2)}) collective-permute-start(bf16[8,512,256]{2,1,0:T(8,128)(2,1)} %bitcast.21), channel_id=1, source_target_pairs={{0,1},{1,0},{2,3},{3,2},{4,5},{5,4},{6,7},{7,6},{8,9},{9,8},{10,11... | collective-permute-start | bytes 6291464 | tf_op jit(solution)/shard_map/ppermute | solution.py:58
  89.5 3.5 %collective-permute-start.8 = (bf16[256,8,256]{0,2,1:T(8,128)(2,1)}, bf16[256,8,256]{0,2,1:T(8,128)(2,1)S(1)}, u32[]{:S(2)}, u32[]{:S(2)}) collective-permute-start(bf16[256,8,256]{0,2,1:T(8,128)(2,1)} %constant_dynamic-slice_fusion), channel_id=1, source_target_pairs={{0,1},{1,0},{2,3},{3,2},{4,5},{5,4},{6,7},{7,6},{8,9},{9,8},{10,11... | collective-permute-start | bytes 3145736 | tf_op jit(solution)/shard_map/ppermute | solution.py:56
  123.2 2.7 %collective-permute-start.11 = (f32[64,32,64]{2,1,0:T(8,128)S(1)}, f32[64,32,64]{2,1,0:T(8,128)S(1)}, u32[]{:S(2)}, u32[]{:S(2)}) collective-permute-start(f32[64,32,64]{2,1,0:T(8,128)S(1)} %fusion.10), channel_id=1, source_target_pairs={{0,1},{1,0},{2,3},{3,2},{4,5},{5,4},{6,7},{7,6},{8,9},{9,8},{10,11... | collective-permute-start | bytes 1572872 | tf_op jit(solution)/shard_map/ppermute | solution.py:73

commit v9 on v7

--- a/solution.py
+++ b/solution.py
@@ -2,6 +2,7 @@
 import jax.numpy as jnp
 from jax import lax
 from jax.sharding import PartitionSpec as P
+from jax.experimental.layout import Layout, with_layout_constraint
 
 
 def swap_halves(local, axis):
@@ -23,8 +24,14 @@
 
     upstream = cotangent.reshape(row_count, right_local, order_right)
     right_full = swap_halves(right_factor, 1)
+    eye = jnp.eye(row_count, dtype=jnp.bfloat16)
+    upstream_t = jnp.einsum(
+        "rc,rs->cs", cotangent, eye, preferred_element_type=jnp.float32
+    ).astype(jnp.bfloat16)
+    upstream_t = with_layout_constraint(upstream_t, Layout((0, 1)))
+    upstream_t = upstream_t.reshape(right_local, order_right, row_count)
     back_grad = jnp.einsum(
-        "rjm,jkm->kjr", upstream, right_full, preferred_element_type=jnp.float32
+        "jmr,jkm->kjr", upstream_t, right_full, preferred_element_type=jnp.float32
     ).astype(jnp.bfloat16)
     back_sent = back_grad.reshape(peer_count, local_blocks, right_local, row_count)
     back_got = lax.all_to_all(back_sent, "blk", 0, 0, tiled=True)

time: 122 us -> 121 us (level)
  matrix products: 9.99 us -> 12.6 us
  waiting for transfers between devices: 70.1 us -> 68.3 us
  local copies, waits for them, and re-layouts: 21.9 us -> 20.2 us
    dot_general x1 -> x2, matrix products: 0.68 us -> 3.3 us  [the longest x1 2.61 us: on_device(): jnp.einsum('rc,rs->cs', cotangent, eye, preferred_element_type=jnp.float32)]
    transpose x1, local copies, waits for them, and re-layouts: 3.41 us -> 1.8 us  [on_device(): back_got.transpose(1, 0, 2, 3).reshape(local_blocks, block_size, row_count)]
    all_to_all x1, waiting for transfers between devices: 35 us -> 33.7 us  [on_device(): mixed_got = lax.all_to_all(mixed_sent, 'blk', 0, 0, tiled=True)]
  transfers between devices with their start and end apart: 7 -> 7, of which waited for: 4 -> 3; matrix products, arithmetic and copies ran while one was open for 26% -> 27% of each run, Pallas kernels for 0% -> 0%
where the time goes in v9:
time: 121 us; the launch traced here: 120 us
  waiting for transfers between devices  68.3 us (56%)
  local copies, waits for them, and re-layouts  20.2 us (17%)
  matrix products  12.6 us (10%)
  starting transfers between devices  12.5 us (10%)
  other arithmetic  6.02 us (5%)
    all_to_all x1, waiting for transfers between devices, on_device(): mixed_got = lax.all_to_all(mixed_sent, 'blk', 0, 0, tiled=True)  33.7 us
    all_to_all x1, waiting for transfers between devices, on_device(): back_got = lax.all_to_all(back_sent, 'blk', 0, 0, tiled=True)  32.8 us
    unnamed x11, local copies, waits for them, and re-layouts  11.4 us
    all_to_all x1, starting transfers between devices, on_device(): back_got = lax.all_to_all(back_sent, 'blk', 0, 0, tiled=True)  6.82 us
    all_to_all x1, starting transfers between devices, on_device(): mixed_got = lax.all_to_all(mixed_sent, 'blk', 0, 0, tiled=True)  4.35 us
    dot_general x1, matrix products, on_device(): jnp.einsum('rki,kjr->kij', partner_part, partner_back, preferred_element_...  3.72 us
    select_n x2, other arithmetic, swap_halves(): first = jnp.where(core == 0, local, other)  2.85 us
    dot_general x1, matrix products, on_device(): jnp.einsum('rki,kjr->kij', own_part, back_t, preferred_element_type=jnp.f...  2.67 us
  transfers between devices with their start and end apart: 7, of which 3 were waited for; matrix products, arithmetic and copies ran while one was open for 27% of the time, Pallas kernels for 0%

profile of v9, /device:TPU:0, one launch (start us, length us, event | category | flops | bytes accessed | tf_op | source)
XLA Modules:
  0.0 120.4 jit_solution(14476125080178167691)
XLA Ops:
  0.6 0.5 collective-permute-start.1
  1.1 2.6 %convolution_convert_fusion = bf16[256,4096]{0,1:T(8,128)(2,1)S(1)} fusion(bf16[256,4096]{1,0:T(8,128)(2,1)} %param.6), kind=kOutput, calls=%fused_computation | convolution fusion | flops 537985024 | bytes 4194304 | tf_op jit(solution)/shard_map/rc,rs->cs/dot_general | solution.py:28
  3.8 0.1 broadcast_select_fusion.3
  3.9 0.7 convert_bitcast_fusion
  4.6 1.5 %copy.32 = bf16[8,8,64,256]{3,1,2,0:T(8,128)(2,1)} copy(bf16[8,8,64,256]{3,1,0,2:T(8,128)(2,1)S(1)} %convert_bitcast_fusion) | data formatting | bytes 4194304 | tf_op jit(solution)/shard_map/reshape | solution.py:36
  6.0 6.8 %all-to-all-start = ((bf16[8,8,64,256]{3,1,2,0:T(8,128)(2,1)}), bf16[8,8,64,256]{3,1,2,0:T(8,128)(2,1)S(1)}, u32[]{:S(2)}, u32[]{:S(2)}) async-start(bf16[8,8,64,256]{3,1,2,0:T(8,128)(2,1)} %copy.32), calls=%async_computation | async-start | bytes 4194304 | tf_op jit(solution)/shard_map/all_to_all | solution.py:37
  12.8 3.9 %copy.28 = bf16[8,256,512]{1,2,0:T(8,128)(2,1)} copy(bf16[8,256,512]{2,1,0:T(8,128)(2,1)} %param.7) | data formatting | bytes 4194304 | tf_op args[2]
  16.8 0.2 collective-permute-start
  17.0 4.1 %copy.26 = bf16[256,4096]{0,1:T(8,128)(2,1)} copy(bf16[256,4096]{1,0:T(8,128)(2,1)} %param.5) | data formatting | bytes 4194304 | tf_op args[0]
  21.0 0.1 fusion.18
  21.1 2.1 %broadcast_multiply_fusion = bf16[256,8,512]{0,2,1:T(8,128)(2,1)S(1)} fusion(bf16[256,8,512]{0,2,1:T(8,128)(2,1)} %bitcast.39, bf16[8,512]{1,0:T(8,128)(2,1)S(1)} %fusion.18), kind=kLoop, calls=%fused_computation.25 | loop fusion | flops 1048576 | bytes 4202496 | tf_op jit(solution)/shard_map/mul | solution.py:40
  23.2 0.0 collective-permute-done
  23.2 0.1 copy-done.1
  23.3 2.8 %broadcast_select_fusion.1 = (bf16[8,256,512]{1,2,0:T(8,128)(2,1)S(1)}, bf16[8,256,512]{1,2,0:T(8,128)(2,1)S(1)}) fusion(bf16[8,256,512]{1,2,0:T(8,128)(2,1)S(1)} %copy-done.1, bf16[8,256,512]{1,2,0:T(8,128)(2,1)} %collective-permute-done, pred[]{:T(512)S(6)} %eq.4), kind=kLoop, calls=%fused_computation.9 | loop fusion | flops 2097152 | bytes 8388609 | tf_op jit(solution)/shard_map/jit(_where)/select_n | solution.py:11
  26.1 1.3 %fusion.4 = bf16[8,512,256]{2,1,0:T(8,128)(2,1)S(1)} fusion(bf16[256,8,512]{0,2,1:T(8,128)(2,1)S(1)} %broadcast_multiply_fusion, bf16[8,256,512]{1,2,0:T(8,128)(2,1)S(1)} %get-tuple-element.11, bf16[8,256,512]{1,2,0:T(8,128)(2,1)S(1)} %get-tuple-element.10), kind=kOutput, calls=%fused_computation.10 | convolution fusion | flops 1083179008 | bytes 8388608 | tf_op jit(solution)/shard_map/rki,kij->jkr/dot_general | solution.py:42
  27.4 1.6 %copy.47 = bf16[8,64,8,256]{3,1,2,0:T(8,128)(2,1)} copy(bf16[8,64,8,256]{3,1,0,2:T(8,128)(2,1)S(1)} %bitcast.40) | data formatting | bytes 4194304 | tf_op jit(solution)/shard_map/reshape | solution.py:45
  29.0 32.8 %all-to-all-done = bf16[8,8,64,256]{3,1,2,0:T(8,128)(2,1)S(1)} async-done(((bf16[8,8,64,256]{3,1,2,0:T(8,128)(2,1)}), bf16[8,8,64,256]{3,1,2,0:T(8,128)(2,1)S(1)}, u32[]{:S(2)}, u32[]{:S(2)}) %all-to-all-start) | async-done | bytes 2097184 | tf_op jit(solution)/shard_map/all_to_all | solution.py:37
  61.7 4.3 %all-to-all-start.1 = ((bf16[8,8,64,256]{3,2,1,0:T(8,128)(2,1)}), bf16[8,8,64,256]{3,2,1,0:T(8,128)(2,1)}, u32[]{:S(2)}, u32[]{:S(2)}) async-start(bf16[8,8,64,256]{3,2,1,0:T(8,128)(2,1)} %bitcast.34), calls=%async_computation.1 | async-start | bytes 4194304 | tf_op jit(solution)/shard_map/all_to_all | solution.py:56
  66.1 1.8 %copy.33 = bf16[8,8,64,256]{3,2,1,0:T(8,128)(2,1)} copy(bf16[8,8,64,256]{3,0,2,1:T(8,128)(2,1)S(1)} %bitcast.37) | data formatting | bytes 4194304 | tf_op jit(solution)/shard_map/transpose | solution.py:54
  67.9 0.0 collective-permute-start.3
  67.9 2.4 %constant_dynamic-slice_fusion = bf16[256,8,256]{0,2,1:T(8,128)(2,1)} fusion(bf16[256,8,512]{0,2,1:T(8,128)(2,1)} %copy-done, s32[]{:T(128)S(6)} %select_n.43), kind=kLoop, calls=%fused_computation.31 | loop fusion | bytes 2097156 | tf_op jit(solution)/shard_map/dynamic_slice | solution.py:52
  70.2 0.5 collective-permute-start.2
  70.7 3.3 %copy.35 = bf16[256,4096]{0,1:T(8,128)(2,1)S(1)} copy(bf16[256,4096]{1,0:T(8,128)(2,1)} %param.6) | data formatting | bytes 4194304 | tf_op args[1]
  74.0 2.7 %fusion.16 = f32[8,256,512]{2,1,0:T(8,128)S(1)} fusion(bf16[8,512,256]{2,1,0:T(8,128)(2,1)} %bitcast.9, bf16[256,8,512]{0,2,1:T(8,128)(2,1)} %copy-done, s32[]{:T(128)S(6)} %select_n.36), kind=kOutput, calls=%fused_computation.23 | convolution fusion | flops 536870912 | bytes 7340036 | tf_op jit(solution)/shard_map/rki,kjr->kij/dot_general | solution.py:57
  76.7 3.7 %add_convert_fusion = bf16[8,256,512]{2,1,0:T(8,128)(2,1)} fusion(f32[8,256,512]{2,1,0:T(8,128)S(1)} %fusion.16, bf16[256,8,256]{0,2,1:T(8,128)(2,1)S(1)} %collective-permute-done.2, bf16[8,512,256]{2,1,0:T(8,128)(2,1)} %collective-permute-done.3), kind=kOutput, calls=%fused_computation.5 | convolution fusion | flops 538968064 | bytes 9437184 | tf_op jit(solution)/shard_map/rki,kjr->kij/dot_general | solution.py:58
  80.4 33.7 %all-to-all-done.1 = bf16[8,8,64,256]{3,2,1,0:T(8,128)(2,1)} async-done(((bf16[8,8,64,256]{3,2,1,0:T(8,128)(2,1)}), bf16[8,8,64,256]{3,2,1,0:T(8,128)(2,1)}, u32[]{:S(2)}, u32[]{:S(2)}) %all-to-all-start.1) | async-done | bytes 2097184 | tf_op jit(solution)/shard_map/all_to_all | solution.py:56
  114.1 1.7 %dynamic-slice_bitcast_fusion = (bf16[64,4,8,256]{3,0,2,1:T(8,128)(2,1)S(1)}, bf16[64,4,8,256]{3,0,2,1:T(8,128)(2,1)S(1)}) fusion(bf16[8,8,64,256]{3,2,1,0:T(8,128)(2,1)} %all-to-all-done.1, s32[]{:T(128)S(6)} %select_n.45, s32[]{:T(128)S(6)} %select_n.44), kind=kLoop, calls=%fused_computation.21 | loop fusion | bytes 4194312 | tf_op jit(solution)/shard_map/transpose | solution.py:67
  115.8 0.8 fusion.10
  116.7 0.1 collective-permute-start.4
  116.7 0.8 fusion.12
  117.6 1.8 %collective-permute-done.4 = f32[64,32,64]{2,1,0:T(8,128)S(1)} collective-permute-done((f32[64,32,64]{2,1,0:T(8,128)S(1)}, f32[64,32,64]{2,1,0:T(8,128)S(1)}, u32[]{:S(2)}, u32[]{:S(2)}) %collective-permute-start.4) | collective-permute-done | bytes 524320 | tf_op jit(solution)/shard_map/ppermute | solution.py:70
  119.4 1.0 add_convert_fusion.1
  (10 shorter events, 0.0 us)
Async XLA Ops:
  0.6 3.1 %collective-permute-start.1 = (bf16[64,32,64]{2,1,0:T(8,128)(2,1)}, bf16[64,32,64]{2,1,0:T(8,128)(2,1)S(1)}, u32[]{:S(2)}, u32[]{:S(2)}) collective-permute-start(bf16[64,32,64]{2,1,0:T(8,128)(2,1)} %param.8), channel_id=1, source_target_pairs={{0,1},{1,0},{2,3},{3,2},{4,5},{5,4},{6,7},{7,6},{8,9},{9,8},{10,11... | collective-permute-start | bytes 786440 | tf_op jit(solution)/shard_map/ppermute | solution.py:9
  1.1 2.6 %copy-start.2 = (bf16[64,32,64]{2,1,0:T(8,128)(2,1)S(1)}, bf16[64,32,64]{2,1,0:T(8,128)(2,1)}, u32[]{:S(2)}) copy-start(bf16[64,32,64]{2,1,0:T(8,128)(2,1)} %param.8) | copy-start | bytes 786436
  6.0 55.7 %all-to-all-start = ((bf16[8,8,64,256]{3,1,2,0:T(8,128)(2,1)}), bf16[8,8,64,256]{3,1,2,0:T(8,128)(2,1)S(1)}, u32[]{:S(2)}, u32[]{:S(2)}) async-start(bf16[8,8,64,256]{3,1,2,0:T(8,128)(2,1)} %copy.32), calls=%async_computation | async-start | bytes 4194304 | tf_op jit(solution)/shard_map/all_to_all | solution.py:37
  16.8 4.3 %copy-start.3 = (s32[8]{0:T(128)S(1)}, s32[8]{0:T(128)}, u32[]{:S(2)}) copy-start(s32[8]{0:T(128)} %param.9) | copy-start | bytes 100
  16.8 6.5 %collective-permute-start = (bf16[8,256,512]{1,2,0:T(8,128)(2,1)}, bf16[8,256,512]{1,2,0:T(8,128)(2,1)}, u32[]{:S(2)}, u32[]{:S(2)}) collective-permute-start(bf16[8,256,512]{1,2,0:T(8,128)(2,1)} %copy.28), channel_id=1, source_target_pairs={{0,1},{1,0},{2,3},{3,2},{4,5},{5,4},{6,7},{7,6},{8,9},{9,8},{10,11... | collective-permute-start | bytes 6291464 | tf_op jit(solution)/shard_map/ppermute | solution.py:9
  21.1 2.2 %copy-start.1 = (bf16[8,256,512]{1,2,0:T(8,128)(2,1)S(1)}, bf16[8,256,512]{1,2,0:T(8,128)(2,1)}, u32[]{:S(2)}) copy-start(bf16[8,256,512]{1,2,0:T(8,128)(2,1)} %copy.28) | copy-start | bytes 6291460
  23.2 2.9 %copy-start = (bf16[256,8,512]{0,2,1:T(8,128)(2,1)}, bf16[256,8,512]{0,2,1:T(8,128)(2,1)S(1)}, u32[]{:S(2)}) copy-start(bf16[256,8,512]{0,2,1:T(8,128)(2,1)S(1)} %broadcast_multiply_fusion) | copy-start | bytes 6291460
  61.7 52.4 %all-to-all-start.1 = ((bf16[8,8,64,256]{3,2,1,0:T(8,128)(2,1)}), bf16[8,8,64,256]{3,2,1,0:T(8,128)(2,1)}, u32[]{:S(2)}, u32[]{:S(2)}) async-start(bf16[8,8,64,256]{3,2,1,0:T(8,128)(2,1)} %bitcast.34), calls=%async_computation.1 | async-start | bytes 4194304 | tf_op jit(solution)/shard_map/all_to_all | solution.py:56
  67.9 8.8 %collective-permute-start.3 = (bf16[8,512,256]{2,1,0:T(8,128)(2,1)}, bf16[8,512,256]{2,1,0:T(8,128)(2,1)}, u32[]{:S(2)}, u32[]{:S(2)}) collective-permute-start(bf16[8,512,256]{2,1,0:T(8,128)(2,1)} %bitcast.9), channel_id=1, source_target_pairs={{0,1},{1,0},{2,3},{3,2},{4,5},{5,4},{6,7},{7,6},{8,9},{9,8},{10,11... | collective-permute-start | bytes 6291464 | tf_op jit(solution)/shard_map/ppermute | solution.py:55
  70.2 6.5 %collective-permute-start.2 = (bf16[256,8,256]{0,2,1:T(8,128)(2,1)}, bf16[256,8,256]{0,2,1:T(8,128)(2,1)S(1)}, u32[]{:S(2)}, u32[]{:S(2)}) collective-permute-start(bf16[256,8,256]{0,2,1:T(8,128)(2,1)} %constant_dynamic-slice_fusion), channel_id=1, source_target_pairs={{0,1},{1,0},{2,3},{3,2},{4,5},{5,4},{6,7},{7,6},{8,9},{9,8},{10,11... | collective-permute-start | bytes 3145736 | tf_op jit(solution)/shard_map/ppermute | solution.py:53
  116.7 2.7 %collective-permute-start.4 = (f32[64,32,64]{2,1,0:T(8,128)S(1)}, f32[64,32,64]{2,1,0:T(8,128)S(1)}, u32[]{:S(2)}, u32[]{:S(2)}) collective-permute-start(f32[64,32,64]{2,1,0:T(8,128)S(1)} %fusion.10), channel_id=1, source_target_pairs={{0,1},{1,0},{2,3},{3,2},{4,5},{5,4},{6,7},{7,6},{8,9},{9,8},{10,11... | collective-permute-start | bytes 1572872 | tf_op jit(solution)/shard_map/ppermute | solution.py:70

commit v10 on v9

--- a/solution.py
+++ b/solution.py
@@ -67,7 +67,10 @@
         blocks = blocks.transpose(2, 0, 1, 3).reshape(right_local, half_peers * local_blocks, row_count)
         return jnp.einsum("jkr,rjm->jkm", blocks, upstream, preferred_element_type=jnp.float32)
 
-    got_right = lax.ppermute(right_of((1 - core) * half_peers), "bin", [(0, 1), (1, 0)])
+    theirs_right = right_of((1 - core) * half_peers)
+    theirs_right, own_got = lax.optimization_barrier((theirs_right, mixed_got))
+    got_right = lax.ppermute(theirs_right, "bin", [(0, 1), (1, 0)])
+    mixed_got = own_got
     grad_right = (lax.optimization_barrier(right_of(core * half_peers)) + got_right).astype(
         jnp.bfloat16
     )

time: 121 us -> 122 us (level)
    transpose x1 -> x2, local copies, waits for them, and re-layouts: 1.68 us -> 2.59 us  [right_of(): blocks.transpose(2, 0, 1, 3)]
  transfers between devices with their start and end apart: 7 -> 7, of which waited for: 3 -> 3; matrix products, arithmetic and copies ran while one was open for 27% -> 28% of each run, Pallas kernels for 0% -> 0%
where the time goes in v10:
time: 122 us; the launch traced here: 121 us
  waiting for transfers between devices  67.2 us (55%)
  local copies, waits for them, and re-layouts  21.1 us (17%)
  matrix products  13.6 us (11%)
  starting transfers between devices  12.4 us (10%)
  other arithmetic  6.02 us (5%)
    all_to_all x1, waiting for transfers between devices, on_device(): mixed_got = lax.all_to_all(mixed_sent, 'blk', 0, 0, tiled=True)  33.7 us
    all_to_all x1, waiting for transfers between devices, on_device(): back_got = lax.all_to_all(back_sent, 'blk', 0, 0, tiled=True)  32.8 us
    unnamed x11, local copies, waits for them, and re-layouts  11.4 us
    all_to_all x1, starting transfers between devices, on_device(): back_got = lax.all_to_all(back_sent, 'blk', 0, 0, tiled=True)  6.82 us
    all_to_all x1, starting transfers between devices, on_device(): mixed_got = lax.all_to_all(mixed_sent, 'blk', 0, 0, tiled=True)  4.35 us
    dot_general x1, matrix products, on_device(): jnp.einsum('rki,kjr->kij', partner_part, partner_back, preferred_element_...  3.72 us
    select_n x2, other arithmetic, swap_halves(): first = jnp.where(core == 0, local, other)  2.85 us
    dot_general x2, matrix products, right_of(): jnp.einsum('jkr,rjm->jkm', blocks, upstream, preferred_element_type=jnp.f...  2.67 us
  transfers between devices with their start and end apart: 7, of which 3 were waited for; matrix products, arithmetic and copies ran while one was open for 28% of the time, Pallas kernels for 0%

profile of v10, /device:TPU:0, one launch (start us, length us, event | category | flops | bytes accessed | tf_op | source)
XLA Modules:
  0.0 121.2 jit_solution(3250351354037558497)
XLA Ops:
  0.6 0.5 collective-permute-start.1
  1.1 2.6 %convolution_convert_fusion = bf16[256,4096]{0,1:T(8,128)(2,1)S(1)} fusion(bf16[256,4096]{1,0:T(8,128)(2,1)} %param.6), kind=kOutput, calls=%fused_computation | convolution fusion | flops 537985024 | bytes 4194304 | tf_op jit(solution)/shard_map/rc,rs->cs/dot_general | solution.py:28
  3.8 0.0 collective-permute-done.1
  3.8 0.1 broadcast_select_fusion.3
  3.9 0.7 convert_bitcast_fusion
  4.6 1.5 %copy.32 = bf16[8,8,64,256]{3,1,2,0:T(8,128)(2,1)} copy(bf16[8,8,64,256]{3,1,0,2:T(8,128)(2,1)S(1)} %convert_bitcast_fusion) | data formatting | bytes 4194304 | tf_op jit(solution)/shard_map/reshape | solution.py:36
  6.0 6.8 %all-to-all-start = ((bf16[8,8,64,256]{3,1,2,0:T(8,128)(2,1)}), bf16[8,8,64,256]{3,1,2,0:T(8,128)(2,1)S(1)}, u32[]{:S(2)}, u32[]{:S(2)}) async-start(bf16[8,8,64,256]{3,1,2,0:T(8,128)(2,1)} %copy.32), calls=%async_computation | async-start | bytes 4194304 | tf_op jit(solution)/shard_map/all_to_all | solution.py:37
  12.8 3.9 %copy.28 = bf16[8,256,512]{1,2,0:T(8,128)(2,1)} copy(bf16[8,256,512]{2,1,0:T(8,128)(2,1)} %param.7) | data formatting | bytes 4194304 | tf_op args[2]
  16.8 0.2 collective-permute-start
  17.0 4.1 %copy.26 = bf16[256,4096]{0,1:T(8,128)(2,1)} copy(bf16[256,4096]{1,0:T(8,128)(2,1)} %param.5) | data formatting | bytes 4194304 | tf_op args[0]
  21.0 0.1 fusion.18
  21.1 2.1 %broadcast_multiply_fusion = bf16[256,8,512]{0,2,1:T(8,128)(2,1)S(1)} fusion(bf16[256,8,512]{0,2,1:T(8,128)(2,1)} %bitcast.39, bf16[8,512]{1,0:T(8,128)(2,1)S(1)} %fusion.18), kind=kLoop, calls=%fused_computation.25 | loop fusion | flops 1048576 | bytes 4202496 | tf_op jit(solution)/shard_map/mul | solution.py:40
  23.2 0.1 copy-done.1
  23.3 2.8 %broadcast_select_fusion.1 = (bf16[8,256,512]{1,2,0:T(8,128)(2,1)S(1)}, bf16[8,256,512]{1,2,0:T(8,128)(2,1)S(1)}) fusion(bf16[8,256,512]{1,2,0:T(8,128)(2,1)S(1)} %copy-done.1, bf16[8,256,512]{1,2,0:T(8,128)(2,1)} %collective-permute-done, pred[]{:T(512)S(6)} %eq.4), kind=kLoop, calls=%fused_computation.9 | loop fusion | flops 2097152 | bytes 8388609 | tf_op jit(solution)/shard_map/jit(_where)/select_n | solution.py:11
  26.1 1.3 %fusion.4 = bf16[8,512,256]{2,1,0:T(8,128)(2,1)S(1)} fusion(bf16[256,8,512]{0,2,1:T(8,128)(2,1)S(1)} %broadcast_multiply_fusion, bf16[8,256,512]{1,2,0:T(8,128)(2,1)S(1)} %get-tuple-element.15, bf16[8,256,512]{1,2,0:T(8,128)(2,1)S(1)} %get-tuple-element.14), kind=kOutput, calls=%fused_computation.10 | convolution fusion | flops 1083179008 | bytes 8388608 | tf_op jit(solution)/shard_map/rki,kij->jkr/dot_general | solution.py:42
  27.4 1.6 %copy.47 = bf16[8,64,8,256]{3,1,2,0:T(8,128)(2,1)} copy(bf16[8,64,8,256]{3,1,0,2:T(8,128)(2,1)S(1)} %bitcast.40) | data formatting | bytes 4194304 | tf_op jit(solution)/shard_map/reshape | solution.py:45
  29.0 32.8 %all-to-all-done = bf16[8,8,64,256]{3,1,2,0:T(8,128)(2,1)S(1)} async-done(((bf16[8,8,64,256]{3,1,2,0:T(8,128)(2,1)}), bf16[8,8,64,256]{3,1,2,0:T(8,128)(2,1)S(1)}, u32[]{:S(2)}, u32[]{:S(2)}) %all-to-all-start) | async-done | bytes 2097184 | tf_op jit(solution)/shard_map/all_to_all | solution.py:37
  61.7 4.4 %all-to-all-start.1 = ((bf16[8,8,64,256]{3,2,1,0:T(8,128)(2,1)}), bf16[8,8,64,256]{3,2,1,0:T(8,128)(2,1)}, u32[]{:S(2)}, u32[]{:S(2)}) async-start(bf16[8,8,64,256]{3,2,1,0:T(8,128)(2,1)} %bitcast.34), calls=%async_computation.1 | async-start | bytes 4194304 | tf_op jit(solution)/shard_map/all_to_all | solution.py:56
  66.1 1.8 %copy.33 = bf16[8,8,64,256]{3,2,1,0:T(8,128)(2,1)} copy(bf16[8,8,64,256]{3,0,2,1:T(8,128)(2,1)S(1)} %bitcast.37) | data formatting | bytes 4194304 | tf_op jit(solution)/shard_map/transpose | solution.py:54
  67.9 0.0 collective-permute-start.3
  67.9 2.4 %constant_dynamic-slice_fusion = bf16[256,8,256]{0,2,1:T(8,128)(2,1)} fusion(bf16[256,8,512]{0,2,1:T(8,128)(2,1)} %copy-done, s32[]{:T(128)S(6)} %select_n.43), kind=kLoop, calls=%fused_computation.31 | loop fusion | bytes 2097156 | tf_op jit(solution)/shard_map/dynamic_slice | solution.py:52
  70.3 0.5 collective-permute-start.2
  70.8 3.3 %copy.35 = bf16[256,4096]{0,1:T(8,128)(2,1)S(1)} copy(bf16[256,4096]{1,0:T(8,128)(2,1)} %param.6) | data formatting | bytes 4194304 | tf_op args[1]
  74.0 2.7 %fusion.16 = f32[8,256,512]{2,1,0:T(8,128)S(1)} fusion(bf16[8,512,256]{2,1,0:T(8,128)(2,1)} %bitcast.9, bf16[256,8,512]{0,2,1:T(8,128)(2,1)} %copy-done, s32[]{:T(128)S(6)} %select_n.36), kind=kOutput, calls=%fused_computation.23 | convolution fusion | flops 536870912 | bytes 7340036 | tf_op jit(solution)/shard_map/rki,kjr->kij/dot_general | solution.py:57
  76.7 3.7 %add_convert_fusion = bf16[8,256,512]{2,1,0:T(8,128)(2,1)} fusion(f32[8,256,512]{2,1,0:T(8,128)S(1)} %fusion.16, bf16[256,8,256]{0,2,1:T(8,128)(2,1)S(1)} %collective-permute-done.2, bf16[8,512,256]{2,1,0:T(8,128)(2,1)} %collective-permute-done.3), kind=kOutput, calls=%fused_computation.5 | convolution fusion | flops 538968064 | bytes 9437184 | tf_op jit(solution)/shard_map/rki,kjr->kij/dot_general | solution.py:58
  80.4 33.7 %all-to-all-done.1 = bf16[8,8,64,256]{3,2,1,0:T(8,128)(2,1)} async-done(((bf16[8,8,64,256]{3,2,1,0:T(8,128)(2,1)}), bf16[8,8,64,256]{3,2,1,0:T(8,128)(2,1)}, u32[]{:S(2)}, u32[]{:S(2)}) %all-to-all-start.1) | async-done | bytes 2097184 | tf_op jit(solution)/shard_map/all_to_all | solution.py:56
  114.2 1.3 %dynamic-slice_bitcast_fusion.1 = bf16[64,4,8,256]{3,0,2,1:T(8,128)(2,1)S(1)} fusion(bf16[8,8,64,256]{3,2,1,0:T(8,128)(2,1)} %all-to-all-done.1, s32[]{:T(128)S(6)} %select_n.44), kind=kLoop, calls=%fused_computation.22 | loop fusion | bytes 2097156 | tf_op jit(solution)/shard_map/transpose | solution.py:67
  115.4 1.8 %fusion.12 = f32[64,32,64]{2,1,0:T(8,128)} fusion(bf16[256,64,64]{0,2,1:T(8,128)(2,1)S(1)} %bitcast.35, bf16[64,4,8,256]{3,0,2,1:T(8,128)(2,1)S(1)} %dynamic-slice_bitcast_fusion.1), kind=kOutput, calls=%fused_computation.16 | convolution fusion | flops 67108864 | bytes 3670016 | tf_op jit(solution)/shard_map/jkr,rjm->jkm/dot_general | solution.py:68
  117.3 1.3 %dynamic-slice_bitcast_fusion = bf16[64,4,8,256]{3,0,2,1:T(8,128)(2,1)S(1)} fusion(bf16[8,8,64,256]{3,2,1,0:T(8,128)(2,1)} %all-to-all-done.1, s32[]{:T(128)S(6)} %select_n.45), kind=kLoop, calls=%fused_computation.21 | loop fusion | bytes 2097156 | tf_op jit(solution)/shard_map/transpose | solution.py:67
  118.6 0.8 fusion.10
  119.4 0.7 collective-permute-done.4
  120.2 1.0 add_convert_fusion.1
  (11 shorter events, 0.0 us)
Async XLA Ops:
  0.6 3.1 %collective-permute-start.1 = (bf16[64,32,64]{2,1,0:T(8,128)(2,1)}, bf16[64,32,64]{2,1,0:T(8,128)(2,1)S(1)}, u32[]{:S(2)}, u32[]{:S(2)}) collective-permute-start(bf16[64,32,64]{2,1,0:T(8,128)(2,1)} %param.8), channel_id=1, source_target_pairs={{0,1},{1,0},{2,3},{3,2},{4,5},{5,4},{6,7},{7,6},{8,9},{9,8},{10,11... | collective-permute-start | bytes 786440 | tf_op jit(solution)/shard_map/ppermute | solution.py:9
  1.1 2.6 %copy-start.2 = (bf16[64,32,64]{2,1,0:T(8,128)(2,1)S(1)}, bf16[64,32,64]{2,1,0:T(8,128)(2,1)}, u32[]{:S(2)}) copy-start(bf16[64,32,64]{2,1,0:T(8,128)(2,1)} %param.8) | copy-start | bytes 786436
  6.0 55.7 %all-to-all-start = ((bf16[8,8,64,256]{3,1,2,0:T(8,128)(2,1)}), bf16[8,8,64,256]{3,1,2,0:T(8,128)(2,1)S(1)}, u32[]{:S(2)}, u32[]{:S(2)}) async-start(bf16[8,8,64,256]{3,1,2,0:T(8,128)(2,1)} %copy.32), calls=%async_computation | async-start | bytes 4194304 | tf_op jit(solution)/shard_map/all_to_all | solution.py:37
  16.8 4.3 %copy-start.3 = (s32[8]{0:T(128)S(1)}, s32[8]{0:T(128)}, u32[]{:S(2)}) copy-start(s32[8]{0:T(128)} %param.9) | copy-start | bytes 100
  16.8 6.5 %collective-permute-start = (bf16[8,256,512]{1,2,0:T(8,128)(2,1)}, bf16[8,256,512]{1,2,0:T(8,128)(2,1)}, u32[]{:S(2)}, u32[]{:S(2)}) collective-permute-start(bf16[8,256,512]{1,2,0:T(8,128)(2,1)} %copy.28), channel_id=1, source_target_pairs={{0,1},{1,0},{2,3},{3,2},{4,5},{5,4},{6,7},{7,6},{8,9},{9,8},{10,11... | collective-permute-start | bytes 6291464 | tf_op jit(solution)/shard_map/ppermute | solution.py:9
  21.1 2.2 %copy-start.1 = (bf16[8,256,512]{1,2,0:T(8,128)(2,1)S(1)}, bf16[8,256,512]{1,2,0:T(8,128)(2,1)}, u32[]{:S(2)}) copy-start(bf16[8,256,512]{1,2,0:T(8,128)(2,1)} %copy.28) | copy-start | bytes 6291460
  23.2 2.9 %copy-start = (bf16[256,8,512]{0,2,1:T(8,128)(2,1)}, bf16[256,8,512]{0,2,1:T(8,128)(2,1)S(1)}, u32[]{:S(2)}) copy-start(bf16[256,8,512]{0,2,1:T(8,128)(2,1)S(1)} %broadcast_multiply_fusion) | copy-start | bytes 6291460
  61.7 52.4 %all-to-all-start.1 = ((bf16[8,8,64,256]{3,2,1,0:T(8,128)(2,1)}), bf16[8,8,64,256]{3,2,1,0:T(8,128)(2,1)}, u32[]{:S(2)}, u32[]{:S(2)}) async-start(bf16[8,8,64,256]{3,2,1,0:T(8,128)(2,1)} %bitcast.34), calls=%async_computation.1 | async-start | bytes 4194304 | tf_op jit(solution)/shard_map/all_to_all | solution.py:56
  67.9 8.8 %collective-permute-start.3 = (bf16[8,512,256]{2,1,0:T(8,128)(2,1)}, bf16[8,512,256]{2,1,0:T(8,128)(2,1)}, u32[]{:S(2)}, u32[]{:S(2)}) collective-permute-start(bf16[8,512,256]{2,1,0:T(8,128)(2,1)} %bitcast.9), channel_id=1, source_target_pairs={{0,1},{1,0},{2,3},{3,2},{4,5},{5,4},{6,7},{7,6},{8,9},{9,8},{10,11... | collective-permute-start | bytes 6291464 | tf_op jit(solution)/shard_map/ppermute | solution.py:55
  70.3 6.5 %collective-permute-start.2 = (bf16[256,8,256]{0,2,1:T(8,128)(2,1)}, bf16[256,8,256]{0,2,1:T(8,128)(2,1)S(1)}, u32[]{:S(2)}, u32[]{:S(2)}) collective-permute-start(bf16[256,8,256]{0,2,1:T(8,128)(2,1)} %constant_dynamic-slice_fusion), channel_id=1, source_target_pairs={{0,1},{1,0},{2,3},{3,2},{4,5},{5,4},{6,7},{7,6},{8,9},{9,8},{10,11... | collective-permute-start | bytes 3145736 | tf_op jit(solution)/shard_map/ppermute | solution.py:53
  117.3 2.9 %collective-permute-start.4 = (f32[64,32,64]{2,1,0:T(8,128)}, f32[64,32,64]{2,1,0:T(8,128)S(1)}, u32[]{:S(2)}, u32[]{:S(2)}) collective-permute-start(f32[64,32,64]{2,1,0:T(8,128)} %fusion.12), channel_id=1, source_target_pairs={{0,1},{1,0},{2,3},{3,2},{4,5},{5,4},{6,7},{7,6},{8,9},{9,8},{10,11... | collective-permute-start | bytes 1572872 | tf_op jit(solution)/shard_map/ppermute | solution.py:72

commit v11 on v9

--- a/solution.py
+++ b/solution.py
@@ -61,16 +61,17 @@
     grad_left = left_term.astype(jnp.bfloat16)
     grad_left, mixed_got = lax.optimization_barrier((grad_left, mixed_got))
     half_peers = peer_count // 2
+    partner_up = lax.ppermute(upstream, "bin", swap)
 
-    def right_of(start):
-        blocks = lax.dynamic_slice_in_dim(mixed_got, start, half_peers, axis=0)
-        blocks = blocks.transpose(2, 0, 1, 3).reshape(right_local, half_peers * local_blocks, row_count)
-        return jnp.einsum("jkr,rjm->jkm", blocks, upstream, preferred_element_type=jnp.float32)
+    def right_of(got, rows):
+        blocks = got.transpose(2, 0, 1, 3).reshape(right_local, half_peers * local_blocks, row_count)
+        return jnp.einsum("jkr,rjm->jkm", blocks, rows, preferred_element_type=jnp.float32)
 
-    got_right = lax.ppermute(right_of((1 - core) * half_peers), "bin", [(0, 1), (1, 0)])
-    grad_right = (lax.optimization_barrier(right_of(core * half_peers)) + got_right).astype(
-        jnp.bfloat16
-    )
+    own_blocks = lax.dynamic_slice_in_dim(mixed_got, core * half_peers, half_peers, axis=0)
+    their_blocks = lax.dynamic_slice_in_dim(mixed_got, (1 - core) * half_peers, half_peers, axis=0)
+    partner_blocks = lax.ppermute(their_blocks, "bin", swap)
+    own_term = lax.optimization_barrier(right_of(own_blocks, upstream))
+    grad_right = (own_term + right_of(partner_blocks, partner_up)).astype(jnp.bfloat16)
     return (grad_left, grad_right)
 
 

time: 121 us -> 122 us (level)
  local copies, waits for them, and re-layouts: 20.2 us -> 23.8 us
  waiting for transfers between devices: 68.3 us -> 64.9 us
  matrix products: 12.6 us -> 15 us
    unnamed x11 -> x15, local copies, waits for them, and re-layouts: 11.4 us -> 14.9 us
    dot_general x2, matrix products: 1.68 us -> 4.12 us  [right_of(): jnp.einsum('jkr,rjm->jkm', blocks, rows, preferred_element_type=jnp.float32)]
    all_to_all x1, waiting for transfers between devices: 33.7 us -> 31.7 us  [on_device(): mixed_got = lax.all_to_all(mixed_sent, 'blk', 0, 0, tiled=True)]
    transpose x1, local copies, waits for them, and re-layouts: 1.8 us -> 3.48 us  [on_device(): back_got.transpose(1, 0, 2, 3).reshape(local_blocks, block_size, row_count)]
    transpose x1 -> x0, local copies, waits for them, and re-layouts: 1.68 us -> none  [right_of(): blocks.transpose(2, 0, 1, 3)]
    ppermute x1 -> x2, waiting for transfers between devices: 1.81 us -> 0.48 us  [the longest x1 0.47 us: on_device(): partner_blocks = lax.ppermute(their_blocks, 'bin', swap)]
  transfers between devices with their start and end apart: 7 -> 8, of which waited for: 3 -> 3; matrix products, arithmetic and copies ran while one was open for 27% -> 29% of each run, Pallas kernels for 0% -> 0%
where the time goes in v11:
time: 122 us; the launch traced here: 121 us
  waiting for transfers between devices  64.9 us (53%)
  local copies, waits for them, and re-layouts  23.8 us (20%)
  matrix products  15 us (12%)
  starting transfers between devices  11.8 us (10%)
  other arithmetic  5.01 us (4%)
    all_to_all x1, waiting for transfers between devices, on_device(): back_got = lax.all_to_all(back_sent, 'blk', 0, 0, tiled=True)  32.8 us
    all_to_all x1, waiting for transfers between devices, on_device(): mixed_got = lax.all_to_all(mixed_sent, 'blk', 0, 0, tiled=True)  31.7 us
    unnamed x15, local copies, waits for them, and re-layouts  14.9 us
    all_to_all x1, starting transfers between devices, on_device(): back_got = lax.all_to_all(back_sent, 'blk', 0, 0, tiled=True)  6.83 us
    dot_general x2, matrix products, right_of(): jnp.einsum('jkr,rjm->jkm', blocks, rows, preferred_element_type=jnp.float32)  4.12 us
    dot_general x1, matrix products, on_device(): jnp.einsum('rki,kjr->kij', partner_part, partner_back, preferred_element_...  3.72 us
    all_to_all x1, starting transfers between devices, on_device(): mixed_got = lax.all_to_all(mixed_sent, 'blk', 0, 0, tiled=True)  3.64 us
    transpose x1, local copies, waits for them, and re-layouts, on_device(): back_got.transpose(1, 0, 2, 3).reshape(local_blocks, block_size, row_count)  3.48 us
  transfers between devices with their start and end apart: 8, of which 3 were waited for; matrix products, arithmetic and copies ran while one was open for 29% of the time, Pallas kernels for 0%

profile of v11, /device:TPU:0, one launch (start us, length us, event | category | flops | bytes accessed | tf_op | source)
XLA Modules:
  0.0 121.3 jit_solution(3694435042305776545)
XLA Ops:
  0.6 0.5 collective-permute-start.1
  1.1 2.6 %convolution_convert_fusion = bf16[256,4096]{0,1:T(8,128)(2,1)S(1)} fusion(bf16[256,4096]{1,0:T(8,128)(2,1)} %param.6), kind=kOutput, calls=%fused_computation | convolution fusion | flops 537985024 | bytes 4194304 | tf_op jit(solution)/shard_map/rc,rs->cs/dot_general | solution.py:28
  3.8 0.1 broadcast_select_fusion.3
  3.9 0.7 convert_bitcast_fusion
  4.6 1.5 %copy.22 = bf16[8,8,64,256]{3,1,2,0:T(8,128)(2,1)} copy(bf16[8,8,64,256]{3,1,0,2:T(8,128)(2,1)S(1)} %convert_bitcast_fusion) | data formatting | bytes 4194304 | tf_op jit(solution)/shard_map/reshape | solution.py:36
  6.0 6.8 %all-to-all-start = ((bf16[8,8,64,256]{3,1,2,0:T(8,128)(2,1)}), bf16[8,8,64,256]{3,1,2,0:T(8,128)(2,1)S(1)}, u32[]{:S(2)}, u32[]{:S(2)}) async-start(bf16[8,8,64,256]{3,1,2,0:T(8,128)(2,1)} %copy.22), calls=%async_computation | async-start | bytes 4194304 | tf_op jit(solution)/shard_map/all_to_all | solution.py:37
  12.8 3.9 %copy.18 = bf16[8,256,512]{1,2,0:T(8,128)(2,1)} copy(bf16[8,256,512]{2,1,0:T(8,128)(2,1)} %param.7) | data formatting | bytes 4194304 | tf_op args[2]
  16.8 0.2 collective-permute-start
  17.0 4.1 %copy.16 = bf16[256,4096]{0,1:T(8,128)(2,1)} copy(bf16[256,4096]{1,0:T(8,128)(2,1)} %param.5) | data formatting | bytes 4194304 | tf_op args[0]
  21.0 0.1 fusion.18
  21.1 2.1 %broadcast_multiply_fusion = bf16[256,8,512]{0,2,1:T(8,128)(2,1)S(1)} fusion(bf16[256,8,512]{0,2,1:T(8,128)(2,1)} %bitcast.39, bf16[8,512]{1,0:T(8,128)(2,1)S(1)} %fusion.18), kind=kLoop, calls=%fused_computation.24 | loop fusion | flops 1048576 | bytes 4202496 | tf_op jit(solution)/shard_map/mul | solution.py:40
  23.2 0.1 copy-done.3
  23.3 2.8 %broadcast_select_fusion.1 = (bf16[8,256,512]{1,2,0:T(8,128)(2,1)S(1)}, bf16[8,256,512]{1,2,0:T(8,128)(2,1)S(1)}) fusion(bf16[8,256,512]{1,2,0:T(8,128)(2,1)S(1)} %copy-done.3, bf16[8,256,512]{1,2,0:T(8,128)(2,1)} %collective-permute-done, pred[]{:T(512)S(6)} %eq.4), kind=kLoop, calls=%fused_computation.9 | loop fusion | flops 2097152 | bytes 8388609 | tf_op jit(solution)/shard_map/jit(_where)/select_n | solution.py:11
  26.1 1.3 %fusion.4 = bf16[8,512,256]{2,1,0:T(8,128)(2,1)S(1)} fusion(bf16[256,8,512]{0,2,1:T(8,128)(2,1)S(1)} %broadcast_multiply_fusion, bf16[8,256,512]{1,2,0:T(8,128)(2,1)S(1)} %get-tuple-element.11, bf16[8,256,512]{1,2,0:T(8,128)(2,1)S(1)} %get-tuple-element.10), kind=kOutput, calls=%fused_computation.10 | convolution fusion | flops 1083179008 | bytes 8388608 | tf_op jit(solution)/shard_map/rki,kij->jkr/dot_general | solution.py:42
  27.4 1.6 %copy.37 = bf16[8,64,8,256]{3,1,2,0:T(8,128)(2,1)} copy(bf16[8,64,8,256]{3,1,0,2:T(8,128)(2,1)S(1)} %bitcast.40) | data formatting | bytes 4194304 | tf_op jit(solution)/shard_map/reshape | solution.py:45
  29.0 32.8 %all-to-all-done = bf16[8,8,64,256]{3,1,2,0:T(8,128)(2,1)S(1)} async-done(((bf16[8,8,64,256]{3,1,2,0:T(8,128)(2,1)}), bf16[8,8,64,256]{3,1,2,0:T(8,128)(2,1)S(1)}, u32[]{:S(2)}, u32[]{:S(2)}) %all-to-all-start) | async-done | bytes 2097184 | tf_op jit(solution)/shard_map/all_to_all | solution.py:37
  61.7 1.3 %copy-done.1 = bf16[8,8,64,256]{3,1,2,0:T(8,128)(2,1)} copy-done((bf16[8,8,64,256]{3,1,2,0:T(8,128)(2,1)}, bf16[8,8,64,256]{3,1,2,0:T(8,128)(2,1)S(1)}, u32[]{:S(2)}) %copy-start.1) | copy-done | bytes 2097176
  63.0 3.6 %all-to-all-start.1 = ((bf16[8,8,64,256]{3,2,1,0:T(8,128)(2,1)}), bf16[8,8,64,256]{3,2,1,0:T(8,128)(2,1)S(1)}, u32[]{:S(2)}, u32[]{:S(2)}) async-start(bf16[8,8,64,256]{3,2,1,0:T(8,128)(2,1)} %bitcast.34), calls=%async_computation.1 | async-start | bytes 4194304 | tf_op jit(solution)/shard_map/all_to_all | solution.py:56
  66.7 3.5 %copy.23 = bf16[8,8,64,256]{3,2,1,0:T(8,128)(2,1)} copy(bf16[8,8,64,256]{3,0,2,1:T(8,128)(2,1)} %bitcast.37) | data formatting | bytes 4194304 | tf_op jit(solution)/shard_map/transpose | solution.py:54
  70.2 2.3 %constant_dynamic-slice_fusion.1 = bf16[256,8,256]{0,2,1:T(8,128)(2,1)} fusion(bf16[256,8,512]{0,2,1:T(8,128)(2,1)} %copy-done.2, s32[]{:T(128)S(6)} %select_n.43), kind=kLoop, calls=%fused_computation.31 | loop fusion | bytes 2097156 | tf_op jit(solution)/shard_map/dynamic_slice | solution.py:52
  72.4 0.5 collective-permute-start.2
  72.9 4.1 %copy.25 = bf16[256,4096]{0,1:T(8,128)(2,1)} copy(bf16[256,4096]{1,0:T(8,128)(2,1)} %param.6) | data formatting | bytes 4194304 | tf_op args[1]
  77.0 0.0 collective-permute-start.5
  77.0 2.7 %fusion.16 = f32[8,256,512]{2,1,0:T(8,128)S(1)} fusion(bf16[8,512,256]{2,1,0:T(8,128)(2,1)} %bitcast.9, bf16[256,8,512]{0,2,1:T(8,128)(2,1)} %copy-done.2, s32[]{:T(128)S(6)} %select_n.36), kind=kOutput, calls=%fused_computation.22 | convolution fusion | flops 536870912 | bytes 7340036 | tf_op jit(solution)/shard_map/rki,kjr->kij/dot_general | solution.py:57
  79.7 3.7 %add_convert_fusion = bf16[8,256,512]{2,1,0:T(8,128)(2,1)} fusion(f32[8,256,512]{2,1,0:T(8,128)S(1)} %fusion.16, bf16[256,8,256]{0,2,1:T(8,128)(2,1)S(1)} %collective-permute-done.2, bf16[8,512,256]{2,1,0:T(8,128)(2,1)} %collective-permute-done.3), kind=kOutput, calls=%fused_computation.5 | convolution fusion | flops 538968064 | bytes 9437184 | tf_op jit(solution)/shard_map/rki,kjr->kij/dot_general | solution.py:58
  83.4 31.7 %all-to-all-done.1 = bf16[8,8,64,256]{3,2,1,0:T(8,128)(2,1)S(1)} async-done(((bf16[8,8,64,256]{3,2,1,0:T(8,128)(2,1)}), bf16[8,8,64,256]{3,2,1,0:T(8,128)(2,1)S(1)}, u32[]{:S(2)}, u32[]{:S(2)}) %all-to-all-start.1) | async-done | bytes 2097184 | tf_op jit(solution)/shard_map/all_to_all | solution.py:56
  115.1 0.1 constant_dynamic-slice_fusion
  115.3 0.1 collective-permute-start.4
  115.4 1.4 %copy-done = bf16[256,4096]{0,1:T(8,128)(2,1)S(1)} copy-done((bf16[256,4096]{0,1:T(8,128)(2,1)S(1)}, bf16[256,4096]{0,1:T(8,128)(2,1)}, u32[]{:S(2)}) %copy-start) | copy-done | bytes 2097176
  116.7 0.8 fusion.12
  117.5 0.5 collective-permute-done.4
  118.0 3.3 %fusion.7 = bf16[64,32,64]{2,1,0:T(8,128)(2,1)} fusion(f32[64,32,64]{2,1,0:T(8,128)S(1)} %fusion.12, bf16[256,64,64]{0,2,1:T(8,128)(2,1)} %collective-permute-done.5, bf16[64,4,8,256]{3,0,2,1:T(8,128)(2,1)S(1)} %bitcast.41), kind=kOutput, calls=%fused_computation.12 | convolution fusion | flops 67371008 | bytes 3932160 | tf_op jit(solution)/shard_map/jkr,rjm->jkm/dot_general | solution.py:68
  (15 shorter events, 0.0 us)
Async XLA Ops:
  0.6 3.1 %collective-permute-start.1 = (bf16[64,32,64]{2,1,0:T(8,128)(2,1)}, bf16[64,32,64]{2,1,0:T(8,128)(2,1)S(1)}, u32[]{:S(2)}, u32[]{:S(2)}) collective-permute-start(bf16[64,32,64]{2,1,0:T(8,128)(2,1)} %param.8), channel_id=1, source_target_pairs={{0,1},{1,0},{2,3},{3,2},{4,5},{5,4},{6,7},{7,6},{8,9},{9,8},{10,11... | collective-permute-start | bytes 786440 | tf_op jit(solution)/shard_map/ppermute | solution.py:9
  1.1 2.6 %copy-start.4 = (bf16[64,32,64]{2,1,0:T(8,128)(2,1)S(1)}, bf16[64,32,64]{2,1,0:T(8,128)(2,1)}, u32[]{:S(2)}) copy-start(bf16[64,32,64]{2,1,0:T(8,128)(2,1)} %param.8) | copy-start | bytes 786436
  6.0 55.7 %all-to-all-start = ((bf16[8,8,64,256]{3,1,2,0:T(8,128)(2,1)}), bf16[8,8,64,256]{3,1,2,0:T(8,128)(2,1)S(1)}, u32[]{:S(2)}, u32[]{:S(2)}) async-start(bf16[8,8,64,256]{3,1,2,0:T(8,128)(2,1)} %copy.22), calls=%async_computation | async-start | bytes 4194304 | tf_op jit(solution)/shard_map/all_to_all | solution.py:37
  16.8 4.3 %copy-start.5 = (s32[8]{0:T(128)S(1)}, s32[8]{0:T(128)}, u32[]{:S(2)}) copy-start(s32[8]{0:T(128)} %param.9) | copy-start | bytes 100
  16.8 6.5 %collective-permute-start = (bf16[8,256,512]{1,2,0:T(8,128)(2,1)}, bf16[8,256,512]{1,2,0:T(8,128)(2,1)}, u32[]{:S(2)}, u32[]{:S(2)}) collective-permute-start(bf16[8,256,512]{1,2,0:T(8,128)(2,1)} %copy.18), channel_id=1, source_target_pairs={{0,1},{1,0},{2,3},{3,2},{4,5},{5,4},{6,7},{7,6},{8,9},{9,8},{10,11... | collective-permute-start | bytes 6291464 | tf_op jit(solution)/shard_map/ppermute | solution.py:9
  21.1 2.2 %copy-start.3 = (bf16[8,256,512]{1,2,0:T(8,128)(2,1)S(1)}, bf16[8,256,512]{1,2,0:T(8,128)(2,1)}, u32[]{:S(2)}) copy-start(bf16[8,256,512]{1,2,0:T(8,128)(2,1)} %copy.18) | copy-start | bytes 6291460
  23.2 2.9 %copy-start.2 = (bf16[256,8,512]{0,2,1:T(8,128)(2,1)}, bf16[256,8,512]{0,2,1:T(8,128)(2,1)S(1)}, u32[]{:S(2)}) copy-start(bf16[256,8,512]{0,2,1:T(8,128)(2,1)S(1)} %broadcast_multiply_fusion) | copy-start | bytes 6291460
  61.7 1.3 %copy-start.1 = (bf16[8,8,64,256]{3,1,2,0:T(8,128)(2,1)}, bf16[8,8,64,256]{3,1,2,0:T(8,128)(2,1)S(1)}, u32[]{:S(2)}) copy-start(bf16[8,8,64,256]{3,1,2,0:T(8,128)(2,1)S(1)} %all-to-all-done) | copy-start | bytes 6291460
  63.0 52.1 %all-to-all-start.1 = ((bf16[8,8,64,256]{3,2,1,0:T(8,128)(2,1)}), bf16[8,8,64,256]{3,2,1,0:T(8,128)(2,1)S(1)}, u32[]{:S(2)}, u32[]{:S(2)}) async-start(bf16[8,8,64,256]{3,2,1,0:T(8,128)(2,1)} %bitcast.34), calls=%async_computation.1 | async-start | bytes 4194304 | tf_op jit(solution)/shard_map/all_to_all | solution.py:56
  70.2 9.6 %collective-permute-start.3 = (bf16[8,512,256]{2,1,0:T(8,128)(2,1)}, bf16[8,512,256]{2,1,0:T(8,128)(2,1)}, u32[]{:S(2)}, u32[]{:S(2)}) collective-permute-start(bf16[8,512,256]{2,1,0:T(8,128)(2,1)} %bitcast.9), channel_id=1, source_target_pairs={{0,1},{1,0},{2,3},{3,2},{4,5},{5,4},{6,7},{7,6},{8,9},{9,8},{10,11... | collective-permute-start | bytes 6291464 | tf_op jit(solution)/shard_map/ppermute | solution.py:55
  72.4 7.3 %collective-permute-start.2 = (bf16[256,8,256]{0,2,1:T(8,128)(2,1)}, bf16[256,8,256]{0,2,1:T(8,128)(2,1)S(1)}, u32[]{:S(2)}, u32[]{:S(2)}) collective-permute-start(bf16[256,8,256]{0,2,1:T(8,128)(2,1)} %constant_dynamic-slice_fusion.1), channel_id=1, source_target_pairs={{0,1},{1,0},{2,3},{3,2},{4,5},{5,4},{6,7},{7,6},{8,9},{9,8},{10,11... | collective-permute-start | bytes 3145736 | tf_op jit(solution)/shard_map/ppermute | solution.py:53
  77.0 40.5 %collective-permute-start.5 = (bf16[256,64,64]{0,2,1:T(8,128)(2,1)}, bf16[256,64,64]{0,2,1:T(8,128)(2,1)}, u32[]{:S(2)}, u32[]{:S(2)}) collective-permute-start(bf16[256,64,64]{0,2,1:T(8,128)(2,1)} %bitcast.35), channel_id=1, source_target_pairs={{0,1},{1,0},{2,3},{3,2},{4,5},{5,4},{6,7},{7,6},{8,9},{9,8},{10,11... | collective-permute-start | bytes 6291464 | tf_op jit(solution)/shard_map/ppermute | solution.py:64
  115.1 1.6 %copy-start = (bf16[256,4096]{0,1:T(8,128)(2,1)S(1)}, bf16[256,4096]{0,1:T(8,128)(2,1)}, u32[]{:S(2)}) copy-start(bf16[256,4096]{0,1:T(8,128)(2,1)} %copy.25) | copy-start | bytes 6291460
  115.3 2.7 %collective-permute-start.4 = (bf16[4,8,64,256]{3,2,1,0:T(8,128)(2,1)S(1)}, bf16[4,8,64,256]{3,2,1,0:T(8,128)(2,1)S(1)}, u32[]{:S(2)}, u32[]{:S(2)}) collective-permute-start(bf16[4,8,64,256]{3,2,1,0:T(8,128)(2,1)S(1)} %get-tuple-element.12), channel_id=1, source_target_pairs={{0,1},{1,0},{2,3},{3,2},{4,5},{5,4},{6,7},{7,6},{8,9},{9,8},{10,11... | collective-permute-start | bytes 3145736 | tf_op jit(solution)/shard_map/ppermute | solution.py:72

commit v12 on v9

--- a/solution.py
+++ b/solution.py
@@ -42,7 +42,7 @@
     mixed = jnp.einsum(
         "rki,kij->jkr", inputs, left_full, preferred_element_type=jnp.float32
     ).astype(jnp.bfloat16)
-    mixed_sent = mixed.reshape(peer_count, right_local, local_blocks, row_count).transpose(0, 2, 1, 3)
+    mixed_sent = mixed.reshape(peer_count, right_local, local_blocks, row_count)
     mixed_sent, back_got = lax.optimization_barrier((mixed_sent, back_got))
 
     half_size = block_size // 2
@@ -53,7 +53,9 @@
     partner_part = lax.ppermute(their_part, "bin", swap)
     back_t = back_got.transpose(1, 0, 2, 3).reshape(local_blocks, block_size, row_count)
     partner_back = lax.ppermute(back_t, "bin", swap)
+    mixed_sent = with_layout_constraint(mixed_sent, Layout((0, 1, 2, 3)))
     mixed_got = lax.all_to_all(mixed_sent, "blk", 0, 0, tiled=True)
+    mixed_got = with_layout_constraint(mixed_got, Layout((0, 1, 2, 3)))
     left_term = jnp.einsum("rki,kjr->kij", own_part, back_t, preferred_element_type=jnp.float32)
     left_term = left_term + jnp.einsum(
         "rki,kjr->kij", partner_part, partner_back, preferred_element_type=jnp.float32
@@ -63,9 +65,16 @@
     half_peers = peer_count // 2
 
     def right_of(start):
-        blocks = lax.dynamic_slice_in_dim(mixed_got, start, half_peers, axis=0)
-        blocks = blocks.transpose(2, 0, 1, 3).reshape(right_local, half_peers * local_blocks, row_count)
-        return jnp.einsum("jkr,rjm->jkm", blocks, upstream, preferred_element_type=jnp.float32)
+        parts = [
+            jnp.einsum(
+                "jkr,jmr->jkm",
+                lax.dynamic_index_in_dim(mixed_got, start + q, 0, keepdims=False),
+                upstream_t,
+                preferred_element_type=jnp.float32,
+            )
+            for q in range(half_peers)
+        ]
+        return jnp.concatenate(parts, axis=1)
 
     got_right = lax.ppermute(right_of((1 - core) * half_peers), "bin", [(0, 1), (1, 0)])
     grad_right = (lax.optimization_barrier(right_of(core * half_peers)) + got_right).astype(

time: 121 us -> 130 us (1.074)
  matrix products: 12.6 us -> 23 us
  waiting for transfers between devices: 68.3 us -> 66.6 us
    dot_general x2 -> x8, matrix products: 1.68 us -> 13.7 us  [right_of(): jnp.einsum('jkr,jmr->jkm', lax.dynamic_index_in_dim(mixed_got, start + q,...]
    convert_element_type x0 -> x1, local copies, waits for them, and re-layouts: none -> 2.57 us  [on_device(): mixed = jnp.einsum('rki,kij->jkr', inputs, left_full, preferred_element_t...]
    ppermute x1, waiting for transfers between devices: 1.81 us -> 0.01 us  [on_device(): lax.ppermute(right_of((1 - core) * half_peers), 'bin', [(0, 1), (1, 0)])]
    transpose x1 -> x0, local copies, waits for them, and re-layouts: 1.68 us -> none  [right_of(): blocks.transpose(2, 0, 1, 3)]
    dot_general x1, matrix products: 2.61 us -> 0.96 us  [on_device(): jnp.einsum('rc,rs->cs', cotangent, eye, preferred_element_type=jnp.float32)]
    transpose x1, local copies, waits for them, and re-layouts: 1.8 us -> 3.41 us  [on_device(): back_got.transpose(1, 0, 2, 3).reshape(local_blocks, block_size, row_count)]
    reshape x1 -> x0, local copies, waits for them, and re-layouts: 1.59 us -> none  [on_device(): mixed.reshape(peer_count, right_local, local_blocks, row_count)]
    unnamed x11 -> x16, local copies, waits for them, and re-layouts: 11.4 us -> 9.81 us
  transfers between devices with their start and end apart: 7 -> 7, of which waited for: 3 -> 3; matrix products, arithmetic and copies ran while one was open for 27% -> 26% of each run, Pallas kernels for 0% -> 0%
where the time goes in v12:
time: 130 us; the launch traced here: 129 us
  waiting for transfers between devices  66.6 us (51%)
  matrix products  23 us (18%)
  local copies, waits for them, and re-layouts  19.5 us (15%)
  starting transfers between devices  12.7 us (10%)
  other arithmetic  6.2 us (5%)
    all_to_all x1, waiting for transfers between devices, on_device(): mixed_got = lax.all_to_all(mixed_sent, 'blk', 0, 0, tiled=True)  34.8 us
    all_to_all x1, waiting for transfers between devices, on_device(): back_got = lax.all_to_all(back_sent, 'blk', 0, 0, tiled=True)  31.4 us
    dot_general x8, matrix products, right_of(): jnp.einsum('jkr,jmr->jkm', lax.dynamic_index_in_dim(mixed_got, start + q,...  13.7 us
    unnamed x16, local copies, waits for them, and re-layouts  9.81 us
    all_to_all x1, starting transfers between devices, on_device(): back_got = lax.all_to_all(back_sent, 'blk', 0, 0, tiled=True)  7.25 us
    all_to_all x1, starting transfers between devices, on_device(): mixed_got = lax.all_to_all(mixed_sent, 'blk', 0, 0, tiled=True)  4.35 us
    dot_general x1, matrix products, on_device(): jnp.einsum('rki,kjr->kij', partner_part, partner_back, preferred_element_...  3.72 us
    transpose x1, local copies, waits for them, and re-layouts, on_device(): back_got.transpose(1, 0, 2, 3).reshape(local_blocks, block_size, row_count)  3.41 us
  transfers between devices with their start and end apart: 7, of which 3 were waited for; matrix products, arithmetic and copies ran while one was open for 26% of the time, Pallas kernels for 0%

profile of v12, /device:TPU:0, one launch (start us, length us, event | category | flops | bytes accessed | tf_op | source)
XLA Modules:
  0.0 128.8 jit_solution(9839965053213310067)
XLA Ops:
  0.6 0.5 collective-permute-start.1
  1.2 1.1 copy-done
  2.2 1.0 convolution_convert_fusion
  3.3 0.7 convert_bitcast_fusion
  4.0 0.5 copy-done.1
  4.5 1.5 %copy.20 = bf16[8,8,64,256]{3,1,2,0:T(8,128)(2,1)} copy(bf16[8,8,64,256]{3,1,0,2:T(8,128)(2,1)S(1)} %convert_bitcast_fusion) | data formatting | bytes 4194304 | tf_op jit(solution)/shard_map/reshape | solution.py:36
  6.0 7.3 %all-to-all-start = ((bf16[8,8,64,256]{3,1,2,0:T(8,128)(2,1)}), bf16[8,8,64,256]{3,1,2,0:T(8,128)(2,1)}, u32[]{:S(2)}, u32[]{:S(2)}) async-start(bf16[8,8,64,256]{3,1,2,0:T(8,128)(2,1)} %copy.20), calls=%async_computation | async-start | bytes 4194304 | tf_op jit(solution)/shard_map/all_to_all | solution.py:37
  13.2 3.9 %copy.16 = bf16[8,256,512]{1,2,0:T(8,128)(2,1)} copy(bf16[8,256,512]{2,1,0:T(8,128)(2,1)} %param.7) | data formatting | bytes 4194304 | tf_op args[2]
  17.2 4.1 %copy.14 = bf16[256,4096]{0,1:T(8,128)(2,1)} copy(bf16[256,4096]{1,0:T(8,128)(2,1)} %param.5) | data formatting | bytes 4194304 | tf_op args[0]
  21.4 2.1 %broadcast_multiply_fusion = bf16[256,8,512]{0,2,1:T(8,128)(2,1)S(1)} fusion(bf16[256,8,512]{0,2,1:T(8,128)(2,1)} %bitcast.61, bf16[8,512]{1,0:T(8,128)(2,1)S(1)} %fusion.35), kind=kLoop, calls=%fused_computation.18 | loop fusion | flops 1048576 | bytes 4202496 | tf_op jit(solution)/shard_map/mul | solution.py:40
  23.5 0.1 copy-done.4
  23.6 2.8 %broadcast_select_fusion.1 = (bf16[8,256,512]{1,2,0:T(8,128)(2,1)S(1)}, bf16[8,256,512]{1,2,0:T(8,128)(2,1)S(1)}) fusion(bf16[8,256,512]{1,2,0:T(8,128)(2,1)S(1)} %copy-done.4, bf16[8,256,512]{1,2,0:T(8,128)(2,1)} %collective-permute-done, pred[]{:T(512)S(6)} %eq.4), kind=kLoop, calls=%fused_computation.9 | loop fusion | flops 2097152 | bytes 8388609 | tf_op jit(solution)/shard_map/jit(_where)/select_n | solution.py:11
  26.4 1.3 convert_bitcast_fusion.1
  27.7 2.6 %copy.19 = bf16[512,8,256]{2,1,0:T(8,128)(2,1)} copy(bf16[512,8,256]{2,0,1:T(8,128)(2,1)S(1)} %convert_bitcast_fusion.1) | data formatting | bytes 4194304 | tf_op jit(solution)/shard_map/convert_element_type | solution.py:44
  30.2 31.4 %all-to-all-done = bf16[8,8,64,256]{3,1,2,0:T(8,128)(2,1)} async-done(((bf16[8,8,64,256]{3,1,2,0:T(8,128)(2,1)}), bf16[8,8,64,256]{3,1,2,0:T(8,128)(2,1)}, u32[]{:S(2)}, u32[]{:S(2)}) %all-to-all-start) | async-done | bytes 2097184 | tf_op jit(solution)/shard_map/all_to_all | solution.py:37
  61.6 4.4 %all-to-all-start.1 = ((bf16[8,64,8,256]{3,2,1,0:T(8,128)(2,1)}), bf16[8,64,8,256]{3,2,1,0:T(8,128)(2,1)}, u32[]{:S(2)}, u32[]{:S(2)}) async-start(bf16[8,64,8,256]{3,2,1,0:T(8,128)(2,1)} %bitcast.60), calls=%async_computation.1 | async-start | bytes 4194304 | tf_op jit(solution)/shard_map/all_to_all | solution.py:57
  65.9 3.4 %copy.21 = bf16[8,8,64,256]{3,2,1,0:T(8,128)(2,1)} copy(bf16[8,8,64,256]{3,0,2,1:T(8,128)(2,1)} %bitcast.7) | data formatting | bytes 4194304 | tf_op jit(solution)/shard_map/transpose | solution.py:54
  69.4 2.3 %constant_dynamic-slice_fusion = bf16[256,8,256]{0,2,1:T(8,128)(2,1)} fusion(bf16[256,8,512]{0,2,1:T(8,128)(2,1)} %copy-done.3, s32[]{:T(128)S(6)} %select_n.62), kind=kLoop, calls=%fused_computation.56 | loop fusion | bytes 2097156 | tf_op jit(solution)/shard_map/dynamic_slice | solution.py:52
  71.6 0.5 collective-permute-start.2
  72.1 2.7 %fusion.9 = f32[8,256,512]{2,1,0:T(8,128)S(1)} fusion(bf16[8,512,256]{2,1,0:T(8,128)(2,1)} %bitcast.8, bf16[256,8,512]{0,2,1:T(8,128)(2,1)} %copy-done.3, s32[]{:T(128)S(6)} %select_n.55), kind=kOutput, calls=%fused_computation.16 | convolution fusion | flops 536870912 | bytes 7340036 | tf_op jit(solution)/shard_map/rki,kjr->kij/dot_general | solution.py:59
  74.8 0.4 collective-permute-done.2
  75.2 3.7 %add_convert_fusion = bf16[8,256,512]{2,1,0:T(8,128)(2,1)} fusion(f32[8,256,512]{2,1,0:T(8,128)S(1)} %fusion.9, bf16[256,8,256]{0,2,1:T(8,128)(2,1)S(1)} %collective-permute-done.2, bf16[8,512,256]{2,1,0:T(8,128)(2,1)} %collective-permute-done.3), kind=kOutput, calls=%fused_computation.5 | convolution fusion | flops 538968064 | bytes 9437184 | tf_op jit(solution)/shard_map/rki,kjr->kij/dot_general | solution.py:60
  78.9 34.8 %all-to-all-done.1 = bf16[8,64,8,256]{3,2,1,0:T(8,128)(2,1)} async-done(((bf16[8,64,8,256]{3,2,1,0:T(8,128)(2,1)}), bf16[8,64,8,256]{3,2,1,0:T(8,128)(2,1)}, u32[]{:S(2)}, u32[]{:S(2)}) %all-to-all-start.1) | async-done | bytes 2097184 | tf_op jit(solution)/shard_map/all_to_all | solution.py:57
  113.8 2.5 %fusion.19 = f32[64,8,64]{2,1,0:T(8,128)S(1)} fusion(bf16[64,64,256]{2,1,0:T(8,128)(2,1)} %bitcast.52, bf16[8,64,8,256]{3,2,1,0:T(8,128)(2,1)} %all-to-all-done.1, s32[]{:T(128)S(6)} %select_n.66), kind=kOutput, calls=%fused_computation.29 | convolution fusion | flops 16777216 | bytes 2490372 | tf_op jit(solution)/shard_map/jkr,jmr->jkm/dot_general | solution.py:69
  116.2 1.6 %fusion.21 = f32[64,8,64]{2,1,0:T(8,128)S(1)} fusion(bf16[64,64,256]{2,1,0:T(8,128)(2,1)S(1)} %bitcast.53, bf16[8,64,8,256]{3,2,1,0:T(8,128)(2,1)} %all-to-all-done.1, s32[]{:T(128)S(6)} %select_n.65), kind=kOutput, calls=%fused_computation.31 | convolution fusion | flops 16777216 | bytes 2490372 | tf_op jit(solution)/shard_map/jkr,jmr->jkm/dot_general | solution.py:69
  117.8 1.6 %fusion.11 = f32[64,8,64]{2,1,0:T(8,128)S(1)} fusion(bf16[64,64,256]{2,1,0:T(8,128)(2,1)S(1)} %bitcast.54, bf16[8,64,8,256]{3,2,1,0:T(8,128)(2,1)} %all-to-all-done.1, s32[]{:T(128)S(6)} %select_n.70), kind=kOutput, calls=%fused_computation.21 | convolution fusion | flops 16777216 | bytes 2490372 | tf_op jit(solution)/shard_map/jkr,jmr->jkm/dot_general | solution.py:69
  119.4 1.6 %fusion.13 = f32[64,8,64]{2,1,0:T(8,128)S(1)} fusion(bf16[64,64,256]{2,1,0:T(8,128)(2,1)S(1)} %bitcast.55, bf16[8,64,8,256]{3,2,1,0:T(8,128)(2,1)} %all-to-all-done.1, s32[]{:T(128)S(6)} %select_n.69), kind=kOutput, calls=%fused_computation.23 | convolution fusion | flops 16777216 | bytes 2490372 | tf_op jit(solution)/shard_map/jkr,jmr->jkm/dot_general | solution.py:69
  121.0 1.6 %fusion.15 = f32[64,8,64]{2,1,0:T(8,128)S(1)} fusion(bf16[64,64,256]{2,1,0:T(8,128)(2,1)S(1)} %bitcast.56, bf16[8,64,8,256]{3,2,1,0:T(8,128)(2,1)} %all-to-all-done.1, s32[]{:T(128)S(6)} %select_n.68), kind=kOutput, calls=%fused_computation.25 | convolution fusion | flops 16777216 | bytes 2490372 | tf_op jit(solution)/shard_map/jkr,jmr->jkm/dot_general | solution.py:69
  122.6 1.6 %fusion.17 = f32[64,8,64]{2,1,0:T(8,128)S(1)} fusion(bf16[64,64,256]{2,1,0:T(8,128)(2,1)S(1)} %bitcast.57, bf16[8,64,8,256]{3,2,1,0:T(8,128)(2,1)} %all-to-all-done.1, s32[]{:T(128)S(6)} %select_n.67), kind=kOutput, calls=%fused_computation.27 | convolution fusion | flops 16777216 | bytes 2490372 | tf_op jit(solution)/shard_map/jkr,jmr->jkm/dot_general | solution.py:69
  124.4 1.6 %fusion.23 = f32[64,8,64]{2,1,0:T(8,128)S(1)} fusion(bf16[64,64,256]{2,1,0:T(8,128)(2,1)S(1)} %bitcast.58, bf16[8,64,8,256]{3,2,1,0:T(8,128)(2,1)} %all-to-all-done.1, s32[]{:T(128)S(6)} %select_n.64), kind=kOutput, calls=%fused_computation.33 | convolution fusion | flops 16777216 | bytes 2490372 | tf_op jit(solution)/shard_map/jkr,jmr->jkm/dot_general | solution.py:69
  126.0 1.6 %fusion.25 = f32[64,8,64]{2,1,0:T(8,128)S(1)} fusion(bf16[64,64,256]{2,1,0:T(8,128)(2,1)S(1)} %bitcast.59, bf16[8,64,8,256]{3,2,1,0:T(8,128)(2,1)} %all-to-all-done.1, s32[]{:T(128)S(6)} %select_n.63), kind=kOutput, calls=%fused_computation.35 | convolution fusion | flops 16777216 | bytes 2490372 | tf_op jit(solution)/shard_map/jkr,jmr->jkm/dot_general | solution.py:69
  127.7 1.0 add_convert_fusion.1
  (22 shorter events, 0.5 us)
Async XLA Ops:
  0.6 1.6 %copy-start = (bf16[256,4096]{1,0:T(8,128)(2,1)S(1)}, bf16[256,4096]{1,0:T(8,128)(2,1)}, u32[]{:S(2)}) copy-start(bf16[256,4096]{1,0:T(8,128)(2,1)} %param.6) | copy-start | bytes 6291460
  0.6 2.6 %collective-permute-start.1 = (bf16[64,32,64]{2,1,0:T(8,128)(2,1)}, bf16[64,32,64]{2,1,0:T(8,128)(2,1)S(1)}, u32[]{:S(2)}, u32[]{:S(2)}) collective-permute-start(bf16[64,32,64]{2,1,0:T(8,128)(2,1)} %param.8), channel_id=1, source_target_pairs={{0,1},{1,0},{2,3},{3,2},{4,5},{5,4},{6,7},{7,6},{8,9},{9,8},{10,11... | collective-permute-start | bytes 786440 | tf_op jit(solution)/shard_map/ppermute | solution.py:9
  2.2 1.0 copy-start.5
  3.2 1.3 %copy-start.1 = (bf16[256,4096]{0,1:T(8,128)(2,1)}, bf16[256,4096]{0,1:T(8,128)(2,1)S(1)}, u32[]{:S(2)}) copy-start(bf16[256,4096]{0,1:T(8,128)(2,1)S(1)} %convolution_convert_fusion) | copy-start | bytes 6291460
  6.0 55.6 %all-to-all-start = ((bf16[8,8,64,256]{3,1,2,0:T(8,128)(2,1)}), bf16[8,8,64,256]{3,1,2,0:T(8,128)(2,1)}, u32[]{:S(2)}, u32[]{:S(2)}) async-start(bf16[8,8,64,256]{3,1,2,0:T(8,128)(2,1)} %copy.20), calls=%async_computation | async-start | bytes 4194304 | tf_op jit(solution)/shard_map/all_to_all | solution.py:37
  17.2 4.2 %copy-start.6 = (s32[8]{0:T(128)S(1)}, s32[8]{0:T(128)}, u32[]{:S(2)}) copy-start(s32[8]{0:T(128)} %param.9) | copy-start | bytes 100
  17.2 6.3 %collective-permute-start = (bf16[8,256,512]{1,2,0:T(8,128)(2,1)}, bf16[8,256,512]{1,2,0:T(8,128)(2,1)}, u32[]{:S(2)}, u32[]{:S(2)}) collective-permute-start(bf16[8,256,512]{1,2,0:T(8,128)(2,1)} %copy.16), channel_id=1, source_target_pairs={{0,1},{1,0},{2,3},{3,2},{4,5},{5,4},{6,7},{7,6},{8,9},{9,8},{10,11... | collective-permute-start | bytes 6291464 | tf_op jit(solution)/shard_map/ppermute | solution.py:9
  21.4 2.2 %copy-start.4 = (bf16[8,256,512]{1,2,0:T(8,128)(2,1)S(1)}, bf16[8,256,512]{1,2,0:T(8,128)(2,1)}, u32[]{:S(2)}) copy-start(bf16[8,256,512]{1,2,0:T(8,128)(2,1)} %copy.16) | copy-start | bytes 6291460
  23.5 2.9 %copy-start.3 = (bf16[256,8,512]{0,2,1:T(8,128)(2,1)}, bf16[256,8,512]{0,2,1:T(8,128)(2,1)S(1)}, u32[]{:S(2)}) copy-start(bf16[256,8,512]{0,2,1:T(8,128)(2,1)S(1)} %broadcast_multiply_fusion) | copy-start | bytes 6291460
  61.6 52.2 %all-to-all-start.1 = ((bf16[8,64,8,256]{3,2,1,0:T(8,128)(2,1)}), bf16[8,64,8,256]{3,2,1,0:T(8,128)(2,1)}, u32[]{:S(2)}, u32[]{:S(2)}) async-start(bf16[8,64,8,256]{3,2,1,0:T(8,128)(2,1)} %bitcast.60), calls=%async_computation.1 | async-start | bytes 4194304 | tf_op jit(solution)/shard_map/all_to_all | solution.py:57
  69.4 5.9 %collective-permute-start.3 = (bf16[8,512,256]{2,1,0:T(8,128)(2,1)}, bf16[8,512,256]{2,1,0:T(8,128)(2,1)}, u32[]{:S(2)}, u32[]{:S(2)}) collective-permute-start(bf16[8,512,256]{2,1,0:T(8,128)(2,1)} %bitcast.8), channel_id=1, source_target_pairs={{0,1},{1,0},{2,3},{3,2},{4,5},{5,4},{6,7},{7,6},{8,9},{9,8},{10,11... | collective-permute-start | bytes 6291464 | tf_op jit(solution)/shard_map/ppermute | solution.py:55
  71.6 3.6 %collective-permute-start.2 = (bf16[256,8,256]{0,2,1:T(8,128)(2,1)}, bf16[256,8,256]{0,2,1:T(8,128)(2,1)S(1)}, u32[]{:S(2)}, u32[]{:S(2)}) collective-permute-start(bf16[256,8,256]{0,2,1:T(8,128)(2,1)} %constant_dynamic-slice_fusion), channel_id=1, source_target_pairs={{0,1},{1,0},{2,3},{3,2},{4,5},{5,4},{6,7},{7,6},{8,9},{9,8},{10,11... | collective-permute-start | bytes 3145736 | tf_op jit(solution)/shard_map/ppermute | solution.py:53
  113.8 2.5 %copy-start.2 = (bf16[256,4096]{0,1:T(8,128)(2,1)S(1)}, bf16[256,4096]{0,1:T(8,128)(2,1)}, u32[]{:S(2)}) copy-start(bf16[256,4096]{0,1:T(8,128)(2,1)} %copy-done.1) | copy-start | bytes 6291460
  124.3 3.4 %collective-permute-start.4 = (f32[64,32,64]{2,1,0:T(8,128)S(1)}, f32[64,32,64]{2,1,0:T(8,128)S(1)}, u32[]{:S(2)}, u32[]{:S(2)}) collective-permute-start(f32[64,32,64]{2,1,0:T(8,128)S(1)} %pad_maximum_fusion.1), channel_id=1, source_target_pairs={{0,1},{1,0},{2,3},{3,2},{4,5},{5,4},{6,7},{7,6},{8,9},{9,8},{10,11... | collective-permute-start | bytes 1572872 | tf_op jit(solution)/shard_map/ppermute | solution.py:79

commit v13 on v9

--- a/solution.py
+++ b/solution.py
@@ -42,7 +42,7 @@
     mixed = jnp.einsum(
         "rki,kij->jkr", inputs, left_full, preferred_element_type=jnp.float32
     ).astype(jnp.bfloat16)
-    mixed_sent = mixed.reshape(peer_count, right_local, local_blocks, row_count).transpose(0, 2, 1, 3)
+    mixed_sent = mixed.reshape(peer_count, right_local, local_blocks, row_count)
     mixed_sent, back_got = lax.optimization_barrier((mixed_sent, back_got))
 
     half_size = block_size // 2
@@ -53,7 +53,9 @@
     partner_part = lax.ppermute(their_part, "bin", swap)
     back_t = back_got.transpose(1, 0, 2, 3).reshape(local_blocks, block_size, row_count)
     partner_back = lax.ppermute(back_t, "bin", swap)
+    mixed_sent = with_layout_constraint(mixed_sent, Layout((0, 1, 2, 3)))
     mixed_got = lax.all_to_all(mixed_sent, "blk", 0, 0, tiled=True)
+    mixed_got = with_layout_constraint(mixed_got, Layout((0, 1, 2, 3)))
     left_term = jnp.einsum("rki,kjr->kij", own_part, back_t, preferred_element_type=jnp.float32)
     left_term = left_term + jnp.einsum(
         "rki,kjr->kij", partner_part, partner_back, preferred_element_type=jnp.float32
@@ -64,7 +66,7 @@
 
     def right_of(start):
         blocks = lax.dynamic_slice_in_dim(mixed_got, start, half_peers, axis=0)
-        blocks = blocks.transpose(2, 0, 1, 3).reshape(right_local, half_peers * local_blocks, row_count)
+        blocks = blocks.transpose(1, 0, 2, 3).reshape(right_local, half_peers * local_blocks, row_count)
         return jnp.einsum("jkr,rjm->jkm", blocks, upstream, preferred_element_type=jnp.float32)
 
     got_right = lax.ppermute(right_of((1 - core) * half_peers), "bin", [(0, 1), (1, 0)])

time: 121 us -> 121 us (level)
    convert_element_type x0 -> x1, local copies, waits for them, and re-layouts: none -> 2.54 us  [on_device(): mixed = jnp.einsum('rki,kij->jkr', inputs, left_full, preferred_element_t...]
    reshape x1 -> x0, local copies, waits for them, and re-layouts: 1.59 us -> none  [on_device(): mixed.reshape(peer_count, right_local, local_blocks, row_count)]
  transfers between devices with their start and end apart: 7 -> 7, of which waited for: 3 -> 3; matrix products, arithmetic and copies ran while one was open for 27% -> 28% of each run, Pallas kernels for 0% -> 0%
where the time goes in v13:
time: 121 us; the launch traced here: 120 us
  waiting for transfers between devices  67.5 us (56%)
  local copies, waits for them, and re-layouts  21.2 us (18%)
  starting transfers between devices  12.5 us (10%)
  matrix products  12.3 us (10%)
  other arithmetic  6.02 us (5%)
    all_to_all x1, waiting for transfers between devices, on_device(): mixed_got = lax.all_to_all(mixed_sent, 'blk', 0, 0, tiled=True)  33.7 us
    all_to_all x1, waiting for transfers between devices, on_device(): back_got = lax.all_to_all(back_sent, 'blk', 0, 0, tiled=True)  31.8 us
    unnamed x11, local copies, waits for them, and re-layouts  11.4 us
    all_to_all x1, starting transfers between devices, on_device(): back_got = lax.all_to_all(back_sent, 'blk', 0, 0, tiled=True)  6.83 us
    all_to_all x1, starting transfers between devices, on_device(): mixed_got = lax.all_to_all(mixed_sent, 'blk', 0, 0, tiled=True)  4.35 us
    dot_general x1, matrix products, on_device(): jnp.einsum('rki,kjr->kij', partner_part, partner_back, preferred_element_...  3.72 us
    select_n x2, other arithmetic, swap_halves(): first = jnp.where(core == 0, local, other)  2.85 us
    dot_general x1, matrix products, on_device(): jnp.einsum('rki,kjr->kij', own_part, back_t, preferred_element_type=jnp.f...  2.67 us
  transfers between devices with their start and end apart: 7, of which 3 were waited for; matrix products, arithmetic and copies ran while one was open for 28% of the time, Pallas kernels for 0%

profile of v13, /device:TPU:0, one launch (start us, length us, event | category | flops | bytes accessed | tf_op | source)
XLA Modules:
  0.0 120.2 jit_solution(16376968593552932255)
XLA Ops:
  0.6 0.5 collective-permute-start.1
  1.1 2.6 %convolution_convert_fusion = bf16[256,4096]{0,1:T(8,128)(2,1)S(1)} fusion(bf16[256,4096]{1,0:T(8,128)(2,1)} %param.6), kind=kOutput, calls=%fused_computation | convolution fusion | flops 537985024 | bytes 4194304 | tf_op jit(solution)/shard_map/rc,rs->cs/dot_general | solution.py:28
  3.8 0.0 collective-permute-done.1
  3.8 0.1 broadcast_select_fusion.3
  3.9 0.7 convert_bitcast_fusion
  4.6 1.5 %copy.32 = bf16[8,8,64,256]{3,1,2,0:T(8,128)(2,1)} copy(bf16[8,8,64,256]{3,1,0,2:T(8,128)(2,1)S(1)} %convert_bitcast_fusion) | data formatting | bytes 4194304 | tf_op jit(solution)/shard_map/reshape | solution.py:36
  6.0 6.8 %all-to-all-start = ((bf16[8,8,64,256]{3,1,2,0:T(8,128)(2,1)}), bf16[8,8,64,256]{3,1,2,0:T(8,128)(2,1)S(1)}, u32[]{:S(2)}, u32[]{:S(2)}) async-start(bf16[8,8,64,256]{3,1,2,0:T(8,128)(2,1)} %copy.32), calls=%async_computation | async-start | bytes 4194304 | tf_op jit(solution)/shard_map/all_to_all | solution.py:37
  12.8 3.9 %copy.28 = bf16[8,256,512]{1,2,0:T(8,128)(2,1)} copy(bf16[8,256,512]{2,1,0:T(8,128)(2,1)} %param.7) | data formatting | bytes 4194304 | tf_op args[2]
  16.8 0.2 collective-permute-start
  17.0 4.1 %copy.26 = bf16[256,4096]{0,1:T(8,128)(2,1)} copy(bf16[256,4096]{1,0:T(8,128)(2,1)} %param.5) | data formatting | bytes 4194304 | tf_op args[0]
  21.0 0.1 fusion.17
  21.1 2.1 %broadcast_multiply_fusion = bf16[256,8,512]{0,2,1:T(8,128)(2,1)S(1)} fusion(bf16[256,8,512]{0,2,1:T(8,128)(2,1)} %bitcast.36, bf16[8,512]{1,0:T(8,128)(2,1)S(1)} %fusion.17), kind=kLoop, calls=%fused_computation.24 | loop fusion | flops 1048576 | bytes 4202496 | tf_op jit(solution)/shard_map/mul | solution.py:40
  23.2 0.1 copy-done.1
  23.3 2.8 %broadcast_select_fusion.1 = (bf16[8,256,512]{1,2,0:T(8,128)(2,1)S(1)}, bf16[8,256,512]{1,2,0:T(8,128)(2,1)S(1)}) fusion(bf16[8,256,512]{1,2,0:T(8,128)(2,1)S(1)} %copy-done.1, bf16[8,256,512]{1,2,0:T(8,128)(2,1)} %collective-permute-done, pred[]{:T(512)S(6)} %eq.4), kind=kLoop, calls=%fused_computation.9 | loop fusion | flops 2097152 | bytes 8388609 | tf_op jit(solution)/shard_map/jit(_where)/select_n | solution.py:11
  26.1 1.3 %convert_bitcast_fusion.1 = bf16[512,8,256]{2,0,1:T(8,128)(2,1)S(1)} fusion(bf16[256,8,512]{0,2,1:T(8,128)(2,1)S(1)} %broadcast_multiply_fusion, bf16[8,256,512]{1,2,0:T(8,128)(2,1)S(1)} %get-tuple-element.11, bf16[8,256,512]{1,2,0:T(8,128)(2,1)S(1)} %get-tuple-element.10), kind=kOutput, calls=%fused_computation.7 | convolution fusion | flops 1083179008 | bytes 8388608 | tf_op jit(solution)/shard_map/rki,kij->jkr/dot_general | solution.py:42
  27.4 2.5 %copy.31 = bf16[512,8,256]{2,1,0:T(8,128)(2,1)} copy(bf16[512,8,256]{2,0,1:T(8,128)(2,1)S(1)} %convert_bitcast_fusion.1) | data formatting | bytes 4194304 | tf_op jit(solution)/shard_map/convert_element_type | solution.py:44
  29.9 31.8 %all-to-all-done = bf16[8,8,64,256]{3,1,2,0:T(8,128)(2,1)S(1)} async-done(((bf16[8,8,64,256]{3,1,2,0:T(8,128)(2,1)}), bf16[8,8,64,256]{3,1,2,0:T(8,128)(2,1)S(1)}, u32[]{:S(2)}, u32[]{:S(2)}) %all-to-all-start) | async-done | bytes 2097184 | tf_op jit(solution)/shard_map/all_to_all | solution.py:37
  61.7 4.3 %all-to-all-start.1 = ((bf16[8,64,8,256]{3,2,1,0:T(8,128)(2,1)}), bf16[8,64,8,256]{3,2,1,0:T(8,128)(2,1)}, u32[]{:S(2)}, u32[]{:S(2)}) async-start(bf16[8,64,8,256]{3,2,1,0:T(8,128)(2,1)} %bitcast.2), calls=%async_computation.1 | async-start | bytes 4194304 | tf_op jit(solution)/shard_map/all_to_all | solution.py:57
  66.1 1.8 %copy.33 = bf16[8,8,64,256]{3,2,1,0:T(8,128)(2,1)} copy(bf16[8,8,64,256]{3,0,2,1:T(8,128)(2,1)S(1)} %bitcast.34) | data formatting | bytes 4194304 | tf_op jit(solution)/shard_map/transpose | solution.py:54
  67.9 2.4 %constant_dynamic-slice_fusion = bf16[256,8,256]{0,2,1:T(8,128)(2,1)} fusion(bf16[256,8,512]{0,2,1:T(8,128)(2,1)} %copy-done, s32[]{:T(128)S(6)} %select_n.43), kind=kLoop, calls=%fused_computation.30 | loop fusion | bytes 2097156 | tf_op jit(solution)/shard_map/dynamic_slice | solution.py:52
  70.2 0.5 collective-permute-start.2
  70.7 3.3 %copy.35 = bf16[256,4096]{0,1:T(8,128)(2,1)S(1)} copy(bf16[256,4096]{1,0:T(8,128)(2,1)} %param.6) | data formatting | bytes 4194304 | tf_op args[1]
  74.0 2.7 %fusion.15 = f32[8,256,512]{2,1,0:T(8,128)S(1)} fusion(bf16[8,512,256]{2,1,0:T(8,128)(2,1)} %bitcast.8, bf16[256,8,512]{0,2,1:T(8,128)(2,1)} %copy-done, s32[]{:T(128)S(6)} %select_n.36), kind=kOutput, calls=%fused_computation.22 | convolution fusion | flops 536870912 | bytes 7340036 | tf_op jit(solution)/shard_map/rki,kjr->kij/dot_general | solution.py:59
  76.7 0.0 collective-permute-done.3
  76.7 3.7 %add_convert_fusion = bf16[8,256,512]{2,1,0:T(8,128)(2,1)} fusion(f32[8,256,512]{2,1,0:T(8,128)S(1)} %fusion.15, bf16[256,8,256]{0,2,1:T(8,128)(2,1)S(1)} %collective-permute-done.2, bf16[8,512,256]{2,1,0:T(8,128)(2,1)} %collective-permute-done.3), kind=kOutput, calls=%fused_computation.5 | convolution fusion | flops 538968064 | bytes 9437184 | tf_op jit(solution)/shard_map/rki,kjr->kij/dot_general | solution.py:60
  80.4 33.7 %all-to-all-done.1 = bf16[8,64,8,256]{3,2,1,0:T(8,128)(2,1)} async-done(((bf16[8,64,8,256]{3,2,1,0:T(8,128)(2,1)}), bf16[8,64,8,256]{3,2,1,0:T(8,128)(2,1)}, u32[]{:S(2)}, u32[]{:S(2)}) %all-to-all-start.1) | async-done | bytes 2097184 | tf_op jit(solution)/shard_map/all_to_all | solution.py:57
  114.1 1.7 %dynamic-slice_bitcast_fusion = (bf16[64,4,8,256]{3,2,0,1:T(8,128)(2,1)S(1)}, bf16[64,4,8,256]{3,2,0,1:T(8,128)(2,1)S(1)}) fusion(bf16[8,64,8,256]{3,2,1,0:T(8,128)(2,1)} %all-to-all-done.1, s32[]{:T(128)S(6)} %select_n.45, s32[]{:T(128)S(6)} %select_n.44), kind=kLoop, calls=%fused_computation.20 | loop fusion | bytes 4194312 | tf_op jit(solution)/shard_map/transpose | solution.py:69
  115.8 0.7 fusion.9
  116.5 0.1 collective-permute-start.4
  116.6 0.7 fusion.11
  117.2 2.0 %collective-permute-done.4 = f32[64,32,64]{2,1,0:T(8,128)S(1)} collective-permute-done((f32[64,32,64]{2,1,0:T(8,128)S(1)}, f32[64,32,64]{2,1,0:T(8,128)S(1)}, u32[]{:S(2)}, u32[]{:S(2)}) %collective-permute-start.4) | collective-permute-done | bytes 524320 | tf_op jit(solution)/shard_map/ppermute | solution.py:72
  119.2 1.0 add_convert_fusion.1
  (10 shorter events, 0.0 us)
Async XLA Ops:
  0.6 3.1 %collective-permute-start.1 = (bf16[64,32,64]{2,1,0:T(8,128)(2,1)}, bf16[64,32,64]{2,1,0:T(8,128)(2,1)S(1)}, u32[]{:S(2)}, u32[]{:S(2)}) collective-permute-start(bf16[64,32,64]{2,1,0:T(8,128)(2,1)} %param.8), channel_id=1, source_target_pairs={{0,1},{1,0},{2,3},{3,2},{4,5},{5,4},{6,7},{7,6},{8,9},{9,8},{10,11... | collective-permute-start | bytes 786440 | tf_op jit(solution)/shard_map/ppermute | solution.py:9
  1.1 2.6 %copy-start.2 = (bf16[64,32,64]{2,1,0:T(8,128)(2,1)S(1)}, bf16[64,32,64]{2,1,0:T(8,128)(2,1)}, u32[]{:S(2)}) copy-start(bf16[64,32,64]{2,1,0:T(8,128)(2,1)} %param.8) | copy-start | bytes 786436
  6.0 55.7 %all-to-all-start = ((bf16[8,8,64,256]{3,1,2,0:T(8,128)(2,1)}), bf16[8,8,64,256]{3,1,2,0:T(8,128)(2,1)S(1)}, u32[]{:S(2)}, u32[]{:S(2)}) async-start(bf16[8,8,64,256]{3,1,2,0:T(8,128)(2,1)} %copy.32), calls=%async_computation | async-start | bytes 4194304 | tf_op jit(solution)/shard_map/all_to_all | solution.py:37
  16.8 4.3 %copy-start.3 = (s32[8]{0:T(128)S(1)}, s32[8]{0:T(128)}, u32[]{:S(2)}) copy-start(s32[8]{0:T(128)} %param.9) | copy-start | bytes 100
  16.8 6.5 %collective-permute-start = (bf16[8,256,512]{1,2,0:T(8,128)(2,1)}, bf16[8,256,512]{1,2,0:T(8,128)(2,1)}, u32[]{:S(2)}, u32[]{:S(2)}) collective-permute-start(bf16[8,256,512]{1,2,0:T(8,128)(2,1)} %copy.28), channel_id=1, source_target_pairs={{0,1},{1,0},{2,3},{3,2},{4,5},{5,4},{6,7},{7,6},{8,9},{9,8},{10,11... | collective-permute-start | bytes 6291464 | tf_op jit(solution)/shard_map/ppermute | solution.py:9
  21.1 2.2 %copy-start.1 = (bf16[8,256,512]{1,2,0:T(8,128)(2,1)S(1)}, bf16[8,256,512]{1,2,0:T(8,128)(2,1)}, u32[]{:S(2)}) copy-start(bf16[8,256,512]{1,2,0:T(8,128)(2,1)} %copy.28) | copy-start | bytes 6291460
  23.2 2.9 %copy-start = (bf16[256,8,512]{0,2,1:T(8,128)(2,1)}, bf16[256,8,512]{0,2,1:T(8,128)(2,1)S(1)}, u32[]{:S(2)}) copy-start(bf16[256,8,512]{0,2,1:T(8,128)(2,1)S(1)} %broadcast_multiply_fusion) | copy-start | bytes 6291460
  61.7 52.4 %all-to-all-start.1 = ((bf16[8,64,8,256]{3,2,1,0:T(8,128)(2,1)}), bf16[8,64,8,256]{3,2,1,0:T(8,128)(2,1)}, u32[]{:S(2)}, u32[]{:S(2)}) async-start(bf16[8,64,8,256]{3,2,1,0:T(8,128)(2,1)} %bitcast.2), calls=%async_computation.1 | async-start | bytes 4194304 | tf_op jit(solution)/shard_map/all_to_all | solution.py:57
  67.9 8.8 %collective-permute-start.3 = (bf16[8,512,256]{2,1,0:T(8,128)(2,1)}, bf16[8,512,256]{2,1,0:T(8,128)(2,1)}, u32[]{:S(2)}, u32[]{:S(2)}) collective-permute-start(bf16[8,512,256]{2,1,0:T(8,128)(2,1)} %bitcast.8), channel_id=1, source_target_pairs={{0,1},{1,0},{2,3},{3,2},{4,5},{5,4},{6,7},{7,6},{8,9},{9,8},{10,11... | collective-permute-start | bytes 6291464 | tf_op jit(solution)/shard_map/ppermute | solution.py:55
  70.2 6.5 %collective-permute-start.2 = (bf16[256,8,256]{0,2,1:T(8,128)(2,1)}, bf16[256,8,256]{0,2,1:T(8,128)(2,1)S(1)}, u32[]{:S(2)}, u32[]{:S(2)}) collective-permute-start(bf16[256,8,256]{0,2,1:T(8,128)(2,1)} %constant_dynamic-slice_fusion), channel_id=1, source_target_pairs={{0,1},{1,0},{2,3},{3,2},{4,5},{5,4},{6,7},{7,6},{8,9},{9,8},{10,11... | collective-permute-start | bytes 3145736 | tf_op jit(solution)/shard_map/ppermute | solution.py:53
  116.5 2.7 %collective-permute-start.4 = (f32[64,32,64]{2,1,0:T(8,128)S(1)}, f32[64,32,64]{2,1,0:T(8,128)S(1)}, u32[]{:S(2)}, u32[]{:S(2)}) collective-permute-start(f32[64,32,64]{2,1,0:T(8,128)S(1)} %fusion.9), channel_id=1, source_target_pairs={{0,1},{1,0},{2,3},{3,2},{4,5},{5,4},{6,7},{7,6},{8,9},{9,8},{10,11... | collective-permute-start | bytes 1572872 | tf_op jit(solution)/shard_map/ppermute | solution.py:72

commit v14 on v13

--- a/solution.py
+++ b/solution.py
@@ -38,9 +38,14 @@
 
     unit_mask = (jnp.arange(block_size)[None, :] < session_units[:, None]).astype(jnp.bfloat16)
     inputs = units.reshape(row_count, local_blocks, block_size) * unit_mask[None]
-    left_full = swap_halves(left_factor, 1)
-    mixed = jnp.einsum(
-        "rki,kij->jkr", inputs, left_full, preferred_element_type=jnp.float32
+    half_rows = block_size // 2
+    core_here = lax.axis_index("bin")
+    left_other = lax.ppermute(left_factor, "bin", [(0, 1), (1, 0)])
+    own_inputs = lax.dynamic_slice_in_dim(inputs, core_here * half_rows, half_rows, axis=2)
+    other_inputs = lax.dynamic_slice_in_dim(inputs, (1 - core_here) * half_rows, half_rows, axis=2)
+    mixed = (
+        jnp.einsum("rki,kij->jkr", own_inputs, left_factor, preferred_element_type=jnp.float32)
+        + jnp.einsum("rki,kij->jkr", other_inputs, left_other, preferred_element_type=jnp.float32)
     ).astype(jnp.bfloat16)
     mixed_sent = mixed.reshape(peer_count, right_local, local_blocks, row_count)
     mixed_sent, back_got = lax.optimization_barrier((mixed_sent, back_got))

time: 121 us -> 121 us (level)
  matrix products: 12.3 us -> 15.9 us
  other arithmetic: 6.02 us -> 2.9 us
  waiting for transfers between devices: 67.5 us -> 65.2 us
  local copies, waits for them, and re-layouts: 21.2 us -> 23 us
    all_to_all x1, waiting for transfers between devices: 31.8 us -> 27.5 us  [on_device(): back_got = lax.all_to_all(back_sent, 'blk', 0, 0, tiled=True)]
    reshape x0 -> x1, local copies, waits for them, and re-layouts: none -> 3.95 us  [on_device(): units.reshape(row_count, local_blocks, block_size) * unit_mask[None]]
    dot_general x1 -> x2, matrix products: 1.25 us -> 4.44 us  [the longest x1 3.73 us: on_device(): jnp.einsum('rki,kij->jkr', other_inputs, left_other, preferred_element_ty...]
    select_n x2 -> x1, other arithmetic: 2.85 us -> 0.07 us  [swap_halves(): first = jnp.where(core == 0, local, other)]
    dynamic_slice x1, local copies, waits for them, and re-layouts: 2.35 us -> 0.08 us  [on_device(): lax.dynamic_slice_in_dim(inputs, (1 - core_here) * half_rows, half_rows,...]
    convert_element_type x1, local copies, waits for them, and re-layouts: 2.54 us -> 4.49 us  [on_device(): mixed = (jnp.einsum('rki,kij->jkr', own_inputs, left_factor, preferred_el...]
    all_to_all x1, waiting for transfers between devices: 33.7 us -> 35.6 us  [on_device(): mixed_got = lax.all_to_all(mixed_sent, 'blk', 0, 0, tiled=True)]
    unnamed x11 -> x10, local copies, waits for them, and re-layouts: 11.4 us -> 9.6 us
where the time goes in v14:
time: 121 us; the launch traced here: 120 us
  waiting for transfers between devices  65.2 us (54%)
  local copies, waits for them, and re-layouts  23 us (19%)
  matrix products  15.9 us (13%)
  starting transfers between devices  12.5 us (10%)
  other arithmetic  2.9 us (2%)
    all_to_all x1, waiting for transfers between devices, on_device(): mixed_got = lax.all_to_all(mixed_sent, 'blk', 0, 0, tiled=True)  35.6 us
    all_to_all x1, waiting for transfers between devices, on_device(): back_got = lax.all_to_all(back_sent, 'blk', 0, 0, tiled=True)  27.5 us
    unnamed x10, local copies, waits for them, and re-layouts  9.6 us
    all_to_all x1, starting transfers between devices, on_device(): back_got = lax.all_to_all(back_sent, 'blk', 0, 0, tiled=True)  6.83 us
    convert_element_type x1, local copies, waits for them, and re-layouts, on_device(): mixed = (jnp.einsum('rki,kij->jkr', own_inputs, left_factor, preferred_el...  4.49 us
    all_to_all x1, starting transfers between devices, on_device(): mixed_got = lax.all_to_all(mixed_sent, 'blk', 0, 0, tiled=True)  4.36 us
    dot_general x1, matrix products, on_device(): jnp.einsum('rki,kjr->kij', partner_part, partner_back, preferred_element_...  4.11 us
    reshape x1, local copies, waits for them, and re-layouts, on_device(): units.reshape(row_count, local_blocks, block_size) * unit_mask[None]  3.95 us
  transfers between devices with their start and end apart: 7, of which 3 were waited for; matrix products, arithmetic and copies ran while one was open for 28% of the time, Pallas kernels for 0%

profile of v14, /device:TPU:0, one launch (start us, length us, event | category | flops | bytes accessed | tf_op | source)
XLA Modules:
  0.0 120.2 jit_solution(11062931891300330458)
XLA Ops:
  0.6 0.5 collective-permute-start.1
  1.1 2.6 %convolution_convert_fusion = bf16[256,4096]{0,1:T(8,128)(2,1)S(1)} fusion(bf16[256,4096]{1,0:T(8,128)(2,1)} %param.6), kind=kOutput, calls=%fused_computation | convolution fusion | flops 537985024 | bytes 4194304 | tf_op jit(solution)/shard_map/rc,rs->cs/dot_general | solution.py:28
  3.8 0.0 collective-permute-done.1
  3.8 0.1 broadcast_select_fusion.1
  3.9 0.7 convert_bitcast_fusion
  4.6 1.5 %copy.25 = bf16[8,8,64,256]{3,1,2,0:T(8,128)(2,1)} copy(bf16[8,8,64,256]{3,1,0,2:T(8,128)(2,1)S(1)} %convert_bitcast_fusion) | data formatting | bytes 4194304 | tf_op jit(solution)/shard_map/reshape | solution.py:36
  6.0 6.8 %all-to-all-start = ((bf16[8,8,64,256]{3,1,2,0:T(8,128)(2,1)}), bf16[8,8,64,256]{3,1,2,0:T(8,128)(2,1)S(1)}, u32[]{:S(2)}, u32[]{:S(2)}) async-start(bf16[8,8,64,256]{3,1,2,0:T(8,128)(2,1)} %copy.25), calls=%async_computation | async-start | bytes 4194304 | tf_op jit(solution)/shard_map/all_to_all | solution.py:37
  12.8 0.2 collective-permute-start
  13.0 4.1 %copy.22 = bf16[256,4096]{0,1:T(8,128)(2,1)} copy(bf16[256,4096]{1,0:T(8,128)(2,1)} %param.5) | data formatting | bytes 4194304 | tf_op args[0]
  17.1 3.9 %copy.23 = bf16[256,8,512]{2,0,1:T(8,128)(2,1)} copy(bf16[256,8,512]{0,2,1:T(8,128)(2,1)} %bitcast.38) | data formatting | bytes 4194304 | tf_op jit(solution)/shard_map/reshape | solution.py:40
  21.1 0.1 fusion.14
  21.1 1.7 %broadcast_multiply_fusion = bf16[256,8,512]{2,0,1:T(8,128)(2,1)S(1)} fusion(bf16[256,8,512]{2,0,1:T(8,128)(2,1)} %copy.23, bf16[8,512]{1,0:T(8,128)(2,1)S(1)} %fusion.14), kind=kLoop, calls=%fused_computation.17 | loop fusion | flops 1048576 | bytes 4202496 | tf_op jit(solution)/shard_map/mul | solution.py:40
  22.9 0.0 copy-start.1
  22.9 0.1 constant_dynamic-slice_fusion
  23.0 2.3 %copy-done.1 = bf16[8,256,512]{2,1,0:T(8,128)(2,1)S(1)} copy-done((bf16[8,256,512]{2,1,0:T(8,128)(2,1)S(1)}, bf16[8,256,512]{2,1,0:T(8,128)(2,1)}, u32[]{:S(2)}) %copy-start.1) | copy-done | bytes 2097176
  25.2 0.7 fusion.12
  26.0 3.7 %fusion = bf16[512,8,256]{0,2,1:T(8,128)(2,1)} fusion(f32[8,256,512]{2,1,0:T(8,128)S(1)} %fusion.12, bf16[256,8,256]{2,0,1:T(8,128)(2,1)S(1)} %constant_dynamic-slice_fusion, bf16[8,256,512]{2,1,0:T(8,128)(2,1)} %collective-permute-done), kind=kOutput, calls=%fused_computation.4 | convolution fusion | flops 538968064 | bytes 9437184 | tf_op jit(solution)/shard_map/rki,kij->jkr/dot_general | solution.py:48
  29.7 4.5 %copy.24 = bf16[512,8,256]{2,1,0:T(8,128)(2,1)} copy(bf16[512,8,256]{0,2,1:T(8,128)(2,1)} %fusion) | data formatting | bytes 4194304 | tf_op jit(solution)/shard_map/convert_element_type | solution.py:49
  34.2 27.5 %all-to-all-done = bf16[8,8,64,256]{3,1,2,0:T(8,128)(2,1)S(1)} async-done(((bf16[8,8,64,256]{3,1,2,0:T(8,128)(2,1)}), bf16[8,8,64,256]{3,1,2,0:T(8,128)(2,1)S(1)}, u32[]{:S(2)}, u32[]{:S(2)}) %all-to-all-start) | async-done | bytes 2097184 | tf_op jit(solution)/shard_map/all_to_all | solution.py:37
  61.7 4.4 %all-to-all-start.1 = ((bf16[8,64,8,256]{3,2,1,0:T(8,128)(2,1)}), bf16[8,64,8,256]{3,2,1,0:T(8,128)(2,1)}, u32[]{:S(2)}, u32[]{:S(2)}) async-start(bf16[8,64,8,256]{3,2,1,0:T(8,128)(2,1)} %bitcast.2), calls=%async_computation.1 | async-start | bytes 4194304 | tf_op jit(solution)/shard_map/all_to_all | solution.py:62
  66.1 1.8 %copy.26 = bf16[8,8,64,256]{3,2,1,0:T(8,128)(2,1)} copy(bf16[8,8,64,256]{3,0,2,1:T(8,128)(2,1)S(1)} %bitcast.36) | data formatting | bytes 4194304 | tf_op jit(solution)/shard_map/transpose | solution.py:59
  67.9 0.5 collective-permute-start.2
  68.4 3.3 %copy.30 = bf16[256,4096]{0,1:T(8,128)(2,1)S(1)} copy(bf16[256,4096]{1,0:T(8,128)(2,1)} %param.6) | data formatting | bytes 4194304 | tf_op args[1]
  71.7 2.7 %fusion.10 = f32[8,256,512]{2,1,0:T(8,128)S(1)} fusion(bf16[8,512,256]{2,1,0:T(8,128)(2,1)} %bitcast.8, bf16[256,8,512]{2,0,1:T(8,128)(2,1)} %copy-done, s32[]{:T(128)S(6)} %select_n.26), kind=kOutput, calls=%fused_computation.18 | convolution fusion | flops 536870912 | bytes 7340036 | tf_op jit(solution)/shard_map/rki,kjr->kij/dot_general | solution.py:64
  74.4 4.1 %add_convert_fusion = bf16[8,256,512]{2,1,0:T(8,128)(2,1)} fusion(f32[8,256,512]{2,1,0:T(8,128)S(1)} %fusion.10, bf16[256,8,256]{2,0,1:T(8,128)(2,1)} %collective-permute-done.2, bf16[8,512,256]{2,1,0:T(8,128)(2,1)} %collective-permute-done.3), kind=kOutput, calls=%fused_computation.1 | convolution fusion | flops 538968064 | bytes 9437184 | tf_op jit(solution)/shard_map/rki,kjr->kij/dot_general | solution.py:65
  78.5 35.6 %all-to-all-done.1 = bf16[8,64,8,256]{3,2,1,0:T(8,128)(2,1)} async-done(((bf16[8,64,8,256]{3,2,1,0:T(8,128)(2,1)}), bf16[8,64,8,256]{3,2,1,0:T(8,128)(2,1)}, u32[]{:S(2)}, u32[]{:S(2)}) %all-to-all-start.1) | async-done | bytes 2097184 | tf_op jit(solution)/shard_map/all_to_all | solution.py:62
  114.2 1.7 %dynamic-slice_bitcast_fusion = (bf16[64,4,8,256]{3,2,0,1:T(8,128)(2,1)S(1)}, bf16[64,4,8,256]{3,2,0,1:T(8,128)(2,1)S(1)}) fusion(bf16[8,64,8,256]{3,2,1,0:T(8,128)(2,1)} %all-to-all-done.1, s32[]{:T(128)S(6)} %select_n.32, s32[]{:T(128)S(6)} %select_n.31), kind=kLoop, calls=%fused_computation.15 | loop fusion | bytes 4194312 | tf_op jit(solution)/shard_map/transpose | solution.py:74
  115.8 0.7 fusion.4
  116.5 0.1 collective-permute-start.4
  116.6 0.7 fusion.6
  117.3 2.0 %collective-permute-done.4 = f32[64,32,64]{2,1,0:T(8,128)S(1)} collective-permute-done((f32[64,32,64]{2,1,0:T(8,128)S(1)}, f32[64,32,64]{2,1,0:T(8,128)S(1)}, u32[]{:S(2)}, u32[]{:S(2)}) %collective-permute-start.4) | collective-permute-done | bytes 524320 | tf_op jit(solution)/shard_map/ppermute | solution.py:77
  119.2 1.0 add_convert_fusion.2
  (10 shorter events, 0.0 us)
Async XLA Ops:
  0.6 3.1 %collective-permute-start.1 = (bf16[64,32,64]{2,1,0:T(8,128)(2,1)}, bf16[64,32,64]{2,1,0:T(8,128)(2,1)S(1)}, u32[]{:S(2)}, u32[]{:S(2)}) collective-permute-start(bf16[64,32,64]{2,1,0:T(8,128)(2,1)} %param.8), channel_id=1, source_target_pairs={{0,1},{1,0},{2,3},{3,2},{4,5},{5,4},{6,7},{7,6},{8,9},{9,8},{10,11... | collective-permute-start | bytes 786440 | tf_op jit(solution)/shard_map/ppermute | solution.py:9
  1.1 2.6 %copy-start.2 = (bf16[64,32,64]{2,1,0:T(8,128)(2,1)S(1)}, bf16[64,32,64]{2,1,0:T(8,128)(2,1)}, u32[]{:S(2)}) copy-start(bf16[64,32,64]{2,1,0:T(8,128)(2,1)} %param.8) | copy-start | bytes 786436
  6.0 55.7 %all-to-all-start = ((bf16[8,8,64,256]{3,1,2,0:T(8,128)(2,1)}), bf16[8,8,64,256]{3,1,2,0:T(8,128)(2,1)S(1)}, u32[]{:S(2)}, u32[]{:S(2)}) async-start(bf16[8,8,64,256]{3,1,2,0:T(8,128)(2,1)} %copy.25), calls=%async_computation | async-start | bytes 4194304 | tf_op jit(solution)/shard_map/all_to_all | solution.py:37
  12.8 13.1 %collective-permute-start = (bf16[8,256,512]{2,1,0:T(8,128)(2,1)}, bf16[8,256,512]{2,1,0:T(8,128)(2,1)}, u32[]{:S(2)}, u32[]{:S(2)}) collective-permute-start(bf16[8,256,512]{2,1,0:T(8,128)(2,1)} %param.7), channel_id=1, source_target_pairs={{0,1},{1,0},{2,3},{3,2},{4,5},{5,4},{6,7},{7,6},{8,9},{9,8},{10,11... | collective-permute-start | bytes 6291464 | tf_op jit(solution)/shard_map/ppermute | solution.py:43
  17.1 4.0 %copy-start.3 = (s32[8]{0:T(128)S(1)}, s32[8]{0:T(128)}, u32[]{:S(2)}) copy-start(s32[8]{0:T(128)} %param.9) | copy-start | bytes 100
  22.9 3.1 %copy-start = (bf16[256,8,512]{2,0,1:T(8,128)(2,1)}, bf16[256,8,512]{2,0,1:T(8,128)(2,1)S(1)}, u32[]{:S(2)}) copy-start(bf16[256,8,512]{2,0,1:T(8,128)(2,1)S(1)} %broadcast_multiply_fusion) | copy-start | bytes 6291460
  22.9 2.4 %copy-start.1 = (bf16[8,256,512]{2,1,0:T(8,128)(2,1)S(1)}, bf16[8,256,512]{2,1,0:T(8,128)(2,1)}, u32[]{:S(2)}) copy-start(bf16[8,256,512]{2,1,0:T(8,128)(2,1)} %param.7) | copy-start | bytes 6291460
  61.7 52.4 %all-to-all-start.1 = ((bf16[8,64,8,256]{3,2,1,0:T(8,128)(2,1)}), bf16[8,64,8,256]{3,2,1,0:T(8,128)(2,1)}, u32[]{:S(2)}, u32[]{:S(2)}) async-start(bf16[8,64,8,256]{3,2,1,0:T(8,128)(2,1)} %bitcast.2), calls=%async_computation.1 | async-start | bytes 4194304 | tf_op jit(solution)/shard_map/all_to_all | solution.py:62
  67.9 6.5 %collective-permute-start.3 = (bf16[8,512,256]{2,1,0:T(8,128)(2,1)}, bf16[8,512,256]{2,1,0:T(8,128)(2,1)}, u32[]{:S(2)}, u32[]{:S(2)}) collective-permute-start(bf16[8,512,256]{2,1,0:T(8,128)(2,1)} %bitcast.8), channel_id=1, source_target_pairs={{0,1},{1,0},{2,3},{3,2},{4,5},{5,4},{6,7},{7,6},{8,9},{9,8},{10,11... | collective-permute-start | bytes 6291464 | tf_op jit(solution)/shard_map/ppermute | solution.py:60
  67.9 6.5 %collective-permute-start.2 = (bf16[256,8,256]{2,0,1:T(8,128)(2,1)S(1)}, bf16[256,8,256]{2,0,1:T(8,128)(2,1)}, u32[]{:S(2)}, u32[]{:S(2)}) collective-permute-start(bf16[256,8,256]{2,0,1:T(8,128)(2,1)S(1)} %constant_dynamic-slice_fusion), channel_id=1, source_target_pairs={{0,1},{1,0},{2,3},{3,2},{4,5},{5,4},{6,7},{7,6},{8,9},{9,8},{10,11... | collective-permute-start | bytes 3145736 | tf_op jit(solution)/shard_map/ppermute | solution.py:58
  116.5 2.7 %collective-permute-start.4 = (f32[64,32,64]{2,1,0:T(8,128)S(1)}, f32[64,32,64]{2,1,0:T(8,128)S(1)}, u32[]{:S(2)}, u32[]{:S(2)}) collective-permute-start(f32[64,32,64]{2,1,0:T(8,128)S(1)} %fusion.4), channel_id=1, source_target_pairs={{0,1},{1,0},{2,3},{3,2},{4,5},{5,4},{6,7},{7,6},{8,9},{9,8},{10,11... | collective-permute-start | bytes 1572872 | tf_op jit(solution)/shard_map/ppermute | solution.py:77

commit v15 on v13

--- a/solution.py
+++ b/solution.py
@@ -64,15 +64,22 @@
     grad_left, mixed_got = lax.optimization_barrier((grad_left, mixed_got))
     half_peers = peer_count // 2
 
-    def right_of(start):
-        blocks = lax.dynamic_slice_in_dim(mixed_got, start, half_peers, axis=0)
-        blocks = blocks.transpose(1, 0, 2, 3).reshape(right_local, half_peers * local_blocks, row_count)
-        return jnp.einsum("jkr,rjm->jkm", blocks, upstream, preferred_element_type=jnp.float32)
+    def right_of(start, j_start, j_count):
+        blocks = lax.dynamic_slice_in_dim(mixed_got, start, half_peers, axis=0)[:, j_start:j_start + j_count]
+        blocks = blocks.transpose(1, 0, 2, 3).reshape(j_count, half_peers * local_blocks, row_count)
+        rows = upstream[:, j_start:j_start + j_count]
+        return jnp.einsum("jkr,rjm->jkm", blocks, rows, preferred_element_type=jnp.float32)
 
-    got_right = lax.ppermute(right_of((1 - core) * half_peers), "bin", [(0, 1), (1, 0)])
-    grad_right = (lax.optimization_barrier(right_of(core * half_peers)) + got_right).astype(
-        jnp.bfloat16
+    half_j = right_local // 2
+    got_right = jnp.concatenate(
+        [
+            lax.ppermute(right_of((1 - core) * half_peers, j0, half_j), "bin", [(0, 1), (1, 0)])
+            for j0 in (0, half_j)
+        ],
+        axis=0,
     )
+    own_right = lax.optimization_barrier(right_of(core * half_peers, 0, right_local))
+    grad_right = (own_right + got_right).astype(jnp.bfloat16)
     return (grad_left, grad_right)
 
 

time: 121 us -> 120 us (level)
  waiting for transfers between devices: 67.5 us -> 65.5 us
  matrix products: 12.3 us -> 13.6 us
    ppermute x1 -> x2, waiting for transfers between devices: 1.97 us -> 0.01 us  [on_device(): lax.ppermute(right_of((1 - core) * half_peers, j0, half_j), 'bin', [(0, 1...]
    dot_general x2 -> x3, matrix products: 1.35 us -> 2.69 us  [right_of(): jnp.einsum('jkr,rjm->jkm', blocks, rows, preferred_element_type=jnp.float32)]
  transfers between devices with their start and end apart: 7 -> 8, of which waited for: 3 -> 2; matrix products, arithmetic and copies ran while one was open for 28% -> 30% of each run, Pallas kernels for 0% -> 0%
where the time goes in v15:
time: 120 us
  waiting for transfers between devices  65.5 us (55%)
  local copies, waits for them, and re-layouts  20.8 us (17%)
  matrix products  13.6 us (11%)
  starting transfers between devices  13 us (11%)
  other arithmetic  6.03 us (5%)
    all_to_all x1, waiting for transfers between devices, on_device(): mixed_got = lax.all_to_all(mixed_sent, 'blk', 0, 0, tiled=True)  33.7 us
    all_to_all x1, waiting for transfers between devices, on_device(): back_got = lax.all_to_all(back_sent, 'blk', 0, 0, tiled=True)  31.8 us
    unnamed x11, local copies, waits for them, and re-layouts  11.4 us
    all_to_all x1, starting transfers between devices, on_device(): back_got = lax.all_to_all(back_sent, 'blk', 0, 0, tiled=True)  6.83 us
    all_to_all x1, starting transfers between devices, on_device(): mixed_got = lax.all_to_all(mixed_sent, 'blk', 0, 0, tiled=True)  4.34 us
    dot_general x1, matrix products, on_device(): jnp.einsum('rki,kjr->kij', partner_part, partner_back, preferred_element_...  3.72 us
    select_n x2, other arithmetic, swap_halves(): first = jnp.where(core == 0, local, other)  2.85 us
    dot_general x3, matrix products, right_of(): jnp.einsum('jkr,rjm->jkm', blocks, rows, preferred_element_type=jnp.float32)  2.69 us
  transfers between devices with their start and end apart: 8, of which 2 were waited for; matrix products, arithmetic and copies ran while one was open for 30% of the time, Pallas kernels for 0%

profile of v15, /device:TPU:0, one launch (start us, length us, event | category | flops | bytes accessed | tf_op | source)
XLA Modules:
  0.0 119.8 jit_solution(5619022432675812468)
XLA Ops:
  0.6 0.5 collective-permute-start.1
  1.1 2.6 %convolution_convert_fusion = bf16[256,4096]{0,1:T(8,128)(2,1)S(1)} fusion(bf16[256,4096]{1,0:T(8,128)(2,1)} %param.6), kind=kOutput, calls=%fused_computation | convolution fusion | flops 537985024 | bytes 4194304 | tf_op jit(solution)/shard_map/rc,rs->cs/dot_general | solution.py:28
  3.8 0.1 broadcast_select_fusion.3
  3.9 0.7 convert_bitcast_fusion
  4.6 1.5 %copy.32 = bf16[8,8,64,256]{3,1,2,0:T(8,128)(2,1)} copy(bf16[8,8,64,256]{3,1,0,2:T(8,128)(2,1)S(1)} %convert_bitcast_fusion) | data formatting | bytes 4194304 | tf_op jit(solution)/shard_map/reshape | solution.py:36
  6.0 6.8 %all-to-all-start = ((bf16[8,8,64,256]{3,1,2,0:T(8,128)(2,1)}), bf16[8,8,64,256]{3,1,2,0:T(8,128)(2,1)S(1)}, u32[]{:S(2)}, u32[]{:S(2)}) async-start(bf16[8,8,64,256]{3,1,2,0:T(8,128)(2,1)} %copy.32), calls=%async_computation | async-start | bytes 4194304 | tf_op jit(solution)/shard_map/all_to_all | solution.py:37
  12.8 3.9 %copy.28 = bf16[8,256,512]{1,2,0:T(8,128)(2,1)} copy(bf16[8,256,512]{2,1,0:T(8,128)(2,1)} %param.7) | data formatting | bytes 4194304 | tf_op args[2]
  16.8 0.2 collective-permute-start
  17.0 4.1 %copy.26 = bf16[256,4096]{0,1:T(8,128)(2,1)} copy(bf16[256,4096]{1,0:T(8,128)(2,1)} %param.5) | data formatting | bytes 4194304 | tf_op args[0]
  21.1 0.1 fusion.23
  21.1 2.1 %broadcast_multiply_fusion = bf16[256,8,512]{0,2,1:T(8,128)(2,1)S(1)} fusion(bf16[256,8,512]{0,2,1:T(8,128)(2,1)} %bitcast.43, bf16[8,512]{1,0:T(8,128)(2,1)S(1)} %fusion.23), kind=kLoop, calls=%fused_computation.25 | loop fusion | flops 1048576 | bytes 4202496 | tf_op jit(solution)/shard_map/mul | solution.py:40
  23.2 0.0 collective-permute-done
  23.3 0.1 copy-done.1
  23.4 2.8 %broadcast_select_fusion.1 = (bf16[8,256,512]{1,2,0:T(8,128)(2,1)S(1)}, bf16[8,256,512]{1,2,0:T(8,128)(2,1)S(1)}) fusion(bf16[8,256,512]{1,2,0:T(8,128)(2,1)S(1)} %copy-done.1, bf16[8,256,512]{1,2,0:T(8,128)(2,1)} %collective-permute-done, pred[]{:T(512)S(6)} %eq.4), kind=kLoop, calls=%fused_computation.9 | loop fusion | flops 2097152 | bytes 8388609 | tf_op jit(solution)/shard_map/jit(_where)/select_n | solution.py:11
  26.1 1.3 %convert_bitcast_fusion.1 = bf16[512,8,256]{2,0,1:T(8,128)(2,1)S(1)} fusion(bf16[256,8,512]{0,2,1:T(8,128)(2,1)S(1)} %broadcast_multiply_fusion, bf16[8,256,512]{1,2,0:T(8,128)(2,1)S(1)} %get-tuple-element.11, bf16[8,256,512]{1,2,0:T(8,128)(2,1)S(1)} %get-tuple-element.10), kind=kOutput, calls=%fused_computation.7 | convolution fusion | flops 1083179008 | bytes 8388608 | tf_op jit(solution)/shard_map/rki,kij->jkr/dot_general | solution.py:42
  27.4 2.5 %copy.31 = bf16[512,8,256]{2,1,0:T(8,128)(2,1)} copy(bf16[512,8,256]{2,0,1:T(8,128)(2,1)S(1)} %convert_bitcast_fusion.1) | data formatting | bytes 4194304 | tf_op jit(solution)/shard_map/convert_element_type | solution.py:44
  30.0 31.8 %all-to-all-done = bf16[8,8,64,256]{3,1,2,0:T(8,128)(2,1)S(1)} async-done(((bf16[8,8,64,256]{3,1,2,0:T(8,128)(2,1)}), bf16[8,8,64,256]{3,1,2,0:T(8,128)(2,1)S(1)}, u32[]{:S(2)}, u32[]{:S(2)}) %all-to-all-start) | async-done | bytes 2097184 | tf_op jit(solution)/shard_map/all_to_all | solution.py:37
  61.7 4.3 %all-to-all-start.1 = ((bf16[8,64,8,256]{3,2,1,0:T(8,128)(2,1)}), bf16[8,64,8,256]{3,2,1,0:T(8,128)(2,1)}, u32[]{:S(2)}, u32[]{:S(2)}) async-start(bf16[8,64,8,256]{3,2,1,0:T(8,128)(2,1)} %bitcast.2), calls=%async_computation.1 | async-start | bytes 4194304 | tf_op jit(solution)/shard_map/all_to_all | solution.py:57
  66.1 1.8 %copy.33 = bf16[8,8,64,256]{3,2,1,0:T(8,128)(2,1)} copy(bf16[8,8,64,256]{3,0,2,1:T(8,128)(2,1)S(1)} %bitcast.41) | data formatting | bytes 4194304 | tf_op jit(solution)/shard_map/transpose | solution.py:54
  67.9 2.4 %constant_dynamic-slice_fusion = bf16[256,8,256]{0,2,1:T(8,128)(2,1)} fusion(bf16[256,8,512]{0,2,1:T(8,128)(2,1)} %copy-done, s32[]{:T(128)S(6)} %select_n.44), kind=kLoop, calls=%fused_computation.37 | loop fusion | bytes 2097156 | tf_op jit(solution)/shard_map/dynamic_slice | solution.py:52
  70.2 0.5 collective-permute-start.2
  70.7 3.3 %copy.35 = bf16[256,4096]{0,1:T(8,128)(2,1)S(1)} copy(bf16[256,4096]{1,0:T(8,128)(2,1)} %param.6) | data formatting | bytes 4194304 | tf_op args[1]
  74.0 2.7 %fusion.17 = f32[8,256,512]{2,1,0:T(8,128)S(1)} fusion(bf16[8,512,256]{2,1,0:T(8,128)(2,1)} %bitcast.8, bf16[256,8,512]{0,2,1:T(8,128)(2,1)} %copy-done, s32[]{:T(128)S(6)} %select_n.37), kind=kOutput, calls=%fused_computation.23 | convolution fusion | flops 536870912 | bytes 7340036 | tf_op jit(solution)/shard_map/rki,kjr->kij/dot_general | solution.py:59
  76.7 3.7 %add_convert_fusion = bf16[8,256,512]{2,1,0:T(8,128)(2,1)} fusion(f32[8,256,512]{2,1,0:T(8,128)S(1)} %fusion.17, bf16[256,8,256]{0,2,1:T(8,128)(2,1)S(1)} %collective-permute-done.2, bf16[8,512,256]{2,1,0:T(8,128)(2,1)} %collective-permute-done.3), kind=kOutput, calls=%fused_computation.5 | convolution fusion | flops 538968064 | bytes 9437184 | tf_op jit(solution)/shard_map/rki,kjr->kij/dot_general | solution.py:60
  80.4 33.7 %all-to-all-done.1 = bf16[8,64,8,256]{3,2,1,0:T(8,128)(2,1)} async-done(((bf16[8,64,8,256]{3,2,1,0:T(8,128)(2,1)}), bf16[8,64,8,256]{3,2,1,0:T(8,128)(2,1)}, u32[]{:S(2)}, u32[]{:S(2)}) %all-to-all-start.1) | async-done | bytes 2097184 | tf_op jit(solution)/shard_map/all_to_all | solution.py:57
  114.1 1.3 %dynamic-slice_bitcast_fusion.2 = (bf16[32,4,8,256]{3,2,0,1:T(8,128)(2,1)S(1)}, bf16[32,4,8,256]{3,2,0,1:T(8,128)(2,1)S(1)}) fusion(bf16[8,64,8,256]{3,2,1,0:T(8,128)(2,1)} %all-to-all-done.1, s32[]{:T(128)S(6)} %select_n.46, s32[]{:T(128)S(6)} %add.25), kind=kLoop, calls=%fused_computation.27 | loop fusion | bytes 2097160 | tf_op jit(solution)/shard_map/transpose | solution.py:69
  115.4 0.4 fusion.6
  115.8 0.1 collective-permute-start.5
  115.9 0.4 fusion.8
  116.3 0.6 collective-permute-start.4
  116.8 1.9 %fusion.14 = f32[64,32,64]{2,1,0:T(8,128)S(1)} fusion(bf16[256,64,64]{0,2,1:T(8,128)(2,1)S(1)} %bitcast.40, bf16[8,64,8,256]{3,2,1,0:T(8,128)(2,1)} %all-to-all-done.1, s32[]{:T(128)S(6)} %select_n.45), kind=kOutput, calls=%fused_computation.19 | convolution fusion | flops 67108864 | bytes 3670020 | tf_op jit(solution)/shard_map/jkr,rjm->jkm/dot_general | solution.py:71
  118.7 1.0 fusion.13
  (13 shorter events, 0.0 us)
Async XLA Ops:
  0.6 3.1 %collective-permute-start.1 = (bf16[64,32,64]{2,1,0:T(8,128)(2,1)}, bf16[64,32,64]{2,1,0:T(8,128)(2,1)S(1)}, u32[]{:S(2)}, u32[]{:S(2)}) collective-permute-start(bf16[64,32,64]{2,1,0:T(8,128)(2,1)} %param.8), channel_id=1, source_target_pairs={{0,1},{1,0},{2,3},{3,2},{4,5},{5,4},{6,7},{7,6},{8,9},{9,8},{10,11... | collective-permute-start | bytes 786440 | tf_op jit(solution)/shard_map/ppermute | solution.py:9
  1.1 2.6 %copy-start.2 = (bf16[64,32,64]{2,1,0:T(8,128)(2,1)S(1)}, bf16[64,32,64]{2,1,0:T(8,128)(2,1)}, u32[]{:S(2)}) copy-start(bf16[64,32,64]{2,1,0:T(8,128)(2,1)} %param.8) | copy-start | bytes 786436
  6.0 55.7 %all-to-all-start = ((bf16[8,8,64,256]{3,1,2,0:T(8,128)(2,1)}), bf16[8,8,64,256]{3,1,2,0:T(8,128)(2,1)S(1)}, u32[]{:S(2)}, u32[]{:S(2)}) async-start(bf16[8,8,64,256]{3,1,2,0:T(8,128)(2,1)} %copy.32), calls=%async_computation | async-start | bytes 4194304 | tf_op jit(solution)/shard_map/all_to_all | solution.py:37
  16.8 4.3 %copy-start.3 = (s32[8]{0:T(128)S(1)}, s32[8]{0:T(128)}, u32[]{:S(2)}) copy-start(s32[8]{0:T(128)} %param.9) | copy-start | bytes 100
  16.8 6.5 %collective-permute-start = (bf16[8,256,512]{1,2,0:T(8,128)(2,1)}, bf16[8,256,512]{1,2,0:T(8,128)(2,1)}, u32[]{:S(2)}, u32[]{:S(2)}) collective-permute-start(bf16[8,256,512]{1,2,0:T(8,128)(2,1)} %copy.28), channel_id=1, source_target_pairs={{0,1},{1,0},{2,3},{3,2},{4,5},{5,4},{6,7},{7,6},{8,9},{9,8},{10,11... | collective-permute-start | bytes 6291464 | tf_op jit(solution)/shard_map/ppermute | solution.py:9
  21.1 2.2 %copy-start.1 = (bf16[8,256,512]{1,2,0:T(8,128)(2,1)S(1)}, bf16[8,256,512]{1,2,0:T(8,128)(2,1)}, u32[]{:S(2)}) copy-start(bf16[8,256,512]{1,2,0:T(8,128)(2,1)} %copy.28) | copy-start | bytes 6291460
  23.2 2.9 %copy-start = (bf16[256,8,512]{0,2,1:T(8,128)(2,1)}, bf16[256,8,512]{0,2,1:T(8,128)(2,1)S(1)}, u32[]{:S(2)}) copy-start(bf16[256,8,512]{0,2,1:T(8,128)(2,1)S(1)} %broadcast_multiply_fusion) | copy-start | bytes 6291460
  61.7 52.4 %all-to-all-start.1 = ((bf16[8,64,8,256]{3,2,1,0:T(8,128)(2,1)}), bf16[8,64,8,256]{3,2,1,0:T(8,128)(2,1)}, u32[]{:S(2)}, u32[]{:S(2)}) async-start(bf16[8,64,8,256]{3,2,1,0:T(8,128)(2,1)} %bitcast.2), calls=%async_computation.1 | async-start | bytes 4194304 | tf_op jit(solution)/shard_map/all_to_all | solution.py:57
  67.9 8.8 %collective-permute-start.3 = (bf16[8,512,256]{2,1,0:T(8,128)(2,1)}, bf16[8,512,256]{2,1,0:T(8,128)(2,1)}, u32[]{:S(2)}, u32[]{:S(2)}) collective-permute-start(bf16[8,512,256]{2,1,0:T(8,128)(2,1)} %bitcast.8), channel_id=1, source_target_pairs={{0,1},{1,0},{2,3},{3,2},{4,5},{5,4},{6,7},{7,6},{8,9},{9,8},{10,11... | collective-permute-start | bytes 6291464 | tf_op jit(solution)/shard_map/ppermute | solution.py:55
  70.2 6.5 %collective-permute-start.2 = (bf16[256,8,256]{0,2,1:T(8,128)(2,1)}, bf16[256,8,256]{0,2,1:T(8,128)(2,1)S(1)}, u32[]{:S(2)}, u32[]{:S(2)}) collective-permute-start(bf16[256,8,256]{0,2,1:T(8,128)(2,1)} %constant_dynamic-slice_fusion), channel_id=1, source_target_pairs={{0,1},{1,0},{2,3},{3,2},{4,5},{5,4},{6,7},{7,6},{8,9},{9,8},{10,11... | collective-permute-start | bytes 3145736 | tf_op jit(solution)/shard_map/ppermute | solution.py:53
  115.8 2.9 %collective-permute-start.5 = (f32[32,32,64]{2,1,0:T(8,128)S(1)}, f32[32,32,64]{2,1,0:T(8,128)S(1)}, u32[]{:S(2)}, u32[]{:S(2)}) collective-permute-start(f32[32,32,64]{2,1,0:T(8,128)S(1)} %fusion.6), channel_id=1, source_target_pairs={{0,1},{1,0},{2,3},{3,2},{4,5},{5,4},{6,7},{7,6},{8,9},{9,8},{10,11... | collective-permute-start | bytes 786440 | tf_op jit(solution)/shard_map/ppermute | solution.py:76
  116.3 2.5 %collective-permute-start.4 = (f32[32,32,64]{2,1,0:T(8,128)S(1)}, f32[32,32,64]{2,1,0:T(8,128)S(1)}, u32[]{:S(2)}, u32[]{:S(2)}) collective-permute-start(f32[32,32,64]{2,1,0:T(8,128)S(1)} %fusion.8), channel_id=1, source_target_pairs={{0,1},{1,0},{2,3},{3,2},{4,5},{5,4},{6,7},{7,6},{8,9},{9,8},{10,11... | collective-permute-start | bytes 786440 | tf_op jit(solution)/shard_map/ppermute | solution.py:76

commit v16 on v15

--- a/solution.py
+++ b/solution.py
@@ -78,8 +78,7 @@
         ],
         axis=0,
     )
-    own_right = lax.optimization_barrier(right_of(core * half_peers, 0, right_local))
-    grad_right = (own_right + got_right).astype(jnp.bfloat16)
+    grad_right = (right_of(core * half_peers, 0, right_local) + got_right).astype(jnp.bfloat16)
     return (grad_left, grad_right)
 
 

time: 120 us -> 123 us (1.025)
  matrix products: 13.6 us -> 16 us
  waiting for transfers between devices: 65.5 us -> 67.2 us
    dot_general x3, matrix products: 2.69 us -> 5.11 us  [right_of(): jnp.einsum('jkr,rjm->jkm', blocks, rows, preferred_element_type=jnp.float32)]
    ppermute x2, waiting for transfers between devices: 0.01 us -> 1.75 us  [on_device(): lax.ppermute(right_of((1 - core) * half_peers, j0, half_j), 'bin', [(0, 1...]
  transfers between devices with their start and end apart: 8 -> 8, of which waited for: 2 -> 4; matrix products, arithmetic and copies ran while one was open for 30% -> 28% of each run, Pallas kernels for 0% -> 0%
where the time goes in v16:
time: 123 us
  waiting for transfers between devices  67.2 us (55%)
  local copies, waits for them, and re-layouts  20.8 us (17%)
  matrix products  16 us (13%)
  starting transfers between devices  12.9 us (10%)
  other arithmetic  5.01 us (4%)
    all_to_all x1, waiting for transfers between devices, on_device(): mixed_got = lax.all_to_all(mixed_sent, 'blk', 0, 0, tiled=True)  33.7 us
    all_to_all x1, waiting for transfers between devices, on_device(): back_got = lax.all_to_all(back_sent, 'blk', 0, 0, tiled=True)  31.8 us
    unnamed x11, local copies, waits for them, and re-layouts  11.4 us
    all_to_all x1, starting transfers between devices, on_device(): back_got = lax.all_to_all(back_sent, 'blk', 0, 0, tiled=True)  6.83 us
    dot_general x3, matrix products, right_of(): jnp.einsum('jkr,rjm->jkm', blocks, rows, preferred_element_type=jnp.float32)  5.11 us
    all_to_all x1, starting transfers between devices, on_device(): mixed_got = lax.all_to_all(mixed_sent, 'blk', 0, 0, tiled=True)  4.34 us
    dot_general x1, matrix products, on_device(): jnp.einsum('rki,kjr->kij', partner_part, partner_back, preferred_element_...  3.72 us
    select_n x2, other arithmetic, swap_halves(): first = jnp.where(core == 0, local, other)  2.85 us
  transfers between devices with their start and end apart: 8, of which 4 were waited for; matrix products, arithmetic and copies ran while one was open for 28% of the time, Pallas kernels for 0%

profile of v16, /device:TPU:0, one launch (start us, length us, event | category | flops | bytes accessed | tf_op | source)
XLA Modules:
  0.0 122.8 jit_solution(4473680374474698253)
XLA Ops:
  0.6 0.5 collective-permute-start.1
  1.1 2.6 %convolution_convert_fusion = bf16[256,4096]{0,1:T(8,128)(2,1)S(1)} fusion(bf16[256,4096]{1,0:T(8,128)(2,1)} %param.6), kind=kOutput, calls=%fused_computation | convolution fusion | flops 537985024 | bytes 4194304 | tf_op jit(solution)/shard_map/rc,rs->cs/dot_general | solution.py:28
  3.8 0.0 collective-permute-done.1
  3.8 0.1 broadcast_select_fusion.3
  3.9 0.7 convert_bitcast_fusion
  4.6 1.5 %copy.32 = bf16[8,8,64,256]{3,1,2,0:T(8,128)(2,1)} copy(bf16[8,8,64,256]{3,1,0,2:T(8,128)(2,1)S(1)} %convert_bitcast_fusion) | data formatting | bytes 4194304 | tf_op jit(solution)/shard_map/reshape | solution.py:36
  6.0 6.8 %all-to-all-start = ((bf16[8,8,64,256]{3,1,2,0:T(8,128)(2,1)}), bf16[8,8,64,256]{3,1,2,0:T(8,128)(2,1)S(1)}, u32[]{:S(2)}, u32[]{:S(2)}) async-start(bf16[8,8,64,256]{3,1,2,0:T(8,128)(2,1)} %copy.32), calls=%async_computation | async-start | bytes 4194304 | tf_op jit(solution)/shard_map/all_to_all | solution.py:37
  12.8 3.9 %copy.28 = bf16[8,256,512]{1,2,0:T(8,128)(2,1)} copy(bf16[8,256,512]{2,1,0:T(8,128)(2,1)} %param.7) | data formatting | bytes 4194304 | tf_op args[2]
  16.8 0.2 collective-permute-start
  17.0 4.1 %copy.26 = bf16[256,4096]{0,1:T(8,128)(2,1)} copy(bf16[256,4096]{1,0:T(8,128)(2,1)} %param.5) | data formatting | bytes 4194304 | tf_op args[0]
  21.1 0.1 fusion.25
  21.1 2.1 %broadcast_multiply_fusion = bf16[256,8,512]{0,2,1:T(8,128)(2,1)S(1)} fusion(bf16[256,8,512]{0,2,1:T(8,128)(2,1)} %bitcast.45, bf16[8,512]{1,0:T(8,128)(2,1)S(1)} %fusion.25), kind=kLoop, calls=%fused_computation.25 | loop fusion | flops 1048576 | bytes 4202496 | tf_op jit(solution)/shard_map/mul | solution.py:40
  23.3 0.1 copy-done.1
  23.4 2.8 %broadcast_select_fusion.1 = (bf16[8,256,512]{1,2,0:T(8,128)(2,1)S(1)}, bf16[8,256,512]{1,2,0:T(8,128)(2,1)S(1)}) fusion(bf16[8,256,512]{1,2,0:T(8,128)(2,1)S(1)} %copy-done.1, bf16[8,256,512]{1,2,0:T(8,128)(2,1)} %collective-permute-done, pred[]{:T(512)S(6)} %eq.4), kind=kLoop, calls=%fused_computation.9 | loop fusion | flops 2097152 | bytes 8388609 | tf_op jit(solution)/shard_map/jit(_where)/select_n | solution.py:11
  26.1 1.3 %convert_bitcast_fusion.1 = bf16[512,8,256]{2,0,1:T(8,128)(2,1)S(1)} fusion(bf16[256,8,512]{0,2,1:T(8,128)(2,1)S(1)} %broadcast_multiply_fusion, bf16[8,256,512]{1,2,0:T(8,128)(2,1)S(1)} %get-tuple-element.11, bf16[8,256,512]{1,2,0:T(8,128)(2,1)S(1)} %get-tuple-element.10), kind=kOutput, calls=%fused_computation.7 | convolution fusion | flops 1083179008 | bytes 8388608 | tf_op jit(solution)/shard_map/rki,kij->jkr/dot_general | solution.py:42
  27.4 2.5 %copy.31 = bf16[512,8,256]{2,1,0:T(8,128)(2,1)} copy(bf16[512,8,256]{2,0,1:T(8,128)(2,1)S(1)} %convert_bitcast_fusion.1) | data formatting | bytes 4194304 | tf_op jit(solution)/shard_map/convert_element_type | solution.py:44
  30.0 31.8 %all-to-all-done = bf16[8,8,64,256]{3,1,2,0:T(8,128)(2,1)S(1)} async-done(((bf16[8,8,64,256]{3,1,2,0:T(8,128)(2,1)}), bf16[8,8,64,256]{3,1,2,0:T(8,128)(2,1)S(1)}, u32[]{:S(2)}, u32[]{:S(2)}) %all-to-all-start) | async-done | bytes 2097184 | tf_op jit(solution)/shard_map/all_to_all | solution.py:37
  61.7 4.3 %all-to-all-start.1 = ((bf16[8,64,8,256]{3,2,1,0:T(8,128)(2,1)}), bf16[8,64,8,256]{3,2,1,0:T(8,128)(2,1)}, u32[]{:S(2)}, u32[]{:S(2)}) async-start(bf16[8,64,8,256]{3,2,1,0:T(8,128)(2,1)} %bitcast.2), calls=%async_computation.1 | async-start | bytes 4194304 | tf_op jit(solution)/shard_map/all_to_all | solution.py:57
  66.1 1.8 %copy.33 = bf16[8,8,64,256]{3,2,1,0:T(8,128)(2,1)} copy(bf16[8,8,64,256]{3,0,2,1:T(8,128)(2,1)S(1)} %bitcast.43) | data formatting | bytes 4194304 | tf_op jit(solution)/shard_map/transpose | solution.py:54
  67.9 2.4 %constant_dynamic-slice_fusion = bf16[256,8,256]{0,2,1:T(8,128)(2,1)} fusion(bf16[256,8,512]{0,2,1:T(8,128)(2,1)} %copy-done, s32[]{:T(128)S(6)} %select_n.44), kind=kLoop, calls=%fused_computation.37 | loop fusion | bytes 2097156 | tf_op jit(solution)/shard_map/dynamic_slice | solution.py:52
  70.2 0.5 collective-permute-start.2
  70.7 3.3 %copy.35 = bf16[256,4096]{0,1:T(8,128)(2,1)S(1)} copy(bf16[256,4096]{1,0:T(8,128)(2,1)} %param.6) | data formatting | bytes 4194304 | tf_op args[1]
  74.0 2.7 %fusion.19 = f32[8,256,512]{2,1,0:T(8,128)S(1)} fusion(bf16[8,512,256]{2,1,0:T(8,128)(2,1)} %bitcast.8, bf16[256,8,512]{0,2,1:T(8,128)(2,1)} %copy-done, s32[]{:T(128)S(6)} %select_n.37), kind=kOutput, calls=%fused_computation.23 | convolution fusion | flops 536870912 | bytes 7340036 | tf_op jit(solution)/shard_map/rki,kjr->kij/dot_general | solution.py:59
  76.7 3.7 %add_convert_fusion = bf16[8,256,512]{2,1,0:T(8,128)(2,1)} fusion(f32[8,256,512]{2,1,0:T(8,128)S(1)} %fusion.19, bf16[256,8,256]{0,2,1:T(8,128)(2,1)S(1)} %collective-permute-done.2, bf16[8,512,256]{2,1,0:T(8,128)(2,1)} %collective-permute-done.3), kind=kOutput, calls=%fused_computation.5 | convolution fusion | flops 538968064 | bytes 9437184 | tf_op jit(solution)/shard_map/rki,kjr->kij/dot_general | solution.py:60
  80.4 33.7 %all-to-all-done.1 = bf16[8,64,8,256]{3,2,1,0:T(8,128)(2,1)} async-done(((bf16[8,64,8,256]{3,2,1,0:T(8,128)(2,1)}), bf16[8,64,8,256]{3,2,1,0:T(8,128)(2,1)}, u32[]{:S(2)}, u32[]{:S(2)}) %all-to-all-start.1) | async-done | bytes 2097184 | tf_op jit(solution)/shard_map/all_to_all | solution.py:57
  114.1 1.3 %dynamic-slice_bitcast_fusion.2 = (bf16[32,4,8,256]{3,2,0,1:T(8,128)(2,1)S(1)}, bf16[32,4,8,256]{3,2,0,1:T(8,128)(2,1)S(1)}) fusion(bf16[8,64,8,256]{3,2,1,0:T(8,128)(2,1)} %all-to-all-done.1, s32[]{:T(128)S(6)} %select_n.46, s32[]{:T(128)S(6)} %add.25), kind=kLoop, calls=%fused_computation.27 | loop fusion | bytes 2097160 | tf_op jit(solution)/shard_map/transpose | solution.py:69
  115.4 1.2 fusion.6
  116.6 1.2 fusion.8
  117.8 0.5 collective-permute-start.4
  118.3 0.4 collective-permute-done.5
  118.7 1.4 %collective-permute-done.4 = f32[32,32,64]{2,1,0:T(8,128)S(1)} collective-permute-done((f32[32,32,64]{2,1,0:T(8,128)}, f32[32,32,64]{2,1,0:T(8,128)S(1)}, u32[]{:S(2)}, u32[]{:S(2)}) %collective-permute-start.4) | collective-permute-done | bytes 262176 | tf_op jit(solution)/shard_map/ppermute | solution.py:76
  120.1 2.7 %fusion.13 = bf16[64,32,64]{2,1,0:T(8,128)(2,1)} fusion(f32[32,32,64]{2,1,0:T(8,128)S(1)} %collective-permute-done.5, f32[32,32,64]{2,1,0:T(8,128)S(1)} %collective-permute-done.4, bf16[256,64,64]{0,2,1:T(8,128)(2,1)S(1)} %bitcast.42, bf16[8,64,8,256]{3,2,1,0:T(8,128)(2,1)} %all-to-all-done.1, s32[]{:T(128)S(6)} %select_n.45), kind=kOutput, calls=%fused_computation.18 | convolution fusion | flops 67502080 | bytes 3932164 | tf_op jit(solution)/shard_map/jkr,rjm->jkm/dot_general | solution.py:71
  (12 shorter events, 0.0 us)
Async XLA Ops:
  0.6 3.1 %collective-permute-start.1 = (bf16[64,32,64]{2,1,0:T(8,128)(2,1)}, bf16[64,32,64]{2,1,0:T(8,128)(2,1)S(1)}, u32[]{:S(2)}, u32[]{:S(2)}) collective-permute-start(bf16[64,32,64]{2,1,0:T(8,128)(2,1)} %param.8), channel_id=1, source_target_pairs={{0,1},{1,0},{2,3},{3,2},{4,5},{5,4},{6,7},{7,6},{8,9},{9,8},{10,11... | collective-permute-start | bytes 786440 | tf_op jit(solution)/shard_map/ppermute | solution.py:9
  1.1 2.6 %copy-start.2 = (bf16[64,32,64]{2,1,0:T(8,128)(2,1)S(1)}, bf16[64,32,64]{2,1,0:T(8,128)(2,1)}, u32[]{:S(2)}) copy-start(bf16[64,32,64]{2,1,0:T(8,128)(2,1)} %param.8) | copy-start | bytes 786436
  6.0 55.7 %all-to-all-start = ((bf16[8,8,64,256]{3,1,2,0:T(8,128)(2,1)}), bf16[8,8,64,256]{3,1,2,0:T(8,128)(2,1)S(1)}, u32[]{:S(2)}, u32[]{:S(2)}) async-start(bf16[8,8,64,256]{3,1,2,0:T(8,128)(2,1)} %copy.32), calls=%async_computation | async-start | bytes 4194304 | tf_op jit(solution)/shard_map/all_to_all | solution.py:37
  16.8 4.3 %copy-start.3 = (s32[8]{0:T(128)S(1)}, s32[8]{0:T(128)}, u32[]{:S(2)}) copy-start(s32[8]{0:T(128)} %param.9) | copy-start | bytes 100
  16.8 6.5 %collective-permute-start = (bf16[8,256,512]{1,2,0:T(8,128)(2,1)}, bf16[8,256,512]{1,2,0:T(8,128)(2,1)}, u32[]{:S(2)}, u32[]{:S(2)}) collective-permute-start(bf16[8,256,512]{1,2,0:T(8,128)(2,1)} %copy.28), channel_id=1, source_target_pairs={{0,1},{1,0},{2,3},{3,2},{4,5},{5,4},{6,7},{7,6},{8,9},{9,8},{10,11... | collective-permute-start | bytes 6291464 | tf_op jit(solution)/shard_map/ppermute | solution.py:9
  21.1 2.2 %copy-start.1 = (bf16[8,256,512]{1,2,0:T(8,128)(2,1)S(1)}, bf16[8,256,512]{1,2,0:T(8,128)(2,1)}, u32[]{:S(2)}) copy-start(bf16[8,256,512]{1,2,0:T(8,128)(2,1)} %copy.28) | copy-start | bytes 6291460
  23.2 2.9 %copy-start = (bf16[256,8,512]{0,2,1:T(8,128)(2,1)}, bf16[256,8,512]{0,2,1:T(8,128)(2,1)S(1)}, u32[]{:S(2)}) copy-start(bf16[256,8,512]{0,2,1:T(8,128)(2,1)S(1)} %broadcast_multiply_fusion) | copy-start | bytes 6291460
  61.7 52.4 %all-to-all-start.1 = ((bf16[8,64,8,256]{3,2,1,0:T(8,128)(2,1)}), bf16[8,64,8,256]{3,2,1,0:T(8,128)(2,1)}, u32[]{:S(2)}, u32[]{:S(2)}) async-start(bf16[8,64,8,256]{3,2,1,0:T(8,128)(2,1)} %bitcast.2), calls=%async_computation.1 | async-start | bytes 4194304 | tf_op jit(solution)/shard_map/all_to_all | solution.py:57
  67.9 8.8 %collective-permute-start.3 = (bf16[8,512,256]{2,1,0:T(8,128)(2,1)}, bf16[8,512,256]{2,1,0:T(8,128)(2,1)}, u32[]{:S(2)}, u32[]{:S(2)}) collective-permute-start(bf16[8,512,256]{2,1,0:T(8,128)(2,1)} %bitcast.8), channel_id=1, source_target_pairs={{0,1},{1,0},{2,3},{3,2},{4,5},{5,4},{6,7},{7,6},{8,9},{9,8},{10,11... | collective-permute-start | bytes 6291464 | tf_op jit(solution)/shard_map/ppermute | solution.py:55
  70.2 6.5 %collective-permute-start.2 = (bf16[256,8,256]{0,2,1:T(8,128)(2,1)}, bf16[256,8,256]{0,2,1:T(8,128)(2,1)S(1)}, u32[]{:S(2)}, u32[]{:S(2)}) collective-permute-start(bf16[256,8,256]{0,2,1:T(8,128)(2,1)} %constant_dynamic-slice_fusion), channel_id=1, source_target_pairs={{0,1},{1,0},{2,3},{3,2},{4,5},{5,4},{6,7},{7,6},{8,9},{9,8},{10,11... | collective-permute-start | bytes 3145736 | tf_op jit(solution)/shard_map/ppermute | solution.py:53
  116.6 2.1 %collective-permute-start.5 = (f32[32,32,64]{2,1,0:T(8,128)}, f32[32,32,64]{2,1,0:T(8,128)S(1)}, u32[]{:S(2)}, u32[]{:S(2)}) collective-permute-start(f32[32,32,64]{2,1,0:T(8,128)} %fusion.6), channel_id=1, source_target_pairs={{0,1},{1,0},{2,3},{3,2},{4,5},{5,4},{6,7},{7,6},{8,9},{9,8},{10,11... | collective-permute-start | bytes 786440 | tf_op jit(solution)/shard_map/ppermute | solution.py:76
  117.8 2.3 %collective-permute-start.4 = (f32[32,32,64]{2,1,0:T(8,128)}, f32[32,32,64]{2,1,0:T(8,128)S(1)}, u32[]{:S(2)}, u32[]{:S(2)}) collective-permute-start(f32[32,32,64]{2,1,0:T(8,128)} %fusion.8), channel_id=1, source_target_pairs={{0,1},{1,0},{2,3},{3,2},{4,5},{5,4},{6,7},{7,6},{8,9},{9,8},{10,11... | collective-permute-start | bytes 786440 | tf_op jit(solution)/shard_map/ppermute | solution.py:76

commit v17 on v15

--- a/solution.py
+++ b/solution.py
@@ -71,12 +71,10 @@
         return jnp.einsum("jkr,rjm->jkm", blocks, rows, preferred_element_type=jnp.float32)
 
     half_j = right_local // 2
+    sent_right = [right_of((1 - core) * half_peers, j0, half_j) for j0 in (0, half_j)]
+    sent_right, mixed_got = lax.optimization_barrier((sent_right, mixed_got))
     got_right = jnp.concatenate(
-        [
-            lax.ppermute(right_of((1 - core) * half_peers, j0, half_j), "bin", [(0, 1), (1, 0)])
-            for j0 in (0, half_j)
-        ],
-        axis=0,
+        [lax.ppermute(part, "bin", [(0, 1), (1, 0)]) for part in sent_right], axis=0
     )
     own_right = lax.optimization_barrier(right_of(core * half_peers, 0, right_local))
     grad_right = (own_right + got_right).astype(jnp.bfloat16)

time: 120 us -> 121 us (level)
  transfers between devices with their start and end apart: 8 -> 8, of which waited for: 2 -> 3; matrix products, arithmetic and copies ran while one was open for 30% -> 29% of each run, Pallas kernels for 0% -> 0%
where the time goes in v17:
time: 121 us; the launch traced here: 120 us
  waiting for transfers between devices  65.7 us (54%)
  local copies, waits for them, and re-layouts  20.8 us (17%)
  matrix products  13.6 us (11%)
  starting transfers between devices  13 us (11%)
  other arithmetic  6.03 us (5%)
    all_to_all x1, waiting for transfers between devices, on_device(): mixed_got = lax.all_to_all(mixed_sent, 'blk', 0, 0, tiled=True)  33.7 us
    all_to_all x1, waiting for transfers between devices, on_device(): back_got = lax.all_to_all(back_sent, 'blk', 0, 0, tiled=True)  31.8 us
    unnamed x11, local copies, waits for them, and re-layouts  11.4 us
    all_to_all x1, starting transfers between devices, on_device(): back_got = lax.all_to_all(back_sent, 'blk', 0, 0, tiled=True)  6.83 us
    all_to_all x1, starting transfers between devices, on_device(): mixed_got = lax.all_to_all(mixed_sent, 'blk', 0, 0, tiled=True)  4.34 us
    dot_general x1, matrix products, on_device(): jnp.einsum('rki,kjr->kij', partner_part, partner_back, preferred_element_...  3.72 us
    select_n x2, other arithmetic, swap_halves(): first = jnp.where(core == 0, local, other)  2.85 us
    dot_general x3, matrix products, right_of(): jnp.einsum('jkr,rjm->jkm', blocks, rows, preferred_element_type=jnp.float32)  2.69 us
  transfers between devices with their start and end apart: 8, of which 3 were waited for; matrix products, arithmetic and copies ran while one was open for 29% of the time, Pallas kernels for 0%

profile of v17, /device:TPU:0, one launch (start us, length us, event | category | flops | bytes accessed | tf_op | source)
XLA Modules:
  0.0 120.0 jit_solution(2010212744526778591)
XLA Ops:
  0.6 0.5 collective-permute-start.1
  1.1 2.6 %convolution_convert_fusion = bf16[256,4096]{0,1:T(8,128)(2,1)S(1)} fusion(bf16[256,4096]{1,0:T(8,128)(2,1)} %param.6), kind=kOutput, calls=%fused_computation | convolution fusion | flops 537985024 | bytes 4194304 | tf_op jit(solution)/shard_map/rc,rs->cs/dot_general | solution.py:28
  3.8 0.1 broadcast_select_fusion.3
  3.9 0.7 convert_bitcast_fusion
  4.6 1.5 %copy.32 = bf16[8,8,64,256]{3,1,2,0:T(8,128)(2,1)} copy(bf16[8,8,64,256]{3,1,0,2:T(8,128)(2,1)S(1)} %convert_bitcast_fusion) | data formatting | bytes 4194304 | tf_op jit(solution)/shard_map/reshape | solution.py:36
  6.0 6.8 %all-to-all-start = ((bf16[8,8,64,256]{3,1,2,0:T(8,128)(2,1)}), bf16[8,8,64,256]{3,1,2,0:T(8,128)(2,1)S(1)}, u32[]{:S(2)}, u32[]{:S(2)}) async-start(bf16[8,8,64,256]{3,1,2,0:T(8,128)(2,1)} %copy.32), calls=%async_computation | async-start | bytes 4194304 | tf_op jit(solution)/shard_map/all_to_all | solution.py:37
  12.8 3.9 %copy.28 = bf16[8,256,512]{1,2,0:T(8,128)(2,1)} copy(bf16[8,256,512]{2,1,0:T(8,128)(2,1)} %param.7) | data formatting | bytes 4194304 | tf_op args[2]
  16.8 0.2 collective-permute-start
  17.0 4.1 %copy.26 = bf16[256,4096]{0,1:T(8,128)(2,1)} copy(bf16[256,4096]{1,0:T(8,128)(2,1)} %param.5) | data formatting | bytes 4194304 | tf_op args[0]
  21.1 0.1 fusion.23
  21.1 2.1 %broadcast_multiply_fusion = bf16[256,8,512]{0,2,1:T(8,128)(2,1)S(1)} fusion(bf16[256,8,512]{0,2,1:T(8,128)(2,1)} %bitcast.43, bf16[8,512]{1,0:T(8,128)(2,1)S(1)} %fusion.23), kind=kLoop, calls=%fused_computation.25 | loop fusion | flops 1048576 | bytes 4202496 | tf_op jit(solution)/shard_map/mul | solution.py:40
  23.3 0.1 copy-done.1
  23.4 2.8 %broadcast_select_fusion.1 = (bf16[8,256,512]{1,2,0:T(8,128)(2,1)S(1)}, bf16[8,256,512]{1,2,0:T(8,128)(2,1)S(1)}) fusion(bf16[8,256,512]{1,2,0:T(8,128)(2,1)S(1)} %copy-done.1, bf16[8,256,512]{1,2,0:T(8,128)(2,1)} %collective-permute-done, pred[]{:T(512)S(6)} %eq.4), kind=kLoop, calls=%fused_computation.9 | loop fusion | flops 2097152 | bytes 8388609 | tf_op jit(solution)/shard_map/jit(_where)/select_n | solution.py:11
  26.1 1.3 %convert_bitcast_fusion.1 = bf16[512,8,256]{2,0,1:T(8,128)(2,1)S(1)} fusion(bf16[256,8,512]{0,2,1:T(8,128)(2,1)S(1)} %broadcast_multiply_fusion, bf16[8,256,512]{1,2,0:T(8,128)(2,1)S(1)} %get-tuple-element.17, bf16[8,256,512]{1,2,0:T(8,128)(2,1)S(1)} %get-tuple-element.16), kind=kOutput, calls=%fused_computation.7 | convolution fusion | flops 1083179008 | bytes 8388608 | tf_op jit(solution)/shard_map/rki,kij->jkr/dot_general | solution.py:42
  27.4 2.5 %copy.31 = bf16[512,8,256]{2,1,0:T(8,128)(2,1)} copy(bf16[512,8,256]{2,0,1:T(8,128)(2,1)S(1)} %convert_bitcast_fusion.1) | data formatting | bytes 4194304 | tf_op jit(solution)/shard_map/convert_element_type | solution.py:44
  30.0 31.8 %all-to-all-done = bf16[8,8,64,256]{3,1,2,0:T(8,128)(2,1)S(1)} async-done(((bf16[8,8,64,256]{3,1,2,0:T(8,128)(2,1)}), bf16[8,8,64,256]{3,1,2,0:T(8,128)(2,1)S(1)}, u32[]{:S(2)}, u32[]{:S(2)}) %all-to-all-start) | async-done | bytes 2097184 | tf_op jit(solution)/shard_map/all_to_all | solution.py:37
  61.7 4.3 %all-to-all-start.1 = ((bf16[8,64,8,256]{3,2,1,0:T(8,128)(2,1)}), bf16[8,64,8,256]{3,2,1,0:T(8,128)(2,1)}, u32[]{:S(2)}, u32[]{:S(2)}) async-start(bf16[8,64,8,256]{3,2,1,0:T(8,128)(2,1)} %bitcast.2), calls=%async_computation.1 | async-start | bytes 4194304 | tf_op jit(solution)/shard_map/all_to_all | solution.py:57
  66.1 1.8 %copy.33 = bf16[8,8,64,256]{3,2,1,0:T(8,128)(2,1)} copy(bf16[8,8,64,256]{3,0,2,1:T(8,128)(2,1)S(1)} %bitcast.41) | data formatting | bytes 4194304 | tf_op jit(solution)/shard_map/transpose | solution.py:54
  67.9 2.4 %constant_dynamic-slice_fusion = bf16[256,8,256]{0,2,1:T(8,128)(2,1)} fusion(bf16[256,8,512]{0,2,1:T(8,128)(2,1)} %copy-done, s32[]{:T(128)S(6)} %select_n.44), kind=kLoop, calls=%fused_computation.37 | loop fusion | bytes 2097156 | tf_op jit(solution)/shard_map/dynamic_slice | solution.py:52
  70.2 0.5 collective-permute-start.2
  70.7 3.3 %copy.35 = bf16[256,4096]{0,1:T(8,128)(2,1)S(1)} copy(bf16[256,4096]{1,0:T(8,128)(2,1)} %param.6) | data formatting | bytes 4194304 | tf_op args[1]
  74.0 2.7 %fusion.17 = f32[8,256,512]{2,1,0:T(8,128)S(1)} fusion(bf16[8,512,256]{2,1,0:T(8,128)(2,1)} %bitcast.8, bf16[256,8,512]{0,2,1:T(8,128)(2,1)} %copy-done, s32[]{:T(128)S(6)} %select_n.37), kind=kOutput, calls=%fused_computation.23 | convolution fusion | flops 536870912 | bytes 7340036 | tf_op jit(solution)/shard_map/rki,kjr->kij/dot_general | solution.py:59
  76.7 3.7 %add_convert_fusion = bf16[8,256,512]{2,1,0:T(8,128)(2,1)} fusion(f32[8,256,512]{2,1,0:T(8,128)S(1)} %fusion.17, bf16[256,8,256]{0,2,1:T(8,128)(2,1)S(1)} %collective-permute-done.2, bf16[8,512,256]{2,1,0:T(8,128)(2,1)} %collective-permute-done.3), kind=kOutput, calls=%fused_computation.5 | convolution fusion | flops 538968064 | bytes 9437184 | tf_op jit(solution)/shard_map/rki,kjr->kij/dot_general | solution.py:60
  80.4 33.7 %all-to-all-done.1 = bf16[8,64,8,256]{3,2,1,0:T(8,128)(2,1)} async-done(((bf16[8,64,8,256]{3,2,1,0:T(8,128)(2,1)}), bf16[8,64,8,256]{3,2,1,0:T(8,128)(2,1)}, u32[]{:S(2)}, u32[]{:S(2)}) %all-to-all-start.1) | async-done | bytes 2097184 | tf_op jit(solution)/shard_map/all_to_all | solution.py:57
  114.1 1.3 %dynamic-slice_bitcast_fusion.1 = (bf16[32,4,8,256]{3,2,0,1:T(8,128)(2,1)S(1)}, bf16[32,4,8,256]{3,2,0,1:T(8,128)(2,1)S(1)}) fusion(bf16[8,64,8,256]{3,2,1,0:T(8,128)(2,1)} %all-to-all-done.1, s32[]{:T(128)S(6)} %select_n.45, s32[]{:T(128)S(6)} %add.25), kind=kLoop, calls=%fused_computation.26 | loop fusion | bytes 2097160 | tf_op jit(solution)/shard_map/transpose | solution.py:69
  115.4 0.4 fusion.8
  115.8 0.4 fusion.6
  116.2 0.1 collective-permute-start.5
  116.3 0.5 collective-permute-start.4
  116.8 1.9 %fusion.14 = f32[64,32,64]{2,1,0:T(8,128)S(1)} fusion(bf16[256,64,64]{0,2,1:T(8,128)(2,1)S(1)} %bitcast.40, bf16[8,64,8,256]{3,2,1,0:T(8,128)(2,1)} %all-to-all-done.1, s32[]{:T(128)S(6)} %select_n.46), kind=kOutput, calls=%fused_computation.19 | convolution fusion | flops 67108864 | bytes 3670020 | tf_op jit(solution)/shard_map/jkr,rjm->jkm/dot_general | solution.py:71
  118.7 0.2 collective-permute-done.4
  118.9 1.0 fusion.13
  (13 shorter events, 0.0 us)
Async XLA Ops:
  0.6 3.1 %collective-permute-start.1 = (bf16[64,32,64]{2,1,0:T(8,128)(2,1)}, bf16[64,32,64]{2,1,0:T(8,128)(2,1)S(1)}, u32[]{:S(2)}, u32[]{:S(2)}) collective-permute-start(bf16[64,32,64]{2,1,0:T(8,128)(2,1)} %param.8), channel_id=1, source_target_pairs={{0,1},{1,0},{2,3},{3,2},{4,5},{5,4},{6,7},{7,6},{8,9},{9,8},{10,11... | collective-permute-start | bytes 786440 | tf_op jit(solution)/shard_map/ppermute | solution.py:9
  1.1 2.6 %copy-start.2 = (bf16[64,32,64]{2,1,0:T(8,128)(2,1)S(1)}, bf16[64,32,64]{2,1,0:T(8,128)(2,1)}, u32[]{:S(2)}) copy-start(bf16[64,32,64]{2,1,0:T(8,128)(2,1)} %param.8) | copy-start | bytes 786436
  6.0 55.7 %all-to-all-start = ((bf16[8,8,64,256]{3,1,2,0:T(8,128)(2,1)}), bf16[8,8,64,256]{3,1,2,0:T(8,128)(2,1)S(1)}, u32[]{:S(2)}, u32[]{:S(2)}) async-start(bf16[8,8,64,256]{3,1,2,0:T(8,128)(2,1)} %copy.32), calls=%async_computation | async-start | bytes 4194304 | tf_op jit(solution)/shard_map/all_to_all | solution.py:37
  16.8 4.3 %copy-start.3 = (s32[8]{0:T(128)S(1)}, s32[8]{0:T(128)}, u32[]{:S(2)}) copy-start(s32[8]{0:T(128)} %param.9) | copy-start | bytes 100
  16.8 6.5 %collective-permute-start = (bf16[8,256,512]{1,2,0:T(8,128)(2,1)}, bf16[8,256,512]{1,2,0:T(8,128)(2,1)}, u32[]{:S(2)}, u32[]{:S(2)}) collective-permute-start(bf16[8,256,512]{1,2,0:T(8,128)(2,1)} %copy.28), channel_id=1, source_target_pairs={{0,1},{1,0},{2,3},{3,2},{4,5},{5,4},{6,7},{7,6},{8,9},{9,8},{10,11... | collective-permute-start | bytes 6291464 | tf_op jit(solution)/shard_map/ppermute | solution.py:9
  21.1 2.2 %copy-start.1 = (bf16[8,256,512]{1,2,0:T(8,128)(2,1)S(1)}, bf16[8,256,512]{1,2,0:T(8,128)(2,1)}, u32[]{:S(2)}) copy-start(bf16[8,256,512]{1,2,0:T(8,128)(2,1)} %copy.28) | copy-start | bytes 6291460
  23.2 2.9 %copy-start = (bf16[256,8,512]{0,2,1:T(8,128)(2,1)}, bf16[256,8,512]{0,2,1:T(8,128)(2,1)S(1)}, u32[]{:S(2)}) copy-start(bf16[256,8,512]{0,2,1:T(8,128)(2,1)S(1)} %broadcast_multiply_fusion) | copy-start | bytes 6291460
  61.7 52.4 %all-to-all-start.1 = ((bf16[8,64,8,256]{3,2,1,0:T(8,128)(2,1)}), bf16[8,64,8,256]{3,2,1,0:T(8,128)(2,1)}, u32[]{:S(2)}, u32[]{:S(2)}) async-start(bf16[8,64,8,256]{3,2,1,0:T(8,128)(2,1)} %bitcast.2), calls=%async_computation.1 | async-start | bytes 4194304 | tf_op jit(solution)/shard_map/all_to_all | solution.py:57
  67.9 8.8 %collective-permute-start.3 = (bf16[8,512,256]{2,1,0:T(8,128)(2,1)}, bf16[8,512,256]{2,1,0:T(8,128)(2,1)}, u32[]{:S(2)}, u32[]{:S(2)}) collective-permute-start(bf16[8,512,256]{2,1,0:T(8,128)(2,1)} %bitcast.8), channel_id=1, source_target_pairs={{0,1},{1,0},{2,3},{3,2},{4,5},{5,4},{6,7},{7,6},{8,9},{9,8},{10,11... | collective-permute-start | bytes 6291464 | tf_op jit(solution)/shard_map/ppermute | solution.py:55
  70.2 6.5 %collective-permute-start.2 = (bf16[256,8,256]{0,2,1:T(8,128)(2,1)}, bf16[256,8,256]{0,2,1:T(8,128)(2,1)S(1)}, u32[]{:S(2)}, u32[]{:S(2)}) collective-permute-start(bf16[256,8,256]{0,2,1:T(8,128)(2,1)} %constant_dynamic-slice_fusion), channel_id=1, source_target_pairs={{0,1},{1,0},{2,3},{3,2},{4,5},{5,4},{6,7},{7,6},{8,9},{9,8},{10,11... | collective-permute-start | bytes 3145736 | tf_op jit(solution)/shard_map/ppermute | solution.py:53
  116.2 2.5 %collective-permute-start.5 = (f32[32,32,64]{2,1,0:T(8,128)S(1)}, f32[32,32,64]{2,1,0:T(8,128)S(1)}, u32[]{:S(2)}, u32[]{:S(2)}) collective-permute-start(f32[32,32,64]{2,1,0:T(8,128)S(1)} %fusion.6), channel_id=1, source_target_pairs={{0,1},{1,0},{2,3},{3,2},{4,5},{5,4},{6,7},{7,6},{8,9},{9,8},{10,11... | collective-permute-start | bytes 786440 | tf_op jit(solution)/shard_map/ppermute | solution.py:77
  116.3 2.6 %collective-permute-start.4 = (f32[32,32,64]{2,1,0:T(8,128)S(1)}, f32[32,32,64]{2,1,0:T(8,128)S(1)}, u32[]{:S(2)}, u32[]{:S(2)}) collective-permute-start(f32[32,32,64]{2,1,0:T(8,128)S(1)} %fusion.8), channel_id=1, source_target_pairs={{0,1},{1,0},{2,3},{3,2},{4,5},{5,4},{6,7},{7,6},{8,9},{9,8},{10,11... | collective-permute-start | bytes 786440 | tf_op jit(solution)/shard_map/ppermute | solution.py:77

commit v18 on v17

--- a/solution.py
+++ b/solution.py
@@ -2,7 +2,31 @@
 import jax.numpy as jnp
 from jax import lax
 from jax.sharding import PartitionSpec as P
+from jax.experimental import pallas as pl
+from jax.experimental.pallas import tpu as pltpu
 from jax.experimental.layout import Layout, with_layout_constraint
+
+
+def _transpose_kernel(x_ref, o_ref):
+    width = 128
+
+    def body(step, carry):
+        start = pl.multiple_of(step * width, width)
+        o_ref[pl.ds(start, width), :] = x_ref[:, pl.ds(start, width)].T
+        return carry
+
+    lax.fori_loop(0, x_ref.shape[1] // width, body, 0)
+
+
+def transposed(x):
+    rows, cols = x.shape
+    return pl.pallas_call(
+        _transpose_kernel,
+        out_shape=jax.ShapeDtypeStruct((cols, rows), x.dtype),
+        in_specs=[pl.BlockSpec(memory_space=pltpu.VMEM)],
+        out_specs=pl.BlockSpec(memory_space=pltpu.VMEM),
+        cost_estimate=pl.CostEstimate(flops=0, bytes_accessed=2 * x.size * x.dtype.itemsize, transcendentals=0),
+    )(x)
 
 
 def swap_halves(local, axis):
@@ -24,12 +48,7 @@
 
     upstream = cotangent.reshape(row_count, right_local, order_right)
     right_full = swap_halves(right_factor, 1)
-    eye = jnp.eye(row_count, dtype=jnp.bfloat16)
-    upstream_t = jnp.einsum(
-        "rc,rs->cs", cotangent, eye, preferred_element_type=jnp.float32
-    ).astype(jnp.bfloat16)
-    upstream_t = with_layout_constraint(upstream_t, Layout((0, 1)))
-    upstream_t = upstream_t.reshape(right_local, order_right, row_count)
+    upstream_t = transposed(cotangent).reshape(right_local, order_right, row_count)
     back_grad = jnp.einsum(
         "jmr,jkm->kjr", upstream_t, right_full, preferred_element_type=jnp.float32
     ).astype(jnp.bfloat16)

time: 121 us -> 125 us (1.033)
  Pallas kernels: 0 us -> 5.31 us
  matrix products: 13.6 us -> 11 us
  local copies, waits for them, and re-layouts: 20.8 us -> 22.3 us
    pallas_call x0 -> x1, Pallas kernels: none -> 5.31 us  [transposed(): pl.pallas_call(_transpose_kernel, out_shape=jax.ShapeDtypeStruct((cols, r...]
    dot_general x1 -> x0, matrix products: 2.61 us -> none  [on_device(): jnp.einsum('rc,rs->cs', cotangent, eye, preferred_element_type=jnp.float32)]
    unnamed x11 -> x13, local copies, waits for them, and re-layouts: 11.4 us -> 12.9 us
  transfers between devices with their start and end apart: 8 -> 8, of which waited for: 3 -> 3; matrix products, arithmetic and copies ran while one was open for 29% -> 26% of each run, Pallas kernels for 0% -> 4%
where the time goes in v18:
time: 125 us; the launch traced here: 124 us
  waiting for transfers between devices  65.8 us (53%)
  local copies, waits for them, and re-layouts  22.3 us (18%)
  starting transfers between devices  13 us (10%)
  matrix products  11 us (9%)
  other arithmetic  6.03 us (5%)
  Pallas kernels  5.31 us (4%)
    all_to_all x1, waiting for transfers between devices, on_device(): mixed_got = lax.all_to_all(mixed_sent, 'blk', 0, 0, tiled=True)  33.7 us
    all_to_all x1, waiting for transfers between devices, on_device(): back_got = lax.all_to_all(back_sent, 'blk', 0, 0, tiled=True)  31.8 us
    unnamed x13, local copies, waits for them, and re-layouts  12.9 us
    all_to_all x1, starting transfers between devices, on_device(): back_got = lax.all_to_all(back_sent, 'blk', 0, 0, tiled=True)  6.83 us
    pallas_call x1, Pallas kernels, transposed(): pl.pallas_call(_transpose_kernel, out_shape=jax.ShapeDtypeStruct((cols, r...  5.31 us
    all_to_all x1, starting transfers between devices, on_device(): mixed_got = lax.all_to_all(mixed_sent, 'blk', 0, 0, tiled=True)  4.34 us
    dot_general x1, matrix products, on_device(): jnp.einsum('rki,kjr->kij', partner_part, partner_back, preferred_element_...  3.72 us
    select_n x2, other arithmetic, swap_halves(): first = jnp.where(core == 0, local, other)  2.85 us
  transfers between devices with their start and end apart: 8, of which 3 were waited for; matrix products, arithmetic and copies ran while one was open for 26% of the time, Pallas kernels for 4%

profile of v18, /device:TPU:0, one launch (start us, length us, event | category | flops | bytes accessed | tf_op | source)
XLA Modules:
  0.0 124.1 jit_solution(5364652615163029326)
XLA Ops:
  0.6 0.5 collective-permute-start.1
  1.1 5.3 %shard_map.68 = bf16[4096,256]{1,0:T(8,128)(2,1)} custom-call(bf16[256,4096]{1,0:T(8,128)(2,1)} %x_ref.1), custom_call_target="tpu_custom_call" | custom-call | bytes 4194304 | tf_op jit(solution)/shard_map/pallas_call | solution.py:23
  6.5 0.1 broadcast_select_fusion.3
  6.6 1.5 %copy-done = bf16[4096,256]{1,0:T(8,128)(2,1)S(1)} copy-done((bf16[4096,256]{1,0:T(8,128)(2,1)S(1)}, bf16[4096,256]{1,0:T(8,128)(2,1)}, u32[]{:S(2)}) %copy-start) | copy-done | bytes 2097176
  8.1 0.7 convert_bitcast_fusion
  8.7 1.5 %copy.32 = bf16[8,8,64,256]{3,1,2,0:T(8,128)(2,1)} copy(bf16[8,8,64,256]{3,1,0,2:T(8,128)(2,1)S(1)} %convert_bitcast_fusion) | data formatting | bytes 4194304 | tf_op jit(solution)/shard_map/reshape | solution.py:55
  10.2 6.8 %all-to-all-start = ((bf16[8,8,64,256]{3,1,2,0:T(8,128)(2,1)}), bf16[8,8,64,256]{3,1,2,0:T(8,128)(2,1)S(1)}, u32[]{:S(2)}, u32[]{:S(2)}) async-start(bf16[8,8,64,256]{3,1,2,0:T(8,128)(2,1)} %copy.32), calls=%async_computation | async-start | bytes 4194304 | tf_op jit(solution)/shard_map/all_to_all | solution.py:56
  17.0 3.9 %copy.28 = bf16[8,256,512]{1,2,0:T(8,128)(2,1)} copy(bf16[8,256,512]{2,1,0:T(8,128)(2,1)} %param.7) | data formatting | bytes 4194304 | tf_op args[2]
  21.0 0.2 collective-permute-start
  21.2 4.1 %copy.26 = bf16[256,4096]{0,1:T(8,128)(2,1)} copy(bf16[256,4096]{1,0:T(8,128)(2,1)} %param.5) | data formatting | bytes 4194304 | tf_op args[0]
  25.2 0.1 fusion.23
  25.3 2.1 %broadcast_multiply_fusion = bf16[256,8,512]{0,2,1:T(8,128)(2,1)S(1)} fusion(bf16[256,8,512]{0,2,1:T(8,128)(2,1)} %bitcast.40, bf16[8,512]{1,0:T(8,128)(2,1)S(1)} %fusion.23), kind=kLoop, calls=%fused_computation.24 | loop fusion | flops 1048576 | bytes 4202496 | tf_op jit(solution)/shard_map/mul | solution.py:59
  27.4 0.1 copy-done.2
  27.5 2.8 %broadcast_select_fusion.1 = (bf16[8,256,512]{1,2,0:T(8,128)(2,1)S(1)}, bf16[8,256,512]{1,2,0:T(8,128)(2,1)S(1)}) fusion(bf16[8,256,512]{1,2,0:T(8,128)(2,1)S(1)} %copy-done.2, bf16[8,256,512]{1,2,0:T(8,128)(2,1)} %collective-permute-done, pred[]{:T(512)S(6)} %eq.2), kind=kLoop, calls=%fused_computation.8 | loop fusion | flops 2097152 | bytes 8388609 | tf_op jit(solution)/shard_map/jit(_where)/select_n | solution.py:35
  30.3 1.3 %convert_bitcast_fusion.1 = bf16[512,8,256]{2,0,1:T(8,128)(2,1)S(1)} fusion(bf16[256,8,512]{0,2,1:T(8,128)(2,1)S(1)} %broadcast_multiply_fusion, bf16[8,256,512]{1,2,0:T(8,128)(2,1)S(1)} %get-tuple-element.17, bf16[8,256,512]{1,2,0:T(8,128)(2,1)S(1)} %get-tuple-element.16), kind=kOutput, calls=%fused_computation.6 | convolution fusion | flops 1083179008 | bytes 8388608 | tf_op jit(solution)/shard_map/rki,kij->jkr/dot_general | solution.py:61
  31.6 2.5 %copy.31 = bf16[512,8,256]{2,1,0:T(8,128)(2,1)} copy(bf16[512,8,256]{2,0,1:T(8,128)(2,1)S(1)} %convert_bitcast_fusion.1) | data formatting | bytes 4194304 | tf_op jit(solution)/shard_map/convert_element_type | solution.py:63
  34.1 31.8 %all-to-all-done = bf16[8,8,64,256]{3,1,2,0:T(8,128)(2,1)S(1)} async-done(((bf16[8,8,64,256]{3,1,2,0:T(8,128)(2,1)}), bf16[8,8,64,256]{3,1,2,0:T(8,128)(2,1)S(1)}, u32[]{:S(2)}, u32[]{:S(2)}) %all-to-all-start) | async-done | bytes 2097184 | tf_op jit(solution)/shard_map/all_to_all | solution.py:56
  65.9 4.3 %all-to-all-start.1 = ((bf16[8,64,8,256]{3,2,1,0:T(8,128)(2,1)}), bf16[8,64,8,256]{3,2,1,0:T(8,128)(2,1)}, u32[]{:S(2)}, u32[]{:S(2)}) async-start(bf16[8,64,8,256]{3,2,1,0:T(8,128)(2,1)} %bitcast.2), calls=%async_computation.1 | async-start | bytes 4194304 | tf_op jit(solution)/shard_map/all_to_all | solution.py:76
  70.3 1.8 %copy.33 = bf16[8,8,64,256]{3,2,1,0:T(8,128)(2,1)} copy(bf16[8,8,64,256]{3,0,2,1:T(8,128)(2,1)S(1)} %bitcast.38) | data formatting | bytes 4194304 | tf_op jit(solution)/shard_map/transpose | solution.py:73
  72.1 2.3 %constant_dynamic-slice_fusion = bf16[256,8,256]{0,2,1:T(8,128)(2,1)} fusion(bf16[256,8,512]{0,2,1:T(8,128)(2,1)} %copy-done.1, s32[]{:T(128)S(6)} %select_n.44), kind=kLoop, calls=%fused_computation.35 | loop fusion | bytes 2097156 | tf_op jit(solution)/shard_map/dynamic_slice | solution.py:71
  74.4 0.5 collective-permute-start.2
  74.9 3.3 %copy.35 = bf16[256,4096]{0,1:T(8,128)(2,1)S(1)} copy(bf16[256,4096]{1,0:T(8,128)(2,1)} %x_ref.1) | data formatting | bytes 4194304 | tf_op args[1]
  78.2 2.7 %fusion.17 = f32[8,256,512]{2,1,0:T(8,128)S(1)} fusion(bf16[8,512,256]{2,1,0:T(8,128)(2,1)} %bitcast.7, bf16[256,8,512]{0,2,1:T(8,128)(2,1)} %copy-done.1, s32[]{:T(128)S(6)} %select_n.37), kind=kOutput, calls=%fused_computation.22 | convolution fusion | flops 536870912 | bytes 7340036 | tf_op jit(solution)/shard_map/rki,kjr->kij/dot_general | solution.py:78
  80.9 3.7 %add_convert_fusion = bf16[8,256,512]{2,1,0:T(8,128)(2,1)} fusion(f32[8,256,512]{2,1,0:T(8,128)S(1)} %fusion.17, bf16[256,8,256]{0,2,1:T(8,128)(2,1)S(1)} %collective-permute-done.2, bf16[8,512,256]{2,1,0:T(8,128)(2,1)} %collective-permute-done.3), kind=kOutput, calls=%fused_computation.4 | convolution fusion | flops 538968064 | bytes 9437184 | tf_op jit(solution)/shard_map/rki,kjr->kij/dot_general | solution.py:79
  84.6 33.7 %all-to-all-done.1 = bf16[8,64,8,256]{3,2,1,0:T(8,128)(2,1)} async-done(((bf16[8,64,8,256]{3,2,1,0:T(8,128)(2,1)}), bf16[8,64,8,256]{3,2,1,0:T(8,128)(2,1)}, u32[]{:S(2)}, u32[]{:S(2)}) %all-to-all-start.1) | async-done | bytes 2097184 | tf_op jit(solution)/shard_map/all_to_all | solution.py:76
  118.3 1.3 %dynamic-slice_bitcast_fusion.1 = (bf16[32,4,8,256]{3,2,0,1:T(8,128)(2,1)S(1)}, bf16[32,4,8,256]{3,2,0,1:T(8,128)(2,1)S(1)}) fusion(bf16[8,64,8,256]{3,2,1,0:T(8,128)(2,1)} %all-to-all-done.1, s32[]{:T(128)S(6)} %select_n.45, s32[]{:T(128)S(6)} %add.25), kind=kLoop, calls=%fused_computation.25 | loop fusion | bytes 2097160 | tf_op jit(solution)/shard_map/transpose | solution.py:88
  119.6 0.4 fusion.8
  120.0 0.4 fusion.6
  120.5 0.5 collective-permute-start.4
  121.0 1.9 %fusion.14 = f32[64,32,64]{2,1,0:T(8,128)S(1)} fusion(bf16[256,64,64]{0,2,1:T(8,128)(2,1)S(1)} %bitcast.37, bf16[8,64,8,256]{3,2,1,0:T(8,128)(2,1)} %all-to-all-done.1, s32[]{:T(128)S(6)} %select_n.46), kind=kOutput, calls=%fused_computation.18 | convolution fusion | flops 67108864 | bytes 3670020 | tf_op jit(solution)/shard_map/jkr,rjm->jkm/dot_general | solution.py:90
  122.9 0.2 collective-permute-done.4
  123.1 1.0 fusion.13
  (15 shorter events, 0.1 us)
Async XLA Ops:
  0.6 5.8 %collective-permute-start.1 = (bf16[64,32,64]{2,1,0:T(8,128)(2,1)}, bf16[64,32,64]{2,1,0:T(8,128)(2,1)S(1)}, u32[]{:S(2)}, u32[]{:S(2)}) collective-permute-start(bf16[64,32,64]{2,1,0:T(8,128)(2,1)} %param.8), channel_id=1, source_target_pairs={{0,1},{1,0},{2,3},{3,2},{4,5},{5,4},{6,7},{7,6},{8,9},{9,8},{10,11... | collective-permute-start | bytes 786440 | tf_op jit(solution)/shard_map/ppermute | solution.py:33
  1.1 5.3 %copy-start.3 = (bf16[64,32,64]{2,1,0:T(8,128)(2,1)S(1)}, bf16[64,32,64]{2,1,0:T(8,128)(2,1)}, u32[]{:S(2)}) copy-start(bf16[64,32,64]{2,1,0:T(8,128)(2,1)} %param.8) | copy-start | bytes 786436
  6.5 1.6 %copy-start = (bf16[4096,256]{1,0:T(8,128)(2,1)S(1)}, bf16[4096,256]{1,0:T(8,128)(2,1)}, u32[]{:S(2)}) copy-start(bf16[4096,256]{1,0:T(8,128)(2,1)} %shard_map.68) | copy-start | bytes 6291460
  10.2 55.7 %all-to-all-start = ((bf16[8,8,64,256]{3,1,2,0:T(8,128)(2,1)}), bf16[8,8,64,256]{3,1,2,0:T(8,128)(2,1)S(1)}, u32[]{:S(2)}, u32[]{:S(2)}) async-start(bf16[8,8,64,256]{3,1,2,0:T(8,128)(2,1)} %copy.32), calls=%async_computation | async-start | bytes 4194304 | tf_op jit(solution)/shard_map/all_to_all | solution.py:56
  21.0 4.3 %copy-start.4 = (s32[8]{0:T(128)S(1)}, s32[8]{0:T(128)}, u32[]{:S(2)}) copy-start(s32[8]{0:T(128)} %param.9) | copy-start | bytes 100
  21.0 6.5 %collective-permute-start = (bf16[8,256,512]{1,2,0:T(8,128)(2,1)}, bf16[8,256,512]{1,2,0:T(8,128)(2,1)}, u32[]{:S(2)}, u32[]{:S(2)}) collective-permute-start(bf16[8,256,512]{1,2,0:T(8,128)(2,1)} %copy.28), channel_id=1, source_target_pairs={{0,1},{1,0},{2,3},{3,2},{4,5},{5,4},{6,7},{7,6},{8,9},{9,8},{10,11... | collective-permute-start | bytes 6291464 | tf_op jit(solution)/shard_map/ppermute | solution.py:33
  25.3 2.2 %copy-start.2 = (bf16[8,256,512]{1,2,0:T(8,128)(2,1)S(1)}, bf16[8,256,512]{1,2,0:T(8,128)(2,1)}, u32[]{:S(2)}) copy-start(bf16[8,256,512]{1,2,0:T(8,128)(2,1)} %copy.28) | copy-start | bytes 6291460
  27.4 2.9 %copy-start.1 = (bf16[256,8,512]{0,2,1:T(8,128)(2,1)}, bf16[256,8,512]{0,2,1:T(8,128)(2,1)S(1)}, u32[]{:S(2)}) copy-start(bf16[256,8,512]{0,2,1:T(8,128)(2,1)S(1)} %broadcast_multiply_fusion) | copy-start | bytes 6291460
  65.9 52.4 %all-to-all-start.1 = ((bf16[8,64,8,256]{3,2,1,0:T(8,128)(2,1)}), bf16[8,64,8,256]{3,2,1,0:T(8,128)(2,1)}, u32[]{:S(2)}, u32[]{:S(2)}) async-start(bf16[8,64,8,256]{3,2,1,0:T(8,128)(2,1)} %bitcast.2), calls=%async_computation.1 | async-start | bytes 4194304 | tf_op jit(solution)/shard_map/all_to_all | solution.py:76
  72.1 8.8 %collective-permute-start.3 = (bf16[8,512,256]{2,1,0:T(8,128)(2,1)}, bf16[8,512,256]{2,1,0:T(8,128)(2,1)}, u32[]{:S(2)}, u32[]{:S(2)}) collective-permute-start(bf16[8,512,256]{2,1,0:T(8,128)(2,1)} %bitcast.7), channel_id=1, source_target_pairs={{0,1},{1,0},{2,3},{3,2},{4,5},{5,4},{6,7},{7,6},{8,9},{9,8},{10,11... | collective-permute-start | bytes 6291464 | tf_op jit(solution)/shard_map/ppermute | solution.py:74
  74.4 6.5 %collective-permute-start.2 = (bf16[256,8,256]{0,2,1:T(8,128)(2,1)}, bf16[256,8,256]{0,2,1:T(8,128)(2,1)S(1)}, u32[]{:S(2)}, u32[]{:S(2)}) collective-permute-start(bf16[256,8,256]{0,2,1:T(8,128)(2,1)} %constant_dynamic-slice_fusion), channel_id=1, source_target_pairs={{0,1},{1,0},{2,3},{3,2},{4,5},{5,4},{6,7},{7,6},{8,9},{9,8},{10,11... | collective-permute-start | bytes 3145736 | tf_op jit(solution)/shard_map/ppermute | solution.py:72
  120.4 2.5 %collective-permute-start.5 = (f32[32,32,64]{2,1,0:T(8,128)S(1)}, f32[32,32,64]{2,1,0:T(8,128)S(1)}, u32[]{:S(2)}, u32[]{:S(2)}) collective-permute-start(f32[32,32,64]{2,1,0:T(8,128)S(1)} %fusion.6), channel_id=1, source_target_pairs={{0,1},{1,0},{2,3},{3,2},{4,5},{5,4},{6,7},{7,6},{8,9},{9,8},{10,11... | collective-permute-start | bytes 786440 | tf_op jit(solution)/shard_map/ppermute | solution.py:96
  120.5 2.6 %collective-permute-start.4 = (f32[32,32,64]{2,1,0:T(8,128)S(1)}, f32[32,32,64]{2,1,0:T(8,128)S(1)}, u32[]{:S(2)}, u32[]{:S(2)}) collective-permute-start(f32[32,32,64]{2,1,0:T(8,128)S(1)} %fusion.8), channel_id=1, source_target_pairs={{0,1},{1,0},{2,3},{3,2},{4,5},{5,4},{6,7},{7,6},{8,9},{9,8},{10,11... | collective-permute-start | bytes 786440 | tf_op jit(solution)/shard_map/ppermute | solution.py:96

commit v19 on v15

--- a/solution.py
+++ b/solution.py
@@ -70,11 +70,11 @@
         rows = upstream[:, j_start:j_start + j_count]
         return jnp.einsum("jkr,rjm->jkm", blocks, rows, preferred_element_type=jnp.float32)
 
-    half_j = right_local // 2
+    half_j = right_local // 4 if right_local % 4 == 0 else right_local // 2
     got_right = jnp.concatenate(
         [
             lax.ppermute(right_of((1 - core) * half_peers, j0, half_j), "bin", [(0, 1), (1, 0)])
-            for j0 in (0, half_j)
+            for j0 in range(0, right_local, half_j)
         ],
         axis=0,
     )

time: 120 us -> 121 us (level)
    dot_general x3 -> x5, matrix products: 2.69 us -> 2.93 us  [right_of(): jnp.einsum('jkr,rjm->jkm', blocks, rows, preferred_element_type=jnp.float32)]
  transfers between devices with their start and end apart: 8 -> 10, of which waited for: 2 -> 2; matrix products, arithmetic and copies ran while one was open for 30% -> 30% of each run, Pallas kernels for 0% -> 0%
where the time goes in v19:
time: 121 us
  waiting for transfers between devices  65.5 us (54%)
  local copies, waits for them, and re-layouts  20.8 us (17%)
  matrix products  13.9 us (11%)
  starting transfers between devices  13.7 us (11%)
  other arithmetic  6.03 us (5%)
    all_to_all x1, waiting for transfers between devices, on_device(): mixed_got = lax.all_to_all(mixed_sent, 'blk', 0, 0, tiled=True)  33.7 us
    all_to_all x1, waiting for transfers between devices, on_device(): back_got = lax.all_to_all(back_sent, 'blk', 0, 0, tiled=True)  31.8 us
    unnamed x11, local copies, waits for them, and re-layouts  11.4 us
    all_to_all x1, starting transfers between devices, on_device(): back_got = lax.all_to_all(back_sent, 'blk', 0, 0, tiled=True)  6.82 us
    all_to_all x1, starting transfers between devices, on_device(): mixed_got = lax.all_to_all(mixed_sent, 'blk', 0, 0, tiled=True)  4.35 us
    dot_general x1, matrix products, on_device(): jnp.einsum('rki,kjr->kij', partner_part, partner_back, preferred_element_...  3.72 us
    dot_general x5, matrix products, right_of(): jnp.einsum('jkr,rjm->jkm', blocks, rows, preferred_element_type=jnp.float32)  2.93 us
    select_n x2, other arithmetic, swap_halves(): first = jnp.where(core == 0, local, other)  2.85 us
  transfers between devices with their start and end apart: 10, of which 2 were waited for; matrix products, arithmetic and copies ran while one was open for 30% of the time, Pallas kernels for 0%

profile of v19, /device:TPU:0, one launch (start us, length us, event | category | flops | bytes accessed | tf_op | source)
XLA Modules:
  0.0 120.7 jit_solution(6027673148471773277)
XLA Ops:
  0.6 0.5 collective-permute-start.1
  1.1 2.6 %convolution_convert_fusion = bf16[256,4096]{0,1:T(8,128)(2,1)S(1)} fusion(bf16[256,4096]{1,0:T(8,128)(2,1)} %param.6), kind=kOutput, calls=%fused_computation | convolution fusion | flops 537985024 | bytes 4194304 | tf_op jit(solution)/shard_map/rc,rs->cs/dot_general | solution.py:28
  3.9 0.7 convert_bitcast_fusion
  4.6 1.5 %copy.34 = bf16[8,8,64,256]{3,1,2,0:T(8,128)(2,1)} copy(bf16[8,8,64,256]{3,1,0,2:T(8,128)(2,1)S(1)} %convert_bitcast_fusion) | data formatting | bytes 4194304 | tf_op jit(solution)/shard_map/reshape | solution.py:36
  6.0 6.8 %all-to-all-start = ((bf16[8,8,64,256]{3,1,2,0:T(8,128)(2,1)}), bf16[8,8,64,256]{3,1,2,0:T(8,128)(2,1)S(1)}, u32[]{:S(2)}, u32[]{:S(2)}) async-start(bf16[8,8,64,256]{3,1,2,0:T(8,128)(2,1)} %copy.34), calls=%async_computation | async-start | bytes 4194304 | tf_op jit(solution)/shard_map/all_to_all | solution.py:37
  12.8 3.9 %copy.30 = bf16[8,256,512]{1,2,0:T(8,128)(2,1)} copy(bf16[8,256,512]{2,1,0:T(8,128)(2,1)} %param.7) | data formatting | bytes 4194304 | tf_op args[2]
  16.8 0.2 collective-permute-start
  17.0 4.1 %copy.28 = bf16[256,4096]{0,1:T(8,128)(2,1)} copy(bf16[256,4096]{1,0:T(8,128)(2,1)} %param.5) | data formatting | bytes 4194304 | tf_op args[0]
  21.1 2.1 %broadcast_multiply_fusion = bf16[256,8,512]{0,2,1:T(8,128)(2,1)S(1)} fusion(bf16[256,8,512]{0,2,1:T(8,128)(2,1)} %bitcast.55, bf16[8,512]{1,0:T(8,128)(2,1)S(1)} %fusion.31), kind=kLoop, calls=%fused_computation.21 | loop fusion | flops 1048576 | bytes 4202496 | tf_op jit(solution)/shard_map/mul | solution.py:40
  23.2 0.1 copy-done.1
  23.3 2.8 %broadcast_select_fusion.1 = (bf16[8,256,512]{1,2,0:T(8,128)(2,1)S(1)}, bf16[8,256,512]{1,2,0:T(8,128)(2,1)S(1)}) fusion(bf16[8,256,512]{1,2,0:T(8,128)(2,1)S(1)} %copy-done.1, bf16[8,256,512]{1,2,0:T(8,128)(2,1)} %collective-permute-done, pred[]{:T(512)S(6)} %eq.4), kind=kLoop, calls=%fused_computation.9 | loop fusion | flops 2097152 | bytes 8388609 | tf_op jit(solution)/shard_map/jit(_where)/select_n | solution.py:11
  26.1 1.3 %convert_bitcast_fusion.1 = bf16[512,8,256]{2,0,1:T(8,128)(2,1)S(1)} fusion(bf16[256,8,512]{0,2,1:T(8,128)(2,1)S(1)} %broadcast_multiply_fusion, bf16[8,256,512]{1,2,0:T(8,128)(2,1)S(1)} %get-tuple-element.11, bf16[8,256,512]{1,2,0:T(8,128)(2,1)S(1)} %get-tuple-element.10), kind=kOutput, calls=%fused_computation.7 | convolution fusion | flops 1083179008 | bytes 8388608 | tf_op jit(solution)/shard_map/rki,kij->jkr/dot_general | solution.py:42
  27.4 2.6 %copy.33 = bf16[512,8,256]{2,1,0:T(8,128)(2,1)} copy(bf16[512,8,256]{2,0,1:T(8,128)(2,1)S(1)} %convert_bitcast_fusion.1) | data formatting | bytes 4194304 | tf_op jit(solution)/shard_map/convert_element_type | solution.py:44
  29.9 31.8 %all-to-all-done = bf16[8,8,64,256]{3,1,2,0:T(8,128)(2,1)S(1)} async-done(((bf16[8,8,64,256]{3,1,2,0:T(8,128)(2,1)}), bf16[8,8,64,256]{3,1,2,0:T(8,128)(2,1)S(1)}, u32[]{:S(2)}, u32[]{:S(2)}) %all-to-all-start) | async-done | bytes 2097184 | tf_op jit(solution)/shard_map/all_to_all | solution.py:37
  61.7 4.4 %all-to-all-start.1 = ((bf16[8,64,8,256]{3,2,1,0:T(8,128)(2,1)}), bf16[8,64,8,256]{3,2,1,0:T(8,128)(2,1)}, u32[]{:S(2)}, u32[]{:S(2)}) async-start(bf16[8,64,8,256]{3,2,1,0:T(8,128)(2,1)} %bitcast.2), calls=%async_computation.1 | async-start | bytes 4194304 | tf_op jit(solution)/shard_map/all_to_all | solution.py:57
  66.1 1.8 %copy.35 = bf16[8,8,64,256]{3,2,1,0:T(8,128)(2,1)} copy(bf16[8,8,64,256]{3,0,2,1:T(8,128)(2,1)S(1)} %bitcast.53) | data formatting | bytes 4194304 | tf_op jit(solution)/shard_map/transpose | solution.py:54
  67.9 2.3 %constant_dynamic-slice_fusion = bf16[256,8,256]{0,2,1:T(8,128)(2,1)} fusion(bf16[256,8,512]{0,2,1:T(8,128)(2,1)} %copy-done, s32[]{:T(128)S(6)} %select_n.46), kind=kLoop, calls=%fused_computation.47 | loop fusion | bytes 2097156 | tf_op jit(solution)/shard_map/dynamic_slice | solution.py:52
  70.2 0.5 collective-permute-start.2
  70.7 3.3 %copy.37 = bf16[256,4096]{0,1:T(8,128)(2,1)S(1)} copy(bf16[256,4096]{1,0:T(8,128)(2,1)} %param.6) | data formatting | bytes 4194304 | tf_op args[1]
  74.0 2.7 %fusion.13 = f32[8,256,512]{2,1,0:T(8,128)S(1)} fusion(bf16[8,512,256]{2,1,0:T(8,128)(2,1)} %bitcast.8, bf16[256,8,512]{0,2,1:T(8,128)(2,1)} %copy-done, s32[]{:T(128)S(6)} %select_n.39), kind=kOutput, calls=%fused_computation.19 | convolution fusion | flops 536870912 | bytes 7340036 | tf_op jit(solution)/shard_map/rki,kjr->kij/dot_general | solution.py:59
  76.7 3.7 %add_convert_fusion = bf16[8,256,512]{2,1,0:T(8,128)(2,1)} fusion(f32[8,256,512]{2,1,0:T(8,128)S(1)} %fusion.13, bf16[256,8,256]{0,2,1:T(8,128)(2,1)S(1)} %collective-permute-done.2, bf16[8,512,256]{2,1,0:T(8,128)(2,1)} %collective-permute-done.3), kind=kOutput, calls=%fused_computation.5 | convolution fusion | flops 538968064 | bytes 9437184 | tf_op jit(solution)/shard_map/rki,kjr->kij/dot_general | solution.py:60
  80.4 33.7 %all-to-all-done.1 = bf16[8,64,8,256]{3,2,1,0:T(8,128)(2,1)} async-done(((bf16[8,64,8,256]{3,2,1,0:T(8,128)(2,1)}), bf16[8,64,8,256]{3,2,1,0:T(8,128)(2,1)}, u32[]{:S(2)}, u32[]{:S(2)}) %all-to-all-start.1) | async-done | bytes 2097184 | tf_op jit(solution)/shard_map/all_to_all | solution.py:57
  114.2 1.3 %dynamic-slice_bitcast_fusion.4 = (bf16[16,4,8,256]{3,2,0,1:T(8,128)(2,1)S(1)}, bf16[16,4,8,256]{3,2,0,1:T(8,128)(2,1)S(1)}, bf16[16,4,8,256]{3,2,0,1:T(8,128)(2,1)S(1)}, bf16[16,4,8,256]{3,2,0,1:T(8,128)(2,1)S(1)}) fusion(bf16[8,64,8,256]{3,2,1,0:T(8,128)(2,1)} %all-to-all-done.1, s32[]{:T(128)S(6)} %select_n.48, s32[]{:T(128)S(6)} %add.28, s32[]{:T(128)S(6)} %add.27, ...), kind=kLoop, calls=%fused_computation.35 | loop fusion | bytes 2097168 | tf_op jit(solution)/shard_map/transpose | solution.py:69
  115.4 0.3 fusion.15
  115.8 0.3 fusion.17
  116.0 0.6 collective-permute-start.6
  116.6 0.3 fusion.19
  116.9 0.1 collective-permute-start.5
  116.9 0.3 fusion.21
  117.2 0.6 collective-permute-start.4
  117.7 1.9 %fusion.10 = f32[64,32,64]{2,1,0:T(8,128)S(1)} fusion(bf16[256,64,64]{0,2,1:T(8,128)(2,1)S(1)} %bitcast.52, bf16[8,64,8,256]{3,2,1,0:T(8,128)(2,1)} %all-to-all-done.1, s32[]{:T(128)S(6)} %select_n.47), kind=kOutput, calls=%fused_computation.15 | convolution fusion | flops 67108864 | bytes 3670020 | tf_op jit(solution)/shard_map/jkr,rjm->jkm/dot_general | solution.py:71
  119.7 1.0 fusion.9
  (19 shorter events, 0.3 us)
Async XLA Ops:
  0.6 3.1 %collective-permute-start.1 = (bf16[64,32,64]{2,1,0:T(8,128)(2,1)}, bf16[64,32,64]{2,1,0:T(8,128)(2,1)S(1)}, u32[]{:S(2)}, u32[]{:S(2)}) collective-permute-start(bf16[64,32,64]{2,1,0:T(8,128)(2,1)} %param.8), channel_id=1, source_target_pairs={{0,1},{1,0},{2,3},{3,2},{4,5},{5,4},{6,7},{7,6},{8,9},{9,8},{10,11... | collective-permute-start | bytes 786440 | tf_op jit(solution)/shard_map/ppermute | solution.py:9
  1.1 2.6 %copy-start.2 = (bf16[64,32,64]{2,1,0:T(8,128)(2,1)S(1)}, bf16[64,32,64]{2,1,0:T(8,128)(2,1)}, u32[]{:S(2)}) copy-start(bf16[64,32,64]{2,1,0:T(8,128)(2,1)} %param.8) | copy-start | bytes 786436
  6.0 55.7 %all-to-all-start = ((bf16[8,8,64,256]{3,1,2,0:T(8,128)(2,1)}), bf16[8,8,64,256]{3,1,2,0:T(8,128)(2,1)S(1)}, u32[]{:S(2)}, u32[]{:S(2)}) async-start(bf16[8,8,64,256]{3,1,2,0:T(8,128)(2,1)} %copy.34), calls=%async_computation | async-start | bytes 4194304 | tf_op jit(solution)/shard_map/all_to_all | solution.py:37
  16.8 4.3 %copy-start.3 = (s32[8]{0:T(128)S(1)}, s32[8]{0:T(128)}, u32[]{:S(2)}) copy-start(s32[8]{0:T(128)} %param.9) | copy-start | bytes 100
  16.8 6.5 %collective-permute-start = (bf16[8,256,512]{1,2,0:T(8,128)(2,1)}, bf16[8,256,512]{1,2,0:T(8,128)(2,1)}, u32[]{:S(2)}, u32[]{:S(2)}) collective-permute-start(bf16[8,256,512]{1,2,0:T(8,128)(2,1)} %copy.30), channel_id=1, source_target_pairs={{0,1},{1,0},{2,3},{3,2},{4,5},{5,4},{6,7},{7,6},{8,9},{9,8},{10,11... | collective-permute-start | bytes 6291464 | tf_op jit(solution)/shard_map/ppermute | solution.py:9
  21.1 2.2 %copy-start.1 = (bf16[8,256,512]{1,2,0:T(8,128)(2,1)S(1)}, bf16[8,256,512]{1,2,0:T(8,128)(2,1)}, u32[]{:S(2)}) copy-start(bf16[8,256,512]{1,2,0:T(8,128)(2,1)} %copy.30) | copy-start | bytes 6291460
  23.2 2.9 %copy-start = (bf16[256,8,512]{0,2,1:T(8,128)(2,1)}, bf16[256,8,512]{0,2,1:T(8,128)(2,1)S(1)}, u32[]{:S(2)}) copy-start(bf16[256,8,512]{0,2,1:T(8,128)(2,1)S(1)} %broadcast_multiply_fusion) | copy-start | bytes 6291460
  61.7 52.4 %all-to-all-start.1 = ((bf16[8,64,8,256]{3,2,1,0:T(8,128)(2,1)}), bf16[8,64,8,256]{3,2,1,0:T(8,128)(2,1)}, u32[]{:S(2)}, u32[]{:S(2)}) async-start(bf16[8,64,8,256]{3,2,1,0:T(8,128)(2,1)} %bitcast.2), calls=%async_computation.1 | async-start | bytes 4194304 | tf_op jit(solution)/shard_map/all_to_all | solution.py:57
  67.9 8.8 %collective-permute-start.3 = (bf16[8,512,256]{2,1,0:T(8,128)(2,1)}, bf16[8,512,256]{2,1,0:T(8,128)(2,1)}, u32[]{:S(2)}, u32[]{:S(2)}) collective-permute-start(bf16[8,512,256]{2,1,0:T(8,128)(2,1)} %bitcast.8), channel_id=1, source_target_pairs={{0,1},{1,0},{2,3},{3,2},{4,5},{5,4},{6,7},{7,6},{8,9},{9,8},{10,11... | collective-permute-start | bytes 6291464 | tf_op jit(solution)/shard_map/ppermute | solution.py:55
  70.2 6.5 %collective-permute-start.2 = (bf16[256,8,256]{0,2,1:T(8,128)(2,1)}, bf16[256,8,256]{0,2,1:T(8,128)(2,1)S(1)}, u32[]{:S(2)}, u32[]{:S(2)}) collective-permute-start(bf16[256,8,256]{0,2,1:T(8,128)(2,1)} %constant_dynamic-slice_fusion), channel_id=1, source_target_pairs={{0,1},{1,0},{2,3},{3,2},{4,5},{5,4},{6,7},{7,6},{8,9},{9,8},{10,11... | collective-permute-start | bytes 3145736 | tf_op jit(solution)/shard_map/ppermute | solution.py:53
  115.7 3.9 %collective-permute-start.7 = (f32[16,32,64]{2,1,0:T(8,128)S(1)}, f32[16,32,64]{2,1,0:T(8,128)S(1)}, u32[]{:S(2)}, u32[]{:S(2)}) collective-permute-start(f32[16,32,64]{2,1,0:T(8,128)S(1)} %fusion.15), channel_id=1, source_target_pairs={{0,1},{1,0},{2,3},{3,2},{4,5},{5,4},{6,7},{7,6},{8,9},{9,8},{10,11... | collective-permute-start | bytes 393224 | tf_op jit(solution)/shard_map/ppermute | solution.py:76
  116.0 3.6 %collective-permute-start.6 = (f32[16,32,64]{2,1,0:T(8,128)S(1)}, f32[16,32,64]{2,1,0:T(8,128)S(1)}, u32[]{:S(2)}, u32[]{:S(2)}) collective-permute-start(f32[16,32,64]{2,1,0:T(8,128)S(1)} %fusion.17), channel_id=1, source_target_pairs={{0,1},{1,0},{2,3},{3,2},{4,5},{5,4},{6,7},{7,6},{8,9},{9,8},{10,11... | collective-permute-start | bytes 393224 | tf_op jit(solution)/shard_map/ppermute | solution.py:76
  116.9 2.8 %collective-permute-start.5 = (f32[16,32,64]{2,1,0:T(8,128)S(1)}, f32[16,32,64]{2,1,0:T(8,128)S(1)}, u32[]{:S(2)}, u32[]{:S(2)}) collective-permute-start(f32[16,32,64]{2,1,0:T(8,128)S(1)} %fusion.19), channel_id=1, source_target_pairs={{0,1},{1,0},{2,3},{3,2},{4,5},{5,4},{6,7},{7,6},{8,9},{9,8},{10,11... | collective-permute-start | bytes 393224 | tf_op jit(solution)/shard_map/ppermute | solution.py:76
  117.2 2.5 %collective-permute-start.4 = (f32[16,32,64]{2,1,0:T(8,128)S(1)}, f32[16,32,64]{2,1,0:T(8,128)S(1)}, u32[]{:S(2)}, u32[]{:S(2)}) collective-permute-start(f32[16,32,64]{2,1,0:T(8,128)S(1)} %fusion.21), channel_id=1, source_target_pairs={{0,1},{1,0},{2,3},{3,2},{4,5},{5,4},{6,7},{7,6},{8,9},{9,8},{10,11... | collective-permute-start | bytes 393224 | tf_op jit(solution)/shard_map/ppermute | solution.py:76

commit v20 on v17

--- a/solution.py
+++ b/solution.py
@@ -34,6 +34,7 @@
         "jmr,jkm->kjr", upstream_t, right_full, preferred_element_type=jnp.float32
     ).astype(jnp.bfloat16)
     back_sent = back_grad.reshape(peer_count, local_blocks, right_local, row_count)
+    back_sent = with_layout_constraint(back_sent, Layout((0, 1, 2, 3)))
     back_got = lax.all_to_all(back_sent, "blk", 0, 0, tiled=True)
 
     unit_mask = (jnp.arange(block_size)[None, :] < session_units[:, None]).astype(jnp.bfloat16)

time: 121 us -> 122 us (level)
    convert_element_type x0 -> x1, local copies, waits for them, and re-layouts: none -> 2.51 us  [on_device(): back_grad = jnp.einsum('jmr,jkm->kjr', upstream_t, right_full, preferred_...]
    reshape x1 -> x0, local copies, waits for them, and re-layouts: 1.45 us -> none  [on_device(): back_grad.reshape(peer_count, local_blocks, right_local, row_count)]
where the time goes in v20:
time: 122 us; the launch traced here: 121 us
  waiting for transfers between devices  66.1 us (54%)
  local copies, waits for them, and re-layouts  21.5 us (18%)
  matrix products  13.6 us (11%)
  starting transfers between devices  13 us (11%)
  other arithmetic  6.03 us (5%)
    all_to_all x1, waiting for transfers between devices, on_device(): mixed_got = lax.all_to_all(mixed_sent, 'blk', 0, 0, tiled=True)  34 us
    all_to_all x1, waiting for transfers between devices, on_device(): back_got = lax.all_to_all(back_sent, 'blk', 0, 0, tiled=True)  31.8 us
    unnamed x11, local copies, waits for them, and re-layouts  11.4 us
    all_to_all x1, starting transfers between devices, on_device(): back_got = lax.all_to_all(back_sent, 'blk', 0, 0, tiled=True)  6.83 us
    all_to_all x1, starting transfers between devices, on_device(): mixed_got = lax.all_to_all(mixed_sent, 'blk', 0, 0, tiled=True)  4.34 us
    dot_general x1, matrix products, on_device(): jnp.einsum('rki,kjr->kij', partner_part, partner_back, preferred_element_...  3.72 us
    select_n x2, other arithmetic, swap_halves(): first = jnp.where(core == 0, local, other)  2.85 us
    dot_general x3, matrix products, right_of(): jnp.einsum('jkr,rjm->jkm', blocks, rows, preferred_element_type=jnp.float32)  2.7 us
  transfers between devices with their start and end apart: 8, of which 3 were waited for; matrix products, arithmetic and copies ran while one was open for 29% of the time, Pallas kernels for 0%

profile of v20, /device:TPU:0, one launch (start us, length us, event | category | flops | bytes accessed | tf_op | source)
XLA Modules:
  0.0 121.0 jit_solution(2813624476663871775)
XLA Ops:
  0.6 0.5 collective-permute-start.1
  1.1 2.6 %convolution_convert_fusion = bf16[256,4096]{0,1:T(8,128)(2,1)S(1)} fusion(bf16[256,4096]{1,0:T(8,128)(2,1)} %param.6), kind=kOutput, calls=%fused_computation | convolution fusion | flops 537985024 | bytes 4194304 | tf_op jit(solution)/shard_map/rc,rs->cs/dot_general | solution.py:28
  3.8 0.1 broadcast_select_fusion.3
  3.9 0.7 convert_bitcast_fusion
  4.6 2.5 %copy.21 = bf16[64,64,256]{2,1,0:T(8,128)(2,1)} copy(bf16[64,64,256]{2,0,1:T(8,128)(2,1)S(1)} %convert_bitcast_fusion) | data formatting | bytes 4194304 | tf_op jit(solution)/shard_map/convert_element_type | solution.py:35
  7.1 6.8 %all-to-all-start = ((bf16[8,8,64,256]{3,2,1,0:T(8,128)(2,1)}), bf16[8,8,64,256]{3,2,1,0:T(8,128)(2,1)S(1)}, u32[]{:S(2)}, u32[]{:S(2)}) async-start(bf16[8,8,64,256]{3,2,1,0:T(8,128)(2,1)} %bitcast.41), calls=%async_computation | async-start | bytes 4194304 | tf_op jit(solution)/shard_map/all_to_all | solution.py:38
  13.9 3.9 %copy.17 = bf16[8,256,512]{1,2,0:T(8,128)(2,1)} copy(bf16[8,256,512]{2,1,0:T(8,128)(2,1)} %param.7) | data formatting | bytes 4194304 | tf_op args[2]
  17.8 0.2 collective-permute-start
  18.0 4.1 %copy.15 = bf16[256,4096]{0,1:T(8,128)(2,1)} copy(bf16[256,4096]{1,0:T(8,128)(2,1)} %param.5) | data formatting | bytes 4194304 | tf_op args[0]
  22.1 0.1 fusion.23
  22.2 2.1 %broadcast_multiply_fusion = bf16[256,8,512]{0,2,1:T(8,128)(2,1)S(1)} fusion(bf16[256,8,512]{0,2,1:T(8,128)(2,1)} %bitcast.43, bf16[8,512]{1,0:T(8,128)(2,1)S(1)} %fusion.23), kind=kLoop, calls=%fused_computation.25 | loop fusion | flops 1048576 | bytes 4202496 | tf_op jit(solution)/shard_map/mul | solution.py:41
  24.3 0.1 copy-done.1
  24.4 2.8 %broadcast_select_fusion.1 = (bf16[8,256,512]{1,2,0:T(8,128)(2,1)S(1)}, bf16[8,256,512]{1,2,0:T(8,128)(2,1)S(1)}) fusion(bf16[8,256,512]{1,2,0:T(8,128)(2,1)S(1)} %copy-done.1, bf16[8,256,512]{1,2,0:T(8,128)(2,1)} %collective-permute-done, pred[]{:T(512)S(6)} %eq.4), kind=kLoop, calls=%fused_computation.9 | loop fusion | flops 2097152 | bytes 8388609 | tf_op jit(solution)/shard_map/jit(_where)/select_n | solution.py:11
  27.2 1.3 %convert_bitcast_fusion.1 = bf16[512,8,256]{2,0,1:T(8,128)(2,1)S(1)} fusion(bf16[256,8,512]{0,2,1:T(8,128)(2,1)S(1)} %broadcast_multiply_fusion, bf16[8,256,512]{1,2,0:T(8,128)(2,1)S(1)} %get-tuple-element.17, bf16[8,256,512]{1,2,0:T(8,128)(2,1)S(1)} %get-tuple-element.16), kind=kOutput, calls=%fused_computation.7 | convolution fusion | flops 1083179008 | bytes 8388608 | tf_op jit(solution)/shard_map/rki,kij->jkr/dot_general | solution.py:43
  28.5 2.5 %copy.20 = bf16[512,8,256]{2,1,0:T(8,128)(2,1)} copy(bf16[512,8,256]{2,0,1:T(8,128)(2,1)S(1)} %convert_bitcast_fusion.1) | data formatting | bytes 4194304 | tf_op jit(solution)/shard_map/convert_element_type | solution.py:45
  31.0 31.8 %all-to-all-done = bf16[8,8,64,256]{3,2,1,0:T(8,128)(2,1)S(1)} async-done(((bf16[8,8,64,256]{3,2,1,0:T(8,128)(2,1)}), bf16[8,8,64,256]{3,2,1,0:T(8,128)(2,1)S(1)}, u32[]{:S(2)}, u32[]{:S(2)}) %all-to-all-start) | async-done | bytes 2097184 | tf_op jit(solution)/shard_map/all_to_all | solution.py:38
  62.8 4.3 %all-to-all-start.1 = ((bf16[8,64,8,256]{3,2,1,0:T(8,128)(2,1)}), bf16[8,64,8,256]{3,2,1,0:T(8,128)(2,1)}, u32[]{:S(2)}, u32[]{:S(2)}) async-start(bf16[8,64,8,256]{3,2,1,0:T(8,128)(2,1)} %bitcast.2), calls=%async_computation.1 | async-start | bytes 4194304 | tf_op jit(solution)/shard_map/all_to_all | solution.py:58
  67.1 1.5 %copy.22 = bf16[8,8,64,256]{3,2,1,0:T(8,128)(2,1)} copy(bf16[8,8,64,256]{3,2,0,1:T(8,128)(2,1)S(1)} %bitcast.40) | data formatting | bytes 4194304 | tf_op jit(solution)/shard_map/transpose | solution.py:55
  68.6 2.4 %constant_dynamic-slice_fusion = bf16[256,8,256]{0,2,1:T(8,128)(2,1)} fusion(bf16[256,8,512]{0,2,1:T(8,128)(2,1)} %copy-done, s32[]{:T(128)S(6)} %select_n.44), kind=kLoop, calls=%fused_computation.37 | loop fusion | bytes 2097156 | tf_op jit(solution)/shard_map/dynamic_slice | solution.py:53
  70.9 0.5 collective-permute-start.2
  71.5 3.3 %copy.24 = bf16[256,4096]{0,1:T(8,128)(2,1)S(1)} copy(bf16[256,4096]{1,0:T(8,128)(2,1)} %param.6) | data formatting | bytes 4194304 | tf_op args[1]
  74.7 2.7 %fusion.17 = f32[8,256,512]{2,1,0:T(8,128)S(1)} fusion(bf16[8,512,256]{2,1,0:T(8,128)(2,1)} %bitcast.8, bf16[256,8,512]{0,2,1:T(8,128)(2,1)} %copy-done, s32[]{:T(128)S(6)} %select_n.37), kind=kOutput, calls=%fused_computation.23 | convolution fusion | flops 536870912 | bytes 7340036 | tf_op jit(solution)/shard_map/rki,kjr->kij/dot_general | solution.py:60
  77.4 3.7 %add_convert_fusion = bf16[8,256,512]{2,1,0:T(8,128)(2,1)} fusion(f32[8,256,512]{2,1,0:T(8,128)S(1)} %fusion.17, bf16[256,8,256]{0,2,1:T(8,128)(2,1)S(1)} %collective-permute-done.2, bf16[8,512,256]{2,1,0:T(8,128)(2,1)} %collective-permute-done.3), kind=kOutput, calls=%fused_computation.5 | convolution fusion | flops 538968064 | bytes 9437184 | tf_op jit(solution)/shard_map/rki,kjr->kij/dot_general | solution.py:61
  81.1 34.0 %all-to-all-done.1 = bf16[8,64,8,256]{3,2,1,0:T(8,128)(2,1)} async-done(((bf16[8,64,8,256]{3,2,1,0:T(8,128)(2,1)}), bf16[8,64,8,256]{3,2,1,0:T(8,128)(2,1)}, u32[]{:S(2)}, u32[]{:S(2)}) %all-to-all-start.1) | async-done | bytes 2097184 | tf_op jit(solution)/shard_map/all_to_all | solution.py:58
  115.2 1.3 %dynamic-slice_bitcast_fusion.1 = (bf16[32,4,8,256]{3,2,0,1:T(8,128)(2,1)S(1)}, bf16[32,4,8,256]{3,2,0,1:T(8,128)(2,1)S(1)}) fusion(bf16[8,64,8,256]{3,2,1,0:T(8,128)(2,1)} %all-to-all-done.1, s32[]{:T(128)S(6)} %select_n.45, s32[]{:T(128)S(6)} %add.25), kind=kLoop, calls=%fused_computation.26 | loop fusion | bytes 2097160 | tf_op jit(solution)/shard_map/transpose | solution.py:70
  116.5 0.4 fusion.8
  116.9 0.4 fusion.6
  117.3 0.1 collective-permute-start.5
  117.3 0.5 collective-permute-start.4
  117.8 1.9 %fusion.14 = f32[64,32,64]{2,1,0:T(8,128)S(1)} fusion(bf16[256,64,64]{0,2,1:T(8,128)(2,1)S(1)} %bitcast.39, bf16[8,64,8,256]{3,2,1,0:T(8,128)(2,1)} %all-to-all-done.1, s32[]{:T(128)S(6)} %select_n.46), kind=kOutput, calls=%fused_computation.19 | convolution fusion | flops 67108864 | bytes 3670020 | tf_op jit(solution)/shard_map/jkr,rjm->jkm/dot_general | solution.py:72
  119.7 0.2 collective-permute-done.4
  120.0 1.0 fusion.13
  (13 shorter events, 0.0 us)
Async XLA Ops:
  0.6 3.1 %collective-permute-start.1 = (bf16[64,32,64]{2,1,0:T(8,128)(2,1)}, bf16[64,32,64]{2,1,0:T(8,128)(2,1)S(1)}, u32[]{:S(2)}, u32[]{:S(2)}) collective-permute-start(bf16[64,32,64]{2,1,0:T(8,128)(2,1)} %param.8), channel_id=1, source_target_pairs={{0,1},{1,0},{2,3},{3,2},{4,5},{5,4},{6,7},{7,6},{8,9},{9,8},{10,11... | collective-permute-start | bytes 786440 | tf_op jit(solution)/shard_map/ppermute | solution.py:9
  1.1 2.6 %copy-start.2 = (bf16[64,32,64]{2,1,0:T(8,128)(2,1)S(1)}, bf16[64,32,64]{2,1,0:T(8,128)(2,1)}, u32[]{:S(2)}) copy-start(bf16[64,32,64]{2,1,0:T(8,128)(2,1)} %param.8) | copy-start | bytes 786436
  7.1 55.7 %all-to-all-start = ((bf16[8,8,64,256]{3,2,1,0:T(8,128)(2,1)}), bf16[8,8,64,256]{3,2,1,0:T(8,128)(2,1)S(1)}, u32[]{:S(2)}, u32[]{:S(2)}) async-start(bf16[8,8,64,256]{3,2,1,0:T(8,128)(2,1)} %bitcast.41), calls=%async_computation | async-start | bytes 4194304 | tf_op jit(solution)/shard_map/all_to_all | solution.py:38
  17.8 4.3 %copy-start.3 = (s32[8]{0:T(128)S(1)}, s32[8]{0:T(128)}, u32[]{:S(2)}) copy-start(s32[8]{0:T(128)} %param.9) | copy-start | bytes 100
  17.8 6.5 %collective-permute-start = (bf16[8,256,512]{1,2,0:T(8,128)(2,1)}, bf16[8,256,512]{1,2,0:T(8,128)(2,1)}, u32[]{:S(2)}, u32[]{:S(2)}) collective-permute-start(bf16[8,256,512]{1,2,0:T(8,128)(2,1)} %copy.17), channel_id=1, source_target_pairs={{0,1},{1,0},{2,3},{3,2},{4,5},{5,4},{6,7},{7,6},{8,9},{9,8},{10,11... | collective-permute-start | bytes 6291464 | tf_op jit(solution)/shard_map/ppermute | solution.py:9
  22.2 2.2 %copy-start.1 = (bf16[8,256,512]{1,2,0:T(8,128)(2,1)S(1)}, bf16[8,256,512]{1,2,0:T(8,128)(2,1)}, u32[]{:S(2)}) copy-start(bf16[8,256,512]{1,2,0:T(8,128)(2,1)} %copy.17) | copy-start | bytes 6291460
  24.3 2.9 %copy-start = (bf16[256,8,512]{0,2,1:T(8,128)(2,1)}, bf16[256,8,512]{0,2,1:T(8,128)(2,1)S(1)}, u32[]{:S(2)}) copy-start(bf16[256,8,512]{0,2,1:T(8,128)(2,1)S(1)} %broadcast_multiply_fusion) | copy-start | bytes 6291460
  62.8 52.4 %all-to-all-start.1 = ((bf16[8,64,8,256]{3,2,1,0:T(8,128)(2,1)}), bf16[8,64,8,256]{3,2,1,0:T(8,128)(2,1)}, u32[]{:S(2)}, u32[]{:S(2)}) async-start(bf16[8,64,8,256]{3,2,1,0:T(8,128)(2,1)} %bitcast.2), calls=%async_computation.1 | async-start | bytes 4194304 | tf_op jit(solution)/shard_map/all_to_all | solution.py:58
  68.6 8.8 %collective-permute-start.3 = (bf16[8,512,256]{2,1,0:T(8,128)(2,1)}, bf16[8,512,256]{2,1,0:T(8,128)(2,1)}, u32[]{:S(2)}, u32[]{:S(2)}) collective-permute-start(bf16[8,512,256]{2,1,0:T(8,128)(2,1)} %bitcast.8), channel_id=1, source_target_pairs={{0,1},{1,0},{2,3},{3,2},{4,5},{5,4},{6,7},{7,6},{8,9},{9,8},{10,11... | collective-permute-start | bytes 6291464 | tf_op jit(solution)/shard_map/ppermute | solution.py:56
  70.9 6.5 %collective-permute-start.2 = (bf16[256,8,256]{0,2,1:T(8,128)(2,1)}, bf16[256,8,256]{0,2,1:T(8,128)(2,1)S(1)}, u32[]{:S(2)}, u32[]{:S(2)}) collective-permute-start(bf16[256,8,256]{0,2,1:T(8,128)(2,1)} %constant_dynamic-slice_fusion), channel_id=1, source_target_pairs={{0,1},{1,0},{2,3},{3,2},{4,5},{5,4},{6,7},{7,6},{8,9},{9,8},{10,11... | collective-permute-start | bytes 3145736 | tf_op jit(solution)/shard_map/ppermute | solution.py:54
  117.3 2.5 %collective-permute-start.5 = (f32[32,32,64]{2,1,0:T(8,128)S(1)}, f32[32,32,64]{2,1,0:T(8,128)S(1)}, u32[]{:S(2)}, u32[]{:S(2)}) collective-permute-start(f32[32,32,64]{2,1,0:T(8,128)S(1)} %fusion.6), channel_id=1, source_target_pairs={{0,1},{1,0},{2,3},{3,2},{4,5},{5,4},{6,7},{7,6},{8,9},{9,8},{10,11... | collective-permute-start | bytes 786440 | tf_op jit(solution)/shard_map/ppermute | solution.py:78
  117.3 2.6 %collective-permute-start.4 = (f32[32,32,64]{2,1,0:T(8,128)S(1)}, f32[32,32,64]{2,1,0:T(8,128)S(1)}, u32[]{:S(2)}, u32[]{:S(2)}) collective-permute-start(f32[32,32,64]{2,1,0:T(8,128)S(1)} %fusion.8), channel_id=1, source_target_pairs={{0,1},{1,0},{2,3},{3,2},{4,5},{5,4},{6,7},{7,6},{8,9},{9,8},{10,11... | collective-permute-start | bytes 786440 | tf_op jit(solution)/shard_map/ppermute | solution.py:78

commit v21 on v17

--- a/solution.py
+++ b/solution.py
@@ -38,9 +38,14 @@
 
     unit_mask = (jnp.arange(block_size)[None, :] < session_units[:, None]).astype(jnp.bfloat16)
     inputs = units.reshape(row_count, local_blocks, block_size) * unit_mask[None]
-    left_full = swap_halves(left_factor, 1)
-    mixed = jnp.einsum(
-        "rki,kij->jkr", inputs, left_full, preferred_element_type=jnp.float32
+    half_rows = block_size // 2
+    core_here = lax.axis_index("bin")
+    left_other = lax.ppermute(left_factor, "bin", [(0, 1), (1, 0)])
+    own_inputs = lax.dynamic_slice_in_dim(inputs, core_here * half_rows, half_rows, axis=2)
+    other_inputs = lax.dynamic_slice_in_dim(inputs, (1 - core_here) * half_rows, half_rows, axis=2)
+    mixed = (
+        jnp.einsum("rki,kij->jkr", own_inputs, left_factor, preferred_element_type=jnp.float32)
+        + jnp.einsum("rki,kij->jkr", other_inputs, left_other, preferred_element_type=jnp.float32)
     ).astype(jnp.bfloat16)
     mixed_sent = mixed.reshape(peer_count, right_local, local_blocks, row_count)
     mixed_sent, back_got = lax.optimization_barrier((mixed_sent, back_got))

time: 121 us -> 121 us (level)
  matrix products: 13.6 us -> 17.2 us
  other arithmetic: 6.03 us -> 2.9 us
  waiting for transfers between devices: 65.7 us -> 63.4 us
  local copies, waits for them, and re-layouts: 20.8 us -> 22.7 us
    all_to_all x1, waiting for transfers between devices: 31.8 us -> 27.5 us  [on_device(): back_got = lax.all_to_all(back_sent, 'blk', 0, 0, tiled=True)]
    reshape x0 -> x1, local copies, waits for them, and re-layouts: none -> 3.94 us  [on_device(): units.reshape(row_count, local_blocks, block_size) * unit_mask[None]]
    dot_general x1 -> x2, matrix products: 1.25 us -> 4.45 us  [the longest x1 3.73 us: on_device(): jnp.einsum('rki,kij->jkr', other_inputs, left_other, preferred_element_ty...]
    select_n x2 -> x1, other arithmetic: 2.85 us -> 0.07 us  [swap_halves(): first = jnp.where(core == 0, local, other)]
    dynamic_slice x1, local copies, waits for them, and re-layouts: 2.35 us -> 0.08 us  [on_device(): lax.dynamic_slice_in_dim(inputs, (1 - core_here) * half_rows, half_rows,...]
    convert_element_type x1, local copies, waits for them, and re-layouts: 2.55 us -> 4.51 us  [on_device(): mixed = (jnp.einsum('rki,kij->jkr', own_inputs, left_factor, preferred_el...]
    all_to_all x1, waiting for transfers between devices: 33.7 us -> 35.6 us  [on_device(): mixed_got = lax.all_to_all(mixed_sent, 'blk', 0, 0, tiled=True)]
    unnamed x11 -> x10, local copies, waits for them, and re-layouts: 11.4 us -> 9.61 us
where the time goes in v21:
time: 121 us; the launch traced here: 120 us
  waiting for transfers between devices  63.4 us (52%)
  local copies, waits for them, and re-layouts  22.7 us (19%)
  matrix products  17.2 us (14%)
  starting transfers between devices  13 us (11%)
  other arithmetic  2.9 us (2%)
    all_to_all x1, waiting for transfers between devices, on_device(): mixed_got = lax.all_to_all(mixed_sent, 'blk', 0, 0, tiled=True)  35.6 us
    all_to_all x1, waiting for transfers between devices, on_device(): back_got = lax.all_to_all(back_sent, 'blk', 0, 0, tiled=True)  27.5 us
    unnamed x10, local copies, waits for them, and re-layouts  9.61 us
    all_to_all x1, starting transfers between devices, on_device(): back_got = lax.all_to_all(back_sent, 'blk', 0, 0, tiled=True)  6.83 us
    convert_element_type x1, local copies, waits for them, and re-layouts, on_device(): mixed = (jnp.einsum('rki,kij->jkr', own_inputs, left_factor, preferred_el...  4.51 us
    all_to_all x1, starting transfers between devices, on_device(): mixed_got = lax.all_to_all(mixed_sent, 'blk', 0, 0, tiled=True)  4.35 us
    dot_general x1, matrix products, on_device(): jnp.einsum('rki,kjr->kij', partner_part, partner_back, preferred_element_...  4.1 us
    reshape x1, local copies, waits for them, and re-layouts, on_device(): units.reshape(row_count, local_blocks, block_size) * unit_mask[None]  3.94 us
  transfers between devices with their start and end apart: 8, of which 3 were waited for; matrix products, arithmetic and copies ran while one was open for 29% of the time, Pallas kernels for 0%

profile of v21, /device:TPU:0, one launch (start us, length us, event | category | flops | bytes accessed | tf_op | source)
XLA Modules:
  0.0 120.0 jit_solution(13295033817424708189)
XLA Ops:
  0.6 0.5 collective-permute-start.1
  1.1 2.6 %convolution_convert_fusion = bf16[256,4096]{0,1:T(8,128)(2,1)S(1)} fusion(bf16[256,4096]{1,0:T(8,128)(2,1)} %param.6), kind=kOutput, calls=%fused_computation | convolution fusion | flops 537985024 | bytes 4194304 | tf_op jit(solution)/shard_map/rc,rs->cs/dot_general | solution.py:28
  3.8 0.1 broadcast_select_fusion.1
  3.9 0.7 convert_bitcast_fusion
  4.6 1.5 %copy.25 = bf16[8,8,64,256]{3,1,2,0:T(8,128)(2,1)} copy(bf16[8,8,64,256]{3,1,0,2:T(8,128)(2,1)S(1)} %convert_bitcast_fusion) | data formatting | bytes 4194304 | tf_op jit(solution)/shard_map/reshape | solution.py:36
  6.0 6.8 %all-to-all-start = ((bf16[8,8,64,256]{3,1,2,0:T(8,128)(2,1)}), bf16[8,8,64,256]{3,1,2,0:T(8,128)(2,1)S(1)}, u32[]{:S(2)}, u32[]{:S(2)}) async-start(bf16[8,8,64,256]{3,1,2,0:T(8,128)(2,1)} %copy.25), calls=%async_computation | async-start | bytes 4194304 | tf_op jit(solution)/shard_map/all_to_all | solution.py:37
  12.8 0.2 collective-permute-start
  13.0 4.1 %copy.22 = bf16[256,4096]{0,1:T(8,128)(2,1)} copy(bf16[256,4096]{1,0:T(8,128)(2,1)} %param.5) | data formatting | bytes 4194304 | tf_op args[0]
  17.1 3.9 %copy.23 = bf16[256,8,512]{2,0,1:T(8,128)(2,1)} copy(bf16[256,8,512]{0,2,1:T(8,128)(2,1)} %bitcast.45) | data formatting | bytes 4194304 | tf_op jit(solution)/shard_map/reshape | solution.py:40
  21.1 0.1 fusion.20
  21.1 1.7 %broadcast_multiply_fusion = bf16[256,8,512]{2,0,1:T(8,128)(2,1)S(1)} fusion(bf16[256,8,512]{2,0,1:T(8,128)(2,1)} %copy.23, bf16[8,512]{1,0:T(8,128)(2,1)S(1)} %fusion.20), kind=kLoop, calls=%fused_computation.18 | loop fusion | flops 1048576 | bytes 4202496 | tf_op jit(solution)/shard_map/mul | solution.py:40
  22.9 0.1 constant_dynamic-slice_fusion
  23.0 2.3 %copy-done.1 = bf16[8,256,512]{2,1,0:T(8,128)(2,1)S(1)} copy-done((bf16[8,256,512]{2,1,0:T(8,128)(2,1)S(1)}, bf16[8,256,512]{2,1,0:T(8,128)(2,1)}, u32[]{:S(2)}) %copy-start.1) | copy-done | bytes 2097176
  25.2 0.7 fusion.14
  26.0 3.7 %fusion = bf16[512,8,256]{0,2,1:T(8,128)(2,1)} fusion(f32[8,256,512]{2,1,0:T(8,128)S(1)} %fusion.14, bf16[256,8,256]{2,0,1:T(8,128)(2,1)S(1)} %constant_dynamic-slice_fusion, bf16[8,256,512]{2,1,0:T(8,128)(2,1)} %collective-permute-done), kind=kOutput, calls=%fused_computation.4 | convolution fusion | flops 538968064 | bytes 9437184 | tf_op jit(solution)/shard_map/rki,kij->jkr/dot_general | solution.py:48
  29.7 4.5 %copy.24 = bf16[512,8,256]{2,1,0:T(8,128)(2,1)} copy(bf16[512,8,256]{0,2,1:T(8,128)(2,1)} %fusion) | data formatting | bytes 4194304 | tf_op jit(solution)/shard_map/convert_element_type | solution.py:49
  34.2 27.5 %all-to-all-done = bf16[8,8,64,256]{3,1,2,0:T(8,128)(2,1)S(1)} async-done(((bf16[8,8,64,256]{3,1,2,0:T(8,128)(2,1)}), bf16[8,8,64,256]{3,1,2,0:T(8,128)(2,1)S(1)}, u32[]{:S(2)}, u32[]{:S(2)}) %all-to-all-start) | async-done | bytes 2097184 | tf_op jit(solution)/shard_map/all_to_all | solution.py:37
  61.7 4.3 %all-to-all-start.1 = ((bf16[8,64,8,256]{3,2,1,0:T(8,128)(2,1)}), bf16[8,64,8,256]{3,2,1,0:T(8,128)(2,1)}, u32[]{:S(2)}, u32[]{:S(2)}) async-start(bf16[8,64,8,256]{3,2,1,0:T(8,128)(2,1)} %bitcast.2), calls=%async_computation.1 | async-start | bytes 4194304 | tf_op jit(solution)/shard_map/all_to_all | solution.py:62
  66.1 1.8 %copy.26 = bf16[8,8,64,256]{3,2,1,0:T(8,128)(2,1)} copy(bf16[8,8,64,256]{3,0,2,1:T(8,128)(2,1)S(1)} %bitcast.43) | data formatting | bytes 4194304 | tf_op jit(solution)/shard_map/transpose | solution.py:59
  67.9 0.5 collective-permute-start.2
  68.4 3.3 %copy.30 = bf16[256,4096]{0,1:T(8,128)(2,1)S(1)} copy(bf16[256,4096]{1,0:T(8,128)(2,1)} %param.6) | data formatting | bytes 4194304 | tf_op args[1]
  71.7 2.7 %fusion.12 = f32[8,256,512]{2,1,0:T(8,128)S(1)} fusion(bf16[8,512,256]{2,1,0:T(8,128)(2,1)} %bitcast.8, bf16[256,8,512]{2,0,1:T(8,128)(2,1)} %copy-done, s32[]{:T(128)S(6)} %select_n.27), kind=kOutput, calls=%fused_computation.19 | convolution fusion | flops 536870912 | bytes 7340036 | tf_op jit(solution)/shard_map/rki,kjr->kij/dot_general | solution.py:64
  74.4 4.1 %add_convert_fusion = bf16[8,256,512]{2,1,0:T(8,128)(2,1)} fusion(f32[8,256,512]{2,1,0:T(8,128)S(1)} %fusion.12, bf16[256,8,256]{2,0,1:T(8,128)(2,1)} %collective-permute-done.2, bf16[8,512,256]{2,1,0:T(8,128)(2,1)} %collective-permute-done.3), kind=kOutput, calls=%fused_computation.1 | convolution fusion | flops 538968064 | bytes 9437184 | tf_op jit(solution)/shard_map/rki,kjr->kij/dot_general | solution.py:65
  78.5 35.6 %all-to-all-done.1 = bf16[8,64,8,256]{3,2,1,0:T(8,128)(2,1)} async-done(((bf16[8,64,8,256]{3,2,1,0:T(8,128)(2,1)}), bf16[8,64,8,256]{3,2,1,0:T(8,128)(2,1)}, u32[]{:S(2)}, u32[]{:S(2)}) %all-to-all-start.1) | async-done | bytes 2097184 | tf_op jit(solution)/shard_map/all_to_all | solution.py:62
  114.1 1.3 %dynamic-slice_bitcast_fusion.1 = (bf16[32,4,8,256]{3,2,0,1:T(8,128)(2,1)S(1)}, bf16[32,4,8,256]{3,2,0,1:T(8,128)(2,1)S(1)}) fusion(bf16[8,64,8,256]{3,2,1,0:T(8,128)(2,1)} %all-to-all-done.1, s32[]{:T(128)S(6)} %select_n.32, s32[]{:T(128)S(6)} %add.32), kind=kLoop, calls=%fused_computation.23 | loop fusion | bytes 2097160 | tf_op jit(solution)/shard_map/transpose | solution.py:74
  115.4 0.4 fusion.1
  115.8 0.4 fusion.3
  116.2 0.1 collective-permute-start.4
  116.3 0.5 collective-permute-start.5
  116.8 1.9 %fusion.9 = f32[64,32,64]{2,1,0:T(8,128)S(1)} fusion(bf16[256,64,64]{0,2,1:T(8,128)(2,1)S(1)} %bitcast.42, bf16[8,64,8,256]{3,2,1,0:T(8,128)(2,1)} %all-to-all-done.1, s32[]{:T(128)S(6)} %select_n.33), kind=kOutput, calls=%fused_computation.14 | convolution fusion | flops 67108864 | bytes 3670020 | tf_op jit(solution)/shard_map/jkr,rjm->jkm/dot_general | solution.py:76
  118.7 0.2 collective-permute-done.5
  118.9 1.0 fusion.8
  (13 shorter events, 0.0 us)
Async XLA Ops:
  0.6 3.1 %collective-permute-start.1 = (bf16[64,32,64]{2,1,0:T(8,128)(2,1)}, bf16[64,32,64]{2,1,0:T(8,128)(2,1)S(1)}, u32[]{:S(2)}, u32[]{:S(2)}) collective-permute-start(bf16[64,32,64]{2,1,0:T(8,128)(2,1)} %param.8), channel_id=1, source_target_pairs={{0,1},{1,0},{2,3},{3,2},{4,5},{5,4},{6,7},{7,6},{8,9},{9,8},{10,11... | collective-permute-start | bytes 786440 | tf_op jit(solution)/shard_map/ppermute | solution.py:9
  1.1 2.6 %copy-start.2 = (bf16[64,32,64]{2,1,0:T(8,128)(2,1)S(1)}, bf16[64,32,64]{2,1,0:T(8,128)(2,1)}, u32[]{:S(2)}) copy-start(bf16[64,32,64]{2,1,0:T(8,128)(2,1)} %param.8) | copy-start | bytes 786436
  6.0 55.7 %all-to-all-start = ((bf16[8,8,64,256]{3,1,2,0:T(8,128)(2,1)}), bf16[8,8,64,256]{3,1,2,0:T(8,128)(2,1)S(1)}, u32[]{:S(2)}, u32[]{:S(2)}) async-start(bf16[8,8,64,256]{3,1,2,0:T(8,128)(2,1)} %copy.25), calls=%async_computation | async-start | bytes 4194304 | tf_op jit(solution)/shard_map/all_to_all | solution.py:37
  12.8 13.1 %collective-permute-start = (bf16[8,256,512]{2,1,0:T(8,128)(2,1)}, bf16[8,256,512]{2,1,0:T(8,128)(2,1)}, u32[]{:S(2)}, u32[]{:S(2)}) collective-permute-start(bf16[8,256,512]{2,1,0:T(8,128)(2,1)} %param.7), channel_id=1, source_target_pairs={{0,1},{1,0},{2,3},{3,2},{4,5},{5,4},{6,7},{7,6},{8,9},{9,8},{10,11... | collective-permute-start | bytes 6291464 | tf_op jit(solution)/shard_map/ppermute | solution.py:43
  17.1 3.9 %copy-start.3 = (s32[8]{0:T(128)S(1)}, s32[8]{0:T(128)}, u32[]{:S(2)}) copy-start(s32[8]{0:T(128)} %param.9) | copy-start | bytes 100
  22.9 3.1 %copy-start = (bf16[256,8,512]{2,0,1:T(8,128)(2,1)}, bf16[256,8,512]{2,0,1:T(8,128)(2,1)S(1)}, u32[]{:S(2)}) copy-start(bf16[256,8,512]{2,0,1:T(8,128)(2,1)S(1)} %broadcast_multiply_fusion) | copy-start | bytes 6291460
  22.9 2.4 %copy-start.1 = (bf16[8,256,512]{2,1,0:T(8,128)(2,1)S(1)}, bf16[8,256,512]{2,1,0:T(8,128)(2,1)}, u32[]{:S(2)}) copy-start(bf16[8,256,512]{2,1,0:T(8,128)(2,1)} %param.7) | copy-start | bytes 6291460
  61.7 52.4 %all-to-all-start.1 = ((bf16[8,64,8,256]{3,2,1,0:T(8,128)(2,1)}), bf16[8,64,8,256]{3,2,1,0:T(8,128)(2,1)}, u32[]{:S(2)}, u32[]{:S(2)}) async-start(bf16[8,64,8,256]{3,2,1,0:T(8,128)(2,1)} %bitcast.2), calls=%async_computation.1 | async-start | bytes 4194304 | tf_op jit(solution)/shard_map/all_to_all | solution.py:62
  67.9 6.5 %collective-permute-start.3 = (bf16[8,512,256]{2,1,0:T(8,128)(2,1)}, bf16[8,512,256]{2,1,0:T(8,128)(2,1)}, u32[]{:S(2)}, u32[]{:S(2)}) collective-permute-start(bf16[8,512,256]{2,1,0:T(8,128)(2,1)} %bitcast.8), channel_id=1, source_target_pairs={{0,1},{1,0},{2,3},{3,2},{4,5},{5,4},{6,7},{7,6},{8,9},{9,8},{10,11... | collective-permute-start | bytes 6291464 | tf_op jit(solution)/shard_map/ppermute | solution.py:60
  67.9 6.5 %collective-permute-start.2 = (bf16[256,8,256]{2,0,1:T(8,128)(2,1)S(1)}, bf16[256,8,256]{2,0,1:T(8,128)(2,1)}, u32[]{:S(2)}, u32[]{:S(2)}) collective-permute-start(bf16[256,8,256]{2,0,1:T(8,128)(2,1)S(1)} %constant_dynamic-slice_fusion), channel_id=1, source_target_pairs={{0,1},{1,0},{2,3},{3,2},{4,5},{5,4},{6,7},{7,6},{8,9},{9,8},{10,11... | collective-permute-start | bytes 3145736 | tf_op jit(solution)/shard_map/ppermute | solution.py:58
  116.2 2.5 %collective-permute-start.4 = (f32[32,32,64]{2,1,0:T(8,128)S(1)}, f32[32,32,64]{2,1,0:T(8,128)S(1)}, u32[]{:S(2)}, u32[]{:S(2)}) collective-permute-start(f32[32,32,64]{2,1,0:T(8,128)S(1)} %fusion.3), channel_id=1, source_target_pairs={{0,1},{1,0},{2,3},{3,2},{4,5},{5,4},{6,7},{7,6},{8,9},{9,8},{10,11... | collective-permute-start | bytes 786440 | tf_op jit(solution)/shard_map/ppermute | solution.py:82
  116.3 2.6 %collective-permute-start.5 = (f32[32,32,64]{2,1,0:T(8,128)S(1)}, f32[32,32,64]{2,1,0:T(8,128)S(1)}, u32[]{:S(2)}, u32[]{:S(2)}) collective-permute-start(f32[32,32,64]{2,1,0:T(8,128)S(1)} %fusion.1), channel_id=1, source_target_pairs={{0,1},{1,0},{2,3},{3,2},{4,5},{5,4},{6,7},{7,6},{8,9},{9,8},{10,11... | collective-permute-start | bytes 786440 | tf_op jit(solution)/shard_map/ppermute | solution.py:82

commit v22 on v17

--- a/solution.py
+++ b/solution.py
@@ -71,7 +71,8 @@
         return jnp.einsum("jkr,rjm->jkm", blocks, rows, preferred_element_type=jnp.float32)
 
     half_j = right_local // 2
-    sent_right = [right_of((1 - core) * half_peers, j0, half_j) for j0 in (0, half_j)]
+    theirs_all = right_of((1 - core) * half_peers, 0, right_local)
+    sent_right = [theirs_all[:half_j], theirs_all[half_j:]]
     sent_right, mixed_got = lax.optimization_barrier((sent_right, mixed_got))
     got_right = jnp.concatenate(
         [lax.ppermute(part, "bin", [(0, 1), (1, 0)]) for part in sent_right], axis=0

time: 121 us -> 121 us (level)
    transpose x1 -> x0, local copies, waits for them, and re-layouts: 1.27 us -> none  [right_of(): blocks.transpose(1, 0, 2, 3)]
    dot_general x3 -> x2, matrix products: 2.69 us -> 3.79 us  [right_of(): jnp.einsum('jkr,rjm->jkm', blocks, rows, preferred_element_type=jnp.float32)]
where the time goes in v22:
time: 121 us; the launch traced here: 120 us
  waiting for transfers between devices  65.7 us (54%)
  local copies, waits for them, and re-layouts  19.6 us (16%)
  matrix products  14.7 us (12%)
  starting transfers between devices  13 us (11%)
  other arithmetic  6.03 us (5%)
    all_to_all x1, waiting for transfers between devices, on_device(): mixed_got = lax.all_to_all(mixed_sent, 'blk', 0, 0, tiled=True)  33.7 us
    all_to_all x1, waiting for transfers between devices, on_device(): back_got = lax.all_to_all(back_sent, 'blk', 0, 0, tiled=True)  31.8 us
    unnamed x11, local copies, waits for them, and re-layouts  11.4 us
    all_to_all x1, starting transfers between devices, on_device(): back_got = lax.all_to_all(back_sent, 'blk', 0, 0, tiled=True)  6.83 us
    all_to_all x1, starting transfers between devices, on_device(): mixed_got = lax.all_to_all(mixed_sent, 'blk', 0, 0, tiled=True)  4.34 us
    dot_general x2, matrix products, right_of(): jnp.einsum('jkr,rjm->jkm', blocks, rows, preferred_element_type=jnp.float32)  3.79 us
    dot_general x1, matrix products, on_device(): jnp.einsum('rki,kjr->kij', partner_part, partner_back, preferred_element_...  3.72 us
    select_n x2, other arithmetic, swap_halves(): first = jnp.where(core == 0, local, other)  2.85 us
  transfers between devices with their start and end apart: 8, of which 3 were waited for; matrix products, arithmetic and copies ran while one was open for 29% of the time, Pallas kernels for 0%

profile of v22, /device:TPU:0, one launch (start us, length us, event | category | flops | bytes accessed | tf_op | source)
XLA Modules:
  0.0 119.9 jit_solution(12470647865982865711)
XLA Ops:
  0.6 0.5 collective-permute-start.1
  1.1 2.6 %convolution_convert_fusion = bf16[256,4096]{0,1:T(8,128)(2,1)S(1)} fusion(bf16[256,4096]{1,0:T(8,128)(2,1)} %param.6), kind=kOutput, calls=%fused_computation | convolution fusion | flops 537985024 | bytes 4194304 | tf_op jit(solution)/shard_map/rc,rs->cs/dot_general | solution.py:28
  3.8 0.0 collective-permute-done.1
  3.8 0.1 broadcast_select_fusion.3
  3.9 0.7 convert_bitcast_fusion
  4.6 1.5 %copy.32 = bf16[8,8,64,256]{3,1,2,0:T(8,128)(2,1)} copy(bf16[8,8,64,256]{3,1,0,2:T(8,128)(2,1)S(1)} %convert_bitcast_fusion) | data formatting | bytes 4194304 | tf_op jit(solution)/shard_map/reshape | solution.py:36
  6.0 6.8 %all-to-all-start = ((bf16[8,8,64,256]{3,1,2,0:T(8,128)(2,1)}), bf16[8,8,64,256]{3,1,2,0:T(8,128)(2,1)S(1)}, u32[]{:S(2)}, u32[]{:S(2)}) async-start(bf16[8,8,64,256]{3,1,2,0:T(8,128)(2,1)} %copy.32), calls=%async_computation | async-start | bytes 4194304 | tf_op jit(solution)/shard_map/all_to_all | solution.py:37
  12.8 3.9 %copy.28 = bf16[8,256,512]{1,2,0:T(8,128)(2,1)} copy(bf16[8,256,512]{2,1,0:T(8,128)(2,1)} %param.7) | data formatting | bytes 4194304 | tf_op args[2]
  16.8 0.2 collective-permute-start
  17.0 4.1 %copy.26 = bf16[256,4096]{0,1:T(8,128)(2,1)} copy(bf16[256,4096]{1,0:T(8,128)(2,1)} %param.5) | data formatting | bytes 4194304 | tf_op args[0]
  21.1 0.1 fusion.18
  21.1 2.1 %broadcast_multiply_fusion = bf16[256,8,512]{0,2,1:T(8,128)(2,1)S(1)} fusion(bf16[256,8,512]{0,2,1:T(8,128)(2,1)} %bitcast.40, bf16[8,512]{1,0:T(8,128)(2,1)S(1)} %fusion.18), kind=kLoop, calls=%fused_computation.25 | loop fusion | flops 1048576 | bytes 4202496 | tf_op jit(solution)/shard_map/mul | solution.py:40
  23.3 0.1 copy-done.1
  23.4 2.8 %broadcast_select_fusion.1 = (bf16[8,256,512]{1,2,0:T(8,128)(2,1)S(1)}, bf16[8,256,512]{1,2,0:T(8,128)(2,1)S(1)}) fusion(bf16[8,256,512]{1,2,0:T(8,128)(2,1)S(1)} %copy-done.1, bf16[8,256,512]{1,2,0:T(8,128)(2,1)} %collective-permute-done, pred[]{:T(512)S(6)} %eq.4), kind=kLoop, calls=%fused_computation.9 | loop fusion | flops 2097152 | bytes 8388609 | tf_op jit(solution)/shard_map/jit(_where)/select_n | solution.py:11
  26.1 1.3 %convert_bitcast_fusion.1 = bf16[512,8,256]{2,0,1:T(8,128)(2,1)S(1)} fusion(bf16[256,8,512]{0,2,1:T(8,128)(2,1)S(1)} %broadcast_multiply_fusion, bf16[8,256,512]{1,2,0:T(8,128)(2,1)S(1)} %get-tuple-element.17, bf16[8,256,512]{1,2,0:T(8,128)(2,1)S(1)} %get-tuple-element.16), kind=kOutput, calls=%fused_computation.7 | convolution fusion | flops 1083179008 | bytes 8388608 | tf_op jit(solution)/shard_map/rki,kij->jkr/dot_general | solution.py:42
  27.4 2.5 %copy.31 = bf16[512,8,256]{2,1,0:T(8,128)(2,1)} copy(bf16[512,8,256]{2,0,1:T(8,128)(2,1)S(1)} %convert_bitcast_fusion.1) | data formatting | bytes 4194304 | tf_op jit(solution)/shard_map/convert_element_type | solution.py:44
  30.0 31.8 %all-to-all-done = bf16[8,8,64,256]{3,1,2,0:T(8,128)(2,1)S(1)} async-done(((bf16[8,8,64,256]{3,1,2,0:T(8,128)(2,1)}), bf16[8,8,64,256]{3,1,2,0:T(8,128)(2,1)S(1)}, u32[]{:S(2)}, u32[]{:S(2)}) %all-to-all-start) | async-done | bytes 2097184 | tf_op jit(solution)/shard_map/all_to_all | solution.py:37
  61.7 4.3 %all-to-all-start.1 = ((bf16[8,64,8,256]{3,2,1,0:T(8,128)(2,1)}), bf16[8,64,8,256]{3,2,1,0:T(8,128)(2,1)}, u32[]{:S(2)}, u32[]{:S(2)}) async-start(bf16[8,64,8,256]{3,2,1,0:T(8,128)(2,1)} %bitcast.2), calls=%async_computation.1 | async-start | bytes 4194304 | tf_op jit(solution)/shard_map/all_to_all | solution.py:57
  66.1 1.8 %copy.33 = bf16[8,8,64,256]{3,2,1,0:T(8,128)(2,1)} copy(bf16[8,8,64,256]{3,0,2,1:T(8,128)(2,1)S(1)} %bitcast.38) | data formatting | bytes 4194304 | tf_op jit(solution)/shard_map/transpose | solution.py:54
  67.9 2.4 %constant_dynamic-slice_fusion = bf16[256,8,256]{0,2,1:T(8,128)(2,1)} fusion(bf16[256,8,512]{0,2,1:T(8,128)(2,1)} %copy-done, s32[]{:T(128)S(6)} %select_n.43), kind=kLoop, calls=%fused_computation.31 | loop fusion | bytes 2097156 | tf_op jit(solution)/shard_map/dynamic_slice | solution.py:52
  70.2 0.5 collective-permute-start.2
  70.7 3.3 %copy.35 = bf16[256,4096]{0,1:T(8,128)(2,1)S(1)} copy(bf16[256,4096]{1,0:T(8,128)(2,1)} %param.6) | data formatting | bytes 4194304 | tf_op args[1]
  74.0 2.7 %fusion.16 = f32[8,256,512]{2,1,0:T(8,128)S(1)} fusion(bf16[8,512,256]{2,1,0:T(8,128)(2,1)} %bitcast.8, bf16[256,8,512]{0,2,1:T(8,128)(2,1)} %copy-done, s32[]{:T(128)S(6)} %select_n.36), kind=kOutput, calls=%fused_computation.23 | convolution fusion | flops 536870912 | bytes 7340036 | tf_op jit(solution)/shard_map/rki,kjr->kij/dot_general | solution.py:59
  76.7 3.7 %add_convert_fusion = bf16[8,256,512]{2,1,0:T(8,128)(2,1)} fusion(f32[8,256,512]{2,1,0:T(8,128)S(1)} %fusion.16, bf16[256,8,256]{0,2,1:T(8,128)(2,1)S(1)} %collective-permute-done.2, bf16[8,512,256]{2,1,0:T(8,128)(2,1)} %collective-permute-done.3), kind=kOutput, calls=%fused_computation.5 | convolution fusion | flops 538968064 | bytes 9437184 | tf_op jit(solution)/shard_map/rki,kjr->kij/dot_general | solution.py:60
  80.4 33.7 %all-to-all-done.1 = bf16[8,64,8,256]{3,2,1,0:T(8,128)(2,1)} async-done(((bf16[8,64,8,256]{3,2,1,0:T(8,128)(2,1)}), bf16[8,64,8,256]{3,2,1,0:T(8,128)(2,1)}, u32[]{:S(2)}, u32[]{:S(2)}) %all-to-all-start.1) | async-done | bytes 2097184 | tf_op jit(solution)/shard_map/all_to_all | solution.py:57
  114.1 1.9 %fusion.12 = f32[64,32,64]{2,1,0:T(8,128)S(1)} fusion(bf16[256,64,64]{0,2,1:T(8,128)(2,1)S(1)} %bitcast.36, bf16[8,64,8,256]{3,2,1,0:T(8,128)(2,1)} %all-to-all-done.1, s32[]{:T(128)S(6)} %select_n.44), kind=kOutput, calls=%fused_computation.17 | convolution fusion | flops 67108864 | bytes 3670020 | tf_op jit(solution)/shard_map/jkr,rjm->jkm/dot_general | solution.py:71
  116.0 0.1 fusion.22
  116.1 0.1 collective-permute-start.5
  116.2 0.5 collective-permute-start.4
  116.7 1.9 %fusion.10 = f32[64,32,64]{2,1,0:T(8,128)S(1)} fusion(bf16[256,64,64]{0,2,1:T(8,128)(2,1)S(1)} %bitcast.37, bf16[8,64,8,256]{3,2,1,0:T(8,128)(2,1)} %all-to-all-done.1, s32[]{:T(128)S(6)} %select_n.45), kind=kOutput, calls=%fused_computation.15 | convolution fusion | flops 67108864 | bytes 3670020 | tf_op jit(solution)/shard_map/jkr,rjm->jkm/dot_general | solution.py:71
  118.6 0.2 collective-permute-done.4
  118.8 1.0 fusion.9
  (12 shorter events, 0.0 us)
Async XLA Ops:
  0.6 3.1 %collective-permute-start.1 = (bf16[64,32,64]{2,1,0:T(8,128)(2,1)}, bf16[64,32,64]{2,1,0:T(8,128)(2,1)S(1)}, u32[]{:S(2)}, u32[]{:S(2)}) collective-permute-start(bf16[64,32,64]{2,1,0:T(8,128)(2,1)} %param.8), channel_id=1, source_target_pairs={{0,1},{1,0},{2,3},{3,2},{4,5},{5,4},{6,7},{7,6},{8,9},{9,8},{10,11... | collective-permute-start | bytes 786440 | tf_op jit(solution)/shard_map/ppermute | solution.py:9
  1.1 2.6 %copy-start.2 = (bf16[64,32,64]{2,1,0:T(8,128)(2,1)S(1)}, bf16[64,32,64]{2,1,0:T(8,128)(2,1)}, u32[]{:S(2)}) copy-start(bf16[64,32,64]{2,1,0:T(8,128)(2,1)} %param.8) | copy-start | bytes 786436
  6.0 55.7 %all-to-all-start = ((bf16[8,8,64,256]{3,1,2,0:T(8,128)(2,1)}), bf16[8,8,64,256]{3,1,2,0:T(8,128)(2,1)S(1)}, u32[]{:S(2)}, u32[]{:S(2)}) async-start(bf16[8,8,64,256]{3,1,2,0:T(8,128)(2,1)} %copy.32), calls=%async_computation | async-start | bytes 4194304 | tf_op jit(solution)/shard_map/all_to_all | solution.py:37
  16.8 4.3 %copy-start.3 = (s32[8]{0:T(128)S(1)}, s32[8]{0:T(128)}, u32[]{:S(2)}) copy-start(s32[8]{0:T(128)} %param.9) | copy-start | bytes 100
  16.8 6.5 %collective-permute-start = (bf16[8,256,512]{1,2,0:T(8,128)(2,1)}, bf16[8,256,512]{1,2,0:T(8,128)(2,1)}, u32[]{:S(2)}, u32[]{:S(2)}) collective-permute-start(bf16[8,256,512]{1,2,0:T(8,128)(2,1)} %copy.28), channel_id=1, source_target_pairs={{0,1},{1,0},{2,3},{3,2},{4,5},{5,4},{6,7},{7,6},{8,9},{9,8},{10,11... | collective-permute-start | bytes 6291464 | tf_op jit(solution)/shard_map/ppermute | solution.py:9
  21.1 2.2 %copy-start.1 = (bf16[8,256,512]{1,2,0:T(8,128)(2,1)S(1)}, bf16[8,256,512]{1,2,0:T(8,128)(2,1)}, u32[]{:S(2)}) copy-start(bf16[8,256,512]{1,2,0:T(8,128)(2,1)} %copy.28) | copy-start | bytes 6291460
  23.2 2.9 %copy-start = (bf16[256,8,512]{0,2,1:T(8,128)(2,1)}, bf16[256,8,512]{0,2,1:T(8,128)(2,1)S(1)}, u32[]{:S(2)}) copy-start(bf16[256,8,512]{0,2,1:T(8,128)(2,1)S(1)} %broadcast_multiply_fusion) | copy-start | bytes 6291460
  61.7 52.4 %all-to-all-start.1 = ((bf16[8,64,8,256]{3,2,1,0:T(8,128)(2,1)}), bf16[8,64,8,256]{3,2,1,0:T(8,128)(2,1)}, u32[]{:S(2)}, u32[]{:S(2)}) async-start(bf16[8,64,8,256]{3,2,1,0:T(8,128)(2,1)} %bitcast.2), calls=%async_computation.1 | async-start | bytes 4194304 | tf_op jit(solution)/shard_map/all_to_all | solution.py:57
  67.9 8.8 %collective-permute-start.3 = (bf16[8,512,256]{2,1,0:T(8,128)(2,1)}, bf16[8,512,256]{2,1,0:T(8,128)(2,1)}, u32[]{:S(2)}, u32[]{:S(2)}) collective-permute-start(bf16[8,512,256]{2,1,0:T(8,128)(2,1)} %bitcast.8), channel_id=1, source_target_pairs={{0,1},{1,0},{2,3},{3,2},{4,5},{5,4},{6,7},{7,6},{8,9},{9,8},{10,11... | collective-permute-start | bytes 6291464 | tf_op jit(solution)/shard_map/ppermute | solution.py:55
  70.2 6.5 %collective-permute-start.2 = (bf16[256,8,256]{0,2,1:T(8,128)(2,1)}, bf16[256,8,256]{0,2,1:T(8,128)(2,1)S(1)}, u32[]{:S(2)}, u32[]{:S(2)}) collective-permute-start(bf16[256,8,256]{0,2,1:T(8,128)(2,1)} %constant_dynamic-slice_fusion), channel_id=1, source_target_pairs={{0,1},{1,0},{2,3},{3,2},{4,5},{5,4},{6,7},{7,6},{8,9},{9,8},{10,11... | collective-permute-start | bytes 3145736 | tf_op jit(solution)/shard_map/ppermute | solution.py:53
  116.1 2.5 %collective-permute-start.5 = (f32[32,32,64]{2,1,0:T(8,128)S(1)}, f32[32,32,64]{2,1,0:T(8,128)S(1)}, u32[]{:S(2)}, u32[]{:S(2)}) collective-permute-start(f32[32,32,64]{2,1,0:T(8,128)S(1)} %get-tuple-element.15), channel_id=1, source_target_pairs={{0,1},{1,0},{2,3},{3,2},{4,5},{5,4},{6,7},{7,6},{8,9},{9,8},{10,11... | collective-permute-start | bytes 786440 | tf_op jit(solution)/shard_map/ppermute | solution.py:78
  116.2 2.6 %collective-permute-start.4 = (f32[32,32,64]{2,1,0:T(8,128)S(1)}, f32[32,32,64]{2,1,0:T(8,128)S(1)}, u32[]{:S(2)}, u32[]{:S(2)}) collective-permute-start(f32[32,32,64]{2,1,0:T(8,128)S(1)} %get-tuple-element.14), channel_id=1, source_target_pairs={{0,1},{1,0},{2,3},{3,2},{4,5},{5,4},{6,7},{7,6},{8,9},{9,8},{10,11... | collective-permute-start | bytes 786440 | tf_op jit(solution)/shard_map/ppermute | solution.py:78
